TPU v7x, 256 devices: a whole 4x4x8 slice. The times are simulated.
256 devices in a mesh: ctx: 32 (over x, y, core), head: 8 (over z).
Axes of the slice: x: 4, y: 4, z: 8, core: 2. Of those that a mesh axis runs over, the one named last changes fastest.
Arguments:
- query_rows: bfloat16 [32, 32768, 128], P('head', 'ctx'), parts along dimension 0, may hold values from -1.75 to 1.75
- key_rows: bfloat16 [32, 32768, 128], P('head', 'ctx'), parts along dimension 0, may hold values from -1.75 to 1.75
- value_rows: bfloat16 [32, 32768, 128], P('head', 'ctx'), parts along dimension 0, may hold values from -6 to 6
- out_grad: bfloat16 [32, 32768, 128], P('head', 'ctx'), parts along dimension 0, may hold values from -6 to 6
- level_gate: float32 [16, 32, 32768], P(None, 'head', 'ctx'), parts along dimension 1, may hold values from -12 to 1
- block_levels: int32 [32, 32], replicated, may hold values from -1 to 15, as said below
Outputs:
- attn_out: bfloat16 [32, 32768, 128], P('head', 'ctx'), parts along dimension 0
- grad_query: bfloat16 [32, 32768, 128], P('head', 'ctx'), parts along dimension 0
- grad_key: bfloat16 [32, 32768, 128], P('head', 'ctx'), parts along dimension 0
- grad_value: bfloat16 [32, 32768, 128], P('head', 'ctx'), parts along dimension 0
- grad_gate: float32 [16, 32, 32768], P(None, 'head', 'ctx'), parts along dimension 1
There are 8 independent parts, one for each index of `head`. A program takes and returns all parts, laid end to end along the dimension named above; an argument that names none is the same for every part. Nothing has to cross between parts.
Inputs may be any that keep to these rules, and one draw needn't show every extreme that they name: The sequence packs documents made of whole blocks; block 0 starts one. block_levels[c, c'] = 10 plus the bit length of (c xor c') where c' < c and both blocks lie in one document, else -1.
All inputs are finite; a program needn't handle non-finite values.
Results may differ from a plain program's by a relative error of at most 0.011.
Values may be sent and summed in bfloat16 or wider, within the bound.
No kernel may reach another device: no remote copies, remote signals or barrier semaphores. Data moves between devices by JAX's collectives and lax.ppermute only.
A program may use at most 128 MiB of HBM per device.

v0:
```python
import jax
import jax.numpy as jnp
from jax import lax
from jax.sharding import PartitionSpec as P


def bit_length(numbers, count):
    total = jnp.zeros(numbers.shape, jnp.int32)
    for shift_by in range(count):
        total = total + (jnp.right_shift(numbers, shift_by) > 0).astype(jnp.int32)
    return total


def head_local(inputs, log_block):
    query_h, key_h, value_h, grad_h, weight_h = inputs
    block_len = query_h.shape[0]
    tile_len = min(64, block_len)
    tile_count = block_len // tile_len
    log_tile = tile_len.bit_length() - 1
    positions = jnp.arange(block_len, dtype=jnp.int32)
    row_tile = positions // tile_len
    row_inner = positions % tile_len
    col_inner = jnp.arange(tile_len, dtype=jnp.int32)
    col_tile = jnp.arange(tile_count, dtype=jnp.int32)
    diag_level = jnp.where(
        col_inner[None, :] <= row_inner[:, None],
        bit_length(jnp.bitwise_xor(row_inner[:, None], col_inner[None, :]), log_tile),
        -1,
    )
    tile_level = jnp.where(
        col_tile[None, :] < row_tile[:, None],
        log_tile
        + bit_length(jnp.bitwise_xor(row_tile[:, None], col_tile[None, :]), log_block - log_tile),
        -1,
    )
    diag_weight = jnp.zeros((block_len, tile_len), jnp.float32)
    for level_num in range(log_tile + 1):
        diag_weight = jnp.where(diag_level == level_num, weight_h[level_num][:, None], diag_weight)
    tile_weight = jnp.zeros((block_len, tile_count), jnp.float32)
    for level_num in range(log_tile + 1, log_block + 1):
        tile_weight = jnp.where(tile_level == level_num, weight_h[level_num][:, None], tile_weight)
    same_tile = row_tile[:, None] == col_tile[None, :]
    mask_weight = jnp.where(
        same_tile[:, :, None], diag_weight[:, None, :], tile_weight[:, :, None]
    ).reshape(block_len, block_len)
    scores = jnp.einsum("td,sd->ts", query_h, key_h, preferred_element_type=jnp.float32)
    probs = (mask_weight * scores).astype(jnp.bfloat16)
    back = jnp.einsum("te,se->ts", grad_h, value_h, preferred_element_type=jnp.float32)
    dprobs = (mask_weight * back).astype(jnp.bfloat16)
    out_inner = jnp.dot(probs, value_h, preferred_element_type=jnp.float32)
    dq_inner = jnp.dot(dprobs, key_h, preferred_element_type=jnp.float32)
    dk_inner = jnp.einsum("ts,td->sd", dprobs, query_h, preferred_element_type=jnp.float32)
    dv_inner = jnp.einsum("ts,te->se", probs, grad_h, preferred_element_type=jnp.float32)
    product = (scores * back).reshape(block_len, tile_count, tile_len)
    tile_sums = jnp.sum(product, axis=2)
    diag_sums = jnp.sum(jnp.where(same_tile[:, :, None], product, jnp.float32(0.0)), axis=1)
    level_terms = []
    for level_num in range(log_block + 1):
        if level_num <= log_tile:
            level_terms.append(
                jnp.sum(jnp.where(diag_level == level_num, diag_sums, jnp.float32(0.0)), axis=1)
            )
        else:
            level_terms.append(
                jnp.sum(jnp.where(tile_level == level_num, tile_sums, jnp.float32(0.0)), axis=1)
            )
    return (out_inner, dq_inner, dk_inner, dv_inner, jnp.stack(level_terms))


def per_device(query_rows, key_rows, value_rows, out_grad, level_gate, block_levels):
    level_total = level_gate.shape[0]
    block_len = query_rows.shape[1]
    log_block = block_len.bit_length() - 1
    log_ctx = level_total - log_block - 1
    stretch_place = lax.axis_index("ctx")
    weights = jnp.exp(level_gate)
    inner_weight = weights[: log_block + 1]
    cross_weight = weights[log_block + 1 :]

    def run_head(inputs):
        return head_local(inputs, log_block)

    local_parts = lax.map(
        run_head, (query_rows, key_rows, value_rows, out_grad, inner_weight.transpose(1, 0, 2))
    )
    out_inner, dq_inner, dk_inner, dv_inner, grad_inner = local_parts
    own_state = jnp.einsum(
        "hcd,hce->hde", key_rows, value_rows, preferred_element_type=jnp.float32
    ).astype(jnp.bfloat16)
    scaled = (cross_weight[..., None] * out_grad[None].astype(jnp.float32)).astype(jnp.bfloat16)
    grad_state = jnp.einsum(
        "hcd,bhce->bhde", query_rows, scaled, preferred_element_type=jnp.float32
    ).astype(jnp.bfloat16)
    levels_row = lax.dynamic_index_in_dim(block_levels, stretch_place, 0, keepdims=False)
    cross_ids = log_block + 1 + jnp.arange(log_ctx, dtype=jnp.int32)
    got = levels_row
    match = got[None, :] == cross_ids[:, None]
    level_sum = jnp.sum(
        jnp.where(
            match[:, :, None, None, None],
            lax.all_gather(own_state[None], "ctx", axis=0, tiled=True)[None].astype(jnp.float32),
            jnp.float32(0.0),
        ),
        axis=1,
    )
    got = levels_row
    match = got[:, None] == cross_ids[None, :]
    key_sum = lax.psum_scatter(
        jnp.sum(
            jnp.where(
                match[:, :, None, None, None],
                grad_state[None].astype(jnp.float32),
                jnp.float32(0.0),
            ),
            axis=1,
        ).astype(jnp.bfloat16),
        "ctx",
        scatter_dimension=0,
        tiled=True,
    ).astype(jnp.float32)[0]
    level_state = level_sum.astype(jnp.bfloat16)
    level_out = jnp.einsum(
        "hcd,bhde->bhce", query_rows, level_state, preferred_element_type=jnp.float32
    )
    level_back = jnp.einsum(
        "hce,bhde->bhcd", out_grad, level_state, preferred_element_type=jnp.float32
    )
    attn = out_inner + jnp.sum(cross_weight[..., None] * level_out, axis=0)
    grad_q = dq_inner + jnp.sum(cross_weight[..., None] * level_back, axis=0)
    grad_cross = cross_weight * jnp.sum(level_out * out_grad[None].astype(jnp.float32), axis=3)
    grad_gate = jnp.concatenate([inner_weight * grad_inner.transpose(1, 0, 2), grad_cross], axis=0)
    key_state = key_sum.astype(jnp.bfloat16)
    grad_k = (
        dk_inner
        + jnp.einsum("hde,hce->hcd", key_state, value_rows, preferred_element_type=jnp.float32)
    ).astype(jnp.bfloat16)
    grad_v = (
        dv_inner
        + jnp.einsum("hde,hcd->hce", key_state, key_rows, preferred_element_type=jnp.float32)
    ).astype(jnp.bfloat16)
    return (attn.astype(jnp.bfloat16), grad_q.astype(jnp.bfloat16), grad_k, grad_v, grad_gate)


def solution(mesh):
    in_specs = (
        P("head", "ctx", None),
        P("head", "ctx", None),
        P("head", "ctx", None),
        P("head", "ctx", None),
        P(None, "head", "ctx"),
        P(),
    )
    out_specs = (
        P("head", "ctx", None),
        P("head", "ctx", None),
        P("head", "ctx", None),
        P("head", "ctx", None),
        P(None, "head", "ctx"),
    )
    return jax.shard_map(
        per_device, mesh=mesh, in_specs=in_specs, out_specs=out_specs, check_vma=False
    )
```

profile of v0, /device:TPU:4, one launch (start us, length us, event | category | flops | bytes accessed | tf_op | source)
XLA Modules:
  0.0 201.9 jit_solution(14055313027224400831)
XLA Ops:
  8.4 1.5 copy.44
  10.0 1.3 copy-done.8
  11.3 3.8 %fusion.47 = f32[5,4,128,128]{2,3,0,1:T(8,128)} fusion(f32[4,1024,128]{1,2,0:T(8,128)S(1)} %copy.44, f32[5,4,1024]{2,0,1:T(8,128)S(1)} %slice.86, bf16[4,1024,128]{2,1,0:T(8,128)(2,1)} %param.8), kind=kOutput, calls=%fused_computation.123 | convolution fusion | flops 676986880 | bytes 4538368 | tf_op jit(solution)/shard_map/hcd,bhce->bhde/dot_general | solution.py:91
  15.1 1.7 copy.45
  16.9 10.4 %select_reduce_fusion.12 = bf16[32,4,128,128]{3,2,1,0:T(8,128)(2,1)} fusion(f32[5,4,128,128]{3,2,1,0:T(8,128)S(1)} %copy.45, pred[32,5]{1,0:T(8,128)(4,1)S(1)} %broadcast_compare_fusion.11), kind=kLoop, calls=%fused_computation.103 | loop fusion | flops 18874368 | bytes 5505184 | tf_op jit(solution)/shard_map/reduce_sum | solution.py:109
  30.1 95.7 %while.20 = (s32[]{:T(128)}, f32[4,1024,128]{1,2,0:T(8,128)}, f32[4,1024,128]{1,2,0:T(8,128)}, f32[4,1024,128]{1,2,0:T(8,128)}, f32[4,1024,128]{1,2,0:T(8,128)},...) while((s32[]{:T(128)}, f32[4,1024,128]{1,2,0:T(8,128)}, ...), condition=%wide.region_14.15_spmd, body=%wide.region_0.14_spmd.sunk | while | flops 1626260480 | bytes 108104296 | solution.py:83
  30.2 1.8 fusion.91
  31.9 5.1 %bitcast_reduce_fusion.2 = (f32[1024,16]{0,1:T(8,128)S(1)}, f32[1024,1024]{0,1:T(8,128)}, f32[1024,1024]{0,1:T(8,128)}) fusion(f32[1024,1024]{0,1:T(8,128)S(1)} %fusion.91, bf16[4,1024,128]{2,1,0:T(8,128)(2,1)S(1)} %get-tuple-element.423, s32[]{:T(128)S(6)} %copy.91, bf16[4,1024,128]{2,1,0:T(8,128)(2,1)} %get-tuple-element.422), kind=kOutput, calls=%fused_computation.clone.1 | convolution fusion | flops 270516224 | bytes 13173760 | tf_op jit(solution)/shard_map/while/body/eval_jaxpr/td,sd->ts/dot_general | solution.py:46
  38.2 3.1 %select_reduce_fusion.18 = (f32[1024,64]{0,1:T(8,128)S(1)}, f32[1024,16,64]{0,2,1:T(8,128)S(1)}) fusion(f32[1024,16,64]{0,2,1:T(8,128)} %bitcast.218, pred[1024,16]{0,1:T(8,128)(4,1)S(1)} %iota_compare_fusion.4, f32[1024,16]{0,1:T(8,128)S(1)} %get-tuple-element.344, f32[1024,64]{0,1:T(8,128)S(1)} %select_select_fusion.3), kind=kLoop, calls=%fused_computation.5.clone.1 | loop fusion | flops 3080192 | bytes 8994816 | tf_op jit(solution)/shard_map/while/body/eval_jaxpr/reduce_sum | solution.py:56
  41.7 1.3 copy-done.4
  43.1 1.8 fusion.93
  44.9 1.3 fusion.94
  46.2 1.3 fusion.95
  47.6 2.6 %fusion.96 = f32[4,1024,128]{1,2,0:T(8,128)} fusion(f32[4,1024,128]{1,2,0:T(8,128)} %get-tuple-element.395, s32[]{:T(128)S(6)} %copy.91, bf16[1024,1024]{0,1:T(8,128)(2,1)S(1)} %get-tuple-element.356, bf16[4,1024,128]{2,1,0:T(8,128)(2,1)} %get-tuple-element.422), kind=kOutput, calls=%fused_computation.10.clone.1 | convolution fusion | flops 268435456 | bytes 2884608 | tf_op jit(solution)/shard_map/while/body/eval_jaxpr/ts,td->sd/dot_general | solution.py:52
  50.2 2.7 %fusion.97 = f32[4,1024,128]{1,2,0:T(8,128)} fusion(f32[4,1024,128]{1,2,0:T(8,128)} %get-tuple-element.396, s32[]{:T(128)S(6)} %copy.91, bf16[1024,1024]{0,1:T(8,128)(2,1)S(1)} %get-tuple-element.355, bf16[4,1024,128]{2,1,0:T(8,128)(2,1)} %get-tuple-element.425), kind=kOutput, calls=%fused_computation.8.clone.1 | convolution fusion | flops 268435456 | bytes 2884608 | tf_op jit(solution)/shard_map/while/body/eval_jaxpr/ts,te->se/dot_general | solution.py:53
  54.1 1.8 fusion.91
  55.9 5.1 %bitcast_reduce_fusion.2 = (f32[1024,16]{0,1:T(8,128)S(1)}, f32[1024,1024]{0,1:T(8,128)}, f32[1024,1024]{0,1:T(8,128)}) fusion(f32[1024,1024]{0,1:T(8,128)S(1)} %fusion.91, bf16[4,1024,128]{2,1,0:T(8,128)(2,1)S(1)} %get-tuple-element.423, s32[]{:T(128)S(6)} %copy.91, bf16[4,1024,128]{2,1,0:T(8,128)(2,1)} %get-tuple-element.422), kind=kOutput, calls=%fused_computation.clone.1 | convolution fusion | flops 270516224 | bytes 13173760 | tf_op jit(solution)/shard_map/while/body/eval_jaxpr/td,sd->ts/dot_general | solution.py:46
  62.2 3.2 %select_reduce_fusion.18 = (f32[1024,64]{0,1:T(8,128)S(1)}, f32[1024,16,64]{0,2,1:T(8,128)S(1)}) fusion(f32[1024,16,64]{0,2,1:T(8,128)} %bitcast.218, pred[1024,16]{0,1:T(8,128)(4,1)S(1)} %iota_compare_fusion.4, f32[1024,16]{0,1:T(8,128)S(1)} %get-tuple-element.344, f32[1024,64]{0,1:T(8,128)S(1)} %select_select_fusion.3), kind=kLoop, calls=%fused_computation.5.clone.1 | loop fusion | flops 3080192 | bytes 8994816 | tf_op jit(solution)/shard_map/while/body/eval_jaxpr/reduce_sum | solution.py:56
  65.8 1.4 copy-done.4
  67.2 1.8 fusion.93
  69.1 1.3 fusion.94
  70.4 1.4 fusion.95
  71.8 2.6 %fusion.96 = f32[4,1024,128]{1,2,0:T(8,128)} fusion(f32[4,1024,128]{1,2,0:T(8,128)} %get-tuple-element.395, s32[]{:T(128)S(6)} %copy.91, bf16[1024,1024]{0,1:T(8,128)(2,1)S(1)} %get-tuple-element.356, bf16[4,1024,128]{2,1,0:T(8,128)(2,1)} %get-tuple-element.422), kind=kOutput, calls=%fused_computation.10.clone.1 | convolution fusion | flops 268435456 | bytes 2884608 | tf_op jit(solution)/shard_map/while/body/eval_jaxpr/ts,td->sd/dot_general | solution.py:52
  74.4 2.7 %fusion.97 = f32[4,1024,128]{1,2,0:T(8,128)} fusion(f32[4,1024,128]{1,2,0:T(8,128)} %get-tuple-element.396, s32[]{:T(128)S(6)} %copy.91, bf16[1024,1024]{0,1:T(8,128)(2,1)S(1)} %get-tuple-element.355, bf16[4,1024,128]{2,1,0:T(8,128)(2,1)} %get-tuple-element.425), kind=kOutput, calls=%fused_computation.8.clone.1 | convolution fusion | flops 268435456 | bytes 2884608 | tf_op jit(solution)/shard_map/while/body/eval_jaxpr/ts,te->se/dot_general | solution.py:53
  78.3 1.7 fusion.91
  80.0 5.1 %bitcast_reduce_fusion.2 = (f32[1024,16]{0,1:T(8,128)S(1)}, f32[1024,1024]{0,1:T(8,128)}, f32[1024,1024]{0,1:T(8,128)}) fusion(f32[1024,1024]{0,1:T(8,128)S(1)} %fusion.91, bf16[4,1024,128]{2,1,0:T(8,128)(2,1)S(1)} %get-tuple-element.423, s32[]{:T(128)S(6)} %copy.91, bf16[4,1024,128]{2,1,0:T(8,128)(2,1)} %get-tuple-element.422), kind=kOutput, calls=%fused_computation.clone.1 | convolution fusion | flops 270516224 | bytes 13173760 | tf_op jit(solution)/shard_map/while/body/eval_jaxpr/td,sd->ts/dot_general | solution.py:46
  86.3 3.2 %select_reduce_fusion.18 = (f32[1024,64]{0,1:T(8,128)S(1)}, f32[1024,16,64]{0,2,1:T(8,128)S(1)}) fusion(f32[1024,16,64]{0,2,1:T(8,128)} %bitcast.218, pred[1024,16]{0,1:T(8,128)(4,1)S(1)} %iota_compare_fusion.4, f32[1024,16]{0,1:T(8,128)S(1)} %get-tuple-element.344, f32[1024,64]{0,1:T(8,128)S(1)} %select_select_fusion.3), kind=kLoop, calls=%fused_computation.5.clone.1 | loop fusion | flops 3080192 | bytes 8994816 | tf_op jit(solution)/shard_map/while/body/eval_jaxpr/reduce_sum | solution.py:56
  89.9 1.3 copy-done.4
  91.3 1.8 fusion.93
  95.7 2.6 %fusion.96 = f32[4,1024,128]{1,2,0:T(8,128)} fusion(f32[4,1024,128]{1,2,0:T(8,128)} %get-tuple-element.395, s32[]{:T(128)S(6)} %copy.91, bf16[1024,1024]{0,1:T(8,128)(2,1)S(1)} %get-tuple-element.356, bf16[4,1024,128]{2,1,0:T(8,128)(2,1)} %get-tuple-element.422), kind=kOutput, calls=%fused_computation.10.clone.1 | convolution fusion | flops 268435456 | bytes 2884608 | tf_op jit(solution)/shard_map/while/body/eval_jaxpr/ts,td->sd/dot_general | solution.py:52
  98.3 2.6 %fusion.97 = f32[4,1024,128]{1,2,0:T(8,128)} fusion(f32[4,1024,128]{1,2,0:T(8,128)} %get-tuple-element.396, s32[]{:T(128)S(6)} %copy.91, bf16[1024,1024]{0,1:T(8,128)(2,1)S(1)} %get-tuple-element.355, bf16[4,1024,128]{2,1,0:T(8,128)(2,1)} %get-tuple-element.425), kind=kOutput, calls=%fused_computation.8.clone.1 | convolution fusion | flops 268435456 | bytes 2884608 | tf_op jit(solution)/shard_map/while/body/eval_jaxpr/ts,te->se/dot_general | solution.py:53
  102.1 1.7 fusion.91
  103.9 5.1 %bitcast_reduce_fusion.2 = (f32[1024,16]{0,1:T(8,128)S(1)}, f32[1024,1024]{0,1:T(8,128)}, f32[1024,1024]{0,1:T(8,128)}) fusion(f32[1024,1024]{0,1:T(8,128)S(1)} %fusion.91, bf16[4,1024,128]{2,1,0:T(8,128)(2,1)S(1)} %get-tuple-element.423, s32[]{:T(128)S(6)} %copy.91, bf16[4,1024,128]{2,1,0:T(8,128)(2,1)} %get-tuple-element.422), kind=kOutput, calls=%fused_computation.clone.1 | convolution fusion | flops 270516224 | bytes 13173760 | tf_op jit(solution)/shard_map/while/body/eval_jaxpr/td,sd->ts/dot_general | solution.py:46
  110.2 3.1 %select_reduce_fusion.18 = (f32[1024,64]{0,1:T(8,128)S(1)}, f32[1024,16,64]{0,2,1:T(8,128)S(1)}) fusion(f32[1024,16,64]{0,2,1:T(8,128)} %bitcast.218, pred[1024,16]{0,1:T(8,128)(4,1)S(1)} %iota_compare_fusion.4, f32[1024,16]{0,1:T(8,128)S(1)} %get-tuple-element.344, f32[1024,64]{0,1:T(8,128)S(1)} %select_select_fusion.3), kind=kLoop, calls=%fused_computation.5.clone.1 | loop fusion | flops 3080192 | bytes 8994816 | tf_op jit(solution)/shard_map/while/body/eval_jaxpr/reduce_sum | solution.py:56
  114.9 1.8 fusion.93
  116.8 1.3 fusion.94
  119.4 2.6 %fusion.96 = f32[4,1024,128]{1,2,0:T(8,128)} fusion(f32[4,1024,128]{1,2,0:T(8,128)} %get-tuple-element.395, s32[]{:T(128)S(6)} %copy.91, bf16[1024,1024]{0,1:T(8,128)(2,1)S(1)} %get-tuple-element.356, bf16[4,1024,128]{2,1,0:T(8,128)(2,1)} %get-tuple-element.422), kind=kOutput, calls=%fused_computation.10.clone.1 | convolution fusion | flops 268435456 | bytes 2884608 | tf_op jit(solution)/shard_map/while/body/eval_jaxpr/ts,td->sd/dot_general | solution.py:52
  122.0 2.6 %fusion.97 = f32[4,1024,128]{1,2,0:T(8,128)} fusion(f32[4,1024,128]{1,2,0:T(8,128)} %get-tuple-element.396, s32[]{:T(128)S(6)} %copy.91, bf16[1024,1024]{0,1:T(8,128)(2,1)S(1)} %get-tuple-element.355, bf16[4,1024,128]{2,1,0:T(8,128)(2,1)} %get-tuple-element.425), kind=kOutput, calls=%fused_computation.8.clone.1 | convolution fusion | flops 268435456 | bytes 2884608 | tf_op jit(solution)/shard_map/while/body/eval_jaxpr/ts,te->se/dot_general | solution.py:53
  126.6 1.7 bitcast_multiply_fusion.5
  128.3 2.1 %fusion.44 = bf16[4,1024,128]{1,2,0:T(8,128)(2,1)S(1)} fusion(f32[4,1024,128]{1,2,0:T(8,128)} %get-tuple-element.151, bf16[4,1024,128]{2,1,0:T(8,128)(2,1)S(1)} %get-tuple-element.440, bf16[1,4,128,128]{3,2,1,0:T(8,128)(2,1)} %reduce-scatter.2.cloned.1.call-done), kind=kOutput, calls=%fused_computation.118 | convolution fusion | flops 135266304 | bytes 4325376 | tf_op jit(solution)/shard_map/hde,hce->hcd/dot_general | solution.py:135
  131.7 2.1 %fusion.43 = bf16[4,1024,128]{1,2,0:T(8,128)(2,1)S(1)} fusion(f32[4,1024,128]{1,2,0:T(8,128)} %get-tuple-element.152, bf16[4,1024,128]{2,1,0:T(8,128)(2,1)S(1)} %get-tuple-element.441, bf16[1,4,128,128]{3,2,1,0:T(8,128)(2,1)S(1)} %copy-done.13), kind=kOutput, calls=%fused_computation.116 | convolution fusion | flops 135266304 | bytes 4325376 | tf_op jit(solution)/shard_map/hde,hcd->hce/dot_general | solution.py:139
  135.1 38.1 %all-gather.3.cloned.1.call-done = bf16[128,128,128]{2,1,0:T(8,128)(2,1)} async-done(((bf16[4,128,128]{2,1,0:T(8,128)(2,1)}), bf16[128,128,128]{2,1,0:T(8,128)(2,1)}) %all-gather.3.cloned.1.call-update) | async-done | bytes 4194320 | tf_op jit(solution)/shard_map/all_gather | solution.py:101
  173.2 3.3 %bitcast_convert_fusion = f32[32,4,128,128]{3,2,1,0:T(8,128)S(1)} fusion(bf16[128,128,128]{2,1,0:T(8,128)(2,1)} %all-gather.3.cloned.1.call-done), kind=kLoop, calls=%fused_computation.141 | loop fusion | flops 2097152 | bytes 12582912 | tf_op jit(solution)/shard_map/convert_element_type | solution.py:101
  176.4 5.7 %select_reduce_fusion.13 = bf16[5,4,128,128]{3,2,1,0:T(8,128)(2,1)S(1)} fusion(f32[32,4,128,128]{3,2,1,0:T(8,128)S(1)} %bitcast_convert_fusion, pred[5,32]{1,0:T(8,128)(4,1)S(1)} %broadcast_compare_fusion.12), kind=kLoop, calls=%fused_computation.104 | loop fusion | flops 20643840 | bytes 9044128 | tf_op jit(solution)/shard_map/reduce_sum | solution.py:98
  182.1 3.1 %fusion.37 = f32[4,1024,128]{1,2,0:T(8,128)S(1)} fusion(f32[5,4,1024]{2,0,1:T(8,128)S(1)} %copy-done.18, bf16[4,1024,128]{2,1,0:T(8,128)(2,1)} %param.11, bf16[5,4,128,128]{3,2,1,0:T(8,128)(2,1)S(1)} %select_reduce_fusion.13), kind=kOutput, calls=%fused_computation.106 | convolution fusion | flops 675807232 | bytes 3883008 | tf_op jit(solution)/shard_map/hce,bhde->bhcd/dot_general | solution.py:125
  185.2 3.9 %fusion.39 = (f32[5,4,1024]{2,0,1:T(8,128)S(1)}, f32[4,1024,128]{1,2,0:T(8,128)S(1)}) fusion(f32[4,1024,128]{1,2,0:T(8,128)S(1)} %copy-done.9, f32[5,4,1024]{2,0,1:T(8,128)S(1)} %copy-done.18, bf16[4,1024,128]{2,1,0:T(8,128)(2,1)} %param.8, bf16[5,4,128,128]{3,2,1,0:T(8,128)(2,1)S(1)} %select_reduce_fusion.13), kind=kOutput, calls=%fused_computation.110 | convolution fusion | flops 681029632 | bytes 6062080 | tf_op jit(solution)/shard_map/hcd,bhde->bhce/dot_general | solution.py:122
  189.1 2.4 %add_convert_fusion = (bf16[4,1024,128]{1,2,0:T(8,128)(2,1)S(1)}, bf16[4,1024,128]{1,2,0:T(8,128)(2,1)S(1)}) fusion(f32[4,1024,128]{1,2,0:T(8,128)} %get-tuple-element.150, f32[4,1024,128]{1,2,0:T(8,128)S(1)} %fusion.37, f32[4,1024,128]{1,2,0:T(8,128)S(1)} %copy-done.7, f32[4,1024,128]{1,2,0:T(8,128)S(1)} %get-tuple-element.192), kind=kLoop, calls=%fused_computation.119 | loop fusion | flops 2097152 | bytes 10485760 | tf_op jit(solution)/shard_map/convert_element_type | solution.py:141
  191.5 1.3 copy.49
  (145 shorter events, 25.7 us)
Async XLA Ops:
  7.2 9.7 %copy-start = (s32[32,32]{1,0:T(8,128)S(1)}, s32[32,32]{1,0:T(8,128)}, u32[]{:S(2)}) copy-start(s32[32,32]{1,0:T(8,128)} %param.13) | copy-start | bytes 12292
  7.2 121.1 %reduce-scatter.2.cloned.1.call-start = ((), (), s32[]{:S(2)}) async-start(), calls=%async_computation.1 | async-start | bytes 4325376 | tf_op jit(solution)/shard_map/reduce_scatter | solution.py:108
  7.2 9.6 %copy-start.19 = (s32[5]{0:T(128)}, s32[5]{0:T(128)S(1)}, u32[]{:S(2)}) copy-start(s32[5]{0:T(128)S(1)} %iota_add_fusion) | copy-start | bytes 64
  8.4 6.7 %copy-start.17 = (f32[5,4,1024]{2,0,1:T(8,128)}, f32[5,4,1024]{2,0,1:T(8,128)S(1)}, u32[]{:S(2)}) copy-start(f32[5,4,1024]{2,0,1:T(8,128)S(1)} %slice.86) | copy-start | bytes 245764
  10.0 1.3 copy-start.8
  16.9 10.5 %copy-start.20 = (s32[32]{0:T(128)}, s32[32]{0:T(128)S(1)}, u32[]{:S(2)}) copy-start(s32[32]{0:T(128)S(1)} %dynamic-slice_bitcast_fusion) | copy-start | bytes 388
  27.4 1.2 copy-start.5
  27.4 1.5 copy-start.6
  27.4 145.8 %all-gather.3.cloned.1.call-start = ((), (), s32[]{:S(2)}) async-start(), calls=%async_computation.2 | async-start | bytes 4325376 | tf_op jit(solution)/shard_map/all_gather | solution.py:101
  30.1 6.9 %copy-start.11 = (f32[4,11,1024]{2,1,0:T(8,128)}, f32[4,11,1024]{2,1,0:T(8,128)S(1)}, u32[]{:S(2)}) copy-start(f32[4,11,1024]{2,1,0:T(8,128)S(1)} %get-tuple-element.421) | copy-start | bytes 540676 | tf_op jit(solution)/shard_map/while
  31.9 5.1 %copy-start.2 = (f32[1024,1024]{0,1:T(8,128)}, f32[1024,1024]{0,1:T(8,128)S(1)}, u32[]{:S(2)}) copy-start(f32[1024,1024]{0,1:T(8,128)S(1)} %fusion.91) | copy-start | bytes 12582916 | tf_op jit(solution)/shard_map/while
  38.2 3.5 %copy-start.3 = (f32[1024,1024]{0,1:T(8,128)S(1)}, f32[1024,1024]{0,1:T(8,128)}, u32[]{:S(2)}) copy-start(f32[1024,1024]{0,1:T(8,128)} %copy-done.2) | copy-start | bytes 12582916 | tf_op jit(solution)/shard_map/while
  38.2 4.9 %copy-start.4 = (f32[1024,1024]{0,1:T(8,128)S(1)}, f32[1024,1024]{0,1:T(8,128)}, u32[]{:S(2)}) copy-start(f32[1024,1024]{0,1:T(8,128)} %get-tuple-element.354) | copy-start | bytes 12582916 | tf_op jit(solution)/shard_map/while
  50.2 3.1 %copy-start.14 = (f32[1024]{0:T(1024)S(1)}, f32[1024]{0:T(1024)}, u32[]{:S(2)}) copy-start(f32[1024]{0:T(1024)} %get-tuple-element.367) | copy-start | bytes 12292 | tf_op jit(solution)/shard_map/while
  50.2 3.1 %copy-start.15 = (f32[1024]{0:T(1024)S(1)}, f32[1024]{0:T(1024)}, u32[]{:S(2)}) copy-start(f32[1024]{0:T(1024)} %get-tuple-element.366) | copy-start | bytes 12292 | tf_op jit(solution)/shard_map/while
  50.2 3.1 %copy-start.16 = (f32[1024]{0:T(1024)S(1)}, f32[1024]{0:T(1024)}, u32[]{:S(2)}) copy-start(f32[1024]{0:T(1024)} %get-tuple-element.365) | copy-start | bytes 12292 | tf_op jit(solution)/shard_map/while
  50.2 3.9 %copy-start.12 = (f32[4,11,1024]{2,1,0:T(8,128)S(1)}, f32[4,11,1024]{2,1,0:T(8,128)}, u32[]{:S(2)}) copy-start(f32[4,11,1024]{2,1,0:T(8,128)} %copy-done.11) | copy-start | bytes 540676 | tf_op jit(solution)/shard_map/while
  54.1 6.9 %copy-start.11 = (f32[4,11,1024]{2,1,0:T(8,128)}, f32[4,11,1024]{2,1,0:T(8,128)S(1)}, u32[]{:S(2)}) copy-start(f32[4,11,1024]{2,1,0:T(8,128)S(1)} %get-tuple-element.421) | copy-start | bytes 540676 | tf_op jit(solution)/shard_map/while
  55.9 5.1 %copy-start.2 = (f32[1024,1024]{0,1:T(8,128)}, f32[1024,1024]{0,1:T(8,128)S(1)}, u32[]{:S(2)}) copy-start(f32[1024,1024]{0,1:T(8,128)S(1)} %fusion.91) | copy-start | bytes 12582916 | tf_op jit(solution)/shard_map/while
  62.1 3.7 %copy-start.3 = (f32[1024,1024]{0,1:T(8,128)S(1)}, f32[1024,1024]{0,1:T(8,128)}, u32[]{:S(2)}) copy-start(f32[1024,1024]{0,1:T(8,128)} %copy-done.2) | copy-start | bytes 12582916 | tf_op jit(solution)/shard_map/while
  62.1 5.1 %copy-start.4 = (f32[1024,1024]{0,1:T(8,128)S(1)}, f32[1024,1024]{0,1:T(8,128)}, u32[]{:S(2)}) copy-start(f32[1024,1024]{0,1:T(8,128)} %get-tuple-element.354) | copy-start | bytes 12582916 | tf_op jit(solution)/shard_map/while
  74.4 3.1 %copy-start.14 = (f32[1024]{0:T(1024)S(1)}, f32[1024]{0:T(1024)}, u32[]{:S(2)}) copy-start(f32[1024]{0:T(1024)} %get-tuple-element.367) | copy-start | bytes 12292 | tf_op jit(solution)/shard_map/while
  74.4 3.2 %copy-start.15 = (f32[1024]{0:T(1024)S(1)}, f32[1024]{0:T(1024)}, u32[]{:S(2)}) copy-start(f32[1024]{0:T(1024)} %get-tuple-element.366) | copy-start | bytes 12292 | tf_op jit(solution)/shard_map/while
  74.4 3.2 %copy-start.16 = (f32[1024]{0:T(1024)S(1)}, f32[1024]{0:T(1024)}, u32[]{:S(2)}) copy-start(f32[1024]{0:T(1024)} %get-tuple-element.365) | copy-start | bytes 12292 | tf_op jit(solution)/shard_map/while
  74.4 3.9 %copy-start.12 = (f32[4,11,1024]{2,1,0:T(8,128)S(1)}, f32[4,11,1024]{2,1,0:T(8,128)}, u32[]{:S(2)}) copy-start(f32[4,11,1024]{2,1,0:T(8,128)} %copy-done.11) | copy-start | bytes 540676 | tf_op jit(solution)/shard_map/while
  78.3 6.9 %copy-start.11 = (f32[4,11,1024]{2,1,0:T(8,128)}, f32[4,11,1024]{2,1,0:T(8,128)S(1)}, u32[]{:S(2)}) copy-start(f32[4,11,1024]{2,1,0:T(8,128)S(1)} %get-tuple-element.421) | copy-start | bytes 540676 | tf_op jit(solution)/shard_map/while
  80.0 5.1 %copy-start.2 = (f32[1024,1024]{0,1:T(8,128)}, f32[1024,1024]{0,1:T(8,128)S(1)}, u32[]{:S(2)}) copy-start(f32[1024,1024]{0,1:T(8,128)S(1)} %fusion.91) | copy-start | bytes 12582916 | tf_op jit(solution)/shard_map/while
  86.3 3.6 %copy-start.3 = (f32[1024,1024]{0,1:T(8,128)S(1)}, f32[1024,1024]{0,1:T(8,128)}, u32[]{:S(2)}) copy-start(f32[1024,1024]{0,1:T(8,128)} %copy-done.2) | copy-start | bytes 12582916 | tf_op jit(solution)/shard_map/while
  86.3 4.9 %copy-start.4 = (f32[1024,1024]{0,1:T(8,128)S(1)}, f32[1024,1024]{0,1:T(8,128)}, u32[]{:S(2)}) copy-start(f32[1024,1024]{0,1:T(8,128)} %get-tuple-element.354) | copy-start | bytes 12582916 | tf_op jit(solution)/shard_map/while
  98.3 3.1 %copy-start.14 = (f32[1024]{0:T(1024)S(1)}, f32[1024]{0:T(1024)}, u32[]{:S(2)}) copy-start(f32[1024]{0:T(1024)} %get-tuple-element.367) | copy-start | bytes 12292 | tf_op jit(solution)/shard_map/while
  98.3 3.1 %copy-start.15 = (f32[1024]{0:T(1024)S(1)}, f32[1024]{0:T(1024)}, u32[]{:S(2)}) copy-start(f32[1024]{0:T(1024)} %get-tuple-element.366) | copy-start | bytes 12292 | tf_op jit(solution)/shard_map/while
  98.3 3.1 %copy-start.16 = (f32[1024]{0:T(1024)S(1)}, f32[1024]{0:T(1024)}, u32[]{:S(2)}) copy-start(f32[1024]{0:T(1024)} %get-tuple-element.365) | copy-start | bytes 12292 | tf_op jit(solution)/shard_map/while
  98.3 3.8 %copy-start.12 = (f32[4,11,1024]{2,1,0:T(8,128)S(1)}, f32[4,11,1024]{2,1,0:T(8,128)}, u32[]{:S(2)}) copy-start(f32[4,11,1024]{2,1,0:T(8,128)} %copy-done.11) | copy-start | bytes 540676 | tf_op jit(solution)/shard_map/while
  102.1 6.9 %copy-start.11 = (f32[4,11,1024]{2,1,0:T(8,128)}, f32[4,11,1024]{2,1,0:T(8,128)S(1)}, u32[]{:S(2)}) copy-start(f32[4,11,1024]{2,1,0:T(8,128)S(1)} %get-tuple-element.421) | copy-start | bytes 540676 | tf_op jit(solution)/shard_map/while
  103.9 5.1 %copy-start.2 = (f32[1024,1024]{0,1:T(8,128)}, f32[1024,1024]{0,1:T(8,128)S(1)}, u32[]{:S(2)}) copy-start(f32[1024,1024]{0,1:T(8,128)S(1)} %fusion.91) | copy-start | bytes 12582916 | tf_op jit(solution)/shard_map/while
  110.2 3.5 %copy-start.3 = (f32[1024,1024]{0,1:T(8,128)S(1)}, f32[1024,1024]{0,1:T(8,128)}, u32[]{:S(2)}) copy-start(f32[1024,1024]{0,1:T(8,128)} %copy-done.2) | copy-start | bytes 12582916 | tf_op jit(solution)/shard_map/while
  110.2 4.8 %copy-start.4 = (f32[1024,1024]{0,1:T(8,128)S(1)}, f32[1024,1024]{0,1:T(8,128)}, u32[]{:S(2)}) copy-start(f32[1024,1024]{0,1:T(8,128)} %get-tuple-element.354) | copy-start | bytes 12582916 | tf_op jit(solution)/shard_map/while
  122.0 3.1 %copy-start.14 = (f32[1024]{0:T(1024)S(1)}, f32[1024]{0:T(1024)}, u32[]{:S(2)}) copy-start(f32[1024]{0:T(1024)} %get-tuple-element.367) | copy-start | bytes 12292 | tf_op jit(solution)/shard_map/while
  122.0 3.1 %copy-start.15 = (f32[1024]{0:T(1024)S(1)}, f32[1024]{0:T(1024)}, u32[]{:S(2)}) copy-start(f32[1024]{0:T(1024)} %get-tuple-element.366) | copy-start | bytes 12292 | tf_op jit(solution)/shard_map/while
  122.0 3.1 %copy-start.16 = (f32[1024]{0:T(1024)S(1)}, f32[1024]{0:T(1024)}, u32[]{:S(2)}) copy-start(f32[1024]{0:T(1024)} %get-tuple-element.365) | copy-start | bytes 12292 | tf_op jit(solution)/shard_map/while
  122.0 3.9 %copy-start.12 = (f32[4,11,1024]{2,1,0:T(8,128)S(1)}, f32[4,11,1024]{2,1,0:T(8,128)}, u32[]{:S(2)}) copy-start(f32[4,11,1024]{2,1,0:T(8,128)} %copy-done.11) | copy-start | bytes 540676 | tf_op jit(solution)/shard_map/while
  130.4 1.3 copy-start.13
  176.4 5.7 %copy-start.18 = (f32[5,4,1024]{2,0,1:T(8,128)S(1)}, f32[5,4,1024]{2,0,1:T(8,128)}, u32[]{:S(2)}) copy-start(f32[5,4,1024]{2,0,1:T(8,128)} %copy-done.17) | copy-start | bytes 245764
  182.1 3.1 %copy-start.9 = (f32[4,1024,128]{1,2,0:T(8,128)S(1)}, f32[4,1024,128]{1,2,0:T(8,128)}, u32[]{:S(2)}) copy-start(f32[4,1024,128]{1,2,0:T(8,128)} %copy-done.8) | copy-start | bytes 6291460
  185.2 3.9 %copy-start.7 = (f32[4,1024,128]{1,2,0:T(8,128)S(1)}, f32[4,1024,128]{1,2,0:T(8,128)}, u32[]{:S(2)}) copy-start(f32[4,1024,128]{1,2,0:T(8,128)} %get-tuple-element.149) | copy-start | bytes 6291460
  191.5 2.7 %copy-start.10 = (f32[11,4,1024]{2,0,1:T(8,128)S(1)}, f32[11,4,1024]{2,0,1:T(8,128)}, u32[]{:S(2)}) copy-start(f32[11,4,1024]{2,0,1:T(8,128)} %bitcast_multiply_fusion.5) | copy-start | bytes 540676
  191.5 3.6 %copy-start.1 = (s32[32,32]{1,0:T(8,128)S(1)}, s32[32,32]{1,0:T(8,128)}, u32[]{:S(2)}) copy-start(s32[32,32]{1,0:T(8,128)} %param.13) | copy-start | bytes 12292
Sparse Core Ops, SparseCore 0:
  27.5 92.0 reduce-scatter.1
  123.1 50.0 all-gather.2
where the time goes:
time: 205 us; the launch traced here: 202 us
  matrix products  75.1 us (37%)
  other arithmetic  50.3 us (25%)
  waiting for transfers between devices  38.1 us (19%)
  local copies, waits for them, and re-layouts  23.4 us (11%)
  between operations  14.3 us (7%)
    all_gather x1, waiting for transfers between devices, per_device(): lax.all_gather(own_state[None], 'ctx', axis=0, tiled=True)[None]  38.1 us
    dot_general x4, matrix products, head_local(): jnp.einsum('td,sd->ts', query_h, key_h, preferred_element_type=jnp.float32)  20.5 us
    reduce_sum x4, other arithmetic, head_local(): jnp.sum(jnp.where(same_tile[:, :, None], product, jnp.float32(0.0)), axis=1)  12.7 us
    dot_general x4, matrix products, head_local(): jnp.einsum('ts,te->se', probs, grad_h, preferred_element_type=jnp.float32)  10.6 us
    reduce_sum x1, other arithmetic, per_device(): jnp.sum(jnp.where(match[:, :, None, None, None], grad_state[None].astype(...  10.4 us
    dot_general x4, matrix products, head_local(): jnp.einsum('ts,td->sd', dprobs, query_h, preferred_element_type=jnp.float32)  10.4 us
    unnamed x31, local copies, waits for them, and re-layouts  8.76 us
    convert_element_type x4, other arithmetic, head_local(): dprobs = (mask_weight * back).astype(jnp.bfloat16)  7.39 us
  transfers between devices with their start and end apart: 2, of which 1 were waited for; matrix products, arithmetic and copies ran while one was open for 49% of the time, Pallas kernels for 0%

commit v1 on v0

v1 whole, which is shorter than its diff:
```python
import jax
import jax.numpy as jnp
from jax import lax
from jax.experimental import pallas as pl
from jax.experimental.pallas import tpu as pltpu
from jax.sharding import PartitionSpec as P


TILE = 256


def bit_length_small(numbers, count):
    total = jnp.zeros(numbers.shape, jnp.int32)
    for shift_by in range(count):
        total = total + (numbers >= (1 << shift_by)).astype(jnp.int32)
    return total


def dot_nt(a, b):
    return lax.dot_general(a, b, (((1,), (1,)), ((), ())), preferred_element_type=jnp.float32)


def dot_tn(a, b):
    return lax.dot_general(a, b, (((0,), (0,)), ((), ())), preferred_element_type=jnp.float32)


def dot_nn(a, b):
    return lax.dot_general(a, b, (((1,), (0,)), ((), ())), preferred_element_type=jnp.float32)


def local_kernel(q_ref, k_ref, v_ref, do_ref, g_ref, o_ref, dq_ref, dk_ref, dv_ref, gg_ref):
    block_len = q_ref.shape[0]
    tiles = block_len // TILE
    log_tile = TILE.bit_length() - 1
    nlev = g_ref.shape[1]
    rows = lax.broadcasted_iota(jnp.int32, (TILE, TILE), 0)
    cols = lax.broadcasted_iota(jnp.int32, (TILE, TILE), 1)
    diag_level = jnp.where(
        cols <= rows, bit_length_small(jnp.bitwise_xor(rows, cols), log_tile), -1
    )
    lane = lax.broadcasted_iota(jnp.int32, (TILE, nlev), 1)
    dk_ref[...] = jnp.zeros(dk_ref.shape, jnp.float32)
    dv_ref[...] = jnp.zeros(dv_ref.shape, jnp.float32)
    for i in range(tiles):
        rs = pl.ds(i * TILE, TILE)
        qi = q_ref[rs, :]
        doi = do_ref[rs, :]
        gi = g_ref[rs, :]
        o_acc = jnp.zeros((TILE, q_ref.shape[1]), jnp.float32)
        dq_acc = jnp.zeros((TILE, q_ref.shape[1]), jnp.float32)
        sums = {}
        for j in range(i + 1):
            cs = pl.ds(j * TILE, TILE)
            kj = k_ref[cs, :]
            vj = v_ref[cs, :]
            scores = dot_nt(qi, kj)
            back = dot_nt(doi, vj)
            prod = scores * back
            if j < i:
                level = log_tile + (i ^ j).bit_length()
                weight = gi[:, level : level + 1]
                probs = (scores * weight).astype(jnp.bfloat16)
                dprobs = (back * weight).astype(jnp.bfloat16)
                part = jnp.sum(prod, axis=1, keepdims=True)
                sums[level] = sums[level] + part if level in sums else part
            else:
                weight = jnp.zeros((TILE, TILE), jnp.float32)
                for level in range(log_tile + 1):
                    hit = diag_level == level
                    weight = jnp.where(hit, gi[:, level : level + 1], weight)
                    part = jnp.sum(jnp.where(hit, prod, 0.0), axis=1, keepdims=True)
                    sums[level] = sums[level] + part if level in sums else part
                probs = (scores * weight).astype(jnp.bfloat16)
                dprobs = (back * weight).astype(jnp.bfloat16)
            o_acc = o_acc + dot_nn(probs, vj)
            dq_acc = dq_acc + dot_nn(dprobs, kj)
            dk_ref[cs, :] += dot_tn(dprobs, qi)
            dv_ref[cs, :] += dot_tn(probs, doi)
        o_ref[rs, :] = o_acc
        dq_ref[rs, :] = dq_acc
        gg = jnp.zeros((TILE, nlev), jnp.float32)
        for level, part in sums.items():
            gg = jnp.where(lane == level, part, gg)
        gg_ref[rs, :] = gg * gi


def local_part(query_rows, key_rows, value_rows, out_grad, gate_t):
    heads, block_len, width = query_rows.shape
    nlev = gate_t.shape[2]
    row_spec = pl.BlockSpec((None, block_len, width), lambda h: (h, 0, 0))
    gate_spec = pl.BlockSpec((None, block_len, nlev), lambda h: (h, 0, 0))
    f32 = jnp.float32
    pairs = (block_len // TILE) * (block_len // TILE + 1) // 2
    flops = heads * pairs * 6 * 2 * TILE * TILE * width
    return pl.pallas_call(
        local_kernel,
        grid=(heads,),
        in_specs=[row_spec] * 4 + [gate_spec],
        out_specs=[row_spec] * 4 + [gate_spec],
        out_shape=[jax.ShapeDtypeStruct((heads, block_len, width), f32)] * 4
        + [jax.ShapeDtypeStruct((heads, block_len, nlev), f32)],
        compiler_params=pltpu.CompilerParams(dimension_semantics=("arbitrary",)),
        cost_estimate=pl.CostEstimate(
            flops=flops,
            transcendentals=0,
            bytes_accessed=heads * block_len * (4 * width * 2 + 4 * width * 4 + 2 * nlev * 4),
        ),
    )(query_rows, key_rows, value_rows, out_grad, gate_t)


def same_doc(block_levels, earlier, later):
    return block_levels[later, earlier] >= 0


def level_network(state, block_levels, me, nbits, ctx_len):
    x = state
    levels = []
    for k in range(nbits):
        bit = ((me >> k) & 1) == 1
        lo = (me >> (k + 1)) << (k + 1)
        end_low = lo + (1 << k) - 1
        end_high = lo + (2 << k) - 1
        joined = same_doc(block_levels, end_low, end_high)
        mine = same_doc(block_levels, end_low, me)
        if k < nbits - 1:
            perm = [(j, j ^ (1 << k)) for j in range(ctx_len)]
        else:
            perm = [(j, j ^ (1 << k)) for j in range(ctx_len) if not (j >> k) & 1]
        got = lax.ppermute(x, "ctx", perm)
        levels.append(jnp.where(bit & mine, got, 0.0).astype(jnp.bfloat16))
        if k < nbits - 1:
            x = jnp.where(
                bit, x + jnp.where(joined, got, 0.0), got + jnp.where(joined, x, 0.0)
            )
    return jnp.stack(levels)


def key_network(grad_state, block_levels, me, nbits, ctx_len):
    acc = None
    for k in reversed(range(nbits)):
        bit = ((me >> k) & 1) == 1
        lo = (me >> (k + 1)) << (k + 1)
        end_low = lo + (1 << k) - 1
        end_high = lo + (2 << k) - 1
        joined = same_doc(block_levels, end_low, end_high)
        mine = same_doc(block_levels, end_low, me)
        term = jnp.where(bit & mine, grad_state[k], 0.0)
        if acc is None:
            send = term
            own = None
            perm = [(j, j ^ (1 << k)) for j in range(ctx_len) if (j >> k) & 1]
        else:
            kept = jnp.where(joined, acc, 0.0)
            send = jnp.where(bit, term + kept, acc)
            own = jnp.where(bit, acc, kept)
            perm = [(j, j ^ (1 << k)) for j in range(ctx_len)]
        got = lax.ppermute(send, "ctx", perm)
        acc = got if own is None else own + got
    return acc


def per_device(query_rows, key_rows, value_rows, out_grad, level_gate, block_levels, ctx_len):
    level_total = level_gate.shape[0]
    block_len = query_rows.shape[1]
    log_block = block_len.bit_length() - 1
    nbits = level_total - log_block - 1
    me = lax.axis_index("ctx")
    weights = jnp.exp(level_gate)
    cross_weight = weights[log_block + 1 :]

    own_state = jnp.einsum(
        "hcd,hce->hde", key_rows, value_rows, preferred_element_type=jnp.float32
    ).astype(jnp.bfloat16)
    scaled = (cross_weight[..., None] * out_grad[None].astype(jnp.float32)).astype(jnp.bfloat16)
    grad_state = jnp.einsum(
        "hcd,bhce->bhde", query_rows, scaled, preferred_element_type=jnp.float32
    ).astype(jnp.bfloat16)

    level_state = level_network(
        own_state.astype(jnp.float32), block_levels, me, nbits, ctx_len
    )
    key_state = key_network(
        grad_state.astype(jnp.float32), block_levels, me, nbits, ctx_len
    ).astype(jnp.bfloat16)

    gate_t = weights.transpose(1, 2, 0)
    out_inner, dq_inner, dk_inner, dv_inner, grad_inner = local_part(
        query_rows, key_rows, value_rows, out_grad, gate_t
    )

    level_out = jnp.einsum(
        "hcd,bhde->bhce", query_rows, level_state, preferred_element_type=jnp.float32
    )
    level_back = jnp.einsum(
        "hce,bhde->bhcd", out_grad, level_state, preferred_element_type=jnp.float32
    )
    attn = out_inner + jnp.sum(cross_weight[..., None] * level_out, axis=0)
    grad_q = dq_inner + jnp.sum(cross_weight[..., None] * level_back, axis=0)
    grad_cross = cross_weight * jnp.sum(level_out * out_grad[None].astype(jnp.float32), axis=3)
    grad_gate = jnp.concatenate(
        [grad_inner.transpose(2, 0, 1)[: log_block + 1], grad_cross], axis=0
    )
    grad_k = (
        dk_inner
        + jnp.einsum("hde,hce->hcd", key_state, value_rows, preferred_element_type=jnp.float32)
    ).astype(jnp.bfloat16)
    grad_v = (
        dv_inner
        + jnp.einsum("hde,hcd->hce", key_state, key_rows, preferred_element_type=jnp.float32)
    ).astype(jnp.bfloat16)
    return (attn.astype(jnp.bfloat16), grad_q.astype(jnp.bfloat16), grad_k, grad_v, grad_gate)


def solution(mesh):
    ctx_len = mesh.shape["ctx"]
    in_specs = (
        P("head", "ctx", None),
        P("head", "ctx", None),
        P("head", "ctx", None),
        P("head", "ctx", None),
        P(None, "head", "ctx"),
        P(),
    )
    out_specs = (
        P("head", "ctx", None),
        P("head", "ctx", None),
        P("head", "ctx", None),
        P("head", "ctx", None),
        P(None, "head", "ctx"),
    )

    def body(*args):
        return per_device(*args, ctx_len=ctx_len)

    return jax.shard_map(
        body, mesh=mesh, in_specs=in_specs, out_specs=out_specs, check_vma=False
    )
```

time: 205 us -> 138 us (0.67)
  the two profiles are of different devices: /device:TPU:4 before, /device:TPU:1 now
where the time goes in v1:
time: 138 us; the launch traced here: 137 us
  Pallas kernels  31.7 us (23%)
  local copies, waits for them, and re-layouts  25.6 us (19%)
  starting transfers between devices  23.2 us (17%)
  waiting for transfers between devices  22.6 us (16%)
  matrix products  13.9 us (10%)
  other arithmetic  13.5 us (10%)
  between operations  6.52 us (5%)
    pallas_call x1, Pallas kernels, local_part(): pl.pallas_call(local_kernel, grid=(heads,), in_specs=[row_spec] * 4 + [ga...  31.7 us
    ppermute x5, starting transfers between devices, key_network(): got = lax.ppermute(send, 'ctx', perm)  12.7 us
    ppermute x5, waiting for transfers between devices, level_network(): got = lax.ppermute(x, 'ctx', perm)  12.5 us
    ppermute x5, starting transfers between devices, level_network(): got = lax.ppermute(x, 'ctx', perm)  10.6 us
    ppermute x5, waiting for transfers between devices, key_network(): got = lax.ppermute(send, 'ctx', perm)  10.2 us
    dot_general x1, matrix products, per_device(): jnp.einsum('hcd,bhde->bhce', query_rows, level_state, preferred_element_t...  4.44 us
    convert_element_type x1, other arithmetic, per_device(): grad_q.astype(jnp.bfloat16)  4.25 us
    slice x2, local copies, waits for them, and re-layouts, per_device(): cross_weight = weights[log_block + 1:]  4.16 us
  transfers between devices with their start and end apart: 10, of which 5 were waited for; matrix products, arithmetic and copies ran while one was open for 26% of the time, Pallas kernels for 23%

profile of v1, /device:TPU:1, one launch (start us, length us, event | category | flops | bytes accessed | tf_op | source)
XLA Modules:
  0.0 137.1 jit_solution(7307292304893266456)
XLA Ops:
  0.6 2.1 %fusion.16 = f32[4,128,128]{2,1,0:T(8,128)S(1)} fusion(bf16[4,1024,128]{2,1,0:T(8,128)(2,1)} %k_ref.1, bf16[4,1024,128]{2,1,0:T(8,128)(2,1)} %v_ref.1), kind=kOutput, calls=%fused_computation.19 | convolution fusion | flops 134348800 | bytes 2359296 | tf_op jit(solution)/shard_map/hcd,hce->hde/dot_general | solution.py:171
  2.7 3.3 %collective-permute-start = (f32[4,128,128]{2,1,0:T(8,128)S(1)}, f32[4,128,128]{2,1,0:T(8,128)S(1)}, u32[]{:S(2)}, u32[]{:S(2)}) collective-permute-start(f32[4,128,128]{2,1,0:T(8,128)S(1)} %fusion.16), channel_id=1, source_target_pairs={{0,8},{8,0},{16,24},{24,16},{32,40},{40,32},{48,56},{56,48},{64,72... | collective-permute-start | bytes 786440 | tf_op jit(solution)/shard_map/ppermute | solution.py:129
  6.0 1.6 %fusion.49 = (s32[1,1]{1,0:T(1,128)}, s32[1,1]{1,0:T(1,128)}, s32[1,1]{1,0:T(1,128)}, s32[1,1]{1,0:T(1,128)}, s32[1,1]{1,0:T(1,128)}, /*index=5*/s32[1,1]{1,0:T(...) fusion(s32[32,32]{1,0:T(8,128)} %param.11, s32[]{:T(128)S(6)} %select_n.247, s32[]{:T(128)S(6)} %select_n.278, ...), kind=kLoop, calls=%fused_computation.76 | loop fusion | bytes 112 | tf_op jit(solution)/shard_map/dynamic_slice | solution.py:112
  8.4 0.1 collective-permute-start.1
  9.1 2.0 %copy.38 = f32[16,4,1024]{0,2,1:T(8,128)} copy(f32[16,4,1024]{2,1,0:T(4,128)S(1)} %copy-done.11) | data formatting | bytes 524288 | tf_op args[4]
  11.1 5.3 %collective-permute-done.1 = f32[4,128,128]{2,1,0:T(8,128)S(1)} collective-permute-done((f32[4,128,128]{2,1,0:T(8,128)S(1)}, f32[4,128,128]{2,1,0:T(8,128)S(1)}, u32[]{:S(2)}, u32[]{:S(2)}) %collective-permute-start.1) | collective-permute-done | bytes 262176 | tf_op jit(solution)/shard_map/ppermute | solution.py:129
  16.4 0.8 add_select_fusion.2
  17.2 1.2 collective-permute-start.2
  18.3 3.2 %fusion.48 = (f32[16,4,1024]{0,2,1:T(8,128)S(1)}, f32[4,1024,16]{2,1,0:T(8,128)}) fusion(f32[16,4,1024]{0,2,1:T(8,128)} %copy.38), kind=kLoop, calls=%fused_computation.75 | loop fusion | bytes 786432 | tf_op jit(solution)/shard_map/exp | solution.py:168
  25.9 1.6 %copy.45 = f32[4,1024,128]{1,2,0:T(8,128)} copy(bf16[4,1024,128]{2,1,0:T(8,128)(2,1)S(1)} %copy-done.7) | data formatting | bytes 3145728 | tf_op jit(solution)/shard_map/convert_element_type | solution.py:174
  27.5 1.9 %slice.28 = f32[5,4,1024]{0,2,1:T(8,128)} slice(f32[16,4,1024]{0,2,1:T(8,128)S(1)} %get-tuple-element.35), slice={[11:16], [0:4], [0:1024]} | slice | bytes 163840 | tf_op jit(solution)/shard_map/slice | solution.py:169
  29.4 2.3 %copy.39 = f32[5,4,1024]{2,0,1:T(8,128)S(1)} copy(f32[5,4,1024]{0,2,1:T(8,128)} %slice.28) | data formatting | bytes 163840 | tf_op jit(solution)/shard_map/slice | solution.py:169
  31.7 1.2 add_select_fusion.1
  32.9 1.3 collective-permute-start.3
  34.4 5.3 %collective-permute-done.3 = f32[4,128,128]{2,1,0:T(8,128)S(1)} collective-permute-done((f32[4,128,128]{2,1,0:T(8,128)S(1)}, f32[4,128,128]{2,1,0:T(8,128)S(1)}, u32[]{:S(2)}, u32[]{:S(2)}) %collective-permute-start.3) | collective-permute-done | bytes 262176 | tf_op jit(solution)/shard_map/ppermute | solution.py:129
  39.7 0.1 add_select_fusion
  39.8 4.7 %collective-permute-start.4 = (bf16[4,128,128]{2,1,0:T(8,128)(2,1)S(1)}, bf16[4,128,128]{2,1,0:T(8,128)(2,1)S(1)}, u32[]{:S(2)}, u32[]{:S(2)}) collective-permute-start(bf16[4,128,128]{2,1,0:T(8,128)(2,1)S(1)} %add_select_fusion), channel_id=1, source_target_pairs={{0,128},{8,136},{16,144},{24,152},{32,160},{40,168},{48,176},{56,1... | collective-permute-start | bytes 393224 | tf_op jit(solution)/shard_map/ppermute | solution.py:129
  44.5 1.9 %collective-permute-done.4 = bf16[4,128,128]{2,1,0:T(8,128)(2,1)S(1)} collective-permute-done((bf16[4,128,128]{2,1,0:T(8,128)(2,1)S(1)}, bf16[4,128,128]{2,1,0:T(8,128)(2,1)S(1)}, u32[]{:S(2)}, u32[]{:S(2)}) %collective-permute-start.4) | collective-permute-done | bytes 131104 | tf_op jit(solution)/shard_map/ppermute | solution.py:129
  46.4 0.0 copy-start.12
  46.4 4.4 %fusion.2 = (f32[5,4,1024]{2,0,1:T(8,128)S(1)}, f32[4,1024,128]{1,2,0:T(8,128)}, bf16[5,4,1024,128]{2,3,0,1:T(8,128)(2,1)S(1)}) fusion(f32[4,1024,128]{1,2,0:T(8,128)S(1)} %copy-done.3, f32[5,4,1024]{2,0,1:T(8,128)S(1)} %copy.39, bf16[4,1024,128]{2,1,0:T(8,128)(2,1)S(1)} %copy-done.14, bf16[5,4,128,128]{3,2,1,0:T(8,128)(2,1)S(1)} %fusion.46), kind=kOutput, calls=%fused_computation.5 | convolution fusion | flops 686272512 | bytes 11304960 | tf_op jit(solution)/shard_map/hcd,bhde->bhce/dot_general | solution.py:191
  50.9 1.7 %fusion.13 = f32[5,4,128,128]{3,2,1,0:T(8,128)S(1)} fusion(bf16[5,4,1024,128]{2,3,0,1:T(8,128)(2,1)S(1)} %get-tuple-element.34, bf16[4,1024,128]{2,1,0:T(8,128)(2,1)S(1)} %copy-done.14), kind=kOutput, calls=%fused_computation.17 | convolution fusion | flops 671744000 | bytes 7602176 | tf_op jit(solution)/shard_map/hcd,bhce->bhde/dot_general | solution.py:175
  52.7 1.3 collective-permute-start.5
  54.0 7.3 %collective-permute-done.5 = f32[4,128,128]{2,1,0:T(8,128)S(1)} collective-permute-done((f32[4,128,128]{2,1,0:T(8,128)S(1)}, f32[4,128,128]{2,1,0:T(8,128)S(1)}, u32[]{:S(2)}, u32[]{:S(2)}) %collective-permute-start.5) | collective-permute-done | bytes 262176 | tf_op jit(solution)/shard_map/ppermute | solution.py:157
  61.4 0.6 collective-permute-start.6
  62.0 31.7 %shard_map.101 = (f32[4,1024,128]{2,1,0:T(8,128)}, f32[4,1024,128]{2,1,0:T(8,128)}, f32[4,1024,128]{2,1,0:T(8,128)}, f32[4,1024,128]{2,1,0:T(8,128)}, f32[4,1024,16]{2,1,0:T(8,128)}) custom-call(bf16[4,1024,128]{2,1,0:T(8,128)(2,1)} %q_ref.1, bf16[4,1024,128]{2,1,0:T(8,128)(2,1)} %k_ref.1, bf16[4,1024,128]{2,1,0:T(8,128)(2,1)} %v_ref.1, ...), custom_call_target="tpu_custom_call" | custom-call | flops 4026531840 | bytes 13107200 | tf_op jit(solution)/shard_map/pallas_call | solution.py:95
  93.7 2.2 %copy.51 = f32[11,4,1024]{2,0,1:T(8,128)S(1)} copy(f32[11,4,1024]{0,2,1:T(8,128)} %bitcast.92) | data formatting | bytes 360448 | tf_op jit(solution)/shard_map/slice | solution.py:201
  95.9 2.0 %copy.50 = f32[5,4,1024]{0,2,1:T(8,128)} copy(f32[5,4,1024]{2,0,1:T(8,128)S(1)} %get-tuple-element.30) | data formatting | bytes 163840 | tf_op jit(solution)/shard_map/reduce_sum | solution.py:199
  97.9 1.0 fusion.25
  98.9 0.0 copy-start.8
  98.9 0.0 copy-start.13
  98.9 0.3 collective-permute-start.7
  99.2 3.7 %slice_multiply_fusion = f32[5,4,1024]{0,2,1:T(8,128)} fusion(f32[5,4,1024]{0,2,1:T(8,128)} %copy.50, f32[16,4,1024]{0,2,1:T(8,128)S(1)} %get-tuple-element.35), kind=kLoop, calls=%fused_computation.73 | loop fusion | flops 20480 | bytes 245760 | tf_op jit(solution)/shard_map/mul | solution.py:199
  102.9 2.8 %collective-permute-done.7 = f32[4,128,128]{2,1,0:T(8,128)S(1)} collective-permute-done((f32[4,128,128]{2,1,0:T(8,128)S(1)}, f32[4,128,128]{2,1,0:T(8,128)S(1)}, u32[]{:S(2)}, u32[]{:S(2)}) %collective-permute-start.7) | collective-permute-done | bytes 262176 | tf_op jit(solution)/shard_map/ppermute | solution.py:157
  105.7 1.0 fusion.24
  106.8 0.5 collective-permute-start.8
  107.3 2.9 %fusion = f32[4,1024,128]{1,2,0:T(8,128)} fusion(f32[5,4,1024]{2,0,1:T(8,128)S(1)} %copy.39, bf16[4,1024,128]{2,1,0:T(8,128)(2,1)S(1)} %copy-done.8, bf16[5,4,128,128]{3,2,1,0:T(8,128)(2,1)S(1)} %copy-done.13), kind=kOutput, calls=%fused_computation.1 | convolution fusion | flops 675807232 | bytes 3883008 | tf_op jit(solution)/shard_map/hce,bhde->bhcd/dot_general | solution.py:194
  110.1 1.9 %copy.44 = f32[4,1024,128]{2,1,0:T(8,128)S(1)} copy(f32[4,1024,128]{1,2,0:T(8,128)} %fusion) | data formatting | bytes 4194304 | tf_op jit(solution)/shard_map/reduce_sum | solution.py:198
  112.1 2.2 %copy.52 = f32[5,4,1024]{2,0,1:T(8,128)S(1)} copy(f32[5,4,1024]{0,2,1:T(8,128)} %slice_multiply_fusion) | data formatting | bytes 163840 | tf_op jit(solution)/shard_map/mul | solution.py:199
  114.3 2.9 %copy.42 = f32[4,1024,128]{2,1,0:T(8,128)} copy(f32[4,1024,128]{1,2,0:T(8,128)} %get-tuple-element.31) | data formatting | bytes 4194304 | tf_op jit(solution)/shard_map/reduce_sum | solution.py:197
  117.2 0.9 copy.53
  118.1 1.0 fusion.23
  119.1 10.0 %collective-permute-start.9 = (f32[4,128,128]{2,1,0:T(8,128)S(1)}, f32[4,128,128]{2,1,0:T(8,128)S(1)}, u32[]{:S(2)}, u32[]{:S(2)}) collective-permute-start(f32[4,128,128]{2,1,0:T(8,128)S(1)} %fusion.23), channel_id=1, source_target_pairs={{0,8},{8,0},{16,24},{24,16},{32,40},{40,32},{48,56},{56,48},{64,72... | collective-permute-start | bytes 786440 | tf_op jit(solution)/shard_map/ppermute | solution.py:157
  129.1 4.2 %add_convert_fusion = (bf16[4,1024,128]{2,1,0:T(8,128)(2,1)}, bf16[4,1024,128]{2,1,0:T(8,128)(2,1)}) fusion(f32[4,1024,128]{2,1,0:T(8,128)} %get-tuple-element.11, f32[4,1024,128]{2,1,0:T(8,128)S(1)} %copy.44, f32[4,1024,128]{2,1,0:T(8,128)} %get-tuple-element.10, f32[4,1024,128]{2,1,0:T(8,128)S(1)} %copy-done), kind=kLoop, calls=%fused_computation.13 | loop fusion | flops 2097152 | bytes 10485760 | tf_op jit(solution)/shard_map/convert_element_type | solution.py:211
  133.3 0.1 fusion.31
  133.4 0.0 copy-start.2
  133.5 1.4 %fusion.6 = bf16[4,1024,128]{2,1,0:T(8,128)(2,1)} fusion(f32[4,1024,128]{2,1,0:T(8,128)S(1)} %copy-done.5, bf16[4,128,128]{2,1,0:T(8,128)(2,1)S(1)} %fusion.31, bf16[4,1024,128]{2,1,0:T(8,128)(2,1)S(1)} %copy-done.1), kind=kOutput, calls=%fused_computation.12 | convolution fusion | flops 135266304 | bytes 4325376 | tf_op jit(solution)/shard_map/hde,hce->hcd/dot_general | solution.py:205
  134.9 0.9 copy-done.4
  135.7 1.4 %fusion.5 = bf16[4,1024,128]{2,1,0:T(8,128)(2,1)} fusion(f32[4,1024,128]{2,1,0:T(8,128)S(1)} %copy-done.4, bf16[4,1024,128]{2,1,0:T(8,128)(2,1)S(1)} %copy-done.2, bf16[4,128,128]{2,1,0:T(8,128)(2,1)S(1)} %fusion.31), kind=kOutput, calls=%fused_computation.10 | convolution fusion | flops 135266304 | bytes 4325376 | tf_op jit(solution)/shard_map/hde,hcd->hce/dot_general | solution.py:209
  (39 shorter events, 0.4 us)
Async XLA Ops:
  0.6 8.5 %copy-start.11 = (f32[16,4,1024]{2,1,0:T(4,128)S(1)}, f32[16,4,1024]{2,1,0:T(4,128)}, u32[]{:S(2)}) copy-start(f32[16,4,1024]{2,1,0:T(4,128)} %param.10) | copy-start | bytes 786436
  2.7 5.6 %collective-permute-start = (f32[4,128,128]{2,1,0:T(8,128)S(1)}, f32[4,128,128]{2,1,0:T(8,128)S(1)}, u32[]{:S(2)}, u32[]{:S(2)}) collective-permute-start(f32[4,128,128]{2,1,0:T(8,128)S(1)} %fusion.16), channel_id=1, source_target_pairs={{0,8},{8,0},{16,24},{24,16},{32,40},{40,32},{48,56},{56,48},{64,72... | collective-permute-start | bytes 786440 | tf_op jit(solution)/shard_map/ppermute | solution.py:129
  8.4 8.0 %collective-permute-start.1 = (f32[4,128,128]{2,1,0:T(8,128)S(1)}, f32[4,128,128]{2,1,0:T(8,128)S(1)}, u32[]{:S(2)}, u32[]{:S(2)}) collective-permute-start(f32[4,128,128]{2,1,0:T(8,128)S(1)} %add_select_fusion.3), channel_id=1, source_target_pairs={{0,16},{8,24},{16,0},{24,8},{32,48},{40,56},{48,32},{56,40},{64,80... | collective-permute-start | bytes 786440 | tf_op jit(solution)/shard_map/ppermute | solution.py:129
  16.4 0.8 copy-start.9
  17.2 8.7 %copy-start.7 = (bf16[4,1024,128]{2,1,0:T(8,128)(2,1)S(1)}, bf16[4,1024,128]{2,1,0:T(8,128)(2,1)}, u32[]{:S(2)}) copy-start(bf16[4,1024,128]{2,1,0:T(8,128)(2,1)} %do_ref.1) | copy-start | bytes 3145732
  17.2 14.6 %collective-permute-start.2 = (f32[4,128,128]{2,1,0:T(8,128)}, f32[4,128,128]{2,1,0:T(8,128)}, u32[]{:S(2)}, u32[]{:S(2)}) collective-permute-start(f32[4,128,128]{2,1,0:T(8,128)} %add_select_fusion.2), channel_id=1, source_target_pairs={{0,32},{8,40},{16,48},{24,56},{32,0},{40,8},{48,16},{56,24},{64,96... | collective-permute-start | bytes 786440 | tf_op jit(solution)/shard_map/ppermute | solution.py:129
  29.4 4.9 %copy-start.10 = (f32[4,128,128]{2,1,0:T(8,128)S(1)}, f32[4,128,128]{2,1,0:T(8,128)}, u32[]{:S(2)}) copy-start(f32[4,128,128]{2,1,0:T(8,128)} %copy-done.9) | copy-start | bytes 786436
  31.7 14.8 %copy-start.3 = (f32[4,1024,128]{1,2,0:T(8,128)S(1)}, f32[4,1024,128]{1,2,0:T(8,128)}, u32[]{:S(2)}) copy-start(f32[4,1024,128]{1,2,0:T(8,128)} %copy.45) | copy-start | bytes 6291460
  31.7 14.8 %copy-start.14 = (bf16[4,1024,128]{2,1,0:T(8,128)(2,1)S(1)}, bf16[4,1024,128]{2,1,0:T(8,128)(2,1)}, u32[]{:S(2)}) copy-start(bf16[4,1024,128]{2,1,0:T(8,128)(2,1)} %q_ref.1) | copy-start | bytes 3145732
  32.9 6.8 %collective-permute-start.3 = (f32[4,128,128]{2,1,0:T(8,128)S(1)}, f32[4,128,128]{2,1,0:T(8,128)S(1)}, u32[]{:S(2)}, u32[]{:S(2)}) collective-permute-start(f32[4,128,128]{2,1,0:T(8,128)S(1)} %add_select_fusion.1), channel_id=1, source_target_pairs={{0,64},{8,72},{16,80},{24,88},{32,96},{40,104},{48,112},{56,120},{... | collective-permute-start | bytes 786440 | tf_op jit(solution)/shard_map/ppermute | solution.py:129
  39.8 6.6 %collective-permute-start.4 = (bf16[4,128,128]{2,1,0:T(8,128)(2,1)S(1)}, bf16[4,128,128]{2,1,0:T(8,128)(2,1)S(1)}, u32[]{:S(2)}, u32[]{:S(2)}) collective-permute-start(bf16[4,128,128]{2,1,0:T(8,128)(2,1)S(1)} %add_select_fusion), channel_id=1, source_target_pairs={{0,128},{8,136},{16,144},{24,152},{32,160},{40,168},{48,176},{56,1... | collective-permute-start | bytes 393224 | tf_op jit(solution)/shard_map/ppermute | solution.py:129
  46.4 4.5 %copy-start.12 = (bf16[5,4,128,128]{3,2,1,0:T(8,128)(2,1)}, bf16[5,4,128,128]{3,2,1,0:T(8,128)(2,1)S(1)}, u32[]{:S(2)}) copy-start(bf16[5,4,128,128]{3,2,1,0:T(8,128)(2,1)S(1)} %fusion.46) | copy-start | bytes 1966084
  52.6 8.7 %copy-start.6 = (f32[5,4,128,128]{3,2,1,0:T(8,128)}, f32[5,4,128,128]{3,2,1,0:T(8,128)S(1)}, u32[]{:S(2)}) copy-start(f32[5,4,128,128]{3,2,1,0:T(8,128)S(1)} %fusion.13) | copy-start | bytes 3932164
  52.7 8.6 %collective-permute-start.5 = (f32[4,128,128]{2,1,0:T(8,128)S(1)}, f32[4,128,128]{2,1,0:T(8,128)S(1)}, u32[]{:S(2)}, u32[]{:S(2)}) collective-permute-start(f32[4,128,128]{2,1,0:T(8,128)S(1)} %fusion.36), channel_id=1, source_target_pairs={{128,0},{136,8},{144,16},{152,24},{160,32},{168,40},{176,48},{184,... | collective-permute-start | bytes 786440 | tf_op jit(solution)/shard_map/ppermute | solution.py:157
  61.4 36.5 %collective-permute-start.6 = (f32[4,128,128]{2,1,0:T(8,128)S(1)}, f32[4,128,128]{2,1,0:T(8,128)S(1)}, u32[]{:S(2)}, u32[]{:S(2)}) collective-permute-start(f32[4,128,128]{2,1,0:T(8,128)S(1)} %fusion.26), channel_id=1, source_target_pairs={{0,64},{8,72},{16,80},{24,88},{32,96},{40,104},{48,112},{56,120},{... | collective-permute-start | bytes 786440 | tf_op jit(solution)/shard_map/ppermute | solution.py:157
  98.9 8.4 %copy-start.8 = (bf16[4,1024,128]{2,1,0:T(8,128)(2,1)S(1)}, bf16[4,1024,128]{2,1,0:T(8,128)(2,1)}, u32[]{:S(2)}) copy-start(bf16[4,1024,128]{2,1,0:T(8,128)(2,1)} %do_ref.1) | copy-start | bytes 3145732
  98.9 8.4 %copy-start.13 = (bf16[5,4,128,128]{3,2,1,0:T(8,128)(2,1)S(1)}, bf16[5,4,128,128]{3,2,1,0:T(8,128)(2,1)}, u32[]{:S(2)}) copy-start(bf16[5,4,128,128]{3,2,1,0:T(8,128)(2,1)} %copy-done.12) | copy-start | bytes 1966084
  98.9 6.8 %collective-permute-start.7 = (f32[4,128,128]{2,1,0:T(8,128)S(1)}, f32[4,128,128]{2,1,0:T(8,128)S(1)}, u32[]{:S(2)}, u32[]{:S(2)}) collective-permute-start(f32[4,128,128]{2,1,0:T(8,128)S(1)} %fusion.25), channel_id=1, source_target_pairs={{0,32},{8,40},{16,48},{24,56},{32,0},{40,8},{48,16},{56,24},{64,96... | collective-permute-start | bytes 786440 | tf_op jit(solution)/shard_map/ppermute | solution.py:157
  106.8 11.3 %collective-permute-start.8 = (f32[4,128,128]{2,1,0:T(8,128)S(1)}, f32[4,128,128]{2,1,0:T(8,128)S(1)}, u32[]{:S(2)}, u32[]{:S(2)}) collective-permute-start(f32[4,128,128]{2,1,0:T(8,128)S(1)} %get-tuple-element.32), channel_id=1, source_target_pairs={{0,16},{8,24},{16,0},{24,8},{32,48},{40,56},{48,32},{56,40},{64,80... | collective-permute-start | bytes 786440 | tf_op jit(solution)/shard_map/ppermute | solution.py:157
  117.2 11.9 %copy-start = (f32[4,1024,128]{2,1,0:T(8,128)S(1)}, f32[4,1024,128]{2,1,0:T(8,128)}, u32[]{:S(2)}) copy-start(f32[4,1024,128]{2,1,0:T(8,128)} %copy.42) | copy-start | bytes 6291460
  119.1 14.2 %collective-permute-start.9 = (f32[4,128,128]{2,1,0:T(8,128)S(1)}, f32[4,128,128]{2,1,0:T(8,128)S(1)}, u32[]{:S(2)}, u32[]{:S(2)}) collective-permute-start(f32[4,128,128]{2,1,0:T(8,128)S(1)} %fusion.23), channel_id=1, source_target_pairs={{0,8},{8,0},{16,24},{24,16},{32,40},{40,32},{48,56},{56,48},{64,72... | collective-permute-start | bytes 786440 | tf_op jit(solution)/shard_map/ppermute | solution.py:157
  129.1 4.3 %copy-start.1 = (bf16[4,1024,128]{2,1,0:T(8,128)(2,1)S(1)}, bf16[4,1024,128]{2,1,0:T(8,128)(2,1)}, u32[]{:S(2)}) copy-start(bf16[4,1024,128]{2,1,0:T(8,128)(2,1)} %v_ref.1) | copy-start | bytes 3145732
  129.1 4.3 %copy-start.5 = (f32[4,1024,128]{2,1,0:T(8,128)S(1)}, f32[4,1024,128]{2,1,0:T(8,128)}, u32[]{:S(2)}) copy-start(f32[4,1024,128]{2,1,0:T(8,128)} %get-tuple-element.12) | copy-start | bytes 6291460
  133.4 1.4 %copy-start.2 = (bf16[4,1024,128]{2,1,0:T(8,128)(2,1)S(1)}, bf16[4,1024,128]{2,1,0:T(8,128)(2,1)}, u32[]{:S(2)}) copy-start(bf16[4,1024,128]{2,1,0:T(8,128)(2,1)} %k_ref.1) | copy-start | bytes 3145732
  133.4 2.3 %copy-start.4 = (f32[4,1024,128]{2,1,0:T(8,128)S(1)}, f32[4,1024,128]{2,1,0:T(8,128)}, u32[]{:S(2)}) copy-start(f32[4,1024,128]{2,1,0:T(8,128)} %get-tuple-element.13) | copy-start | bytes 6291460

commit v2 on v1

v2 whole, which is shorter than its diff:
```python
import jax
import jax.numpy as jnp
from jax import lax
from jax.experimental import pallas as pl
from jax.experimental.pallas import tpu as pltpu
from jax.sharding import PartitionSpec as P


TILE = 256
SUB = 128


def bit_length_small(numbers, count):
    total = jnp.zeros(numbers.shape, jnp.int32)
    for shift_by in range(count):
        total = total + (numbers >= (1 << shift_by)).astype(jnp.int32)
    return total


def dot_nt(a, b):
    return lax.dot_general(a, b, (((1,), (1,)), ((), ())), preferred_element_type=jnp.float32)


def dot_tn(a, b):
    return lax.dot_general(a, b, (((0,), (0,)), ((), ())), preferred_element_type=jnp.float32)


def dot_nn(a, b):
    return lax.dot_general(a, b, (((1,), (0,)), ((), ())), preferred_element_type=jnp.float32)


def local_kernel(q_ref, k_ref, v_ref, do_ref, g_ref, *refs):
    o_ref, dq_ref, dk_ref, dv_ref, gg_ref = refs[-5:]
    block_len = q_ref.shape[0]
    tiles = block_len // TILE
    log_tile = TILE.bit_length() - 1
    log_sub = SUB.bit_length() - 1
    keys = lax.broadcasted_iota(jnp.int32, (SUB, SUB), 0)
    queries = lax.broadcasted_iota(jnp.int32, (SUB, SUB), 1)
    diag_level = jnp.where(
        keys <= queries, bit_length_small(jnp.bitwise_xor(keys, queries), log_sub), -1
    )
    for ref in (o_ref, dq_ref, dk_ref, dv_ref, gg_ref):
        ref[...] = jnp.zeros(ref.shape, jnp.float32)

    def pair(t0, s0, size, level):
        ts = pl.ds(t0, size)
        ss = pl.ds(s0, size)
        qi = q_ref[ts, :]
        doi = do_ref[ts, :]
        kj = k_ref[ss, :]
        vj = v_ref[ss, :]
        gi = g_ref[:, ts]
        scores = dot_nt(kj, qi)
        back = dot_nt(vj, doi)
        prod = scores * back
        if level is not None:
            weight = gi[level : level + 1, :]
            gg_ref[level : level + 1, ts] += jnp.sum(prod, axis=0, keepdims=True)
        else:
            weight = jnp.zeros((size, size), jnp.float32)
            for lev in range(log_sub + 1):
                hit = diag_level == lev
                weight = jnp.where(hit, gi[lev : lev + 1, :], weight)
                gg_ref[lev : lev + 1, ts] += jnp.sum(
                    jnp.where(hit, prod, 0.0), axis=0, keepdims=True
                )
        probs = (scores * weight).astype(jnp.bfloat16)
        dprobs = (back * weight).astype(jnp.bfloat16)
        o_ref[ts, :] += dot_tn(probs, vj)
        dq_ref[ts, :] += dot_tn(dprobs, kj)
        dk_ref[ss, :] += dot_nn(dprobs, qi)
        dv_ref[ss, :] += dot_nn(probs, doi)

    for i in range(tiles):
        for j in range(i):
            pair(i * TILE, j * TILE, TILE, log_tile + (i ^ j).bit_length())
        for a in range(TILE // SUB):
            for b in range(a):
                pair(i * TILE + a * SUB, i * TILE + b * SUB, SUB, log_sub + (a ^ b).bit_length())
            pair(i * TILE + a * SUB, i * TILE + a * SUB, SUB, None)
    gg_ref[...] = gg_ref[...] * g_ref[...]


def local_part(query_rows, key_rows, value_rows, out_grad, gate_t):
    heads, block_len, width = query_rows.shape
    nlev = gate_t.shape[1]
    f32 = jnp.float32
    pairs = (block_len // TILE) * (block_len // TILE + 1) // 2
    flops = pairs * 6 * 2 * TILE * TILE * width
    shapes = [jax.ShapeDtypeStruct((heads, block_len, width), f32)] * 4 + [
        jax.ShapeDtypeStruct((heads, nlev, block_len), f32)
    ]
    outs = None
    for h in range(heads):
        row_spec = pl.BlockSpec((None, block_len, width), lambda i, h=h: (h, 0, 0))
        gate_spec = pl.BlockSpec((None, nlev, block_len), lambda i, h=h: (h, 0, 0))
        args = (query_rows, key_rows, value_rows, out_grad, gate_t)
        in_specs = [row_spec] * 4 + [gate_spec]
        aliases = {}
        if outs is not None:
            args = args + tuple(outs)
            in_specs = in_specs + [pl.BlockSpec(memory_space=pl.ANY)] * 5
            aliases = {5 + n: n for n in range(5)}
        outs = pl.pallas_call(
            local_kernel,
            grid=(1,),
            in_specs=in_specs,
            out_specs=[row_spec] * 4 + [gate_spec],
            out_shape=shapes,
            input_output_aliases=aliases,
            compiler_params=pltpu.CompilerParams(dimension_semantics=("arbitrary",)),
            cost_estimate=pl.CostEstimate(
                flops=flops,
                transcendentals=0,
                bytes_accessed=block_len * (4 * width * 2 + 4 * width * 4 + 2 * nlev * 4),
            ),
        )(*args)
    return outs


def final_kernel(q_ref, k_ref, v_ref, do_ref, o_ref, dq_ref, dk_ref, dv_ref, ggl_ref, g_ref,
                 ls_ref, ks_ref, attn_ref, gq_ref, gk_ref, gv_ref, gg_ref):
    block_len = q_ref.shape[0]
    nlev = g_ref.shape[0]
    nbits = ls_ref.shape[0]
    first = nlev - nbits
    gate_cols = jnp.transpose(g_ref[...])
    key_state = ks_ref[...]
    lane = lax.broadcasted_iota(jnp.int32, (TILE, nlev), 1)
    cross_parts = []
    for i in range(block_len // TILE):
        ts = pl.ds(i * TILE, TILE)
        qi = q_ref[ts, :]
        doi = do_ref[ts, :]
        do_f = doi.astype(jnp.float32)
        attn = o_ref[ts, :]
        grad_q = dq_ref[ts, :]
        cross = jnp.zeros((TILE, nlev), jnp.float32)
        for b in range(nbits):
            state = ls_ref[b]
            weight = gate_cols[i * TILE : (i + 1) * TILE, first + b : first + b + 1]
            level_out = dot_nn(qi, state)
            level_back = dot_nt(doi, state)
            attn = attn + weight * level_out
            grad_q = grad_q + weight * level_back
            dotted = jnp.sum(level_out * do_f, axis=1, keepdims=True)
            cross = jnp.where(lane == first + b, weight * dotted, cross)
        attn_ref[ts, :] = attn.astype(attn_ref.dtype)
        gq_ref[ts, :] = grad_q.astype(gq_ref.dtype)
        gk_ref[ts, :] = (dk_ref[ts, :] + dot_nt(v_ref[ts, :], key_state)).astype(gk_ref.dtype)
        gv_ref[ts, :] = (dv_ref[ts, :] + dot_nn(k_ref[ts, :], key_state)).astype(gv_ref.dtype)
        cross_parts.append(cross)
    cross_all = jnp.concatenate(cross_parts, axis=0)
    gg_ref[...] = ggl_ref[...] + jnp.transpose(cross_all)


def final_part(query_rows, key_rows, value_rows, out_grad, partials, gate_t, level_state, key_state):
    heads, block_len, width = query_rows.shape
    nlev = gate_t.shape[1]
    nbits = level_state.shape[0]
    row_spec = pl.BlockSpec((None, block_len, width), lambda h: (h, 0, 0))
    gate_spec = pl.BlockSpec((None, nlev, block_len), lambda h: (h, 0, 0))
    ls_spec = pl.BlockSpec((nbits, None, width, width), lambda h: (0, h, 0, 0))
    ks_spec = pl.BlockSpec((None, width, width), lambda h: (h, 0, 0))
    bf = jnp.bfloat16
    return pl.pallas_call(
        final_kernel,
        grid=(heads,),
        in_specs=[row_spec] * 8 + [gate_spec, gate_spec, ls_spec, ks_spec],
        out_specs=[row_spec] * 4 + [gate_spec],
        out_shape=[jax.ShapeDtypeStruct((heads, block_len, width), bf)] * 4
        + [jax.ShapeDtypeStruct((heads, nlev, block_len), jnp.float32)],
        compiler_params=pltpu.CompilerParams(dimension_semantics=("arbitrary",)),
        cost_estimate=pl.CostEstimate(
            flops=heads * block_len * width * width * 2 * (2 * nbits + 2),
            transcendentals=0,
            bytes_accessed=heads * block_len * (8 * width * 2 + 4 * width * 4 + 4 * nlev * 4),
        ),
    )(query_rows, key_rows, value_rows, out_grad, *partials[:4], partials[4], gate_t,
      level_state, key_state)


def same_doc(block_levels, earlier, later):
    return block_levels[later, earlier] >= 0


def level_network(state, block_levels, me, nbits, ctx_len):
    x = state
    levels = []
    for k in range(nbits):
        bit = ((me >> k) & 1) == 1
        lo = (me >> (k + 1)) << (k + 1)
        end_low = lo + (1 << k) - 1
        end_high = lo + (2 << k) - 1
        joined = same_doc(block_levels, end_low, end_high)
        mine = same_doc(block_levels, end_low, me)
        if k < nbits - 1:
            perm = [(j, j ^ (1 << k)) for j in range(ctx_len)]
        else:
            perm = [(j, j ^ (1 << k)) for j in range(ctx_len) if not (j >> k) & 1]
        got = lax.ppermute(x, "ctx", perm)
        levels.append(jnp.where(bit & mine, got, 0.0).astype(jnp.bfloat16))
        if k < nbits - 1:
            x = jnp.where(
                bit, x + jnp.where(joined, got, 0.0), got + jnp.where(joined, x, 0.0)
            )
    return jnp.stack(levels)


def key_network(grad_state, block_levels, me, nbits, ctx_len):
    acc = None
    for k in reversed(range(nbits)):
        bit = ((me >> k) & 1) == 1
        lo = (me >> (k + 1)) << (k + 1)
        end_low = lo + (1 << k) - 1
        end_high = lo + (2 << k) - 1
        joined = same_doc(block_levels, end_low, end_high)
        mine = same_doc(block_levels, end_low, me)
        term = jnp.where(bit & mine, grad_state[k], 0.0)
        if acc is None:
            send = term
            own = None
            perm = [(j, j ^ (1 << k)) for j in range(ctx_len) if (j >> k) & 1]
        else:
            kept = jnp.where(joined, acc, 0.0)
            send = jnp.where(bit, term + kept, acc)
            own = jnp.where(bit, acc, kept)
            perm = [(j, j ^ (1 << k)) for j in range(ctx_len)]
        got = lax.ppermute(send, "ctx", perm)
        acc = got if own is None else own + got
    return acc


def per_device(query_rows, key_rows, value_rows, out_grad, level_gate, block_levels, ctx_len):
    level_total = level_gate.shape[0]
    block_len = query_rows.shape[1]
    log_block = block_len.bit_length() - 1
    nbits = level_total - log_block - 1
    me = lax.axis_index("ctx")
    weights = jnp.exp(level_gate)
    cross_weight = weights[log_block + 1 :]

    own_state = jnp.einsum(
        "hcd,hce->hde", key_rows, value_rows, preferred_element_type=jnp.float32
    ).astype(jnp.bfloat16)
    scaled = (cross_weight[..., None] * out_grad[None].astype(jnp.float32)).astype(jnp.bfloat16)
    grad_state = jnp.einsum(
        "hcd,bhce->bhde", query_rows, scaled, preferred_element_type=jnp.float32
    ).astype(jnp.bfloat16)

    level_state = level_network(
        own_state.astype(jnp.float32), block_levels, me, nbits, ctx_len
    )
    key_state = key_network(
        grad_state.astype(jnp.float32), block_levels, me, nbits, ctx_len
    ).astype(jnp.bfloat16)

    gate_t = weights.transpose(1, 0, 2)
    partials = local_part(query_rows, key_rows, value_rows, out_grad, gate_t)
    attn, grad_q, grad_k, grad_v, grad_gate = final_part(
        query_rows, key_rows, value_rows, out_grad, partials, gate_t, level_state, key_state
    )
    return (attn, grad_q, grad_k, grad_v, grad_gate.transpose(1, 0, 2))


def solution(mesh):
    ctx_len = mesh.shape["ctx"]
    in_specs = (
        P("head", "ctx", None),
        P("head", "ctx", None),
        P("head", "ctx", None),
        P("head", "ctx", None),
        P(None, "head", "ctx"),
        P(),
    )
    out_specs = (
        P("head", "ctx", None),
        P("head", "ctx", None),
        P("head", "ctx", None),
        P("head", "ctx", None),
        P(None, "head", "ctx"),
    )

    def body(*args):
        return per_device(*args, ctx_len=ctx_len)

    return jax.shard_map(
        body, mesh=mesh, in_specs=in_specs, out_specs=out_specs, check_vma=False
    )
```

time: 138 us -> 109 us (0.79)
  the two profiles are of different devices: /device:TPU:1 before, /device:TPU:4 now
where the time goes in v2:
time: 109 us
  Pallas kernels  47.4 us (43%)
  waiting for transfers between devices  31.3 us (29%)
  starting transfers between devices  12.7 us (12%)
  local copies, waits for them, and re-layouts  7.04 us (6%)
  between operations  6.5 us (6%)
  matrix products  2.23 us (2%)
  other arithmetic  1.57 us (1%)
    pallas_call x4, Pallas kernels, local_part(): pl.pallas_call(local_kernel, grid=(1,), in_specs=in_specs, out_specs=[row...  33.7 us
    ppermute x5, waiting for transfers between devices, key_network(): got = lax.ppermute(send, 'ctx', perm)  16.5 us
    ppermute x5, waiting for transfers between devices, level_network(): got = lax.ppermute(x, 'ctx', perm)  14.8 us
    pallas_call x1, Pallas kernels, final_part(): pl.pallas_call(final_kernel, grid=(heads,), in_specs=[row_spec] * 8 + [ga...  13.7 us
    ppermute x5, starting transfers between devices, key_network(): got = lax.ppermute(send, 'ctx', perm)  6.94 us
    ppermute x5, starting transfers between devices, level_network(): got = lax.ppermute(x, 'ctx', perm)  5.75 us
  transfers between devices with their start and end apart: 10, of which 6 were waited for; matrix products, arithmetic and copies ran while one was open for 1% of the time, Pallas kernels for 31%

profile of v2, /device:TPU:4, one launch (start us, length us, event | category | flops | bytes accessed | tf_op | source)
XLA Modules:
  0.0 108.7 jit_solution(13837423502179655611)
XLA Ops:
  0.6 0.0 copy-start.2
  0.7 1.9 %copy_exponential_fusion = (f32[16,4,1024]{2,0,1:T(8,128)S(1)}, f32[4,16,1024]{2,1,0:T(8,128)}) fusion(f32[16,4,1024]{2,1,0:T(4,128)} %param.10), kind=kLoop, calls=%fused_computation.36 | loop fusion | bytes 786432 | tf_op jit(solution)/shard_map/exp | solution.py:241
  2.6 1.5 %copy.28 = f32[4,1024,128]{1,2,0:T(8,128)S(1)} copy(bf16[4,1024,128]{2,1,0:T(8,128)(2,1)} %do_ref.9) | data formatting | bytes 3145728 | tf_op jit(solution)/shard_map/convert_element_type | solution.py:247
  4.1 1.7 %fusion.39 = (s32[1,1]{1,0:T(1,128)}, s32[1,1]{1,0:T(1,128)}, s32[1,1]{1,0:T(1,128)}, s32[1,1]{1,0:T(1,128)}, s32[1,1]{1,0:T(1,128)}, /*index=5*/s32[1,1]{1,0:T(...) fusion(s32[32,32]{1,0:T(8,128)} %param.11, s32[]{:T(128)S(6)} %select_n.247, s32[]{:T(128)S(6)} %select_n.278, ...), kind=kLoop, calls=%fused_computation.57 | loop fusion | bytes 112 | tf_op jit(solution)/shard_map/dynamic_slice | solution.py:185
  6.4 0.0 copy-done.2
  6.4 0.0 copy-start
  6.4 0.0 copy-start.1
  6.5 1.7 %fusion.8 = f32[5,4,128,128]{3,2,1,0:T(8,128)S(1)} fusion(bf16[4,1024,128]{2,1,0:T(8,128)(2,1)S(1)} %copy-done.2, f32[4,1024,128]{1,2,0:T(8,128)S(1)} %copy.28, f32[5,4,1024]{2,0,1:T(8,128)S(1)} %slice.24), kind=kOutput, calls=%fused_computation.5 | convolution fusion | flops 676986880 | bytes 4538368 | tf_op jit(solution)/shard_map/hcd,bhce->bhde/dot_general | solution.py:248
  8.2 0.0 copy-start.3
  8.2 4.2 %collective-permute-start.5 = (f32[4,128,128]{2,1,0:T(8,128)S(1)}, f32[4,128,128]{2,1,0:T(8,128)S(1)}, u32[]{:S(2)}, u32[]{:S(2)}) collective-permute-start(f32[4,128,128]{2,1,0:T(8,128)S(1)} %fusion.26), channel_id=1, source_target_pairs={{128,0},{136,8},{144,16},{152,24},{160,32},{168,40},{176,48},{184,... | collective-permute-start | bytes 786440 | tf_op jit(solution)/shard_map/ppermute | solution.py:230
  12.4 0.0 copy-done
  12.4 0.0 copy-done.1
  12.4 0.5 fusion.11
  12.9 0.0 copy-done.3
  12.9 0.3 collective-permute-start
  13.2 8.3 %shard_map.101 = (f32[4,1024,128]{2,1,0:T(8,128)}, f32[4,1024,128]{2,1,0:T(8,128)}, f32[4,1024,128]{2,1,0:T(8,128)}, f32[4,1024,128]{2,1,0:T(8,128)}, f32[4,16,1024]{2,1,0:T(8,128)}) custom-call(bf16[4,1024,128]{2,1,0:T(8,128)(2,1)} %q_ref.9, bf16[4,1024,128]{2,1,0:T(8,128)(2,1)} %k_ref.9, bf16[4,1024,128]{2,1,0:T(8,128)(2,1)} %v_ref.9, ...), custom_call_target="tpu_custom_call" | custom-call | flops 1006632960 | bytes 3276800 | tf_op jit(solution)/shard_map/pallas_call | solution.py:105
  21.5 8.3 %shard_map.102 = (f32[4,1024,128]{2,1,0:T(8,128)}, f32[4,1024,128]{2,1,0:T(8,128)}, f32[4,1024,128]{2,1,0:T(8,128)}, f32[4,1024,128]{2,1,0:T(8,128)}, f32[4,16,1024]{2,1,0:T(8,128)}) custom-call(bf16[4,1024,128]{2,1,0:T(8,128)(2,1)} %q_ref.9, ...), custom_call_target="tpu_custom_call", output_to_operand_aliasing={{0}: (5, {}), {1}: (6, {}), {2}: (7, {}), {3}: (8, {}), {4}... | custom-call | flops 1006632960 | bytes 3276800 | tf_op jit(solution)/shard_map/pallas_call | solution.py:105
  29.9 8.5 %shard_map.103 = (f32[4,1024,128]{2,1,0:T(8,128)}, f32[4,1024,128]{2,1,0:T(8,128)}, f32[4,1024,128]{2,1,0:T(8,128)}, f32[4,1024,128]{2,1,0:T(8,128)}, f32[4,16,1024]{2,1,0:T(8,128)}) custom-call(bf16[4,1024,128]{2,1,0:T(8,128)(2,1)} %q_ref.9, ...), custom_call_target="tpu_custom_call", output_to_operand_aliasing={{0}: (5, {}), {1}: (6, {}), {2}: (7, {}), {3}: (8, {}), {4}... | custom-call | flops 1006632960 | bytes 3276800 | tf_op jit(solution)/shard_map/pallas_call | solution.py:105
  38.4 0.0 copy-start.4
  38.4 8.5 %shard_map.104 = (f32[4,1024,128]{2,1,0:T(8,128)}, f32[4,1024,128]{2,1,0:T(8,128)}, f32[4,1024,128]{2,1,0:T(8,128)}, f32[4,1024,128]{2,1,0:T(8,128)}, f32[4,16,1024]{2,1,0:T(8,128)}) custom-call(bf16[4,1024,128]{2,1,0:T(8,128)(2,1)} %q_ref.9, ...), custom_call_target="tpu_custom_call", output_to_operand_aliasing={{0}: (5, {}), {1}: (6, {}), {2}: (7, {}), {3}: (8, {}), {4}... | custom-call | flops 1006632960 | bytes 3276800 | tf_op jit(solution)/shard_map/pallas_call | solution.py:105
  51.9 0.0 collective-permute-done.5
  51.9 0.0 copy-done.4
  52.0 0.5 collective-permute-start.6
  52.4 0.0 collective-permute-done
  52.5 1.7 %collective-permute-start.1 = (f32[4,128,128]{2,1,0:T(8,128)S(1)}, f32[4,128,128]{2,1,0:T(8,128)S(1)}, u32[]{:S(2)}, u32[]{:S(2)}) collective-permute-start(f32[4,128,128]{2,1,0:T(8,128)S(1)} %add_select_fusion.3), channel_id=1, source_target_pairs={{0,16},{8,24},{16,0},{24,8},{32,48},{40,56},{48,32},{56,40},{64,80... | collective-permute-start | bytes 786440 | tf_op jit(solution)/shard_map/ppermute | solution.py:202
  54.2 6.6 %collective-permute-done.6 = f32[4,128,128]{2,1,0:T(8,128)S(1)} collective-permute-done((f32[4,128,128]{2,1,0:T(8,128)S(1)}, f32[4,128,128]{2,1,0:T(8,128)S(1)}, u32[]{:S(2)}, u32[]{:S(2)}) %collective-permute-start.6) | collective-permute-done | bytes 262176 | tf_op jit(solution)/shard_map/ppermute | solution.py:230
  60.8 0.1 fusion.15
  60.8 1.9 %collective-permute-start.7 = (f32[4,128,128]{2,1,0:T(8,128)S(1)}, f32[4,128,128]{2,1,0:T(8,128)S(1)}, u32[]{:S(2)}, u32[]{:S(2)}) collective-permute-start(f32[4,128,128]{2,1,0:T(8,128)S(1)} %fusion.15), channel_id=1, source_target_pairs={{0,32},{8,40},{16,48},{24,56},{32,0},{40,8},{48,16},{56,24},{64,96... | collective-permute-start | bytes 786440 | tf_op jit(solution)/shard_map/ppermute | solution.py:230
  62.8 0.0 collective-permute-done.1
  62.8 1.8 %collective-permute-start.2 = (f32[4,128,128]{2,1,0:T(8,128)S(1)}, f32[4,128,128]{2,1,0:T(8,128)S(1)}, u32[]{:S(2)}, u32[]{:S(2)}) collective-permute-start(f32[4,128,128]{2,1,0:T(8,128)S(1)} %add_select_fusion.2), channel_id=1, source_target_pairs={{0,32},{8,40},{16,48},{24,56},{32,0},{40,8},{48,16},{56,24},{64,96... | collective-permute-start | bytes 786440 | tf_op jit(solution)/shard_map/ppermute | solution.py:202
  64.6 7.0 %collective-permute-done.7 = f32[4,128,128]{2,1,0:T(8,128)S(1)} collective-permute-done((f32[4,128,128]{2,1,0:T(8,128)S(1)}, f32[4,128,128]{2,1,0:T(8,128)S(1)}, u32[]{:S(2)}, u32[]{:S(2)}) %collective-permute-start.7) | collective-permute-done | bytes 262176 | tf_op jit(solution)/shard_map/ppermute | solution.py:230
  71.6 0.1 fusion.14
  71.7 0.3 collective-permute-start.8
  72.0 5.2 %collective-permute-done.2 = f32[4,128,128]{2,1,0:T(8,128)S(1)} collective-permute-done((f32[4,128,128]{2,1,0:T(8,128)S(1)}, f32[4,128,128]{2,1,0:T(8,128)S(1)}, u32[]{:S(2)}, u32[]{:S(2)}) %collective-permute-start.2) | collective-permute-done | bytes 262176 | tf_op jit(solution)/shard_map/ppermute | solution.py:202
  77.3 0.5 collective-permute-start.3
  77.8 2.9 %collective-permute-done.8 = f32[4,128,128]{2,1,0:T(8,128)S(1)} collective-permute-done((f32[4,128,128]{2,1,0:T(8,128)S(1)}, f32[4,128,128]{2,1,0:T(8,128)S(1)}, u32[]{:S(2)}, u32[]{:S(2)}) %collective-permute-start.8) | collective-permute-done | bytes 262176 | tf_op jit(solution)/shard_map/ppermute | solution.py:230
  80.8 0.1 fusion.13
  80.8 0.1 collective-permute-start.9
  80.9 2.8 %collective-permute-done.3 = f32[4,128,128]{2,1,0:T(8,128)S(1)} collective-permute-done((f32[4,128,128]{2,1,0:T(8,128)S(1)}, f32[4,128,128]{2,1,0:T(8,128)S(1)}, u32[]{:S(2)}, u32[]{:S(2)}) %collective-permute-start.3) | collective-permute-done | bytes 262176 | tf_op jit(solution)/shard_map/ppermute | solution.py:202
  83.8 0.1 add_select_fusion
  83.8 1.6 %collective-permute-start.4 = (bf16[4,128,128]{2,1,0:T(8,128)(2,1)S(1)}, bf16[4,128,128]{2,1,0:T(8,128)(2,1)S(1)}, u32[]{:S(2)}, u32[]{:S(2)}) collective-permute-start(bf16[4,128,128]{2,1,0:T(8,128)(2,1)S(1)} %add_select_fusion), channel_id=1, source_target_pairs={{0,128},{8,136},{16,144},{24,152},{32,160},{40,168},{48,176},{56,1... | collective-permute-start | bytes 393224 | tf_op jit(solution)/shard_map/ppermute | solution.py:202
  85.4 6.8 %collective-permute-done.4 = bf16[4,128,128]{2,1,0:T(8,128)(2,1)S(1)} collective-permute-done((bf16[4,128,128]{2,1,0:T(8,128)(2,1)S(1)}, bf16[4,128,128]{2,1,0:T(8,128)(2,1)S(1)}, u32[]{:S(2)}, u32[]{:S(2)}) %collective-permute-start.4) | collective-permute-done | bytes 131104 | tf_op jit(solution)/shard_map/ppermute | solution.py:202
  92.2 0.0 copy-start.5
  92.2 0.0 collective-permute-done.9
  92.3 0.9 fusion.21.ks_ref
  93.1 0.1 copy-done.5
  93.2 13.7 %shard_map.105 = (bf16[4,1024,128]{2,1,0:T(8,128)(2,1)}, bf16[4,1024,128]{2,1,0:T(8,128)(2,1)}, bf16[4,1024,128]{2,1,0:T(8,128)(2,1)}, bf16[4,1024,128]{2,1,0:T(8,128)(2,1)}, f32[4,16,1024]{2,1,0:T(8,128)}) custom-call(bf16[4,1024,128]{2,1,0:T(8,128)(2,1)} %q_ref.9, bf16[4,1024,128]{2,1,0:T(8,128)(2,1)} %k_ref.9, bf16[4,1024,128]{2,1,0:T(8,128)(2,1)} %v_ref.9, ...), custom_call_target="tpu_custom_call" | custom-call | flops 1610612736 | bytes 17825792 | tf_op jit(solution)/shard_map/pallas_call | solution.py:167
  106.9 1.8 %copy.30 = f32[16,4,1024]{2,1,0:T(4,128)} copy(f32[16,4,1024]{2,0,1:T(8,128)} %bitcast.57) | data formatting | bytes 524288
  (11 shorter events, 0.4 us)
Async XLA Ops:
  0.6 5.8 %copy-start.2 = (bf16[4,1024,128]{2,1,0:T(8,128)(2,1)S(1)}, bf16[4,1024,128]{2,1,0:T(8,128)(2,1)}, u32[]{:S(2)}) copy-start(bf16[4,1024,128]{2,1,0:T(8,128)(2,1)} %q_ref.9) | copy-start | bytes 3145732
  6.4 6.0 %copy-start = (bf16[4,1024,128]{2,1,0:T(8,128)(2,1)S(1)}, bf16[4,1024,128]{2,1,0:T(8,128)(2,1)}, u32[]{:S(2)}) copy-start(bf16[4,1024,128]{2,1,0:T(8,128)(2,1)} %k_ref.9) | copy-start | bytes 3145732
  6.4 6.0 %copy-start.1 = (bf16[4,1024,128]{2,1,0:T(8,128)(2,1)S(1)}, bf16[4,1024,128]{2,1,0:T(8,128)(2,1)}, u32[]{:S(2)}) copy-start(bf16[4,1024,128]{2,1,0:T(8,128)(2,1)} %v_ref.9) | copy-start | bytes 3145732
  8.2 4.7 %copy-start.3 = (f32[5,4,128,128]{3,2,1,0:T(8,128)}, f32[5,4,128,128]{3,2,1,0:T(8,128)S(1)}, u32[]{:S(2)}) copy-start(f32[5,4,128,128]{3,2,1,0:T(8,128)S(1)} %fusion.8) | copy-start | bytes 3932164
  8.2 43.7 %collective-permute-start.5 = (f32[4,128,128]{2,1,0:T(8,128)S(1)}, f32[4,128,128]{2,1,0:T(8,128)S(1)}, u32[]{:S(2)}, u32[]{:S(2)}) collective-permute-start(f32[4,128,128]{2,1,0:T(8,128)S(1)} %fusion.26), channel_id=1, source_target_pairs={{128,0},{136,8},{144,16},{152,24},{160,32},{168,40},{176,48},{184,... | collective-permute-start | bytes 786440 | tf_op jit(solution)/shard_map/ppermute | solution.py:230
  12.9 39.5 %collective-permute-start = (f32[4,128,128]{2,1,0:T(8,128)S(1)}, f32[4,128,128]{2,1,0:T(8,128)S(1)}, u32[]{:S(2)}, u32[]{:S(2)}) collective-permute-start(f32[4,128,128]{2,1,0:T(8,128)S(1)} %fusion.11), channel_id=1, source_target_pairs={{0,8},{8,0},{16,24},{24,16},{32,40},{40,32},{48,56},{56,48},{64,72... | collective-permute-start | bytes 786440 | tf_op jit(solution)/shard_map/ppermute | solution.py:202
  38.4 13.5 %copy-start.4 = (f32[5,4,128,128]{3,2,1,0:T(8,128)S(1)}, f32[5,4,128,128]{3,2,1,0:T(8,128)}, u32[]{:S(2)}) copy-start(f32[5,4,128,128]{3,2,1,0:T(8,128)} %copy-done.3) | copy-start | bytes 3932164
  52.0 8.8 %collective-permute-start.6 = (f32[4,128,128]{2,1,0:T(8,128)S(1)}, f32[4,128,128]{2,1,0:T(8,128)S(1)}, u32[]{:S(2)}, u32[]{:S(2)}) collective-permute-start(f32[4,128,128]{2,1,0:T(8,128)S(1)} %fusion.16), channel_id=1, source_target_pairs={{0,64},{8,72},{16,80},{24,88},{32,96},{40,104},{48,112},{56,120},{... | collective-permute-start | bytes 786440 | tf_op jit(solution)/shard_map/ppermute | solution.py:230
  52.5 10.3 %collective-permute-start.1 = (f32[4,128,128]{2,1,0:T(8,128)S(1)}, f32[4,128,128]{2,1,0:T(8,128)S(1)}, u32[]{:S(2)}, u32[]{:S(2)}) collective-permute-start(f32[4,128,128]{2,1,0:T(8,128)S(1)} %add_select_fusion.3), channel_id=1, source_target_pairs={{0,16},{8,24},{16,0},{24,8},{32,48},{40,56},{48,32},{56,40},{64,80... | collective-permute-start | bytes 786440 | tf_op jit(solution)/shard_map/ppermute | solution.py:202
  60.8 10.8 %collective-permute-start.7 = (f32[4,128,128]{2,1,0:T(8,128)S(1)}, f32[4,128,128]{2,1,0:T(8,128)S(1)}, u32[]{:S(2)}, u32[]{:S(2)}) collective-permute-start(f32[4,128,128]{2,1,0:T(8,128)S(1)} %fusion.15), channel_id=1, source_target_pairs={{0,32},{8,40},{16,48},{24,56},{32,0},{40,8},{48,16},{56,24},{64,96... | collective-permute-start | bytes 786440 | tf_op jit(solution)/shard_map/ppermute | solution.py:230
  62.8 14.4 %collective-permute-start.2 = (f32[4,128,128]{2,1,0:T(8,128)S(1)}, f32[4,128,128]{2,1,0:T(8,128)S(1)}, u32[]{:S(2)}, u32[]{:S(2)}) collective-permute-start(f32[4,128,128]{2,1,0:T(8,128)S(1)} %add_select_fusion.2), channel_id=1, source_target_pairs={{0,32},{8,40},{16,48},{24,56},{32,0},{40,8},{48,16},{56,24},{64,96... | collective-permute-start | bytes 786440 | tf_op jit(solution)/shard_map/ppermute | solution.py:202
  71.7 9.0 %collective-permute-start.8 = (f32[4,128,128]{2,1,0:T(8,128)S(1)}, f32[4,128,128]{2,1,0:T(8,128)S(1)}, u32[]{:S(2)}, u32[]{:S(2)}) collective-permute-start(f32[4,128,128]{2,1,0:T(8,128)S(1)} %get-tuple-element.60), channel_id=1, source_target_pairs={{0,16},{8,24},{16,0},{24,8},{32,48},{40,56},{48,32},{56,40},{64,80... | collective-permute-start | bytes 786440 | tf_op jit(solution)/shard_map/ppermute | solution.py:230
  77.3 6.5 %collective-permute-start.3 = (f32[4,128,128]{2,1,0:T(8,128)S(1)}, f32[4,128,128]{2,1,0:T(8,128)S(1)}, u32[]{:S(2)}, u32[]{:S(2)}) collective-permute-start(f32[4,128,128]{2,1,0:T(8,128)S(1)} %add_select_fusion.1), channel_id=1, source_target_pairs={{0,64},{8,72},{16,80},{24,88},{32,96},{40,104},{48,112},{56,120},{... | collective-permute-start | bytes 786440 | tf_op jit(solution)/shard_map/ppermute | solution.py:202
  80.8 11.4 %collective-permute-start.9 = (f32[4,128,128]{2,1,0:T(8,128)S(1)}, f32[4,128,128]{2,1,0:T(8,128)S(1)}, u32[]{:S(2)}, u32[]{:S(2)}) collective-permute-start(f32[4,128,128]{2,1,0:T(8,128)S(1)} %fusion.13), channel_id=1, source_target_pairs={{0,8},{8,0},{16,24},{24,16},{32,40},{40,32},{48,56},{56,48},{64,72... | collective-permute-start | bytes 786440 | tf_op jit(solution)/shard_map/ppermute | solution.py:230
  83.8 8.4 %collective-permute-start.4 = (bf16[4,128,128]{2,1,0:T(8,128)(2,1)S(1)}, bf16[4,128,128]{2,1,0:T(8,128)(2,1)S(1)}, u32[]{:S(2)}, u32[]{:S(2)}) collective-permute-start(bf16[4,128,128]{2,1,0:T(8,128)(2,1)S(1)} %add_select_fusion), channel_id=1, source_target_pairs={{0,128},{8,136},{16,144},{24,152},{32,160},{40,168},{48,176},{56,1... | collective-permute-start | bytes 393224 | tf_op jit(solution)/shard_map/ppermute | solution.py:202
  92.2 1.0 copy-start.5

commit v3 on v2

--- a/solution.py
+++ b/solution.py
@@ -82,7 +82,7 @@
     gg_ref[...] = gg_ref[...] * g_ref[...]
 
 
-def local_part(query_rows, key_rows, value_rows, out_grad, gate_t):
+def local_part(query_rows, key_rows, value_rows, out_grad, gate_t, h, outs):
     heads, block_len, width = query_rows.shape
     nlev = gate_t.shape[1]
     f32 = jnp.float32
@@ -91,32 +91,29 @@
     shapes = [jax.ShapeDtypeStruct((heads, block_len, width), f32)] * 4 + [
         jax.ShapeDtypeStruct((heads, nlev, block_len), f32)
     ]
-    outs = None
-    for h in range(heads):
-        row_spec = pl.BlockSpec((None, block_len, width), lambda i, h=h: (h, 0, 0))
-        gate_spec = pl.BlockSpec((None, nlev, block_len), lambda i, h=h: (h, 0, 0))
-        args = (query_rows, key_rows, value_rows, out_grad, gate_t)
-        in_specs = [row_spec] * 4 + [gate_spec]
-        aliases = {}
-        if outs is not None:
-            args = args + tuple(outs)
-            in_specs = in_specs + [pl.BlockSpec(memory_space=pl.ANY)] * 5
-            aliases = {5 + n: n for n in range(5)}
-        outs = pl.pallas_call(
-            local_kernel,
-            grid=(1,),
-            in_specs=in_specs,
-            out_specs=[row_spec] * 4 + [gate_spec],
-            out_shape=shapes,
-            input_output_aliases=aliases,
-            compiler_params=pltpu.CompilerParams(dimension_semantics=("arbitrary",)),
-            cost_estimate=pl.CostEstimate(
-                flops=flops,
-                transcendentals=0,
-                bytes_accessed=block_len * (4 * width * 2 + 4 * width * 4 + 2 * nlev * 4),
-            ),
-        )(*args)
-    return outs
+    row_spec = pl.BlockSpec((None, block_len, width), lambda i: (h, 0, 0))
+    gate_spec = pl.BlockSpec((None, nlev, block_len), lambda i: (h, 0, 0))
+    args = (query_rows, key_rows, value_rows, out_grad, gate_t)
+    in_specs = [row_spec] * 4 + [gate_spec]
+    aliases = {}
+    if outs is not None:
+        args = args + tuple(outs)
+        in_specs = in_specs + [pl.BlockSpec(memory_space=pl.ANY)] * 5
+        aliases = {5 + n: n for n in range(5)}
+    return pl.pallas_call(
+        local_kernel,
+        grid=(1,),
+        in_specs=in_specs,
+        out_specs=[row_spec] * 4 + [gate_spec],
+        out_shape=shapes,
+        input_output_aliases=aliases,
+        compiler_params=pltpu.CompilerParams(dimension_semantics=("arbitrary",)),
+        cost_estimate=pl.CostEstimate(
+            flops=flops,
+            transcendentals=0,
+            bytes_accessed=block_len * (4 * width * 2 + 4 * width * 4 + 2 * nlev * 4),
+        ),
+    )(*args)
 
 
 def final_kernel(q_ref, k_ref, v_ref, do_ref, o_ref, dq_ref, dk_ref, dv_ref, ggl_ref, g_ref,
@@ -185,51 +182,22 @@
     return block_levels[later, earlier] >= 0
 
 
-def level_network(state, block_levels, me, nbits, ctx_len):
-    x = state
-    levels = []
-    for k in range(nbits):
-        bit = ((me >> k) & 1) == 1
-        lo = (me >> (k + 1)) << (k + 1)
-        end_low = lo + (1 << k) - 1
-        end_high = lo + (2 << k) - 1
-        joined = same_doc(block_levels, end_low, end_high)
-        mine = same_doc(block_levels, end_low, me)
-        if k < nbits - 1:
-            perm = [(j, j ^ (1 << k)) for j in range(ctx_len)]
-        else:
-            perm = [(j, j ^ (1 << k)) for j in range(ctx_len) if not (j >> k) & 1]
-        got = lax.ppermute(x, "ctx", perm)
-        levels.append(jnp.where(bit & mine, got, 0.0).astype(jnp.bfloat16))
-        if k < nbits - 1:
-            x = jnp.where(
-                bit, x + jnp.where(joined, got, 0.0), got + jnp.where(joined, x, 0.0)
-            )
-    return jnp.stack(levels)
-
-
-def key_network(grad_state, block_levels, me, nbits, ctx_len):
-    acc = None
-    for k in reversed(range(nbits)):
-        bit = ((me >> k) & 1) == 1
-        lo = (me >> (k + 1)) << (k + 1)
-        end_low = lo + (1 << k) - 1
-        end_high = lo + (2 << k) - 1
-        joined = same_doc(block_levels, end_low, end_high)
-        mine = same_doc(block_levels, end_low, me)
-        term = jnp.where(bit & mine, grad_state[k], 0.0)
-        if acc is None:
-            send = term
-            own = None
-            perm = [(j, j ^ (1 << k)) for j in range(ctx_len) if (j >> k) & 1]
-        else:
-            kept = jnp.where(joined, acc, 0.0)
-            send = jnp.where(bit, term + kept, acc)
-            own = jnp.where(bit, acc, kept)
-            perm = [(j, j ^ (1 << k)) for j in range(ctx_len)]
-        got = lax.ppermute(send, "ctx", perm)
-        acc = got if own is None else own + got
-    return acc
+def step_masks(block_levels, me, k):
+    bit = ((me >> k) & 1) == 1
+    lo = (me >> (k + 1)) << (k + 1)
+    end_low = lo + (1 << k) - 1
+    end_high = lo + (2 << k) - 1
+    joined = same_doc(block_levels, end_low, end_high)
+    mine = same_doc(block_levels, end_low, me)
+    return bit, joined, mine
+
+
+def pairs_of(k, ctx_len, sender_bit=None):
+    return [
+        (j, j ^ (1 << k))
+        for j in range(ctx_len)
+        if sender_bit is None or ((j >> k) & 1) == sender_bit
+    ]
 
 
 def per_device(query_rows, key_rows, value_rows, out_grad, level_gate, block_levels, ctx_len):
@@ -249,15 +217,44 @@
         "hcd,bhce->bhde", query_rows, scaled, preferred_element_type=jnp.float32
     ).astype(jnp.bfloat16)
 
-    level_state = level_network(
-        own_state.astype(jnp.float32), block_levels, me, nbits, ctx_len
-    )
-    key_state = key_network(
-        grad_state.astype(jnp.float32), block_levels, me, nbits, ctx_len
-    ).astype(jnp.bfloat16)
-
     gate_t = weights.transpose(1, 0, 2)
-    partials = local_part(query_rows, key_rows, value_rows, out_grad, gate_t)
+    grad_wide = grad_state.astype(jnp.float32)
+    heads = query_rows.shape[0]
+    fwd_x = own_state.astype(jnp.float32)
+    bwd_acc = None
+    levels = []
+    partials = None
+    for r in range(nbits):
+        kf = r
+        kb = nbits - 1 - r
+        fwd_got = lax.ppermute(
+            fwd_x, "ctx", pairs_of(kf, ctx_len, None if kf < nbits - 1 else 0)
+        )
+        bit, joined, mine = step_masks(block_levels, me, kb)
+        term = jnp.where(bit & mine, grad_wide[kb], 0.0)
+        if bwd_acc is None:
+            send, own = term, None
+            bwd_pairs = pairs_of(kb, ctx_len, 1)
+        else:
+            kept = jnp.where(joined, bwd_acc, 0.0)
+            send = jnp.where(bit, term + kept, bwd_acc)
+            own = jnp.where(bit, bwd_acc, kept)
+            bwd_pairs = pairs_of(kb, ctx_len)
+        bwd_got = lax.ppermute(send, "ctx", bwd_pairs)
+        if r < heads:
+            partials = local_part(query_rows, key_rows, value_rows, out_grad, gate_t, r, partials)
+            fwd_got, bwd_got, partials = lax.optimization_barrier((fwd_got, bwd_got, partials))
+        bwd_acc = bwd_got if own is None else own + bwd_got
+        bit, joined, mine = step_masks(block_levels, me, kf)
+        levels.append(jnp.where(bit & mine, fwd_got, 0.0).astype(jnp.bfloat16))
+        if kf < nbits - 1:
+            fwd_x = jnp.where(
+                bit, fwd_x + jnp.where(joined, fwd_got, 0.0), fwd_got + jnp.where(joined, fwd_x, 0.0)
+            )
+    for h in range(nbits, heads):
+        partials = local_part(query_rows, key_rows, value_rows, out_grad, gate_t, h, partials)
+    level_state = jnp.stack(levels)
+    key_state = bwd_acc.astype(jnp.bfloat16)
     attn, grad_q, grad_k, grad_v, grad_gate = final_part(
         query_rows, key_rows, value_rows, out_grad, partials, gate_t, level_state, key_state
     )

time: 109 us -> 95.2 us (0.87)
  waiting for transfers between devices: 31.3 us -> 10.6 us
  matrix products: 2.23 us -> 6.16 us
  other arithmetic: 1.57 us -> 4.29 us
  starting transfers between devices: 12.7 us -> 14 us
    ppermute x10, waiting for transfers between devices: 31.3 us -> 10.6 us  [the longest x5 10.6 us: per_device(): lax.ppermute(fwd_x, 'ctx', pairs_of(kf, ctx_len, None if kf < nbits - 1 e...]
    select_n x9, other arithmetic: 0.52 us -> 3.19 us  [the longest x4 1.94 us: per_device(): send = jnp.where(bit, term + kept, bwd_acc)]
    dot_general x1, matrix products: 0.48 us -> 2.82 us  [per_device(): jnp.einsum('hcd,hce->hde', key_rows, value_rows, preferred_element_type=j...]
    exp x1 -> x0, local copies, waits for them, and re-layouts: 1.92 us -> none  [per_device(): weights = jnp.exp(level_gate)]
    dot_general x1, matrix products: 1.75 us -> 3.34 us  [per_device(): jnp.einsum('hcd,bhce->bhde', query_rows, scaled, preferred_element_type=j...]
    ppermute x10, starting transfers between devices: 12.7 us -> 14 us  [the longest x5 7.74 us: per_device(): bwd_got = lax.ppermute(send, 'ctx', bwd_pairs)]
  transfers between devices with their start and end apart: 10 -> 10, of which waited for: 6 -> 2; matrix products, arithmetic and copies ran while one was open for 1% -> 9% of each run, Pallas kernels for 31% -> 35%
where the time goes in v3:
time: 95.2 us; the launch traced here: 94.7 us
  Pallas kernels  47.1 us (49%)
  starting transfers between devices  14 us (15%)
  waiting for transfers between devices  10.6 us (11%)
  between operations  6.5 us (7%)
  matrix products  6.16 us (6%)
  local copies, waits for them, and re-layouts  6.06 us (6%)
  other arithmetic  4.29 us (5%)
    pallas_call x4, Pallas kernels, local_part(): pl.pallas_call(local_kernel, grid=(1,), in_specs=in_specs, out_specs=[row...  33.4 us
    pallas_call x1, Pallas kernels, final_part(): pl.pallas_call(final_kernel, grid=(heads,), in_specs=[row_spec] * 8 + [ga...  13.7 us
    ppermute x5, waiting for transfers between devices, per_device(): lax.ppermute(fwd_x, 'ctx', pairs_of(kf, ctx_len, None if kf < nbits - 1 e...  10.6 us
    ppermute x5, starting transfers between devices, per_device(): bwd_got = lax.ppermute(send, 'ctx', bwd_pairs)  7.74 us
    ppermute x5, starting transfers between devices, per_device(): lax.ppermute(fwd_x, 'ctx', pairs_of(kf, ctx_len, None if kf < nbits - 1 e...  6.25 us
    dot_general x1, matrix products, per_device(): jnp.einsum('hcd,bhce->bhde', query_rows, scaled, preferred_element_type=j...  3.34 us
    dot_general x1, matrix products, per_device(): jnp.einsum('hcd,hce->hde', key_rows, value_rows, preferred_element_type=j...  2.82 us
    select_n x4, other arithmetic, per_device(): send = jnp.where(bit, term + kept, bwd_acc)  1.94 us
  transfers between devices with their start and end apart: 10, of which 2 were waited for; matrix products, arithmetic and copies ran while one was open for 9% of the time, Pallas kernels for 35%

profile of v3, /device:TPU:4, one launch (start us, length us, event | category | flops | bytes accessed | tf_op | source)
XLA Modules:
  0.0 94.7 jit_solution(13953211376066114780)
XLA Ops:
  0.6 0.0 copy-start.3
  0.6 0.0 copy-start
  0.7 2.8 %fusion.11 = f32[4,128,128]{2,1,0:T(8,128)} fusion(bf16[4,1024,128]{2,1,0:T(8,128)(2,1)} %k_ref.9, bf16[4,1024,128]{2,1,0:T(8,128)(2,1)} %v_ref.9), kind=kOutput, calls=%fused_computation.7 | convolution fusion | flops 134348800 | bytes 2359296 | tf_op jit(solution)/shard_map/hcd,hce->hde/dot_general | solution.py:212
  3.5 0.0 collective-permute-start
  3.5 0.0 copy-done.3
  3.5 0.0 copy-start.1
  3.5 0.9 fusion.37
  4.4 0.0 copy-done
  4.4 1.6 %copy.28 = f32[4,1024,128]{1,2,0:T(8,128)} copy(bf16[4,1024,128]{2,1,0:T(8,128)(2,1)S(1)} %copy-done) | data formatting | bytes 3145728 | tf_op jit(solution)/shard_map/convert_element_type | solution.py:215
  6.0 1.7 %fusion.39 = (s32[1,1]{1,0:T(1,128)}, s32[1,1]{1,0:T(1,128)}, s32[1,1]{1,0:T(1,128)}, s32[1,1]{1,0:T(1,128)}, s32[1,1]{1,0:T(1,128)}, /*index=5*/s32[1,1]{1,0:T(...) fusion(s32[32,32]{1,0:T(8,128)} %param.11, s32[]{:T(128)S(6)} %select_n.253, s32[]{:T(128)S(6)} %select_n.251, ...), kind=kLoop, calls=%fused_computation.57 | loop fusion | bytes 112 | tf_op jit(solution)/shard_map/dynamic_slice | solution.py:182
  8.3 0.0 copy-done.1
  8.3 3.3 %fusion.8 = f32[5,4,128,128]{3,2,1,0:T(8,128)S(1)} fusion(bf16[4,1024,128]{2,1,0:T(8,128)(2,1)S(1)} %copy-done.1, f32[4,1024,128]{1,2,0:T(8,128)} %copy.28, f32[5,4,1024]{2,0,1:T(8,128)S(1)} %slice.24), kind=kOutput, calls=%fused_computation.5 | convolution fusion | flops 676986880 | bytes 4538368 | tf_op jit(solution)/shard_map/hcd,bhce->bhde/dot_general | solution.py:216
  11.7 4.2 %collective-permute-start.1 = (f32[4,128,128]{2,1,0:T(8,128)S(1)}, f32[4,128,128]{2,1,0:T(8,128)S(1)}, u32[]{:S(2)}, u32[]{:S(2)}) collective-permute-start(f32[4,128,128]{2,1,0:T(8,128)S(1)} %fusion.26), channel_id=1, source_target_pairs={{128,0},{136,8},{144,16},{152,24},{160,32},{168,40},{176,48},{184,... | collective-permute-start | bytes 786440 | tf_op jit(solution)/shard_map/ppermute | solution.py:243
  20.9 8.3 %shard_map.101 = (f32[4,1024,128]{2,1,0:T(8,128)}, f32[4,1024,128]{2,1,0:T(8,128)}, f32[4,1024,128]{2,1,0:T(8,128)}, f32[4,1024,128]{2,1,0:T(8,128)}, f32[4,16,1024]{2,1,0:T(8,128)}) custom-call(bf16[4,1024,128]{2,1,0:T(8,128)(2,1)} %q_ref.9, bf16[4,1024,128]{2,1,0:T(8,128)(2,1)} %k_ref.9, bf16[4,1024,128]{2,1,0:T(8,128)(2,1)} %v_ref.9, ...), custom_call_target="tpu_custom_call" | custom-call | flops 1006632960 | bytes 3276800 | tf_op jit(solution)/shard_map/pallas_call | solution.py:103
  29.2 0.0 collective-permute-done
  29.2 0.0 collective-permute-done.1
  29.3 0.5 collective-permute-start.3
  29.8 1.1 %add_select_fusion.3 = f32[4,128,128]{2,1,0:T(8,128)S(1)} fusion(f32[4,128,128]{2,1,0:T(8,128)} %collective-permute-done, f32[4,128,128]{2,1,0:T(8,128)} %fusion.11, pred[]{:T(512)} %bitcast, pred[]{:T(512)S(6)} %eq.22), kind=kLoop, calls=%fused_computation.45 | loop fusion | flops 327680 | bytes 786434 | tf_op jit(solution)/shard_map/jit(_where)/select_n | solution.py:251
  30.9 1.8 %collective-permute-start.2 = (f32[4,128,128]{2,1,0:T(8,128)S(1)}, f32[4,128,128]{2,1,0:T(8,128)S(1)}, u32[]{:S(2)}, u32[]{:S(2)}) collective-permute-start(f32[4,128,128]{2,1,0:T(8,128)S(1)} %add_select_fusion.3), channel_id=1, source_target_pairs={{0,16},{8,24},{16,0},{24,8},{32,48},{40,56},{48,32},{56,40},{64,80... | collective-permute-start | bytes 786440 | tf_op jit(solution)/shard_map/ppermute | solution.py:230
  32.7 8.3 %shard_map.102 = (f32[4,1024,128]{2,1,0:T(8,128)}, f32[4,1024,128]{2,1,0:T(8,128)}, f32[4,1024,128]{2,1,0:T(8,128)}, f32[4,1024,128]{2,1,0:T(8,128)}, f32[4,16,1024]{2,1,0:T(8,128)}) custom-call(bf16[4,1024,128]{2,1,0:T(8,128)(2,1)} %q_ref.9, ...), custom_call_target="tpu_custom_call", output_to_operand_aliasing={{0}: (5, {}), {1}: (6, {}), {2}: (7, {}), {3}: (8, {}), {4}... | custom-call | flops 1006632960 | bytes 3276800 | tf_op jit(solution)/shard_map/pallas_call | solution.py:103
  41.1 0.0 collective-permute-done.3
  41.1 0.0 collective-permute-done.2
  41.1 0.8 fusion.15
  41.9 2.9 %collective-permute-start.5 = (f32[4,128,128]{2,1,0:T(8,128)}, f32[4,128,128]{2,1,0:T(8,128)S(1)}, u32[]{:S(2)}, u32[]{:S(2)}) collective-permute-start(f32[4,128,128]{2,1,0:T(8,128)} %fusion.15), channel_id=1, source_target_pairs={{0,32},{8,40},{16,48},{24,56},{32,0},{40,8},{48,16},{56,24},{64,96... | collective-permute-start | bytes 786440 | tf_op jit(solution)/shard_map/ppermute | solution.py:243
  44.8 0.7 collective-permute-start.4
  45.5 8.3 %shard_map.103 = (f32[4,1024,128]{2,1,0:T(8,128)}, f32[4,1024,128]{2,1,0:T(8,128)}, f32[4,1024,128]{2,1,0:T(8,128)}, f32[4,1024,128]{2,1,0:T(8,128)}, f32[4,16,1024]{2,1,0:T(8,128)}) custom-call(bf16[4,1024,128]{2,1,0:T(8,128)(2,1)} %q_ref.9, ...), custom_call_target="tpu_custom_call", output_to_operand_aliasing={{0}: (5, {}), {1}: (6, {}), {2}: (7, {}), {3}: (8, {}), {4}... | custom-call | flops 1006632960 | bytes 3276800 | tf_op jit(solution)/shard_map/pallas_call | solution.py:103
  53.9 0.0 collective-permute-done.5
  53.9 0.0 copy-start.4
  53.9 3.7 %collective-permute-done.4 = f32[4,128,128]{2,1,0:T(8,128)S(1)} collective-permute-done((f32[4,128,128]{2,1,0:T(8,128)S(1)}, f32[4,128,128]{2,1,0:T(8,128)S(1)}, u32[]{:S(2)}, u32[]{:S(2)}) %collective-permute-start.4) | collective-permute-done | bytes 262176 | tf_op jit(solution)/shard_map/ppermute | solution.py:230
  57.7 0.0 copy-done.4
  57.7 1.0 %fusion.14 = (f32[4,128,128]{2,1,0:T(8,128)S(1)}, f32[4,128,128]{2,1,0:T(8,128)S(1)}) fusion(f32[5,4,128,128]{3,2,1,0:T(8,128)S(1)} %fusion.8, pred[]{:T(512)S(6)} %and.49, pred[]{:T(512)} %bitcast.6, pred[]{:T(512)S(6)} %eq.21, f32[4,128,128]{2,1,0:T(8,128)} %copy-done.4, pred[]{:T(512)} %bitcast.10, f32[4,128,128]{2,1,0:T(8,128)S(1)} %collective-permute-done.3, ...), kind=kLoop, calls=%fused_computation.14 | loop fusion | flops 655360 | bytes 1572871 | tf_op jit(solution)/shard_map/jit(_where)/select_n | solution.py:240
  58.8 0.1 collective-permute-start.7
  58.9 2.4 %collective-permute-start.6 = (f32[4,128,128]{2,1,0:T(8,128)S(1)}, f32[4,128,128]{2,1,0:T(8,128)S(1)}, u32[]{:S(2)}, u32[]{:S(2)}) collective-permute-start(f32[4,128,128]{2,1,0:T(8,128)S(1)} %add_select_fusion.1), channel_id=1, source_target_pairs={{0,64},{8,72},{16,80},{24,88},{32,96},{40,104},{48,112},{56,120},{... | collective-permute-start | bytes 786440 | tf_op jit(solution)/shard_map/ppermute | solution.py:230
  61.3 8.4 %shard_map.104 = (f32[4,1024,128]{2,1,0:T(8,128)}, f32[4,1024,128]{2,1,0:T(8,128)}, f32[4,1024,128]{2,1,0:T(8,128)}, f32[4,1024,128]{2,1,0:T(8,128)}, f32[4,16,1024]{2,1,0:T(8,128)}) custom-call(bf16[4,1024,128]{2,1,0:T(8,128)(2,1)} %q_ref.9, ...), custom_call_target="tpu_custom_call", output_to_operand_aliasing={{0}: (5, {}), {1}: (6, {}), {2}: (7, {}), {3}: (8, {}), {4}... | custom-call | flops 1006632960 | bytes 3276800 | tf_op jit(solution)/shard_map/pallas_call | solution.py:103
  69.7 0.0 collective-permute-done.7
  69.7 0.0 collective-permute-done.6
  69.7 0.1 add_select_fusion
  69.8 1.3 %collective-permute-start.8 = (bf16[4,128,128]{2,1,0:T(8,128)(2,1)S(1)}, bf16[4,128,128]{2,1,0:T(8,128)(2,1)S(1)}, u32[]{:S(2)}, u32[]{:S(2)}) collective-permute-start(bf16[4,128,128]{2,1,0:T(8,128)(2,1)S(1)} %add_select_fusion), channel_id=1, source_target_pairs={{0,128},{8,136},{16,144},{24,152},{32,160},{40,168},{48,176},{56,1... | collective-permute-start | bytes 393224 | tf_op jit(solution)/shard_map/ppermute | solution.py:230
  71.1 0.1 fusion.13
  71.2 0.1 collective-permute-start.9
  71.3 6.8 %collective-permute-done.8 = bf16[4,128,128]{2,1,0:T(8,128)(2,1)S(1)} collective-permute-done((bf16[4,128,128]{2,1,0:T(8,128)(2,1)S(1)}, bf16[4,128,128]{2,1,0:T(8,128)(2,1)S(1)}, u32[]{:S(2)}, u32[]{:S(2)}) %collective-permute-start.8) | collective-permute-done | bytes 131104 | tf_op jit(solution)/shard_map/ppermute | solution.py:230
  78.2 0.0 copy-start.2
  78.2 0.0 collective-permute-done.9
  78.2 0.9 fusion.21.ks_ref
  79.2 0.0 copy-done.2
  79.2 13.7 %shard_map.105 = (bf16[4,1024,128]{2,1,0:T(8,128)(2,1)}, bf16[4,1024,128]{2,1,0:T(8,128)(2,1)}, bf16[4,1024,128]{2,1,0:T(8,128)(2,1)}, bf16[4,1024,128]{2,1,0:T(8,128)(2,1)}, f32[4,16,1024]{2,1,0:T(8,128)}) custom-call(bf16[4,1024,128]{2,1,0:T(8,128)(2,1)} %q_ref.9, bf16[4,1024,128]{2,1,0:T(8,128)(2,1)} %k_ref.9, bf16[4,1024,128]{2,1,0:T(8,128)(2,1)} %v_ref.9, ...), custom_call_target="tpu_custom_call" | custom-call | flops 1610612736 | bytes 17825792 | tf_op jit(solution)/shard_map/pallas_call | solution.py:164
  92.9 1.8 %copy.30 = f32[16,4,1024]{2,1,0:T(4,128)} copy(f32[16,4,1024]{2,0,1:T(8,128)} %bitcast.57) | data formatting | bytes 524288
  (10 shorter events, 0.4 us)
Async XLA Ops:
  0.6 2.9 %copy-start.3 = (f32[16,4,1024]{2,1,0:T(4,128)S(1)}, f32[16,4,1024]{2,1,0:T(4,128)}, u32[]{:S(2)}) copy-start(f32[16,4,1024]{2,1,0:T(4,128)} %param.10) | copy-start | bytes 786436
  0.6 3.7 %copy-start = (bf16[4,1024,128]{2,1,0:T(8,128)(2,1)S(1)}, bf16[4,1024,128]{2,1,0:T(8,128)(2,1)}, u32[]{:S(2)}) copy-start(bf16[4,1024,128]{2,1,0:T(8,128)(2,1)} %do_ref.9) | copy-start | bytes 3145732
  3.5 25.8 %collective-permute-start = (f32[4,128,128]{2,1,0:T(8,128)}, f32[4,128,128]{2,1,0:T(8,128)}, u32[]{:S(2)}, u32[]{:S(2)}) collective-permute-start(f32[4,128,128]{2,1,0:T(8,128)} %fusion.11), channel_id=1, source_target_pairs={{0,8},{8,0},{16,24},{24,16},{32,40},{40,32},{48,56},{56,48},{64,72... | collective-permute-start | bytes 786440 | tf_op jit(solution)/shard_map/ppermute | solution.py:230
  3.5 4.8 %copy-start.1 = (bf16[4,1024,128]{2,1,0:T(8,128)(2,1)S(1)}, bf16[4,1024,128]{2,1,0:T(8,128)(2,1)}, u32[]{:S(2)}) copy-start(bf16[4,1024,128]{2,1,0:T(8,128)(2,1)} %q_ref.9) | copy-start | bytes 3145732
  11.7 17.6 %collective-permute-start.1 = (f32[4,128,128]{2,1,0:T(8,128)S(1)}, f32[4,128,128]{2,1,0:T(8,128)S(1)}, u32[]{:S(2)}, u32[]{:S(2)}) collective-permute-start(f32[4,128,128]{2,1,0:T(8,128)S(1)} %fusion.26), channel_id=1, source_target_pairs={{128,0},{136,8},{144,16},{152,24},{160,32},{168,40},{176,48},{184,... | collective-permute-start | bytes 786440 | tf_op jit(solution)/shard_map/ppermute | solution.py:243
  29.3 11.8 %collective-permute-start.3 = (f32[4,128,128]{2,1,0:T(8,128)S(1)}, f32[4,128,128]{2,1,0:T(8,128)S(1)}, u32[]{:S(2)}, u32[]{:S(2)}) collective-permute-start(f32[4,128,128]{2,1,0:T(8,128)S(1)} %fusion.16), channel_id=1, source_target_pairs={{0,64},{8,72},{16,80},{24,88},{32,96},{40,104},{48,112},{56,120},{... | collective-permute-start | bytes 786440 | tf_op jit(solution)/shard_map/ppermute | solution.py:243
  30.9 10.2 %collective-permute-start.2 = (f32[4,128,128]{2,1,0:T(8,128)S(1)}, f32[4,128,128]{2,1,0:T(8,128)S(1)}, u32[]{:S(2)}, u32[]{:S(2)}) collective-permute-start(f32[4,128,128]{2,1,0:T(8,128)S(1)} %add_select_fusion.3), channel_id=1, source_target_pairs={{0,16},{8,24},{16,0},{24,8},{32,48},{40,56},{48,32},{56,40},{64,80... | collective-permute-start | bytes 786440 | tf_op jit(solution)/shard_map/ppermute | solution.py:230
  41.9 12.0 %collective-permute-start.5 = (f32[4,128,128]{2,1,0:T(8,128)}, f32[4,128,128]{2,1,0:T(8,128)S(1)}, u32[]{:S(2)}, u32[]{:S(2)}) collective-permute-start(f32[4,128,128]{2,1,0:T(8,128)} %fusion.15), channel_id=1, source_target_pairs={{0,32},{8,40},{16,48},{24,56},{32,0},{40,8},{48,16},{56,24},{64,96... | collective-permute-start | bytes 786440 | tf_op jit(solution)/shard_map/ppermute | solution.py:243
  44.8 12.9 %collective-permute-start.4 = (f32[4,128,128]{2,1,0:T(8,128)S(1)}, f32[4,128,128]{2,1,0:T(8,128)S(1)}, u32[]{:S(2)}, u32[]{:S(2)}) collective-permute-start(f32[4,128,128]{2,1,0:T(8,128)S(1)} %add_select_fusion.2), channel_id=1, source_target_pairs={{0,32},{8,40},{16,48},{24,56},{32,0},{40,8},{48,16},{56,24},{64,96... | collective-permute-start | bytes 786440 | tf_op jit(solution)/shard_map/ppermute | solution.py:230
  53.9 3.8 %copy-start.4 = (f32[4,128,128]{2,1,0:T(8,128)}, f32[4,128,128]{2,1,0:T(8,128)S(1)}, u32[]{:S(2)}) copy-start(f32[4,128,128]{2,1,0:T(8,128)S(1)} %collective-permute-done.5) | copy-start | bytes 786436
  58.8 11.0 %collective-permute-start.7 = (f32[4,128,128]{2,1,0:T(8,128)S(1)}, f32[4,128,128]{2,1,0:T(8,128)S(1)}, u32[]{:S(2)}, u32[]{:S(2)}) collective-permute-start(f32[4,128,128]{2,1,0:T(8,128)S(1)} %get-tuple-element.116), channel_id=1, source_target_pairs={{0,16},{8,24},{16,0},{24,8},{32,48},{40,56},{48,32},{56,40},{64,80... | collective-permute-start | bytes 786440 | tf_op jit(solution)/shard_map/ppermute | solution.py:243
  58.9 10.9 %collective-permute-start.6 = (f32[4,128,128]{2,1,0:T(8,128)S(1)}, f32[4,128,128]{2,1,0:T(8,128)S(1)}, u32[]{:S(2)}, u32[]{:S(2)}) collective-permute-start(f32[4,128,128]{2,1,0:T(8,128)S(1)} %add_select_fusion.1), channel_id=1, source_target_pairs={{0,64},{8,72},{16,80},{24,88},{32,96},{40,104},{48,112},{56,120},{... | collective-permute-start | bytes 786440 | tf_op jit(solution)/shard_map/ppermute | solution.py:230
  69.8 8.4 %collective-permute-start.8 = (bf16[4,128,128]{2,1,0:T(8,128)(2,1)S(1)}, bf16[4,128,128]{2,1,0:T(8,128)(2,1)S(1)}, u32[]{:S(2)}, u32[]{:S(2)}) collective-permute-start(bf16[4,128,128]{2,1,0:T(8,128)(2,1)S(1)} %add_select_fusion), channel_id=1, source_target_pairs={{0,128},{8,136},{16,144},{24,152},{32,160},{40,168},{48,176},{56,1... | collective-permute-start | bytes 393224 | tf_op jit(solution)/shard_map/ppermute | solution.py:230
  71.2 7.0 %collective-permute-start.9 = (f32[4,128,128]{2,1,0:T(8,128)S(1)}, f32[4,128,128]{2,1,0:T(8,128)S(1)}, u32[]{:S(2)}, u32[]{:S(2)}) collective-permute-start(f32[4,128,128]{2,1,0:T(8,128)S(1)} %fusion.13), channel_id=1, source_target_pairs={{0,8},{8,0},{16,24},{24,16},{32,40},{40,32},{48,56},{56,48},{64,72... | collective-permute-start | bytes 786440 | tf_op jit(solution)/shard_map/ppermute | solution.py:243
  78.2 1.0 %copy-start.2 = (bf16[5,4,128,128]{3,2,1,0:T(8,128)(2,1)}, bf16[5,4,128,128]{3,2,1,0:T(8,128)(2,1)S(1)}, u32[]{:S(2)}) copy-start(bf16[5,4,128,128]{3,2,1,0:T(8,128)(2,1)S(1)} %fusion.36.ls_ref) | copy-start | bytes 1966084

commit v4 on v3

--- a/solution.py
+++ b/solution.py
@@ -67,8 +67,8 @@
                 )
         probs = (scores * weight).astype(jnp.bfloat16)
         dprobs = (back * weight).astype(jnp.bfloat16)
-        o_ref[ts, :] += dot_tn(probs, vj)
-        dq_ref[ts, :] += dot_tn(dprobs, kj)
+        o_ref[:, ts] += dot_tn(vj, probs)
+        dq_ref[:, ts] += dot_tn(kj, dprobs)
         dk_ref[ss, :] += dot_nn(dprobs, qi)
         dv_ref[ss, :] += dot_nn(probs, doi)
 
@@ -88,10 +88,11 @@
     f32 = jnp.float32
     pairs = (block_len // TILE) * (block_len // TILE + 1) // 2
     flops = pairs * 6 * 2 * TILE * TILE * width
-    shapes = [jax.ShapeDtypeStruct((heads, block_len, width), f32)] * 4 + [
-        jax.ShapeDtypeStruct((heads, nlev, block_len), f32)
-    ]
+    shapes = [jax.ShapeDtypeStruct((heads, width, block_len), f32)] * 2 + [
+        jax.ShapeDtypeStruct((heads, block_len, width), f32)
+    ] * 2 + [jax.ShapeDtypeStruct((heads, nlev, block_len), f32)]
     row_spec = pl.BlockSpec((None, block_len, width), lambda i: (h, 0, 0))
+    col_spec = pl.BlockSpec((None, width, block_len), lambda i: (h, 0, 0))
     gate_spec = pl.BlockSpec((None, nlev, block_len), lambda i: (h, 0, 0))
     args = (query_rows, key_rows, value_rows, out_grad, gate_t)
     in_specs = [row_spec] * 4 + [gate_spec]
@@ -104,7 +105,7 @@
         local_kernel,
         grid=(1,),
         in_specs=in_specs,
-        out_specs=[row_spec] * 4 + [gate_spec],
+        out_specs=[col_spec] * 2 + [row_spec] * 2 + [gate_spec],
         out_shape=shapes,
         input_output_aliases=aliases,
         compiler_params=pltpu.CompilerParams(dimension_semantics=("arbitrary",)),
@@ -116,55 +117,90 @@
     )(*args)
 
 
+def state_kernel(q_ref, k_ref, v_ref, do_ref, g_ref, st_ref, gs_ref):
+    nlev = g_ref.shape[0]
+    nbits = gs_ref.shape[0]
+    first = nlev - nbits
+    st_ref[...] = dot_tn(k_ref[...], v_ref[...]).astype(st_ref.dtype)
+    do_t = jnp.transpose(do_ref[...].astype(jnp.float32))
+    q = q_ref[...]
+    for b in range(nbits):
+        scaled_t = (g_ref[first + b : first + b + 1, :] * do_t).astype(jnp.bfloat16)
+        gs_ref[b] = dot_nn(scaled_t, q).astype(gs_ref.dtype)
+
+
+def state_part(query_rows, key_rows, value_rows, out_grad, gate_t, nbits):
+    heads, block_len, width = query_rows.shape
+    nlev = gate_t.shape[1]
+    row_spec = pl.BlockSpec((None, block_len, width), lambda h: (h, 0, 0))
+    gate_spec = pl.BlockSpec((None, nlev, block_len), lambda h: (h, 0, 0))
+    bf = jnp.bfloat16
+    return pl.pallas_call(
+        state_kernel,
+        grid=(heads,),
+        in_specs=[row_spec] * 4 + [gate_spec],
+        out_specs=[
+            pl.BlockSpec((None, width, width), lambda h: (h, 0, 0)),
+            pl.BlockSpec((nbits, None, width, width), lambda h: (0, h, 0, 0)),
+        ],
+        out_shape=[
+            jax.ShapeDtypeStruct((heads, width, width), bf),
+            jax.ShapeDtypeStruct((nbits, heads, width, width), bf),
+        ],
+        compiler_params=pltpu.CompilerParams(dimension_semantics=("arbitrary",)),
+        cost_estimate=pl.CostEstimate(
+            flops=heads * block_len * width * width * 2 * (nbits + 1),
+            transcendentals=0,
+            bytes_accessed=heads * block_len * (4 * width * 2 + nlev * 4),
+        ),
+    )(query_rows, key_rows, value_rows, out_grad, gate_t)
+
+
 def final_kernel(q_ref, k_ref, v_ref, do_ref, o_ref, dq_ref, dk_ref, dv_ref, ggl_ref, g_ref,
-                 ls_ref, ks_ref, attn_ref, gq_ref, gk_ref, gv_ref, gg_ref):
+                 ls_ref, lst_ref, kst_ref, attn_ref, gq_ref, gk_ref, gv_ref, gg_ref):
     block_len = q_ref.shape[0]
     nlev = g_ref.shape[0]
     nbits = ls_ref.shape[0]
     first = nlev - nbits
-    gate_cols = jnp.transpose(g_ref[...])
-    key_state = ks_ref[...]
-    lane = lax.broadcasted_iota(jnp.int32, (TILE, nlev), 1)
-    cross_parts = []
+    key_state_t = kst_ref[...]
+    gg_ref[...] = ggl_ref[...]
     for i in range(block_len // TILE):
         ts = pl.ds(i * TILE, TILE)
         qi = q_ref[ts, :]
         doi = do_ref[ts, :]
-        do_f = doi.astype(jnp.float32)
-        attn = o_ref[ts, :]
-        grad_q = dq_ref[ts, :]
-        cross = jnp.zeros((TILE, nlev), jnp.float32)
+        do_t = jnp.transpose(doi.astype(jnp.float32))
+        attn_t = o_ref[:, ts]
+        grad_q_t = dq_ref[:, ts]
         for b in range(nbits):
-            state = ls_ref[b]
-            weight = gate_cols[i * TILE : (i + 1) * TILE, first + b : first + b + 1]
-            level_out = dot_nn(qi, state)
-            level_back = dot_nt(doi, state)
-            attn = attn + weight * level_out
-            grad_q = grad_q + weight * level_back
-            dotted = jnp.sum(level_out * do_f, axis=1, keepdims=True)
-            cross = jnp.where(lane == first + b, weight * dotted, cross)
-        attn_ref[ts, :] = attn.astype(attn_ref.dtype)
-        gq_ref[ts, :] = grad_q.astype(gq_ref.dtype)
-        gk_ref[ts, :] = (dk_ref[ts, :] + dot_nt(v_ref[ts, :], key_state)).astype(gk_ref.dtype)
-        gv_ref[ts, :] = (dv_ref[ts, :] + dot_nn(k_ref[ts, :], key_state)).astype(gv_ref.dtype)
-        cross_parts.append(cross)
-    cross_all = jnp.concatenate(cross_parts, axis=0)
-    gg_ref[...] = ggl_ref[...] + jnp.transpose(cross_all)
-
-
-def final_part(query_rows, key_rows, value_rows, out_grad, partials, gate_t, level_state, key_state):
+            weight = g_ref[first + b : first + b + 1, ts]
+            level_out_t = dot_nt(lst_ref[b], qi)
+            level_back_t = dot_nt(ls_ref[b], doi)
+            attn_t = attn_t + weight * level_out_t
+            grad_q_t = grad_q_t + weight * level_back_t
+            dotted = jnp.sum(level_out_t * do_t, axis=0, keepdims=True)
+            gg_ref[first + b : first + b + 1, ts] = weight * dotted
+        attn_ref[ts, :] = jnp.transpose(attn_t).astype(attn_ref.dtype)
+        gq_ref[ts, :] = jnp.transpose(grad_q_t).astype(gq_ref.dtype)
+        gk_ref[ts, :] = (dk_ref[ts, :] + dot_nn(v_ref[ts, :], key_state_t)).astype(gk_ref.dtype)
+        gv_ref[ts, :] = (dv_ref[ts, :] + dot_nt(k_ref[ts, :], key_state_t)).astype(gv_ref.dtype)
+
+
+def final_part(query_rows, key_rows, value_rows, out_grad, partials, gate_t, level_state, key_state_t):
     heads, block_len, width = query_rows.shape
     nlev = gate_t.shape[1]
     nbits = level_state.shape[0]
     row_spec = pl.BlockSpec((None, block_len, width), lambda h: (h, 0, 0))
+    col_spec = pl.BlockSpec((None, width, block_len), lambda h: (h, 0, 0))
     gate_spec = pl.BlockSpec((None, nlev, block_len), lambda h: (h, 0, 0))
     ls_spec = pl.BlockSpec((nbits, None, width, width), lambda h: (0, h, 0, 0))
     ks_spec = pl.BlockSpec((None, width, width), lambda h: (h, 0, 0))
     bf = jnp.bfloat16
+    level_state_t = jnp.swapaxes(level_state, 2, 3)
     return pl.pallas_call(
         final_kernel,
         grid=(heads,),
-        in_specs=[row_spec] * 8 + [gate_spec, gate_spec, ls_spec, ks_spec],
+        in_specs=[row_spec] * 4 + [col_spec] * 2 + [row_spec] * 2
+        + [gate_spec, gate_spec, ls_spec, ls_spec, ks_spec],
         out_specs=[row_spec] * 4 + [gate_spec],
         out_shape=[jax.ShapeDtypeStruct((heads, block_len, width), bf)] * 4
         + [jax.ShapeDtypeStruct((heads, nlev, block_len), jnp.float32)],
@@ -175,7 +211,7 @@
             bytes_accessed=heads * block_len * (8 * width * 2 + 4 * width * 4 + 4 * nlev * 4),
         ),
     )(query_rows, key_rows, value_rows, out_grad, *partials[:4], partials[4], gate_t,
-      level_state, key_state)
+      level_state, level_state_t, key_state_t)
 
 
 def same_doc(block_levels, earlier, later):
@@ -209,15 +245,8 @@
     weights = jnp.exp(level_gate)
     cross_weight = weights[log_block + 1 :]
 
-    own_state = jnp.einsum(
-        "hcd,hce->hde", key_rows, value_rows, preferred_element_type=jnp.float32
-    ).astype(jnp.bfloat16)
-    scaled = (cross_weight[..., None] * out_grad[None].astype(jnp.float32)).astype(jnp.bfloat16)
-    grad_state = jnp.einsum(
-        "hcd,bhce->bhde", query_rows, scaled, preferred_element_type=jnp.float32
-    ).astype(jnp.bfloat16)
-
     gate_t = weights.transpose(1, 0, 2)
+    own_state, grad_state = state_part(query_rows, key_rows, value_rows, out_grad, gate_t, nbits)
     grad_wide = grad_state.astype(jnp.float32)
     heads = query_rows.shape[0]
     fwd_x = own_state.astype(jnp.float32)
@@ -254,9 +283,9 @@
     for h in range(nbits, heads):
         partials = local_part(query_rows, key_rows, value_rows, out_grad, gate_t, h, partials)
     level_state = jnp.stack(levels)
-    key_state = bwd_acc.astype(jnp.bfloat16)
+    key_state_t = bwd_acc.astype(jnp.bfloat16)
     attn, grad_q, grad_k, grad_v, grad_gate = final_part(
-        query_rows, key_rows, value_rows, out_grad, partials, gate_t, level_state, key_state
+        query_rows, key_rows, value_rows, out_grad, partials, gate_t, level_state, key_state_t
     )
     return (attn, grad_q, grad_k, grad_v, grad_gate.transpose(1, 0, 2))
 

time: 95.2 us -> 87.1 us (0.915)
  matrix products: 6.16 us -> 0 us
  Pallas kernels: 47.1 us -> 43.9 us
    dot_general x2 -> x0, matrix products: 6.16 us -> none  [the longest x1 3.34 us: per_device(): jnp.einsum('hcd,bhce->bhde', query_rows, scaled, preferred_element_type=j...]
    pallas_call x5 -> x6, Pallas kernels: 47.1 us -> 43.9 us  [the longest x4 29.7 us: local_part(): pl.pallas_call(local_kernel, grid=(1,), in_specs=in_specs, out_specs=[col...]
    convert_element_type x1 -> x3, other arithmetic: 0.91 us -> 2.85 us  [the longest x1 1.22 us: per_device(): grad_wide = grad_state.astype(jnp.float32)]
    convert_element_type x1 -> x0, local copies, waits for them, and re-layouts: 1.63 us -> none  [per_device(): out_grad[None].astype(jnp.float32)]
    transpose x0 -> x1, local copies, waits for them, and re-layouts: none -> 1.14 us  [final_part(): level_state_t = jnp.swapaxes(level_state, 2, 3)]
    select_n x4, other arithmetic: 1.22 us -> 0.2 us  [per_device(): jnp.where(bit, fwd_x + jnp.where(joined, fwd_got, 0.0), fwd_got + jnp.whe...]
  transfers between devices with their start and end apart: 10 -> 10, of which waited for: 2 -> 2; matrix products, arithmetic and copies ran while one was open for 9% -> 5% of each run, Pallas kernels for 35% -> 34%
where the time goes in v4:
time: 87.1 us; the launch traced here: 86.5 us
  Pallas kernels  43.9 us (50%)
  starting transfers between devices  13.7 us (16%)
  waiting for transfers between devices  10.8 us (12%)
  local copies, waits for them, and re-layouts  6.5 us (7%)
  between operations  6.48 us (7%)
  other arithmetic  5.21 us (6%)
    pallas_call x4, Pallas kernels, local_part(): pl.pallas_call(local_kernel, grid=(1,), in_specs=in_specs, out_specs=[col...  29.7 us
    ppermute x5, waiting for transfers between devices, per_device(): lax.ppermute(fwd_x, 'ctx', pairs_of(kf, ctx_len, None if kf < nbits - 1 e...  10.7 us
    pallas_call x1, Pallas kernels, final_part(): pl.pallas_call(final_kernel, grid=(heads,), in_specs=[row_spec] * 4 + [co...  9.01 us
    ppermute x5, starting transfers between devices, per_device(): bwd_got = lax.ppermute(send, 'ctx', bwd_pairs)  8.16 us
    ppermute x5, starting transfers between devices, per_device(): lax.ppermute(fwd_x, 'ctx', pairs_of(kf, ctx_len, None if kf < nbits - 1 e...  5.58 us
    pallas_call x1, Pallas kernels, state_part(): pl.pallas_call(state_kernel, grid=(heads,), in_specs=[row_spec] * 4 + [ga...  5.18 us
    select_n x4, other arithmetic, per_device(): send = jnp.where(bit, term + kept, bwd_acc)  1.94 us
    unnamed x5, local copies, waits for them, and re-layouts  1.83 us
  transfers between devices with their start and end apart: 10, of which 2 were waited for; matrix products, arithmetic and copies ran while one was open for 5% of the time, Pallas kernels for 34%

profile of v4, /device:TPU:4, one launch (start us, length us, event | category | flops | bytes accessed | tf_op | source)
XLA Modules:
  0.0 86.5 jit_solution(2191737231019096571)
XLA Ops:
  0.6 1.8 %fusion.14.g_ref = f32[4,16,1024]{2,1,0:T(8,128)} fusion(f32[16,4,1024]{2,1,0:T(4,128)} %param.10), kind=kLoop, calls=%fused_computation.28 | loop fusion | bytes 524288 | tf_op jit(solution)/shard_map/transpose | solution.py:248
  2.5 5.2 %shard_map.101 = (bf16[4,128,128]{2,1,0:T(8,128)(2,1)}, bf16[5,4,128,128]{3,2,1,0:T(8,128)(2,1)}) custom-call(bf16[4,1024,128]{2,1,0:T(8,128)(2,1)} %q_ref.11, bf16[4,1024,128]{2,1,0:T(8,128)(2,1)} %k_ref.11, bf16[4,1024,128]{2,1,0:T(8,128)(2,1)} %v_ref.11, bf16[4,1024,128]{2,1,0:T(8,128)(2,1)} %do_ref.11, f32[4,16,1024]{2,1,0:T(8,128)} %fusion.14.g_ref), custom_call_target="tpu_custom_call" | custom-call | flops 805306368 | bytes 4456448 | tf_op jit(solution)/shard_map/pallas_call | solution.py:138
  7.6 0.9 %convert_element_type.24 = f32[4,128,128]{2,1,0:T(8,128)S(1)} convert(bf16[4,128,128]{2,1,0:T(8,128)(2,1)} %get-tuple-element.60) | non-fusion elementwise | flops 65536 | bytes 393216 | tf_op jit(solution)/shard_map/convert_element_type | solution.py:252
  8.6 0.1 collective-permute-start
  8.7 1.2 %convert_element_type.25 = f32[5,4,128,128]{3,2,1,0:T(8,128)S(1)} convert(bf16[5,4,128,128]{3,2,1,0:T(8,128)(2,1)} %get-tuple-element.61) | non-fusion elementwise | flops 327680 | bytes 1966080 | tf_op jit(solution)/shard_map/convert_element_type | solution.py:250
  9.9 1.7 %fusion.26 = (s32[1,1]{1,0:T(1,128)}, s32[1,1]{1,0:T(1,128)}, s32[1,1]{1,0:T(1,128)}, s32[1,1]{1,0:T(1,128)}, s32[1,1]{1,0:T(1,128)}, /*index=5*/s32[1,1]{1,0:T(...) fusion(s32[32,32]{1,0:T(8,128)} %param.11, s32[]{:T(128)S(6)} %select_n.253, s32[]{:T(128)S(6)} %select_n.251, ...), kind=kLoop, calls=%fused_computation.48 | loop fusion | bytes 112 | tf_op jit(solution)/shard_map/dynamic_slice | solution.py:218
  12.3 4.2 %collective-permute-start.1 = (f32[4,128,128]{2,1,0:T(8,128)S(1)}, f32[4,128,128]{2,1,0:T(8,128)S(1)}, u32[]{:S(2)}, u32[]{:S(2)}) collective-permute-start(f32[4,128,128]{2,1,0:T(8,128)S(1)} %fusion.13), channel_id=1, source_target_pairs={{128,0},{136,8},{144,16},{152,24},{160,32},{168,40},{176,48},{184,... | collective-permute-start | bytes 786440 | tf_op jit(solution)/shard_map/ppermute | solution.py:272
  21.5 0.0 copy-start.1
  21.5 7.4 %shard_map.102 = (f32[4,128,1024]{2,1,0:T(8,128)}, f32[4,128,1024]{2,1,0:T(8,128)}, f32[4,1024,128]{2,1,0:T(8,128)}, f32[4,1024,128]{2,1,0:T(8,128)}, f32[4,16,1024]{2,1,0:T(8,128)}) custom-call(bf16[4,1024,128]{2,1,0:T(8,128)(2,1)} %q_ref.11, bf16[4,1024,128]{2,1,0:T(8,128)(2,1)} %k_ref.11, bf16[4,1024,128]{2,1,0:T(8,128)(2,1)} %v_ref.11, ...), custom_call_target="tpu_custom_call" | custom-call | flops 1006632960 | bytes 3276800 | tf_op jit(solution)/shard_map/pallas_call | solution.py:104
  28.9 0.0 collective-permute-done
  28.9 0.0 collective-permute-done.1
  29.0 0.5 collective-permute-start.3
  29.4 0.0 copy-done.1
  29.4 0.1 add_select_fusion.3
  29.5 1.7 %collective-permute-start.2 = (f32[4,128,128]{2,1,0:T(8,128)S(1)}, f32[4,128,128]{2,1,0:T(8,128)S(1)}, u32[]{:S(2)}, u32[]{:S(2)}) collective-permute-start(f32[4,128,128]{2,1,0:T(8,128)S(1)} %add_select_fusion.3), channel_id=1, source_target_pairs={{0,16},{8,24},{16,0},{24,8},{32,48},{40,56},{48,32},{56,40},{64,80... | collective-permute-start | bytes 786440 | tf_op jit(solution)/shard_map/ppermute | solution.py:259
  31.2 7.4 %shard_map.103 = (f32[4,128,1024]{2,1,0:T(8,128)}, f32[4,128,1024]{2,1,0:T(8,128)}, f32[4,1024,128]{2,1,0:T(8,128)}, f32[4,1024,128]{2,1,0:T(8,128)}, f32[4,16,1024]{2,1,0:T(8,128)}) custom-call(bf16[4,1024,128]{2,1,0:T(8,128)(2,1)} %q_ref.11, ...), custom_call_target="tpu_custom_call", output_to_operand_aliasing={{0}: (5, {}), {1}: (6, {}), {2}: (7, {}), {3}: (8, {}), {4}... | custom-call | flops 1006632960 | bytes 3276800 | tf_op jit(solution)/shard_map/pallas_call | solution.py:104
  38.6 0.0 collective-permute-done.3
  38.6 0.0 collective-permute-done.2
  38.6 0.8 fusion.2
  39.4 2.9 %collective-permute-start.5 = (f32[4,128,128]{2,1,0:T(8,128)}, f32[4,128,128]{2,1,0:T(8,128)}, u32[]{:S(2)}, u32[]{:S(2)}) collective-permute-start(f32[4,128,128]{2,1,0:T(8,128)} %fusion.2), channel_id=1, source_target_pairs={{0,32},{8,40},{16,48},{24,56},{32,0},{40,8},{48,16},{56,24},{64,96... | collective-permute-start | bytes 786440 | tf_op jit(solution)/shard_map/ppermute | solution.py:272
  42.3 0.9 %collective-permute-start.4 = (f32[4,128,128]{2,1,0:T(8,128)S(1)}, f32[4,128,128]{2,1,0:T(8,128)S(1)}, u32[]{:S(2)}, u32[]{:S(2)}) collective-permute-start(f32[4,128,128]{2,1,0:T(8,128)S(1)} %add_select_fusion.2), channel_id=1, source_target_pairs={{0,32},{8,40},{16,48},{24,56},{32,0},{40,8},{48,16},{56,24},{64,96... | collective-permute-start | bytes 786440 | tf_op jit(solution)/shard_map/ppermute | solution.py:259
  43.2 7.4 %shard_map.104 = (f32[4,128,1024]{2,1,0:T(8,128)}, f32[4,128,1024]{2,1,0:T(8,128)}, f32[4,1024,128]{2,1,0:T(8,128)}, f32[4,1024,128]{2,1,0:T(8,128)}, f32[4,16,1024]{2,1,0:T(8,128)}) custom-call(bf16[4,1024,128]{2,1,0:T(8,128)(2,1)} %q_ref.11, ...), custom_call_target="tpu_custom_call", output_to_operand_aliasing={{0}: (5, {}), {1}: (6, {}), {2}: (7, {}), {3}: (8, {}), {4}... | custom-call | flops 1006632960 | bytes 3276800 | tf_op jit(solution)/shard_map/pallas_call | solution.py:104
  50.6 0.0 collective-permute-done.5
  50.7 3.9 %collective-permute-done.4 = f32[4,128,128]{2,1,0:T(8,128)S(1)} collective-permute-done((f32[4,128,128]{2,1,0:T(8,128)S(1)}, f32[4,128,128]{2,1,0:T(8,128)S(1)}, u32[]{:S(2)}, u32[]{:S(2)}) %collective-permute-start.4) | collective-permute-done | bytes 262176 | tf_op jit(solution)/shard_map/ppermute | solution.py:259
  54.6 1.0 %fusion.1 = (f32[4,128,128]{2,1,0:T(8,128)S(1)}, f32[4,128,128]{2,1,0:T(8,128)S(1)}) fusion(f32[5,4,128,128]{3,2,1,0:T(8,128)S(1)} %convert_element_type.25, pred[]{:T(512)S(6)} %and.49, pred[]{:T(512)} %bitcast.4, pred[]{:T(512)S(6)} %eq.21, f32[4,128,128]{2,1,0:T(8,128)} %collective-permute-done.5, pred[]{:T(512)} %bitcast.8, ...), kind=kLoop, calls=%fused_computation.5 | loop fusion | flops 655360 | bytes 1572871 | tf_op jit(solution)/shard_map/jit(_where)/select_n | solution.py:269
  55.6 0.5 collective-permute-start.7
  56.2 1.6 %collective-permute-start.6 = (f32[4,128,128]{2,1,0:T(8,128)S(1)}, f32[4,128,128]{2,1,0:T(8,128)S(1)}, u32[]{:S(2)}, u32[]{:S(2)}) collective-permute-start(f32[4,128,128]{2,1,0:T(8,128)S(1)} %add_select_fusion.1), channel_id=1, source_target_pairs={{0,64},{8,72},{16,80},{24,88},{32,96},{40,104},{48,112},{56,120},{... | collective-permute-start | bytes 786440 | tf_op jit(solution)/shard_map/ppermute | solution.py:259
  57.8 7.5 %shard_map.105 = (f32[4,128,1024]{2,1,0:T(8,128)}, f32[4,128,1024]{2,1,0:T(8,128)}, f32[4,1024,128]{2,1,0:T(8,128)}, f32[4,1024,128]{2,1,0:T(8,128)}, f32[4,16,1024]{2,1,0:T(8,128)}) custom-call(bf16[4,1024,128]{2,1,0:T(8,128)(2,1)} %q_ref.11, ...), custom_call_target="tpu_custom_call", output_to_operand_aliasing={{0}: (5, {}), {1}: (6, {}), {2}: (7, {}), {3}: (8, {}), {4}... | custom-call | flops 1006632960 | bytes 3276800 | tf_op jit(solution)/shard_map/pallas_call | solution.py:104
  65.3 0.0 collective-permute-done.7
  65.3 0.0 collective-permute-done.6
  65.3 0.1 add_select_fusion
  65.4 1.3 %collective-permute-start.8 = (bf16[4,128,128]{2,1,0:T(8,128)(2,1)S(1)}, bf16[4,128,128]{2,1,0:T(8,128)(2,1)S(1)}, u32[]{:S(2)}, u32[]{:S(2)}) collective-permute-start(bf16[4,128,128]{2,1,0:T(8,128)(2,1)S(1)} %add_select_fusion), channel_id=1, source_target_pairs={{0,128},{8,136},{16,144},{24,152},{32,160},{40,168},{48,176},{56,1... | collective-permute-start | bytes 393224 | tf_op jit(solution)/shard_map/ppermute | solution.py:259
  66.7 0.1 fusion
  66.8 0.1 collective-permute-start.9
  66.9 6.8 %collective-permute-done.8 = bf16[4,128,128]{2,1,0:T(8,128)(2,1)S(1)} collective-permute-done((bf16[4,128,128]{2,1,0:T(8,128)(2,1)S(1)}, bf16[4,128,128]{2,1,0:T(8,128)(2,1)S(1)}, u32[]{:S(2)}, u32[]{:S(2)}) %collective-permute-start.8) | collective-permute-done | bytes 131104 | tf_op jit(solution)/shard_map/ppermute | solution.py:259
  73.8 0.0 copy-start
  73.8 1.1 %copy.27.lst_ref = bf16[5,4,128,128]{3,2,1,0:T(8,128)(2,1)} copy(bf16[5,4,128,128]{2,3,1,0:T(8,128)(2,1)S(1)} %bitcast.51) | data formatting | bytes 1310720 | tf_op jit(solution)/shard_map/transpose | solution.py:198
  75.0 0.0 collective-permute-done.9
  75.0 0.7 fusion.8.kst_ref
  75.7 0.0 copy-done
  75.7 9.0 %shard_map.106 = (bf16[4,1024,128]{2,1,0:T(8,128)(2,1)}, bf16[4,1024,128]{2,1,0:T(8,128)(2,1)}, bf16[4,1024,128]{2,1,0:T(8,128)(2,1)}, bf16[4,1024,128]{2,1,0:T(8,128)(2,1)}, f32[4,16,1024]{2,1,0:T(8,128)}) custom-call(bf16[4,1024,128]{2,1,0:T(8,128)(2,1)} %q_ref.11, bf16[4,1024,128]{2,1,0:T(8,128)(2,1)} %k_ref.11, bf16[4,1024,128]{2,1,0:T(8,128)(2,1)} %v_ref.11, ...), custom_call_target="tpu_custom_call" | custom-call | flops 1610612736 | bytes 17825792 | tf_op jit(solution)/shard_map/pallas_call | solution.py:199
  84.7 1.8 %copy.28 = f32[16,4,1024]{2,1,0:T(4,128)} copy(f32[16,4,1024]{2,0,1:T(8,128)} %bitcast.52) | data formatting | bytes 524288
  (9 shorter events, 0.4 us)
Async XLA Ops:
  8.6 20.3 %collective-permute-start = (f32[4,128,128]{2,1,0:T(8,128)S(1)}, f32[4,128,128]{2,1,0:T(8,128)S(1)}, u32[]{:S(2)}, u32[]{:S(2)}) collective-permute-start(f32[4,128,128]{2,1,0:T(8,128)S(1)} %convert_element_type.24), channel_id=1, source_target_pairs={{0,8},{8,0},{16,24},{24,16},{32,40},{40,32},{48,56},{56,48},{64,72... | collective-permute-start | bytes 786440 | tf_op jit(solution)/shard_map/ppermute | solution.py:259
  12.3 16.6 %collective-permute-start.1 = (f32[4,128,128]{2,1,0:T(8,128)S(1)}, f32[4,128,128]{2,1,0:T(8,128)S(1)}, u32[]{:S(2)}, u32[]{:S(2)}) collective-permute-start(f32[4,128,128]{2,1,0:T(8,128)S(1)} %fusion.13), channel_id=1, source_target_pairs={{128,0},{136,8},{144,16},{152,24},{160,32},{168,40},{176,48},{184,... | collective-permute-start | bytes 786440 | tf_op jit(solution)/shard_map/ppermute | solution.py:272
  21.5 8.0 %copy-start.1 = (bf16[4,128,128]{2,1,0:T(8,128)(2,1)S(1)}, bf16[4,128,128]{2,1,0:T(8,128)(2,1)}, u32[]{:S(2)}) copy-start(bf16[4,128,128]{2,1,0:T(8,128)(2,1)} %get-tuple-element.60) | copy-start | bytes 393220
  29.0 9.6 %collective-permute-start.3 = (f32[4,128,128]{2,1,0:T(8,128)S(1)}, f32[4,128,128]{2,1,0:T(8,128)S(1)}, u32[]{:S(2)}, u32[]{:S(2)}) collective-permute-start(f32[4,128,128]{2,1,0:T(8,128)S(1)} %fusion.3), channel_id=1, source_target_pairs={{0,64},{8,72},{16,80},{24,88},{32,96},{40,104},{48,112},{56,120},{... | collective-permute-start | bytes 786440 | tf_op jit(solution)/shard_map/ppermute | solution.py:272
  29.5 9.1 %collective-permute-start.2 = (f32[4,128,128]{2,1,0:T(8,128)S(1)}, f32[4,128,128]{2,1,0:T(8,128)S(1)}, u32[]{:S(2)}, u32[]{:S(2)}) collective-permute-start(f32[4,128,128]{2,1,0:T(8,128)S(1)} %add_select_fusion.3), channel_id=1, source_target_pairs={{0,16},{8,24},{16,0},{24,8},{32,48},{40,56},{48,32},{56,40},{64,80... | collective-permute-start | bytes 786440 | tf_op jit(solution)/shard_map/ppermute | solution.py:259
  39.4 11.3 %collective-permute-start.5 = (f32[4,128,128]{2,1,0:T(8,128)}, f32[4,128,128]{2,1,0:T(8,128)}, u32[]{:S(2)}, u32[]{:S(2)}) collective-permute-start(f32[4,128,128]{2,1,0:T(8,128)} %fusion.2), channel_id=1, source_target_pairs={{0,32},{8,40},{16,48},{24,56},{32,0},{40,8},{48,16},{56,24},{64,96... | collective-permute-start | bytes 786440 | tf_op jit(solution)/shard_map/ppermute | solution.py:272
  42.3 12.2 %collective-permute-start.4 = (f32[4,128,128]{2,1,0:T(8,128)S(1)}, f32[4,128,128]{2,1,0:T(8,128)S(1)}, u32[]{:S(2)}, u32[]{:S(2)}) collective-permute-start(f32[4,128,128]{2,1,0:T(8,128)S(1)} %add_select_fusion.2), channel_id=1, source_target_pairs={{0,32},{8,40},{16,48},{24,56},{32,0},{40,8},{48,16},{56,24},{64,96... | collective-permute-start | bytes 786440 | tf_op jit(solution)/shard_map/ppermute | solution.py:259
  55.6 9.7 %collective-permute-start.7 = (f32[4,128,128]{2,1,0:T(8,128)S(1)}, f32[4,128,128]{2,1,0:T(8,128)S(1)}, u32[]{:S(2)}, u32[]{:S(2)}) collective-permute-start(f32[4,128,128]{2,1,0:T(8,128)S(1)} %get-tuple-element.120), channel_id=1, source_target_pairs={{0,16},{8,24},{16,0},{24,8},{32,48},{40,56},{48,32},{56,40},{64,80... | collective-permute-start | bytes 786440 | tf_op jit(solution)/shard_map/ppermute | solution.py:272
  56.2 9.2 %collective-permute-start.6 = (f32[4,128,128]{2,1,0:T(8,128)S(1)}, f32[4,128,128]{2,1,0:T(8,128)S(1)}, u32[]{:S(2)}, u32[]{:S(2)}) collective-permute-start(f32[4,128,128]{2,1,0:T(8,128)S(1)} %add_select_fusion.1), channel_id=1, source_target_pairs={{0,64},{8,72},{16,80},{24,88},{32,96},{40,104},{48,112},{56,120},{... | collective-permute-start | bytes 786440 | tf_op jit(solution)/shard_map/ppermute | solution.py:259
  65.4 8.4 %collective-permute-start.8 = (bf16[4,128,128]{2,1,0:T(8,128)(2,1)S(1)}, bf16[4,128,128]{2,1,0:T(8,128)(2,1)S(1)}, u32[]{:S(2)}, u32[]{:S(2)}) collective-permute-start(bf16[4,128,128]{2,1,0:T(8,128)(2,1)S(1)} %add_select_fusion), channel_id=1, source_target_pairs={{0,128},{8,136},{16,144},{24,152},{32,160},{40,168},{48,176},{56,1... | collective-permute-start | bytes 393224 | tf_op jit(solution)/shard_map/ppermute | solution.py:259
  66.8 8.2 %collective-permute-start.9 = (f32[4,128,128]{2,1,0:T(8,128)S(1)}, f32[4,128,128]{2,1,0:T(8,128)S(1)}, u32[]{:S(2)}, u32[]{:S(2)}) collective-permute-start(f32[4,128,128]{2,1,0:T(8,128)S(1)} %fusion), channel_id=1, source_target_pairs={{0,8},{8,0},{16,24},{24,16},{32,40},{40,32},{48,56},{56,48},{64,72... | collective-permute-start | bytes 786440 | tf_op jit(solution)/shard_map/ppermute | solution.py:272
  73.8 1.9 %copy-start = (bf16[5,4,128,128]{3,2,1,0:T(8,128)(2,1)}, bf16[5,4,128,128]{3,2,1,0:T(8,128)(2,1)S(1)}, u32[]{:S(2)}) copy-start(bf16[5,4,128,128]{3,2,1,0:T(8,128)(2,1)S(1)} %fusion.24.ls_ref) | copy-start | bytes 1966084

commit v5 on v4

--- a/solution.py
+++ b/solution.py
@@ -243,7 +243,6 @@
     nbits = level_total - log_block - 1
     me = lax.axis_index("ctx")
     weights = jnp.exp(level_gate)
-    cross_weight = weights[log_block + 1 :]
 
     gate_t = weights.transpose(1, 0, 2)
     own_state, grad_state = state_part(query_rows, key_rows, value_rows, out_grad, gate_t, nbits)
@@ -256,9 +255,13 @@
     for r in range(nbits):
         kf = r
         kb = nbits - 1 - r
-        fwd_got = lax.ppermute(
-            fwd_x, "ctx", pairs_of(kf, ctx_len, None if kf < nbits - 1 else 0)
-        )
+        if kf == 0 or kf == nbits - 1:
+            fwd_got = lax.ppermute(
+                fwd_x.astype(jnp.bfloat16), "ctx",
+                pairs_of(kf, ctx_len, None if kf < nbits - 1 else 0),
+            ).astype(jnp.float32)
+        else:
+            fwd_got = lax.ppermute(fwd_x, "ctx", pairs_of(kf, ctx_len))
         bit, joined, mine = step_masks(block_levels, me, kb)
         term = jnp.where(bit & mine, grad_wide[kb], 0.0)
         if bwd_acc is None:
@@ -269,7 +272,10 @@
             send = jnp.where(bit, term + kept, bwd_acc)
             own = jnp.where(bit, bwd_acc, kept)
             bwd_pairs = pairs_of(kb, ctx_len)
-        bwd_got = lax.ppermute(send, "ctx", bwd_pairs)
+        if own is None:
+            bwd_got = lax.ppermute(send.astype(jnp.bfloat16), "ctx", bwd_pairs).astype(jnp.float32)
+        else:
+            bwd_got = lax.ppermute(send, "ctx", bwd_pairs)
         if r < heads:
             partials = local_part(query_rows, key_rows, value_rows, out_grad, gate_t, r, partials)
             fwd_got, bwd_got, partials = lax.optimization_barrier((fwd_got, bwd_got, partials))

time: 87.1 us -> 86.1 us (0.989)
  other arithmetic: 5.21 us -> 4.33 us
    ppermute x5 -> x4, starting transfers between devices: 8.16 us -> 4.01 us  [per_device(): bwd_got = lax.ppermute(send, 'ctx', bwd_pairs)]
    ppermute x5 -> x6, starting transfers between devices: 5.58 us -> 9.65 us  [the longest x3 4.2 us: per_device(): fwd_got = lax.ppermute(fwd_x, 'ctx', pairs_of(kf, ctx_len))]
    ppermute x5 -> x6, waiting for transfers between devices: 10.7 us -> 10.8 us  [the longest x2 6.84 us: per_device(): lax.ppermute(fwd_x.astype(jnp.bfloat16), 'ctx', pairs_of(kf, ctx_len, Non...]
  transfers between devices with their start and end apart: 10 -> 10, of which waited for: 2 -> 2; matrix products, arithmetic and copies ran while one was open for 5% -> 5% of each run, Pallas kernels for 34% -> 35%
where the time goes in v5:
time: 86.1 us; the launch traced here: 85.6 us
  Pallas kernels  43.8 us (51%)
  starting transfers between devices  13.7 us (16%)
  waiting for transfers between devices  10.8 us (13%)
  local copies, waits for them, and re-layouts  6.5 us (8%)
  between operations  6.47 us (8%)
  other arithmetic  4.33 us (5%)
    pallas_call x4, Pallas kernels, local_part(): pl.pallas_call(local_kernel, grid=(1,), in_specs=in_specs, out_specs=[col...  29.7 us
    pallas_call x1, Pallas kernels, final_part(): pl.pallas_call(final_kernel, grid=(heads,), in_specs=[row_spec] * 4 + [co...  9.01 us
    ppermute x2, waiting for transfers between devices, per_device(): lax.ppermute(fwd_x.astype(jnp.bfloat16), 'ctx', pairs_of(kf, ctx_len, Non...  6.84 us
    pallas_call x1, Pallas kernels, state_part(): pl.pallas_call(state_kernel, grid=(heads,), in_specs=[row_spec] * 4 + [ga...  5.18 us
    ppermute x3, starting transfers between devices, per_device(): fwd_got = lax.ppermute(fwd_x, 'ctx', pairs_of(kf, ctx_len))  4.2 us
    ppermute x1, starting transfers between devices, per_device(): lax.ppermute(send.astype(jnp.bfloat16), 'ctx', bwd_pairs)  4.15 us
    ppermute x4, starting transfers between devices, per_device(): bwd_got = lax.ppermute(send, 'ctx', bwd_pairs)  4.01 us
    ppermute x3, waiting for transfers between devices, per_device(): fwd_got = lax.ppermute(fwd_x, 'ctx', pairs_of(kf, ctx_len))  3.91 us
  transfers between devices with their start and end apart: 10, of which 2 were waited for; matrix products, arithmetic and copies ran while one was open for 5% of the time, Pallas kernels for 35%

profile of v5, /device:TPU:4, one launch (start us, length us, event | category | flops | bytes accessed | tf_op | source)
XLA Modules:
  0.0 85.6 jit_solution(9538258017439652962)
XLA Ops:
  0.6 1.8 %fusion.16.g_ref = f32[4,16,1024]{2,1,0:T(8,128)} fusion(f32[16,4,1024]{2,1,0:T(4,128)} %param.10), kind=kLoop, calls=%fused_computation.32 | loop fusion | bytes 524288 | tf_op jit(solution)/shard_map/transpose | solution.py:247
  2.5 5.2 %shard_map.101 = (bf16[4,128,128]{2,1,0:T(8,128)(2,1)}, bf16[5,4,128,128]{3,2,1,0:T(8,128)(2,1)}) custom-call(bf16[4,1024,128]{2,1,0:T(8,128)(2,1)} %q_ref.11, bf16[4,1024,128]{2,1,0:T(8,128)(2,1)} %k_ref.11, bf16[4,1024,128]{2,1,0:T(8,128)(2,1)} %v_ref.11, bf16[4,1024,128]{2,1,0:T(8,128)(2,1)} %do_ref.11, f32[4,16,1024]{2,1,0:T(8,128)} %fusion.16.g_ref), custom_call_target="tpu_custom_call" | custom-call | flops 805306368 | bytes 4456448 | tf_op jit(solution)/shard_map/pallas_call | solution.py:138
  7.6 0.0 collective-permute-start
  7.6 1.2 %convert_element_type.45 = f32[5,4,128,128]{3,2,1,0:T(8,128)S(1)} convert(bf16[5,4,128,128]{3,2,1,0:T(8,128)(2,1)} %get-tuple-element.61) | non-fusion elementwise | flops 327680 | bytes 1966080 | tf_op jit(solution)/shard_map/convert_element_type | solution.py:249
  8.9 1.7 %fusion.29 = (s32[1,1]{1,0:T(1,128)}, s32[1,1]{1,0:T(1,128)}, s32[1,1]{1,0:T(1,128)}, s32[1,1]{1,0:T(1,128)}, s32[1,1]{1,0:T(1,128)}, /*index=5*/s32[1,1]{1,0:T(...) fusion(s32[32,32]{1,0:T(8,128)} %param.11, s32[]{:T(128)S(6)} %select_n.251, s32[]{:T(128)S(6)} %select_n.249, ...), kind=kLoop, calls=%fused_computation.52 | loop fusion | bytes 112 | tf_op jit(solution)/shard_map/dynamic_slice | solution.py:218
  11.3 4.2 %collective-permute-start.1 = (bf16[4,128,128]{2,1,0:T(8,128)(2,1)S(1)}, bf16[4,128,128]{2,1,0:T(8,128)(2,1)S(1)}, u32[]{:S(2)}, u32[]{:S(2)}) collective-permute-start(bf16[4,128,128]{2,1,0:T(8,128)(2,1)S(1)} %fusion.27), channel_id=1, source_target_pairs={{128,0},{136,8},{144,16},{152,24},{160,32},{168,40},{176,48},{184,... | collective-permute-start | bytes 393224 | tf_op jit(solution)/shard_map/ppermute | solution.py:276
  20.4 0.0 copy-start.1
  20.4 7.4 %shard_map.102 = (f32[4,128,1024]{2,1,0:T(8,128)}, f32[4,128,1024]{2,1,0:T(8,128)}, f32[4,1024,128]{2,1,0:T(8,128)}, f32[4,1024,128]{2,1,0:T(8,128)}, f32[4,16,1024]{2,1,0:T(8,128)}) custom-call(bf16[4,1024,128]{2,1,0:T(8,128)(2,1)} %q_ref.11, bf16[4,1024,128]{2,1,0:T(8,128)(2,1)} %k_ref.11, bf16[4,1024,128]{2,1,0:T(8,128)(2,1)} %v_ref.11, ...), custom_call_target="tpu_custom_call" | custom-call | flops 1006632960 | bytes 3276800 | tf_op jit(solution)/shard_map/pallas_call | solution.py:104
  27.8 0.0 collective-permute-done
  27.9 0.0 collective-permute-done.1
  28.0 0.5 collective-permute-start.3
  28.5 0.0 copy-done.1
  28.5 0.1 fusion.4
  28.5 1.7 %collective-permute-start.2 = (f32[4,128,128]{2,1,0:T(8,128)S(1)}, f32[4,128,128]{2,1,0:T(8,128)S(1)}, u32[]{:S(2)}, u32[]{:S(2)}) collective-permute-start(f32[4,128,128]{2,1,0:T(8,128)S(1)} %fusion.4), channel_id=1, source_target_pairs={{0,16},{8,24},{16,0},{24,8},{32,48},{40,56},{48,32},{56,40},{64,80... | collective-permute-start | bytes 786440 | tf_op jit(solution)/shard_map/ppermute | solution.py:264
  30.2 7.4 %shard_map.103 = (f32[4,128,1024]{2,1,0:T(8,128)}, f32[4,128,1024]{2,1,0:T(8,128)}, f32[4,1024,128]{2,1,0:T(8,128)}, f32[4,1024,128]{2,1,0:T(8,128)}, f32[4,16,1024]{2,1,0:T(8,128)}) custom-call(bf16[4,1024,128]{2,1,0:T(8,128)(2,1)} %q_ref.11, ...), custom_call_target="tpu_custom_call", output_to_operand_aliasing={{0}: (5, {}), {1}: (6, {}), {2}: (7, {}), {3}: (8, {}), {4}... | custom-call | flops 1006632960 | bytes 3276800 | tf_op jit(solution)/shard_map/pallas_call | solution.py:104
  37.6 0.0 collective-permute-done.3
  37.6 0.0 collective-permute-done.2
  37.6 0.8 fusion.2
  38.4 2.9 %collective-permute-start.5 = (f32[4,128,128]{2,1,0:T(8,128)}, f32[4,128,128]{2,1,0:T(8,128)}, u32[]{:S(2)}, u32[]{:S(2)}) collective-permute-start(f32[4,128,128]{2,1,0:T(8,128)} %fusion.2), channel_id=1, source_target_pairs={{0,32},{8,40},{16,48},{24,56},{32,0},{40,8},{48,16},{56,24},{64,96... | collective-permute-start | bytes 786440 | tf_op jit(solution)/shard_map/ppermute | solution.py:278
  41.3 0.9 %collective-permute-start.4 = (f32[4,128,128]{2,1,0:T(8,128)S(1)}, f32[4,128,128]{2,1,0:T(8,128)S(1)}, u32[]{:S(2)}, u32[]{:S(2)}) collective-permute-start(f32[4,128,128]{2,1,0:T(8,128)S(1)} %add_select_fusion.1), channel_id=1, source_target_pairs={{0,32},{8,40},{16,48},{24,56},{32,0},{40,8},{48,16},{56,24},{64,96... | collective-permute-start | bytes 786440 | tf_op jit(solution)/shard_map/ppermute | solution.py:264
  42.2 7.4 %shard_map.104 = (f32[4,128,1024]{2,1,0:T(8,128)}, f32[4,128,1024]{2,1,0:T(8,128)}, f32[4,1024,128]{2,1,0:T(8,128)}, f32[4,1024,128]{2,1,0:T(8,128)}, f32[4,16,1024]{2,1,0:T(8,128)}) custom-call(bf16[4,1024,128]{2,1,0:T(8,128)(2,1)} %q_ref.11, ...), custom_call_target="tpu_custom_call", output_to_operand_aliasing={{0}: (5, {}), {1}: (6, {}), {2}: (7, {}), {3}: (8, {}), {4}... | custom-call | flops 1006632960 | bytes 3276800 | tf_op jit(solution)/shard_map/pallas_call | solution.py:104
  49.7 0.0 collective-permute-done.5
  49.7 3.9 %collective-permute-done.4 = f32[4,128,128]{2,1,0:T(8,128)S(1)} collective-permute-done((f32[4,128,128]{2,1,0:T(8,128)S(1)}, f32[4,128,128]{2,1,0:T(8,128)S(1)}, u32[]{:S(2)}, u32[]{:S(2)}) %collective-permute-start.4) | collective-permute-done | bytes 262176 | tf_op jit(solution)/shard_map/ppermute | solution.py:264
  53.6 1.0 %fusion.1 = (f32[4,128,128]{2,1,0:T(8,128)S(1)}, f32[4,128,128]{2,1,0:T(8,128)S(1)}) fusion(f32[5,4,128,128]{3,2,1,0:T(8,128)S(1)} %convert_element_type.45, pred[]{:T(512)S(6)} %and.49, pred[]{:T(512)} %bitcast.4, pred[]{:T(512)S(6)} %eq.21, f32[4,128,128]{2,1,0:T(8,128)} %collective-permute-done.5, pred[]{:T(512)} %bitcast.8, ...), kind=kLoop, calls=%fused_computation.5 | loop fusion | flops 655360 | bytes 1572871 | tf_op jit(solution)/shard_map/jit(_where)/select_n | solution.py:272
  54.7 0.5 collective-permute-start.7
  55.2 1.6 %collective-permute-start.6 = (f32[4,128,128]{2,1,0:T(8,128)S(1)}, f32[4,128,128]{2,1,0:T(8,128)S(1)}, u32[]{:S(2)}, u32[]{:S(2)}) collective-permute-start(f32[4,128,128]{2,1,0:T(8,128)S(1)} %add_select_fusion), channel_id=1, source_target_pairs={{0,64},{8,72},{16,80},{24,88},{32,96},{40,104},{48,112},{56,120},{... | collective-permute-start | bytes 786440 | tf_op jit(solution)/shard_map/ppermute | solution.py:264
  56.8 7.5 %shard_map.105 = (f32[4,128,1024]{2,1,0:T(8,128)}, f32[4,128,1024]{2,1,0:T(8,128)}, f32[4,1024,128]{2,1,0:T(8,128)}, f32[4,1024,128]{2,1,0:T(8,128)}, f32[4,16,1024]{2,1,0:T(8,128)}) custom-call(bf16[4,1024,128]{2,1,0:T(8,128)(2,1)} %q_ref.11, ...), custom_call_target="tpu_custom_call", output_to_operand_aliasing={{0}: (5, {}), {1}: (6, {}), {2}: (7, {}), {3}: (8, {}), {4}... | custom-call | flops 1006632960 | bytes 3276800 | tf_op jit(solution)/shard_map/pallas_call | solution.py:104
  64.4 0.0 collective-permute-done.7
  64.4 0.0 collective-permute-done.6
  64.4 0.1 select_convert_fusion.1
  64.4 1.3 %collective-permute-start.8 = (bf16[4,128,128]{2,1,0:T(8,128)(2,1)S(1)}, bf16[4,128,128]{2,1,0:T(8,128)(2,1)S(1)}, u32[]{:S(2)}, u32[]{:S(2)}) collective-permute-start(bf16[4,128,128]{2,1,0:T(8,128)(2,1)S(1)} %select_convert_fusion.1), channel_id=1, source_target_pairs={{0,128},{8,136},{16,144},{24,152},{32,160},{40,168},{48,176},{56,1... | collective-permute-start | bytes 393224 | tf_op jit(solution)/shard_map/ppermute | solution.py:259
  65.7 0.1 fusion
  65.8 0.1 collective-permute-start.9
  66.0 6.8 %collective-permute-done.8 = bf16[4,128,128]{2,1,0:T(8,128)(2,1)S(1)} collective-permute-done((bf16[4,128,128]{2,1,0:T(8,128)(2,1)S(1)}, bf16[4,128,128]{2,1,0:T(8,128)(2,1)S(1)}, u32[]{:S(2)}, u32[]{:S(2)}) %collective-permute-start.8) | collective-permute-done | bytes 131104 | tf_op jit(solution)/shard_map/ppermute | solution.py:259
  72.9 0.0 copy-start
  72.9 1.1 %copy.27.lst_ref = bf16[5,4,128,128]{3,2,1,0:T(8,128)(2,1)} copy(bf16[5,4,128,128]{2,3,1,0:T(8,128)(2,1)S(1)} %bitcast.51) | data formatting | bytes 1310720 | tf_op jit(solution)/shard_map/transpose | solution.py:198
  74.0 0.0 collective-permute-done.9
  74.0 0.7 fusion.10.kst_ref
  74.7 0.0 copy-done
  74.7 9.0 %shard_map.106 = (bf16[4,1024,128]{2,1,0:T(8,128)(2,1)}, bf16[4,1024,128]{2,1,0:T(8,128)(2,1)}, bf16[4,1024,128]{2,1,0:T(8,128)(2,1)}, bf16[4,1024,128]{2,1,0:T(8,128)(2,1)}, f32[4,16,1024]{2,1,0:T(8,128)}) custom-call(bf16[4,1024,128]{2,1,0:T(8,128)(2,1)} %q_ref.11, bf16[4,1024,128]{2,1,0:T(8,128)(2,1)} %k_ref.11, bf16[4,1024,128]{2,1,0:T(8,128)(2,1)} %v_ref.11, ...), custom_call_target="tpu_custom_call" | custom-call | flops 1610612736 | bytes 17825792 | tf_op jit(solution)/shard_map/pallas_call | solution.py:199
  83.8 1.8 %copy.28 = f32[16,4,1024]{2,1,0:T(4,128)} copy(f32[16,4,1024]{2,0,1:T(8,128)} %bitcast.52) | data formatting | bytes 524288
  (11 shorter events, 0.4 us)
Async XLA Ops:
  7.6 20.2 %collective-permute-start = (bf16[4,128,128]{2,1,0:T(8,128)(2,1)}, bf16[4,128,128]{2,1,0:T(8,128)(2,1)S(1)}, u32[]{:S(2)}, u32[]{:S(2)}) collective-permute-start(bf16[4,128,128]{2,1,0:T(8,128)(2,1)} %get-tuple-element.60), channel_id=1, source_target_pairs={{0,8},{8,0},{16,24},{24,16},{32,40},{40,32},{48,56},{56,48},{64,72... | collective-permute-start | bytes 393224 | tf_op jit(solution)/shard_map/ppermute | solution.py:259
  11.3 16.6 %collective-permute-start.1 = (bf16[4,128,128]{2,1,0:T(8,128)(2,1)S(1)}, bf16[4,128,128]{2,1,0:T(8,128)(2,1)S(1)}, u32[]{:S(2)}, u32[]{:S(2)}) collective-permute-start(bf16[4,128,128]{2,1,0:T(8,128)(2,1)S(1)} %fusion.27), channel_id=1, source_target_pairs={{128,0},{136,8},{144,16},{152,24},{160,32},{168,40},{176,48},{184,... | collective-permute-start | bytes 393224 | tf_op jit(solution)/shard_map/ppermute | solution.py:276
  20.4 8.0 %copy-start.1 = (bf16[4,128,128]{2,1,0:T(8,128)(2,1)S(1)}, bf16[4,128,128]{2,1,0:T(8,128)(2,1)}, u32[]{:S(2)}) copy-start(bf16[4,128,128]{2,1,0:T(8,128)(2,1)} %get-tuple-element.60) | copy-start | bytes 393220
  28.0 9.6 %collective-permute-start.3 = (f32[4,128,128]{2,1,0:T(8,128)S(1)}, f32[4,128,128]{2,1,0:T(8,128)S(1)}, u32[]{:S(2)}, u32[]{:S(2)}) collective-permute-start(f32[4,128,128]{2,1,0:T(8,128)S(1)} %fusion.3), channel_id=1, source_target_pairs={{0,64},{8,72},{16,80},{24,88},{32,96},{40,104},{48,112},{56,120},{... | collective-permute-start | bytes 786440 | tf_op jit(solution)/shard_map/ppermute | solution.py:278
  28.5 9.1 %collective-permute-start.2 = (f32[4,128,128]{2,1,0:T(8,128)S(1)}, f32[4,128,128]{2,1,0:T(8,128)S(1)}, u32[]{:S(2)}, u32[]{:S(2)}) collective-permute-start(f32[4,128,128]{2,1,0:T(8,128)S(1)} %fusion.4), channel_id=1, source_target_pairs={{0,16},{8,24},{16,0},{24,8},{32,48},{40,56},{48,32},{56,40},{64,80... | collective-permute-start | bytes 786440 | tf_op jit(solution)/shard_map/ppermute | solution.py:264
  38.4 11.3 %collective-permute-start.5 = (f32[4,128,128]{2,1,0:T(8,128)}, f32[4,128,128]{2,1,0:T(8,128)}, u32[]{:S(2)}, u32[]{:S(2)}) collective-permute-start(f32[4,128,128]{2,1,0:T(8,128)} %fusion.2), channel_id=1, source_target_pairs={{0,32},{8,40},{16,48},{24,56},{32,0},{40,8},{48,16},{56,24},{64,96... | collective-permute-start | bytes 786440 | tf_op jit(solution)/shard_map/ppermute | solution.py:278
  41.3 12.3 %collective-permute-start.4 = (f32[4,128,128]{2,1,0:T(8,128)S(1)}, f32[4,128,128]{2,1,0:T(8,128)S(1)}, u32[]{:S(2)}, u32[]{:S(2)}) collective-permute-start(f32[4,128,128]{2,1,0:T(8,128)S(1)} %add_select_fusion.1), channel_id=1, source_target_pairs={{0,32},{8,40},{16,48},{24,56},{32,0},{40,8},{48,16},{56,24},{64,96... | collective-permute-start | bytes 786440 | tf_op jit(solution)/shard_map/ppermute | solution.py:264
  54.7 9.7 %collective-permute-start.7 = (f32[4,128,128]{2,1,0:T(8,128)S(1)}, f32[4,128,128]{2,1,0:T(8,128)S(1)}, u32[]{:S(2)}, u32[]{:S(2)}) collective-permute-start(f32[4,128,128]{2,1,0:T(8,128)S(1)} %get-tuple-element.120), channel_id=1, source_target_pairs={{0,16},{8,24},{16,0},{24,8},{32,48},{40,56},{48,32},{56,40},{64,80... | collective-permute-start | bytes 786440 | tf_op jit(solution)/shard_map/ppermute | solution.py:278
  55.2 9.2 %collective-permute-start.6 = (f32[4,128,128]{2,1,0:T(8,128)S(1)}, f32[4,128,128]{2,1,0:T(8,128)S(1)}, u32[]{:S(2)}, u32[]{:S(2)}) collective-permute-start(f32[4,128,128]{2,1,0:T(8,128)S(1)} %add_select_fusion), channel_id=1, source_target_pairs={{0,64},{8,72},{16,80},{24,88},{32,96},{40,104},{48,112},{56,120},{... | collective-permute-start | bytes 786440 | tf_op jit(solution)/shard_map/ppermute | solution.py:264
  64.4 8.4 %collective-permute-start.8 = (bf16[4,128,128]{2,1,0:T(8,128)(2,1)S(1)}, bf16[4,128,128]{2,1,0:T(8,128)(2,1)S(1)}, u32[]{:S(2)}, u32[]{:S(2)}) collective-permute-start(bf16[4,128,128]{2,1,0:T(8,128)(2,1)S(1)} %select_convert_fusion.1), channel_id=1, source_target_pairs={{0,128},{8,136},{16,144},{24,152},{32,160},{40,168},{48,176},{56,1... | collective-permute-start | bytes 393224 | tf_op jit(solution)/shard_map/ppermute | solution.py:259
  65.8 8.2 %collective-permute-start.9 = (f32[4,128,128]{2,1,0:T(8,128)S(1)}, f32[4,128,128]{2,1,0:T(8,128)S(1)}, u32[]{:S(2)}, u32[]{:S(2)}) collective-permute-start(f32[4,128,128]{2,1,0:T(8,128)S(1)} %fusion), channel_id=1, source_target_pairs={{0,8},{8,0},{16,24},{24,16},{32,40},{40,32},{48,56},{56,48},{64,72... | collective-permute-start | bytes 786440 | tf_op jit(solution)/shard_map/ppermute | solution.py:278
  72.9 1.9 %copy-start = (bf16[5,4,128,128]{3,2,1,0:T(8,128)(2,1)}, bf16[5,4,128,128]{3,2,1,0:T(8,128)(2,1)S(1)}, u32[]{:S(2)}) copy-start(bf16[5,4,128,128]{3,2,1,0:T(8,128)(2,1)S(1)} %fusion.26.ls_ref) | copy-start | bytes 1966084

commit v6 on v5

--- a/solution.py
+++ b/solution.py
@@ -258,7 +258,7 @@
         if kf == 0 or kf == nbits - 1:
             fwd_got = lax.ppermute(
                 fwd_x.astype(jnp.bfloat16), "ctx",
-                pairs_of(kf, ctx_len, None if kf < nbits - 1 else 0),
+                pairs_of(kf, ctx_len),
             ).astype(jnp.float32)
         else:
             fwd_got = lax.ppermute(fwd_x, "ctx", pairs_of(kf, ctx_len))
@@ -266,7 +266,7 @@
         term = jnp.where(bit & mine, grad_wide[kb], 0.0)
         if bwd_acc is None:
             send, own = term, None
-            bwd_pairs = pairs_of(kb, ctx_len, 1)
+            bwd_pairs = pairs_of(kb, ctx_len)
         else:
             kept = jnp.where(joined, bwd_acc, 0.0)
             send = jnp.where(bit, term + kept, bwd_acc)

time: 86.1 us -> 83.2 us (0.966)
  waiting for transfers between devices: 10.8 us -> 8.89 us
  starting transfers between devices: 13.7 us -> 11.9 us
    ppermute x2, waiting for transfers between devices: 6.84 us -> 4.97 us  [per_device(): lax.ppermute(fwd_x.astype(jnp.bfloat16), 'ctx', pairs_of(kf, ctx_len))]
    ppermute x1, starting transfers between devices: 4.15 us -> 2.33 us  [per_device(): lax.ppermute(send.astype(jnp.bfloat16), 'ctx', bwd_pairs)]
  transfers between devices with their start and end apart: 10 -> 10, of which waited for: 2 -> 2; matrix products, arithmetic and copies ran while one was open for 5% -> 5% of each run, Pallas kernels for 35% -> 36%
where the time goes in v6:
time: 83.2 us; the launch traced here: 81.9 us
  Pallas kernels  43.9 us (53%)
  starting transfers between devices  11.9 us (14%)
  waiting for transfers between devices  8.89 us (11%)
  local copies, waits for them, and re-layouts  6.5 us (8%)
  between operations  6.45 us (8%)
  other arithmetic  4.32 us (5%)
    pallas_call x4, Pallas kernels, local_part(): pl.pallas_call(local_kernel, grid=(1,), in_specs=in_specs, out_specs=[col...  29.7 us
    pallas_call x1, Pallas kernels, final_part(): pl.pallas_call(final_kernel, grid=(heads,), in_specs=[row_spec] * 4 + [co...  9.01 us
    pallas_call x1, Pallas kernels, state_part(): pl.pallas_call(state_kernel, grid=(heads,), in_specs=[row_spec] * 4 + [ga...  5.18 us
    ppermute x2, waiting for transfers between devices, per_device(): lax.ppermute(fwd_x.astype(jnp.bfloat16), 'ctx', pairs_of(kf, ctx_len))  4.97 us
    ppermute x3, starting transfers between devices, per_device(): fwd_got = lax.ppermute(fwd_x, 'ctx', pairs_of(kf, ctx_len))  4.2 us
    ppermute x4, starting transfers between devices, per_device(): bwd_got = lax.ppermute(send, 'ctx', bwd_pairs)  4 us
    ppermute x3, waiting for transfers between devices, per_device(): fwd_got = lax.ppermute(fwd_x, 'ctx', pairs_of(kf, ctx_len))  3.91 us
    ppermute x1, starting transfers between devices, per_device(): lax.ppermute(send.astype(jnp.bfloat16), 'ctx', bwd_pairs)  2.33 us
  transfers between devices with their start and end apart: 10, of which 2 were waited for; matrix products, arithmetic and copies ran while one was open for 5% of the time, Pallas kernels for 36%

profile of v6, /device:TPU:4, one launch (start us, length us, event | category | flops | bytes accessed | tf_op | source)
XLA Modules:
  0.0 81.9 jit_solution(4279954109952471446)
XLA Ops:
  0.6 1.8 %fusion.16.g_ref = f32[4,16,1024]{2,1,0:T(8,128)} fusion(f32[16,4,1024]{2,1,0:T(4,128)} %param.10), kind=kLoop, calls=%fused_computation.32 | loop fusion | bytes 524288 | tf_op jit(solution)/shard_map/transpose | solution.py:247
  2.5 5.2 %shard_map.101 = (bf16[4,128,128]{2,1,0:T(8,128)(2,1)}, bf16[5,4,128,128]{3,2,1,0:T(8,128)(2,1)}) custom-call(bf16[4,1024,128]{2,1,0:T(8,128)(2,1)} %q_ref.11, bf16[4,1024,128]{2,1,0:T(8,128)(2,1)} %k_ref.11, bf16[4,1024,128]{2,1,0:T(8,128)(2,1)} %v_ref.11, bf16[4,1024,128]{2,1,0:T(8,128)(2,1)} %do_ref.11, f32[4,16,1024]{2,1,0:T(8,128)} %fusion.16.g_ref), custom_call_target="tpu_custom_call" | custom-call | flops 805306368 | bytes 4456448 | tf_op jit(solution)/shard_map/pallas_call | solution.py:138
  7.6 0.0 collective-permute-start
  7.6 1.2 %convert_element_type.45 = f32[5,4,128,128]{3,2,1,0:T(8,128)S(1)} convert(bf16[5,4,128,128]{3,2,1,0:T(8,128)(2,1)} %get-tuple-element.61) | non-fusion elementwise | flops 327680 | bytes 1966080 | tf_op jit(solution)/shard_map/convert_element_type | solution.py:249
  8.9 1.7 %fusion.29 = (s32[1,1]{1,0:T(1,128)}, s32[1,1]{1,0:T(1,128)}, s32[1,1]{1,0:T(1,128)}, s32[1,1]{1,0:T(1,128)}, s32[1,1]{1,0:T(1,128)}, /*index=5*/s32[1,1]{1,0:T(...) fusion(s32[32,32]{1,0:T(8,128)} %param.11, s32[]{:T(128)S(6)} %select_n.251, s32[]{:T(128)S(6)} %select_n.249, ...), kind=kLoop, calls=%fused_computation.52 | loop fusion | bytes 112 | tf_op jit(solution)/shard_map/dynamic_slice | solution.py:218
  11.3 2.3 %collective-permute-start.1 = (bf16[4,128,128]{2,1,0:T(8,128)(2,1)S(1)}, bf16[4,128,128]{2,1,0:T(8,128)(2,1)S(1)}, u32[]{:S(2)}, u32[]{:S(2)}) collective-permute-start(bf16[4,128,128]{2,1,0:T(8,128)(2,1)S(1)} %fusion.27), channel_id=1, source_target_pairs={{0,128},{8,136},{16,144},{24,152},{32,160},{40,168},{48,176},{56,1... | collective-permute-start | bytes 393224 | tf_op jit(solution)/shard_map/ppermute | solution.py:276
  18.6 0.0 copy-start.1
  18.6 7.4 %shard_map.102 = (f32[4,128,1024]{2,1,0:T(8,128)}, f32[4,128,1024]{2,1,0:T(8,128)}, f32[4,1024,128]{2,1,0:T(8,128)}, f32[4,1024,128]{2,1,0:T(8,128)}, f32[4,16,1024]{2,1,0:T(8,128)}) custom-call(bf16[4,1024,128]{2,1,0:T(8,128)(2,1)} %q_ref.11, bf16[4,1024,128]{2,1,0:T(8,128)(2,1)} %k_ref.11, bf16[4,1024,128]{2,1,0:T(8,128)(2,1)} %v_ref.11, ...), custom_call_target="tpu_custom_call" | custom-call | flops 1006632960 | bytes 3276800 | tf_op jit(solution)/shard_map/pallas_call | solution.py:104
  26.0 0.0 collective-permute-done
  26.0 0.0 collective-permute-done.1
  26.1 0.5 collective-permute-start.3
  26.6 0.0 copy-done.1
  26.6 0.1 fusion.4
  26.7 1.7 %collective-permute-start.2 = (f32[4,128,128]{2,1,0:T(8,128)S(1)}, f32[4,128,128]{2,1,0:T(8,128)S(1)}, u32[]{:S(2)}, u32[]{:S(2)}) collective-permute-start(f32[4,128,128]{2,1,0:T(8,128)S(1)} %fusion.4), channel_id=1, source_target_pairs={{0,16},{8,24},{16,0},{24,8},{32,48},{40,56},{48,32},{56,40},{64,80... | collective-permute-start | bytes 786440 | tf_op jit(solution)/shard_map/ppermute | solution.py:264
  28.3 7.4 %shard_map.103 = (f32[4,128,1024]{2,1,0:T(8,128)}, f32[4,128,1024]{2,1,0:T(8,128)}, f32[4,1024,128]{2,1,0:T(8,128)}, f32[4,1024,128]{2,1,0:T(8,128)}, f32[4,16,1024]{2,1,0:T(8,128)}) custom-call(bf16[4,1024,128]{2,1,0:T(8,128)(2,1)} %q_ref.11, ...), custom_call_target="tpu_custom_call", output_to_operand_aliasing={{0}: (5, {}), {1}: (6, {}), {2}: (7, {}), {3}: (8, {}), {4}... | custom-call | flops 1006632960 | bytes 3276800 | tf_op jit(solution)/shard_map/pallas_call | solution.py:104
  35.7 0.0 collective-permute-done.3
  35.7 0.0 collective-permute-done.2
  35.8 0.8 fusion.2
  36.5 2.9 %collective-permute-start.5 = (f32[4,128,128]{2,1,0:T(8,128)}, f32[4,128,128]{2,1,0:T(8,128)}, u32[]{:S(2)}, u32[]{:S(2)}) collective-permute-start(f32[4,128,128]{2,1,0:T(8,128)} %fusion.2), channel_id=1, source_target_pairs={{0,32},{8,40},{16,48},{24,56},{32,0},{40,8},{48,16},{56,24},{64,96... | collective-permute-start | bytes 786440 | tf_op jit(solution)/shard_map/ppermute | solution.py:278
  39.5 0.9 %collective-permute-start.4 = (f32[4,128,128]{2,1,0:T(8,128)S(1)}, f32[4,128,128]{2,1,0:T(8,128)S(1)}, u32[]{:S(2)}, u32[]{:S(2)}) collective-permute-start(f32[4,128,128]{2,1,0:T(8,128)S(1)} %add_select_fusion.1), channel_id=1, source_target_pairs={{0,32},{8,40},{16,48},{24,56},{32,0},{40,8},{48,16},{56,24},{64,96... | collective-permute-start | bytes 786440 | tf_op jit(solution)/shard_map/ppermute | solution.py:264
  40.4 7.4 %shard_map.104 = (f32[4,128,1024]{2,1,0:T(8,128)}, f32[4,128,1024]{2,1,0:T(8,128)}, f32[4,1024,128]{2,1,0:T(8,128)}, f32[4,1024,128]{2,1,0:T(8,128)}, f32[4,16,1024]{2,1,0:T(8,128)}) custom-call(bf16[4,1024,128]{2,1,0:T(8,128)(2,1)} %q_ref.11, ...), custom_call_target="tpu_custom_call", output_to_operand_aliasing={{0}: (5, {}), {1}: (6, {}), {2}: (7, {}), {3}: (8, {}), {4}... | custom-call | flops 1006632960 | bytes 3276800 | tf_op jit(solution)/shard_map/pallas_call | solution.py:104
  47.8 0.0 collective-permute-done.5
  47.8 3.9 %collective-permute-done.4 = f32[4,128,128]{2,1,0:T(8,128)S(1)} collective-permute-done((f32[4,128,128]{2,1,0:T(8,128)S(1)}, f32[4,128,128]{2,1,0:T(8,128)S(1)}, u32[]{:S(2)}, u32[]{:S(2)}) %collective-permute-start.4) | collective-permute-done | bytes 262176 | tf_op jit(solution)/shard_map/ppermute | solution.py:264
  51.8 1.0 %fusion.1 = (f32[4,128,128]{2,1,0:T(8,128)S(1)}, f32[4,128,128]{2,1,0:T(8,128)S(1)}) fusion(f32[5,4,128,128]{3,2,1,0:T(8,128)S(1)} %convert_element_type.45, pred[]{:T(512)S(6)} %and.49, pred[]{:T(512)} %bitcast.4, pred[]{:T(512)S(6)} %eq.21, f32[4,128,128]{2,1,0:T(8,128)} %collective-permute-done.5, pred[]{:T(512)} %bitcast.8, ...), kind=kLoop, calls=%fused_computation.5 | loop fusion | flops 655360 | bytes 1572871 | tf_op jit(solution)/shard_map/jit(_where)/select_n | solution.py:272
  52.8 0.5 collective-permute-start.7
  53.4 1.6 %collective-permute-start.6 = (f32[4,128,128]{2,1,0:T(8,128)S(1)}, f32[4,128,128]{2,1,0:T(8,128)S(1)}, u32[]{:S(2)}, u32[]{:S(2)}) collective-permute-start(f32[4,128,128]{2,1,0:T(8,128)S(1)} %add_select_fusion), channel_id=1, source_target_pairs={{0,64},{8,72},{16,80},{24,88},{32,96},{40,104},{48,112},{56,120},{... | collective-permute-start | bytes 786440 | tf_op jit(solution)/shard_map/ppermute | solution.py:264
  55.0 7.5 %shard_map.105 = (f32[4,128,1024]{2,1,0:T(8,128)}, f32[4,128,1024]{2,1,0:T(8,128)}, f32[4,1024,128]{2,1,0:T(8,128)}, f32[4,1024,128]{2,1,0:T(8,128)}, f32[4,16,1024]{2,1,0:T(8,128)}) custom-call(bf16[4,1024,128]{2,1,0:T(8,128)(2,1)} %q_ref.11, ...), custom_call_target="tpu_custom_call", output_to_operand_aliasing={{0}: (5, {}), {1}: (6, {}), {2}: (7, {}), {3}: (8, {}), {4}... | custom-call | flops 1006632960 | bytes 3276800 | tf_op jit(solution)/shard_map/pallas_call | solution.py:104
  62.5 0.0 collective-permute-done.7
  62.5 0.0 collective-permute-done.6
  62.5 0.1 select_convert_fusion.1
  62.6 1.4 %collective-permute-start.8 = (bf16[4,128,128]{2,1,0:T(8,128)(2,1)S(1)}, bf16[4,128,128]{2,1,0:T(8,128)(2,1)S(1)}, u32[]{:S(2)}, u32[]{:S(2)}) collective-permute-start(bf16[4,128,128]{2,1,0:T(8,128)(2,1)S(1)} %select_convert_fusion.1), channel_id=1, source_target_pairs={{0,128},{8,136},{16,144},{24,152},{32,160},{40,168},{48,176},{56,1... | collective-permute-start | bytes 393224 | tf_op jit(solution)/shard_map/ppermute | solution.py:259
  64.0 0.1 fusion
  64.1 0.1 collective-permute-start.9
  64.2 5.0 %collective-permute-done.8 = bf16[4,128,128]{2,1,0:T(8,128)(2,1)S(1)} collective-permute-done((bf16[4,128,128]{2,1,0:T(8,128)(2,1)S(1)}, bf16[4,128,128]{2,1,0:T(8,128)(2,1)S(1)}, u32[]{:S(2)}, u32[]{:S(2)}) %collective-permute-start.8) | collective-permute-done | bytes 131104 | tf_op jit(solution)/shard_map/ppermute | solution.py:259
  69.2 0.0 copy-start
  69.2 1.1 %copy.27.lst_ref = bf16[5,4,128,128]{3,2,1,0:T(8,128)(2,1)} copy(bf16[5,4,128,128]{2,3,1,0:T(8,128)(2,1)S(1)} %bitcast.51) | data formatting | bytes 1310720 | tf_op jit(solution)/shard_map/transpose | solution.py:198
  70.4 0.0 collective-permute-done.9
  70.4 0.7 fusion.10.kst_ref
  71.1 0.0 copy-done
  71.1 9.0 %shard_map.106 = (bf16[4,1024,128]{2,1,0:T(8,128)(2,1)}, bf16[4,1024,128]{2,1,0:T(8,128)(2,1)}, bf16[4,1024,128]{2,1,0:T(8,128)(2,1)}, bf16[4,1024,128]{2,1,0:T(8,128)(2,1)}, f32[4,16,1024]{2,1,0:T(8,128)}) custom-call(bf16[4,1024,128]{2,1,0:T(8,128)(2,1)} %q_ref.11, bf16[4,1024,128]{2,1,0:T(8,128)(2,1)} %k_ref.11, bf16[4,1024,128]{2,1,0:T(8,128)(2,1)} %v_ref.11, ...), custom_call_target="tpu_custom_call" | custom-call | flops 1610612736 | bytes 17825792 | tf_op jit(solution)/shard_map/pallas_call | solution.py:199
  80.1 1.8 %copy.28 = f32[16,4,1024]{2,1,0:T(4,128)} copy(f32[16,4,1024]{2,0,1:T(8,128)} %bitcast.52) | data formatting | bytes 524288
  (11 shorter events, 0.4 us)
Async XLA Ops:
  7.6 18.4 %collective-permute-start = (bf16[4,128,128]{2,1,0:T(8,128)(2,1)}, bf16[4,128,128]{2,1,0:T(8,128)(2,1)S(1)}, u32[]{:S(2)}, u32[]{:S(2)}) collective-permute-start(bf16[4,128,128]{2,1,0:T(8,128)(2,1)} %get-tuple-element.60), channel_id=1, source_target_pairs={{0,8},{8,0},{16,24},{24,16},{32,40},{40,32},{48,56},{56,48},{64,72... | collective-permute-start | bytes 393224 | tf_op jit(solution)/shard_map/ppermute | solution.py:259
  11.3 14.8 %collective-permute-start.1 = (bf16[4,128,128]{2,1,0:T(8,128)(2,1)S(1)}, bf16[4,128,128]{2,1,0:T(8,128)(2,1)S(1)}, u32[]{:S(2)}, u32[]{:S(2)}) collective-permute-start(bf16[4,128,128]{2,1,0:T(8,128)(2,1)S(1)} %fusion.27), channel_id=1, source_target_pairs={{0,128},{8,136},{16,144},{24,152},{32,160},{40,168},{48,176},{56,1... | collective-permute-start | bytes 393224 | tf_op jit(solution)/shard_map/ppermute | solution.py:276
  18.6 8.0 %copy-start.1 = (bf16[4,128,128]{2,1,0:T(8,128)(2,1)S(1)}, bf16[4,128,128]{2,1,0:T(8,128)(2,1)}, u32[]{:S(2)}) copy-start(bf16[4,128,128]{2,1,0:T(8,128)(2,1)} %get-tuple-element.60) | copy-start | bytes 393220
  26.1 9.6 %collective-permute-start.3 = (f32[4,128,128]{2,1,0:T(8,128)S(1)}, f32[4,128,128]{2,1,0:T(8,128)S(1)}, u32[]{:S(2)}, u32[]{:S(2)}) collective-permute-start(f32[4,128,128]{2,1,0:T(8,128)S(1)} %fusion.3), channel_id=1, source_target_pairs={{0,64},{8,72},{16,80},{24,88},{32,96},{40,104},{48,112},{56,120},{... | collective-permute-start | bytes 786440 | tf_op jit(solution)/shard_map/ppermute | solution.py:278
  26.7 9.1 %collective-permute-start.2 = (f32[4,128,128]{2,1,0:T(8,128)S(1)}, f32[4,128,128]{2,1,0:T(8,128)S(1)}, u32[]{:S(2)}, u32[]{:S(2)}) collective-permute-start(f32[4,128,128]{2,1,0:T(8,128)S(1)} %fusion.4), channel_id=1, source_target_pairs={{0,16},{8,24},{16,0},{24,8},{32,48},{40,56},{48,32},{56,40},{64,80... | collective-permute-start | bytes 786440 | tf_op jit(solution)/shard_map/ppermute | solution.py:264
  36.5 11.3 %collective-permute-start.5 = (f32[4,128,128]{2,1,0:T(8,128)}, f32[4,128,128]{2,1,0:T(8,128)}, u32[]{:S(2)}, u32[]{:S(2)}) collective-permute-start(f32[4,128,128]{2,1,0:T(8,128)} %fusion.2), channel_id=1, source_target_pairs={{0,32},{8,40},{16,48},{24,56},{32,0},{40,8},{48,16},{56,24},{64,96... | collective-permute-start | bytes 786440 | tf_op jit(solution)/shard_map/ppermute | solution.py:278
  39.5 12.3 %collective-permute-start.4 = (f32[4,128,128]{2,1,0:T(8,128)S(1)}, f32[4,128,128]{2,1,0:T(8,128)S(1)}, u32[]{:S(2)}, u32[]{:S(2)}) collective-permute-start(f32[4,128,128]{2,1,0:T(8,128)S(1)} %add_select_fusion.1), channel_id=1, source_target_pairs={{0,32},{8,40},{16,48},{24,56},{32,0},{40,8},{48,16},{56,24},{64,96... | collective-permute-start | bytes 786440 | tf_op jit(solution)/shard_map/ppermute | solution.py:264
  52.8 9.7 %collective-permute-start.7 = (f32[4,128,128]{2,1,0:T(8,128)S(1)}, f32[4,128,128]{2,1,0:T(8,128)S(1)}, u32[]{:S(2)}, u32[]{:S(2)}) collective-permute-start(f32[4,128,128]{2,1,0:T(8,128)S(1)} %get-tuple-element.120), channel_id=1, source_target_pairs={{0,16},{8,24},{16,0},{24,8},{32,48},{40,56},{48,32},{56,40},{64,80... | collective-permute-start | bytes 786440 | tf_op jit(solution)/shard_map/ppermute | solution.py:278
  53.4 9.2 %collective-permute-start.6 = (f32[4,128,128]{2,1,0:T(8,128)S(1)}, f32[4,128,128]{2,1,0:T(8,128)S(1)}, u32[]{:S(2)}, u32[]{:S(2)}) collective-permute-start(f32[4,128,128]{2,1,0:T(8,128)S(1)} %add_select_fusion), channel_id=1, source_target_pairs={{0,64},{8,72},{16,80},{24,88},{32,96},{40,104},{48,112},{56,120},{... | collective-permute-start | bytes 786440 | tf_op jit(solution)/shard_map/ppermute | solution.py:264
  62.6 6.6 %collective-permute-start.8 = (bf16[4,128,128]{2,1,0:T(8,128)(2,1)S(1)}, bf16[4,128,128]{2,1,0:T(8,128)(2,1)S(1)}, u32[]{:S(2)}, u32[]{:S(2)}) collective-permute-start(bf16[4,128,128]{2,1,0:T(8,128)(2,1)S(1)} %select_convert_fusion.1), channel_id=1, source_target_pairs={{0,128},{8,136},{16,144},{24,152},{32,160},{40,168},{48,176},{56,1... | collective-permute-start | bytes 393224 | tf_op jit(solution)/shard_map/ppermute | solution.py:259
  64.1 6.3 %collective-permute-start.9 = (f32[4,128,128]{2,1,0:T(8,128)S(1)}, f32[4,128,128]{2,1,0:T(8,128)S(1)}, u32[]{:S(2)}, u32[]{:S(2)}) collective-permute-start(f32[4,128,128]{2,1,0:T(8,128)S(1)} %fusion), channel_id=1, source_target_pairs={{0,8},{8,0},{16,24},{24,16},{32,40},{40,32},{48,56},{56,48},{64,72... | collective-permute-start | bytes 786440 | tf_op jit(solution)/shard_map/ppermute | solution.py:278
  69.2 1.9 %copy-start = (bf16[5,4,128,128]{3,2,1,0:T(8,128)(2,1)}, bf16[5,4,128,128]{3,2,1,0:T(8,128)(2,1)S(1)}, u32[]{:S(2)}) copy-start(bf16[5,4,128,128]{3,2,1,0:T(8,128)(2,1)S(1)} %fusion.26.ls_ref) | copy-start | bytes 1966084

commit v7 on v6

--- a/solution.py
+++ b/solution.py
@@ -248,6 +248,18 @@
     own_state, grad_state = state_part(query_rows, key_rows, value_rows, out_grad, gate_t, nbits)
     grad_wide = grad_state.astype(jnp.float32)
     heads = query_rows.shape[0]
+    steps = jnp.arange(nbits, dtype=jnp.int32)
+    bit = ((me >> steps) & 1) == 1
+    lo = (me >> (steps + 1)) << (steps + 1)
+    end_low = lo + (1 << steps) - 1
+    end_high = lo + (2 << steps) - 1
+    joined = block_levels[end_high, end_low] >= 0
+    mine = block_levels[me, end_low] >= 0
+    one = jnp.float32(1.0)
+    zero = jnp.float32(0.0)
+    take = jnp.where(bit & mine, one, zero)
+    keep_own = jnp.where(bit, one, jnp.where(joined, one, zero))
+    keep_got = jnp.where(bit, jnp.where(joined, one, zero), one)
     fwd_x = own_state.astype(jnp.float32)
     bwd_acc = None
     levels = []
@@ -257,35 +269,25 @@
         kb = nbits - 1 - r
         if kf == 0 or kf == nbits - 1:
             fwd_got = lax.ppermute(
-                fwd_x.astype(jnp.bfloat16), "ctx",
-                pairs_of(kf, ctx_len),
+                fwd_x.astype(jnp.bfloat16), "ctx", pairs_of(kf, ctx_len)
             ).astype(jnp.float32)
         else:
             fwd_got = lax.ppermute(fwd_x, "ctx", pairs_of(kf, ctx_len))
-        bit, joined, mine = step_masks(block_levels, me, kb)
-        term = jnp.where(bit & mine, grad_wide[kb], 0.0)
+        term = take[kb] * grad_wide[kb]
         if bwd_acc is None:
             send, own = term, None
-            bwd_pairs = pairs_of(kb, ctx_len)
+            bwd_got = lax.ppermute(send.astype(jnp.bfloat16), "ctx", pairs_of(kb, ctx_len)).astype(jnp.float32)
         else:
-            kept = jnp.where(joined, bwd_acc, 0.0)
-            send = jnp.where(bit, term + kept, bwd_acc)
-            own = jnp.where(bit, bwd_acc, kept)
-            bwd_pairs = pairs_of(kb, ctx_len)
-        if own is None:
-            bwd_got = lax.ppermute(send.astype(jnp.bfloat16), "ctx", bwd_pairs).astype(jnp.float32)
-        else:
-            bwd_got = lax.ppermute(send, "ctx", bwd_pairs)
+            send = term + keep_got[kb] * bwd_acc
+            own = keep_own[kb] * bwd_acc
+            bwd_got = lax.ppermute(send, "ctx", pairs_of(kb, ctx_len))
         if r < heads:
             partials = local_part(query_rows, key_rows, value_rows, out_grad, gate_t, r, partials)
             fwd_got, bwd_got, partials = lax.optimization_barrier((fwd_got, bwd_got, partials))
         bwd_acc = bwd_got if own is None else own + bwd_got
-        bit, joined, mine = step_masks(block_levels, me, kf)
-        levels.append(jnp.where(bit & mine, fwd_got, 0.0).astype(jnp.bfloat16))
+        levels.append((take[kf] * fwd_got).astype(jnp.bfloat16))
         if kf < nbits - 1:
-            fwd_x = jnp.where(
-                bit, fwd_x + jnp.where(joined, fwd_got, 0.0), fwd_got + jnp.where(joined, fwd_x, 0.0)
-            )
+            fwd_x = keep_own[kf] * fwd_x + keep_got[kf] * fwd_got
     for h in range(nbits, heads):
         partials = local_part(query_rows, key_rows, value_rows, out_grad, gate_t, h, partials)
     level_state = jnp.stack(levels)

time: 83.2 us -> 92 us (1.11)
  other arithmetic: 4.32 us -> 21.3 us
  between operations: 6.45 us -> 0.83 us
  waiting for transfers between devices: 8.89 us -> 4.63 us
  local copies, waits for them, and re-layouts: 6.5 us -> 8.11 us
    add x0 -> x7, other arithmetic: none -> 12.9 us  [the longest x4 9.21 us: per_device(): send = term + keep_got[kb] * bwd_acc]
    unnamed x4, other arithmetic: 0.15 us -> 2.66 us
    ppermute x2, waiting for transfers between devices: 4.97 us -> 2.49 us  [per_device(): lax.ppermute(fwd_x.astype(jnp.bfloat16), 'ctx', pairs_of(kf, ctx_len))]
    select_n x7 -> x1, other arithmetic: 2.08 us -> 0.01 us  [per_device(): keep_own = jnp.where(bit, one, jnp.where(joined, one, zero))]
    slice x0 -> x3, local copies, waits for them, and re-layouts: none -> 2 us  [the longest x2 1.32 us: per_device(): fwd_x = keep_own[kf] * fwd_x + keep_got[kf] * fwd_got]
    ppermute x3, waiting for transfers between devices: 3.91 us -> 2.13 us  [per_device(): fwd_got = lax.ppermute(fwd_x, 'ctx', pairs_of(kf, ctx_len))]
    dynamic_slice x1 -> x0, local copies, waits for them, and re-layouts: 1.7 us -> none  [same_doc(): return block_levels[later, earlier] >= 0]
    gather x0 -> x2, local copies, waits for them, and re-layouts: none -> 1.32 us  [the longest x1 0.66 us: per_device(): joined = block_levels[end_high, end_low] >= 0]
  transfers between devices with their start and end apart: 10 -> 10, of which waited for: 2 -> 2; matrix products, arithmetic and copies ran while one was open for 5% -> 15% of each run, Pallas kernels for 36% -> 33%
where the time goes in v7:
time: 92 us; the launch traced here: 90.6 us
  Pallas kernels  43.8 us (48%)
  other arithmetic  21.3 us (23%)
  starting transfers between devices  11.9 us (13%)
  local copies, waits for them, and re-layouts  8.11 us (9%)
  waiting for transfers between devices  4.63 us (5%)
    pallas_call x4, Pallas kernels, local_part(): pl.pallas_call(local_kernel, grid=(1,), in_specs=in_specs, out_specs=[col...  29.6 us
    add x4, other arithmetic, per_device(): send = term + keep_got[kb] * bwd_acc  9.21 us
    pallas_call x1, Pallas kernels, final_part(): pl.pallas_call(final_kernel, grid=(heads,), in_specs=[row_spec] * 4 + [co...  9.01 us
    pallas_call x1, Pallas kernels, state_part(): pl.pallas_call(state_kernel, grid=(heads,), in_specs=[row_spec] * 4 + [ga...  5.17 us
    ppermute x3, starting transfers between devices, per_device(): fwd_got = lax.ppermute(fwd_x, 'ctx', pairs_of(kf, ctx_len))  4.2 us
    ppermute x4, starting transfers between devices, per_device(): bwd_got = lax.ppermute(send, 'ctx', pairs_of(kb, ctx_len))  3.99 us
    add x3, other arithmetic, per_device(): fwd_x = keep_own[kf] * fwd_x + keep_got[kf] * fwd_got  3.69 us
    unnamed x4, other arithmetic  2.66 us
  transfers between devices with their start and end apart: 10, of which 2 were waited for; matrix products, arithmetic and copies ran while one was open for 15% of the time, Pallas kernels for 33%

profile of v7, /device:TPU:4, one launch (start us, length us, event | category | flops | bytes accessed | tf_op | source)
XLA Modules:
  0.0 90.6 jit_solution(6612520384190406407)
XLA Ops:
  0.6 0.0 copy-start
  0.6 1.8 %fusion.9.g_ref = f32[4,16,1024]{2,1,0:T(8,128)} fusion(f32[16,4,1024]{2,1,0:T(4,128)} %param.10), kind=kLoop, calls=%fused_computation.17 | loop fusion | bytes 524288 | tf_op jit(solution)/shard_map/transpose | solution.py:247
  2.5 5.2 %shard_map.101 = (bf16[4,128,128]{2,1,0:T(8,128)(2,1)}, bf16[5,4,128,128]{3,2,1,0:T(8,128)(2,1)}) custom-call(bf16[4,1024,128]{2,1,0:T(8,128)(2,1)} %q_ref.11, bf16[4,1024,128]{2,1,0:T(8,128)(2,1)} %k_ref.11, bf16[4,1024,128]{2,1,0:T(8,128)(2,1)} %v_ref.11, bf16[4,1024,128]{2,1,0:T(8,128)(2,1)} %do_ref.11, f32[4,16,1024]{2,1,0:T(8,128)} %fusion.9.g_ref), custom_call_target="tpu_custom_call" | custom-call | flops 805306368 | bytes 4456448 | tf_op jit(solution)/shard_map/pallas_call | solution.py:138
  7.7 0.0 collective-permute-start
  7.7 0.7 gather_fusion.1
  8.4 0.7 gather_fusion
  9.0 0.7 fusion.24
  9.7 1.2 %convert_element_type.45 = f32[5,4,128,128]{3,2,1,0:T(8,128)S(1)} convert(bf16[5,4,128,128]{3,2,1,0:T(8,128)(2,1)} %get-tuple-element.61) | non-fusion elementwise | flops 327680 | bytes 1966080 | tf_op jit(solution)/shard_map/convert_element_type | solution.py:249
  10.9 0.6 fusion.20
  11.5 2.3 %collective-permute-start.1 = (bf16[4,128,128]{2,1,0:T(8,128)(2,1)S(1)}, bf16[4,128,128]{2,1,0:T(8,128)(2,1)S(1)}, u32[]{:S(2)}, u32[]{:S(2)}) collective-permute-start(bf16[4,128,128]{2,1,0:T(8,128)(2,1)S(1)} %fusion.20), channel_id=1, source_target_pairs={{0,128},{8,136},{16,144},{24,152},{32,160},{40,168},{48,176},{56,1... | collective-permute-start | bytes 393224 | tf_op jit(solution)/shard_map/ppermute | solution.py:279
  13.9 0.7 fusion.25
  14.5 7.4 %shard_map.102 = (f32[4,128,1024]{2,1,0:T(8,128)}, f32[4,128,1024]{2,1,0:T(8,128)}, f32[4,1024,128]{2,1,0:T(8,128)}, f32[4,1024,128]{2,1,0:T(8,128)}, f32[4,16,1024]{2,1,0:T(8,128)}) custom-call(bf16[4,1024,128]{2,1,0:T(8,128)(2,1)} %q_ref.11, bf16[4,1024,128]{2,1,0:T(8,128)(2,1)} %k_ref.11, bf16[4,1024,128]{2,1,0:T(8,128)(2,1)} %v_ref.11, ...), custom_call_target="tpu_custom_call" | custom-call | flops 1006632960 | bytes 3276800 | tf_op jit(solution)/shard_map/pallas_call | solution.py:104
  21.9 0.6 fusion.26
  22.6 0.0 collective-permute-done
  22.6 0.0 collective-permute-done.1
  22.6 1.4 %fusion.7 = f32[4,128,128]{2,1,0:T(8,128)S(1)} fusion(f32[5,4,128,128]{3,2,1,0:T(8,128)S(1)} %convert_element_type.45, f32[4,128,128]{2,1,0:T(8,128)S(1)} %convert_element_type.48, f32[]{:T(128)} %bitcast.12, f32[]{:T(128)} %bitcast.10), kind=kLoop, calls=%fused_computation.13 | loop fusion | flops 196608 | bytes 786440 | tf_op jit(solution)/shard_map/add | solution.py:281
  24.0 0.4 collective-permute-start.3
  24.5 1.3 %multiply_add_fusion.5 = f32[4,128,128]{2,1,0:T(8,128)S(1)} fusion(f32[4,128,128]{2,1,0:T(8,128)S(1)} %convert_element_type.44, bf16[4,128,128]{2,1,0:T(8,128)(2,1)S(1)} %copy-done.2, f32[]{:T(128)} %bitcast.5, f32[]{:T(128)} %bitcast.3), kind=kLoop, calls=%fused_computation.30 | loop fusion | flops 262144 | bytes 655368 | tf_op jit(solution)/shard_map/add | solution.py:290
  25.8 1.7 %collective-permute-start.2 = (f32[4,128,128]{2,1,0:T(8,128)S(1)}, f32[4,128,128]{2,1,0:T(8,128)S(1)}, u32[]{:S(2)}, u32[]{:S(2)}) collective-permute-start(f32[4,128,128]{2,1,0:T(8,128)S(1)} %multiply_add_fusion.5), channel_id=1, source_target_pairs={{0,16},{8,24},{16,0},{24,8},{32,48},{40,56},{48,32},{56,40},{64,80... | collective-permute-start | bytes 786440 | tf_op jit(solution)/shard_map/ppermute | solution.py:275
  27.5 7.4 %shard_map.103 = (f32[4,128,1024]{2,1,0:T(8,128)}, f32[4,128,1024]{2,1,0:T(8,128)}, f32[4,1024,128]{2,1,0:T(8,128)}, f32[4,1024,128]{2,1,0:T(8,128)}, f32[4,16,1024]{2,1,0:T(8,128)}) custom-call(bf16[4,1024,128]{2,1,0:T(8,128)(2,1)} %q_ref.11, ...), custom_call_target="tpu_custom_call", output_to_operand_aliasing={{0}: (5, {}), {1}: (6, {}), {2}: (7, {}), {3}: (8, {}), {4}... | custom-call | flops 1006632960 | bytes 3276800 | tf_op jit(solution)/shard_map/pallas_call | solution.py:104
  34.9 0.7 fusion.11
  35.6 0.0 collective-permute-done.2
  35.6 2.5 %fusion.5 = f32[4,128,128]{2,1,0:T(8,128)} fusion(f32[5,4,128,128]{3,2,1,0:T(8,128)S(1)} %convert_element_type.45, f32[]{:T(128)} %bitcast.14, f32[]{:T(128)} %bitcast.13, f32[4,128,128]{2,1,0:T(8,128)S(1)} %collective-permute-done.3, f32[4,128,128]{2,1,0:T(8,128)S(1)} %convert_element_type.48, f32[]{:T(128)} %bitcast.16), kind=kLoop, calls=%fused_computation.10 | loop fusion | flops 327680 | bytes 1048588 | tf_op jit(solution)/shard_map/add | solution.py:281
  38.1 2.9 %collective-permute-start.5 = (f32[4,128,128]{2,1,0:T(8,128)}, f32[4,128,128]{2,1,0:T(8,128)}, u32[]{:S(2)}, u32[]{:S(2)}) collective-permute-start(f32[4,128,128]{2,1,0:T(8,128)} %fusion.5), channel_id=1, source_target_pairs={{0,32},{8,40},{16,48},{24,56},{32,0},{40,8},{48,16},{56,24},{64,96... | collective-permute-start | bytes 786440 | tf_op jit(solution)/shard_map/ppermute | solution.py:283
  41.0 1.2 %multiply_add_fusion.4 = f32[4,128,128]{2,1,0:T(8,128)S(1)} fusion(f32[4,128,128]{2,1,0:T(8,128)S(1)} %collective-permute-done.2, f32[4,128,128]{2,1,0:T(8,128)S(1)} %multiply_add_fusion.5, f32[]{:T(128)} %bitcast.9, f32[]{:T(128)} %bitcast.2), kind=kLoop, calls=%fused_computation.29 | loop fusion | flops 196608 | bytes 786440 | tf_op jit(solution)/shard_map/add | solution.py:290
  42.2 0.9 collective-permute-start.4
  43.1 7.4 %shard_map.104 = (f32[4,128,1024]{2,1,0:T(8,128)}, f32[4,128,1024]{2,1,0:T(8,128)}, f32[4,1024,128]{2,1,0:T(8,128)}, f32[4,1024,128]{2,1,0:T(8,128)}, f32[4,16,1024]{2,1,0:T(8,128)}) custom-call(bf16[4,1024,128]{2,1,0:T(8,128)(2,1)} %q_ref.11, ...), custom_call_target="tpu_custom_call", output_to_operand_aliasing={{0}: (5, {}), {1}: (6, {}), {2}: (7, {}), {3}: (8, {}), {4}... | custom-call | flops 1006632960 | bytes 3276800 | tf_op jit(solution)/shard_map/pallas_call | solution.py:104
  50.5 0.7 fusion.13
  51.2 2.1 %collective-permute-done.4 = f32[4,128,128]{2,1,0:T(8,128)S(1)} collective-permute-done((f32[4,128,128]{2,1,0:T(8,128)S(1)}, f32[4,128,128]{2,1,0:T(8,128)S(1)}, u32[]{:S(2)}, u32[]{:S(2)}) %collective-permute-start.4) | collective-permute-done | bytes 262176 | tf_op jit(solution)/shard_map/ppermute | solution.py:275
  53.3 1.1 %multiply_add_fusion.2 = f32[4,128,128]{2,1,0:T(8,128)S(1)} fusion(f32[4,128,128]{2,1,0:T(8,128)S(1)} %collective-permute-done.4, f32[4,128,128]{2,1,0:T(8,128)S(1)} %multiply_add_fusion.4, f32[]{:T(128)} %bitcast.13, f32[]{:T(128)} %bitcast.1), kind=kLoop, calls=%fused_computation.27 | loop fusion | flops 196608 | bytes 786440 | tf_op jit(solution)/shard_map/add | solution.py:290
  54.4 3.5 %fusion.3 = (f32[4,128,128]{2,1,0:T(8,128)S(1)}, f32[4,128,128]{2,1,0:T(8,128)S(1)}) fusion(f32[5,4,128,128]{3,2,1,0:T(8,128)S(1)} %convert_element_type.45, f32[]{:T(128)} %bitcast.17, f32[]{:T(128)} %bitcast.9, f32[4,128,128]{2,1,0:T(8,128)} %collective-permute-done.5, f32[4,128,128]{2,1,0:T(8,128)S(1)} %collective-permute-done.3, ...), kind=kLoop, calls=%fused_computation.7 | loop fusion | flops 458752 | bytes 1572880 | tf_op jit(solution)/shard_map/add | solution.py:281
  57.9 0.5 collective-permute-start.7
  58.4 1.7 %collective-permute-start.6 = (f32[4,128,128]{2,1,0:T(8,128)S(1)}, f32[4,128,128]{2,1,0:T(8,128)S(1)}, u32[]{:S(2)}, u32[]{:S(2)}) collective-permute-start(f32[4,128,128]{2,1,0:T(8,128)S(1)} %multiply_add_fusion.2), channel_id=1, source_target_pairs={{0,64},{8,72},{16,80},{24,88},{32,96},{40,104},{48,112},{56,120},{... | collective-permute-start | bytes 786440 | tf_op jit(solution)/shard_map/ppermute | solution.py:275
  60.1 7.4 %shard_map.105 = (f32[4,128,1024]{2,1,0:T(8,128)}, f32[4,128,1024]{2,1,0:T(8,128)}, f32[4,1024,128]{2,1,0:T(8,128)}, f32[4,1024,128]{2,1,0:T(8,128)}, f32[4,16,1024]{2,1,0:T(8,128)}) custom-call(bf16[4,1024,128]{2,1,0:T(8,128)(2,1)} %q_ref.11, ...), custom_call_target="tpu_custom_call", output_to_operand_aliasing={{0}: (5, {}), {1}: (6, {}), {2}: (7, {}), {3}: (8, {}), {4}... | custom-call | flops 1006632960 | bytes 3276800 | tf_op jit(solution)/shard_map/pallas_call | solution.py:104
  67.5 0.6 fusion.15
  68.1 0.0 collective-permute-done.7
  68.1 0.0 collective-permute-done.6
  68.1 1.3 %add_convert_fusion.1 = bf16[4,128,128]{2,1,0:T(8,128)(2,1)S(1)} fusion(f32[4,128,128]{2,1,0:T(8,128)S(1)} %collective-permute-done.6, f32[4,128,128]{2,1,0:T(8,128)S(1)} %multiply_add_fusion.2, f32[]{:T(128)} %bitcast.16, f32[]{:T(128)} %bitcast.12), kind=kLoop, calls=%fused_computation.21 | loop fusion | flops 262144 | bytes 655368 | tf_op jit(solution)/shard_map/convert_element_type | solution.py:272
  69.5 1.4 %collective-permute-start.8 = (bf16[4,128,128]{2,1,0:T(8,128)(2,1)S(1)}, bf16[4,128,128]{2,1,0:T(8,128)(2,1)S(1)}, u32[]{:S(2)}, u32[]{:S(2)}) collective-permute-start(bf16[4,128,128]{2,1,0:T(8,128)(2,1)S(1)} %add_convert_fusion.1), channel_id=1, source_target_pairs={{0,128},{8,136},{16,144},{24,152},{32,160},{40,168},{48,176},{56,1... | collective-permute-start | bytes 393224 | tf_op jit(solution)/shard_map/ppermute | solution.py:271
  70.9 1.9 %fusion.1 = f32[4,128,128]{2,1,0:T(8,128)S(1)} fusion(f32[5,4,128,128]{3,2,1,0:T(8,128)S(1)} %convert_element_type.45, f32[]{:T(128)} %bitcast.19, f32[]{:T(128)} %bitcast.5, f32[4,128,128]{2,1,0:T(8,128)S(1)} %collective-permute-done.7, f32[4,128,128]{2,1,0:T(8,128)S(1)} %get-tuple-element.126, f32[]{:T(128)} %bitcast.2), kind=kLoop, calls=%fused_computation.4 | loop fusion | flops 327680 | bytes 1048588 | tf_op jit(solution)/shard_map/add | solution.py:281
  72.7 0.1 collective-permute-start.9
  72.8 0.7 fusion.17
  73.6 2.5 %collective-permute-done.8 = bf16[4,128,128]{2,1,0:T(8,128)(2,1)S(1)} collective-permute-done((bf16[4,128,128]{2,1,0:T(8,128)(2,1)S(1)}, bf16[4,128,128]{2,1,0:T(8,128)(2,1)S(1)}, u32[]{:S(2)}, u32[]{:S(2)}) %collective-permute-start.8) | collective-permute-done | bytes 131104 | tf_op jit(solution)/shard_map/ppermute | solution.py:271
  76.0 0.6 fusion.19.ls_ref
  76.7 1.1 %copy.30.lst_ref = bf16[5,4,128,128]{3,2,1,0:T(8,128)(2,1)} copy(bf16[5,4,128,128]{2,3,1,0:T(8,128)(2,1)S(1)} %bitcast.59) | data formatting | bytes 1310720 | tf_op jit(solution)/shard_map/transpose | solution.py:198
  77.8 2.0 %add_convert_fusion.kst_ref = bf16[4,128,128]{2,1,0:T(8,128)(2,1)} fusion(f32[4,128,128]{2,1,0:T(8,128)S(1)} %collective-permute-done.9, f32[]{:T(128)} %bitcast.3, f32[4,128,128]{2,1,0:T(8,128)S(1)} %collective-permute-done.7, f32[4,128,128]{2,1,0:T(8,128)S(1)} %get-tuple-element.126, f32[]{:T(128)} %bitcast.2), kind=kLoop, calls=%fused_computation.18 | loop fusion | flops 327680 | bytes 917512 | tf_op jit(solution)/shard_map/convert_element_type | solution.py:294
  79.7 9.0 %shard_map.106 = (bf16[4,1024,128]{2,1,0:T(8,128)(2,1)}, bf16[4,1024,128]{2,1,0:T(8,128)(2,1)}, bf16[4,1024,128]{2,1,0:T(8,128)(2,1)}, bf16[4,1024,128]{2,1,0:T(8,128)(2,1)}, f32[4,16,1024]{2,1,0:T(8,128)}) custom-call(bf16[4,1024,128]{2,1,0:T(8,128)(2,1)} %q_ref.11, bf16[4,1024,128]{2,1,0:T(8,128)(2,1)} %k_ref.11, bf16[4,1024,128]{2,1,0:T(8,128)(2,1)} %v_ref.11, ...), custom_call_target="tpu_custom_call" | custom-call | flops 1610612736 | bytes 17825792 | tf_op jit(solution)/shard_map/pallas_call | solution.py:199
  88.7 1.8 %copy.31 = f32[16,4,1024]{2,1,0:T(4,128)} copy(f32[16,4,1024]{2,0,1:T(8,128)} %bitcast.60) | data formatting | bytes 524288
  (13 shorter events, 0.1 us)
Async XLA Ops:
  0.6 7.1 %copy-start = (s32[32,32]{1,0:T(8,128)S(1)}, s32[32,32]{1,0:T(8,128)}, u32[]{:S(2)}) copy-start(s32[32,32]{1,0:T(8,128)} %param.11) | copy-start | bytes 12292
  7.7 14.9 %collective-permute-start = (bf16[4,128,128]{2,1,0:T(8,128)(2,1)}, bf16[4,128,128]{2,1,0:T(8,128)(2,1)S(1)}, u32[]{:S(2)}, u32[]{:S(2)}) collective-permute-start(bf16[4,128,128]{2,1,0:T(8,128)(2,1)} %get-tuple-element.60), channel_id=1, source_target_pairs={{0,8},{8,0},{16,24},{24,16},{32,40},{40,32},{48,56},{56,48},{64,72... | collective-permute-start | bytes 393224 | tf_op jit(solution)/shard_map/ppermute | solution.py:271
  11.5 11.1 %collective-permute-start.1 = (bf16[4,128,128]{2,1,0:T(8,128)(2,1)S(1)}, bf16[4,128,128]{2,1,0:T(8,128)(2,1)S(1)}, u32[]{:S(2)}, u32[]{:S(2)}) collective-permute-start(bf16[4,128,128]{2,1,0:T(8,128)(2,1)S(1)} %fusion.20), channel_id=1, source_target_pairs={{0,128},{8,136},{16,144},{24,152},{32,160},{40,168},{48,176},{56,1... | collective-permute-start | bytes 393224 | tf_op jit(solution)/shard_map/ppermute | solution.py:279
  14.5 10.0 %copy-start.2 = (bf16[4,128,128]{2,1,0:T(8,128)(2,1)S(1)}, bf16[4,128,128]{2,1,0:T(8,128)(2,1)}, u32[]{:S(2)}) copy-start(bf16[4,128,128]{2,1,0:T(8,128)(2,1)} %get-tuple-element.60) | copy-start | bytes 393220
  24.0 11.5 %collective-permute-start.3 = (f32[4,128,128]{2,1,0:T(8,128)S(1)}, f32[4,128,128]{2,1,0:T(8,128)S(1)}, u32[]{:S(2)}, u32[]{:S(2)}) collective-permute-start(f32[4,128,128]{2,1,0:T(8,128)S(1)} %fusion.7), channel_id=1, source_target_pairs={{0,64},{8,72},{16,80},{24,88},{32,96},{40,104},{48,112},{56,120},{... | collective-permute-start | bytes 786440 | tf_op jit(solution)/shard_map/ppermute | solution.py:283
  25.8 9.7 %collective-permute-start.2 = (f32[4,128,128]{2,1,0:T(8,128)S(1)}, f32[4,128,128]{2,1,0:T(8,128)S(1)}, u32[]{:S(2)}, u32[]{:S(2)}) collective-permute-start(f32[4,128,128]{2,1,0:T(8,128)S(1)} %multiply_add_fusion.5), channel_id=1, source_target_pairs={{0,16},{8,24},{16,0},{24,8},{32,48},{40,56},{48,32},{56,40},{64,80... | collective-permute-start | bytes 786440 | tf_op jit(solution)/shard_map/ppermute | solution.py:275
  38.1 13.1 %collective-permute-start.5 = (f32[4,128,128]{2,1,0:T(8,128)}, f32[4,128,128]{2,1,0:T(8,128)}, u32[]{:S(2)}, u32[]{:S(2)}) collective-permute-start(f32[4,128,128]{2,1,0:T(8,128)} %fusion.5), channel_id=1, source_target_pairs={{0,32},{8,40},{16,48},{24,56},{32,0},{40,8},{48,16},{56,24},{64,96... | collective-permute-start | bytes 786440 | tf_op jit(solution)/shard_map/ppermute | solution.py:283
  42.2 11.1 %collective-permute-start.4 = (f32[4,128,128]{2,1,0:T(8,128)S(1)}, f32[4,128,128]{2,1,0:T(8,128)S(1)}, u32[]{:S(2)}, u32[]{:S(2)}) collective-permute-start(f32[4,128,128]{2,1,0:T(8,128)S(1)} %multiply_add_fusion.4), channel_id=1, source_target_pairs={{0,32},{8,40},{16,48},{24,56},{32,0},{40,8},{48,16},{56,24},{64,96... | collective-permute-start | bytes 786440 | tf_op jit(solution)/shard_map/ppermute | solution.py:275
  57.9 10.2 %collective-permute-start.7 = (f32[4,128,128]{2,1,0:T(8,128)S(1)}, f32[4,128,128]{2,1,0:T(8,128)S(1)}, u32[]{:S(2)}, u32[]{:S(2)}) collective-permute-start(f32[4,128,128]{2,1,0:T(8,128)S(1)} %get-tuple-element.125), channel_id=1, source_target_pairs={{0,16},{8,24},{16,0},{24,8},{32,48},{40,56},{48,32},{56,40},{64,80... | collective-permute-start | bytes 786440 | tf_op jit(solution)/shard_map/ppermute | solution.py:283
  58.4 9.7 %collective-permute-start.6 = (f32[4,128,128]{2,1,0:T(8,128)S(1)}, f32[4,128,128]{2,1,0:T(8,128)S(1)}, u32[]{:S(2)}, u32[]{:S(2)}) collective-permute-start(f32[4,128,128]{2,1,0:T(8,128)S(1)} %multiply_add_fusion.2), channel_id=1, source_target_pairs={{0,64},{8,72},{16,80},{24,88},{32,96},{40,104},{48,112},{56,120},{... | collective-permute-start | bytes 786440 | tf_op jit(solution)/shard_map/ppermute | solution.py:275
  69.5 6.6 %collective-permute-start.8 = (bf16[4,128,128]{2,1,0:T(8,128)(2,1)S(1)}, bf16[4,128,128]{2,1,0:T(8,128)(2,1)S(1)}, u32[]{:S(2)}, u32[]{:S(2)}) collective-permute-start(bf16[4,128,128]{2,1,0:T(8,128)(2,1)S(1)} %add_convert_fusion.1), channel_id=1, source_target_pairs={{0,128},{8,136},{16,144},{24,152},{32,160},{40,168},{48,176},{56,1... | collective-permute-start | bytes 393224 | tf_op jit(solution)/shard_map/ppermute | solution.py:271
  72.7 5.1 %collective-permute-start.9 = (f32[4,128,128]{2,1,0:T(8,128)S(1)}, f32[4,128,128]{2,1,0:T(8,128)S(1)}, u32[]{:S(2)}, u32[]{:S(2)}) collective-permute-start(f32[4,128,128]{2,1,0:T(8,128)S(1)} %fusion.1), channel_id=1, source_target_pairs={{0,8},{8,0},{16,24},{24,16},{32,40},{40,32},{48,56},{56,48},{64,72... | collective-permute-start | bytes 786440 | tf_op jit(solution)/shard_map/ppermute | solution.py:283
  76.6 3.1 %copy-start.1 = (bf16[5,4,128,128]{3,2,1,0:T(8,128)(2,1)}, bf16[5,4,128,128]{3,2,1,0:T(8,128)(2,1)S(1)}, u32[]{:S(2)}) copy-start(bf16[5,4,128,128]{3,2,1,0:T(8,128)(2,1)S(1)} %fusion.19.ls_ref) | copy-start | bytes 1966084

commit v8 on v7

--- a/solution.py
+++ b/solution.py
@@ -260,6 +260,7 @@
     take = jnp.where(bit & mine, one, zero)
     keep_own = jnp.where(bit, one, jnp.where(joined, one, zero))
     keep_got = jnp.where(bit, jnp.where(joined, one, zero), one)
+    take, keep_own, keep_got = lax.optimization_barrier((take, keep_own, keep_got))
     fwd_x = own_state.astype(jnp.float32)
     bwd_acc = None
     levels = []

time: 92 us -> 92 us (level)
  no operation moved by 1% of the time
where the time goes in v8:
time: 92 us; the launch traced here: 90.6 us
  Pallas kernels  43.8 us (48%)
  other arithmetic  21.3 us (23%)
  starting transfers between devices  11.9 us (13%)
  local copies, waits for them, and re-layouts  8.11 us (9%)
  waiting for transfers between devices  4.63 us (5%)
    pallas_call x4, Pallas kernels, local_part(): pl.pallas_call(local_kernel, grid=(1,), in_specs=in_specs, out_specs=[col...  29.6 us
    add x4, other arithmetic, per_device(): send = term + keep_got[kb] * bwd_acc  9.21 us
    pallas_call x1, Pallas kernels, final_part(): pl.pallas_call(final_kernel, grid=(heads,), in_specs=[row_spec] * 4 + [co...  9.01 us
    pallas_call x1, Pallas kernels, state_part(): pl.pallas_call(state_kernel, grid=(heads,), in_specs=[row_spec] * 4 + [ga...  5.17 us
    ppermute x3, starting transfers between devices, per_device(): fwd_got = lax.ppermute(fwd_x, 'ctx', pairs_of(kf, ctx_len))  4.2 us
    ppermute x4, starting transfers between devices, per_device(): bwd_got = lax.ppermute(send, 'ctx', pairs_of(kb, ctx_len))  3.99 us
    add x3, other arithmetic, per_device(): fwd_x = keep_own[kf] * fwd_x + keep_got[kf] * fwd_got  3.69 us
    unnamed x4, other arithmetic  2.66 us
  transfers between devices with their start and end apart: 10, of which 2 were waited for; matrix products, arithmetic and copies ran while one was open for 15% of the time, Pallas kernels for 33%

profile of v8, /device:TPU:4, one launch (start us, length us, event | category | flops | bytes accessed | tf_op | source)
XLA Modules:
  0.0 90.6 jit_solution(16027021670464704317)
XLA Ops:
  0.6 0.0 copy-start
  0.6 1.8 %fusion.9.g_ref = f32[4,16,1024]{2,1,0:T(8,128)} fusion(f32[16,4,1024]{2,1,0:T(4,128)} %param.10), kind=kLoop, calls=%fused_computation.17 | loop fusion | bytes 524288 | tf_op jit(solution)/shard_map/transpose | solution.py:247
  2.5 5.2 %shard_map.101 = (bf16[4,128,128]{2,1,0:T(8,128)(2,1)}, bf16[5,4,128,128]{3,2,1,0:T(8,128)(2,1)}) custom-call(bf16[4,1024,128]{2,1,0:T(8,128)(2,1)} %q_ref.11, bf16[4,1024,128]{2,1,0:T(8,128)(2,1)} %k_ref.11, bf16[4,1024,128]{2,1,0:T(8,128)(2,1)} %v_ref.11, bf16[4,1024,128]{2,1,0:T(8,128)(2,1)} %do_ref.11, f32[4,16,1024]{2,1,0:T(8,128)} %fusion.9.g_ref), custom_call_target="tpu_custom_call" | custom-call | flops 805306368 | bytes 4456448 | tf_op jit(solution)/shard_map/pallas_call | solution.py:138
  7.7 0.0 collective-permute-start
  7.7 0.7 gather_fusion
  8.4 0.7 gather_fusion.1
  9.0 0.7 fusion.24
  9.7 1.2 %convert_element_type.45 = f32[5,4,128,128]{3,2,1,0:T(8,128)S(1)} convert(bf16[5,4,128,128]{3,2,1,0:T(8,128)(2,1)} %get-tuple-element.67) | non-fusion elementwise | flops 327680 | bytes 1966080 | tf_op jit(solution)/shard_map/convert_element_type | solution.py:249
  10.9 0.6 fusion.20
  11.5 2.3 %collective-permute-start.1 = (bf16[4,128,128]{2,1,0:T(8,128)(2,1)S(1)}, bf16[4,128,128]{2,1,0:T(8,128)(2,1)S(1)}, u32[]{:S(2)}, u32[]{:S(2)}) collective-permute-start(bf16[4,128,128]{2,1,0:T(8,128)(2,1)S(1)} %fusion.20), channel_id=1, source_target_pairs={{0,128},{8,136},{16,144},{24,152},{32,160},{40,168},{48,176},{56,1... | collective-permute-start | bytes 393224 | tf_op jit(solution)/shard_map/ppermute | solution.py:280
  13.9 0.7 fusion.25
  14.5 7.4 %shard_map.102 = (f32[4,128,1024]{2,1,0:T(8,128)}, f32[4,128,1024]{2,1,0:T(8,128)}, f32[4,1024,128]{2,1,0:T(8,128)}, f32[4,1024,128]{2,1,0:T(8,128)}, f32[4,16,1024]{2,1,0:T(8,128)}) custom-call(bf16[4,1024,128]{2,1,0:T(8,128)(2,1)} %q_ref.11, bf16[4,1024,128]{2,1,0:T(8,128)(2,1)} %k_ref.11, bf16[4,1024,128]{2,1,0:T(8,128)(2,1)} %v_ref.11, ...), custom_call_target="tpu_custom_call" | custom-call | flops 1006632960 | bytes 3276800 | tf_op jit(solution)/shard_map/pallas_call | solution.py:104
  21.9 0.6 fusion.26
  22.6 0.0 collective-permute-done
  22.6 0.0 collective-permute-done.1
  22.6 1.4 %fusion.7 = f32[4,128,128]{2,1,0:T(8,128)S(1)} fusion(f32[5,4,128,128]{3,2,1,0:T(8,128)S(1)} %convert_element_type.45, f32[4,128,128]{2,1,0:T(8,128)S(1)} %convert_element_type.48, f32[]{:T(128)} %bitcast.12, f32[]{:T(128)} %bitcast.10), kind=kLoop, calls=%fused_computation.13 | loop fusion | flops 196608 | bytes 786440 | tf_op jit(solution)/shard_map/add | solution.py:282
  24.0 0.4 collective-permute-start.3
  24.5 1.3 %multiply_add_fusion.5 = f32[4,128,128]{2,1,0:T(8,128)S(1)} fusion(f32[4,128,128]{2,1,0:T(8,128)S(1)} %convert_element_type.44, bf16[4,128,128]{2,1,0:T(8,128)(2,1)S(1)} %copy-done.2, f32[]{:T(128)} %bitcast.6, f32[]{:T(128)} %bitcast.4), kind=kLoop, calls=%fused_computation.30 | loop fusion | flops 262144 | bytes 655368 | tf_op jit(solution)/shard_map/add | solution.py:291
  25.8 1.7 %collective-permute-start.2 = (f32[4,128,128]{2,1,0:T(8,128)S(1)}, f32[4,128,128]{2,1,0:T(8,128)S(1)}, u32[]{:S(2)}, u32[]{:S(2)}) collective-permute-start(f32[4,128,128]{2,1,0:T(8,128)S(1)} %multiply_add_fusion.5), channel_id=1, source_target_pairs={{0,16},{8,24},{16,0},{24,8},{32,48},{40,56},{48,32},{56,40},{64,80... | collective-permute-start | bytes 786440 | tf_op jit(solution)/shard_map/ppermute | solution.py:276
  27.5 7.4 %shard_map.103 = (f32[4,128,1024]{2,1,0:T(8,128)}, f32[4,128,1024]{2,1,0:T(8,128)}, f32[4,1024,128]{2,1,0:T(8,128)}, f32[4,1024,128]{2,1,0:T(8,128)}, f32[4,16,1024]{2,1,0:T(8,128)}) custom-call(bf16[4,1024,128]{2,1,0:T(8,128)(2,1)} %q_ref.11, ...), custom_call_target="tpu_custom_call", output_to_operand_aliasing={{0}: (5, {}), {1}: (6, {}), {2}: (7, {}), {3}: (8, {}), {4}... | custom-call | flops 1006632960 | bytes 3276800 | tf_op jit(solution)/shard_map/pallas_call | solution.py:104
  34.9 0.7 fusion.11
  35.6 0.0 collective-permute-done.2
  35.6 2.5 %fusion.5 = f32[4,128,128]{2,1,0:T(8,128)} fusion(f32[5,4,128,128]{3,2,1,0:T(8,128)S(1)} %convert_element_type.45, f32[]{:T(128)} %bitcast.14, f32[]{:T(128)} %bitcast.13, f32[4,128,128]{2,1,0:T(8,128)S(1)} %collective-permute-done.3, f32[4,128,128]{2,1,0:T(8,128)S(1)} %convert_element_type.48, f32[]{:T(128)} %bitcast.16), kind=kLoop, calls=%fused_computation.10 | loop fusion | flops 327680 | bytes 1048588 | tf_op jit(solution)/shard_map/add | solution.py:282
  38.1 2.9 %collective-permute-start.5 = (f32[4,128,128]{2,1,0:T(8,128)}, f32[4,128,128]{2,1,0:T(8,128)}, u32[]{:S(2)}, u32[]{:S(2)}) collective-permute-start(f32[4,128,128]{2,1,0:T(8,128)} %fusion.5), channel_id=1, source_target_pairs={{0,32},{8,40},{16,48},{24,56},{32,0},{40,8},{48,16},{56,24},{64,96... | collective-permute-start | bytes 786440 | tf_op jit(solution)/shard_map/ppermute | solution.py:284
  41.0 1.2 %multiply_add_fusion.4 = f32[4,128,128]{2,1,0:T(8,128)S(1)} fusion(f32[4,128,128]{2,1,0:T(8,128)S(1)} %collective-permute-done.2, f32[4,128,128]{2,1,0:T(8,128)S(1)} %multiply_add_fusion.5, f32[]{:T(128)} %bitcast.9, f32[]{:T(128)} %bitcast.3), kind=kLoop, calls=%fused_computation.29 | loop fusion | flops 196608 | bytes 786440 | tf_op jit(solution)/shard_map/add | solution.py:291
  42.2 0.9 collective-permute-start.4
  43.1 7.4 %shard_map.104 = (f32[4,128,1024]{2,1,0:T(8,128)}, f32[4,128,1024]{2,1,0:T(8,128)}, f32[4,1024,128]{2,1,0:T(8,128)}, f32[4,1024,128]{2,1,0:T(8,128)}, f32[4,16,1024]{2,1,0:T(8,128)}) custom-call(bf16[4,1024,128]{2,1,0:T(8,128)(2,1)} %q_ref.11, ...), custom_call_target="tpu_custom_call", output_to_operand_aliasing={{0}: (5, {}), {1}: (6, {}), {2}: (7, {}), {3}: (8, {}), {4}... | custom-call | flops 1006632960 | bytes 3276800 | tf_op jit(solution)/shard_map/pallas_call | solution.py:104
  50.5 0.7 fusion.13
  51.2 2.1 %collective-permute-done.4 = f32[4,128,128]{2,1,0:T(8,128)S(1)} collective-permute-done((f32[4,128,128]{2,1,0:T(8,128)S(1)}, f32[4,128,128]{2,1,0:T(8,128)S(1)}, u32[]{:S(2)}, u32[]{:S(2)}) %collective-permute-start.4) | collective-permute-done | bytes 262176 | tf_op jit(solution)/shard_map/ppermute | solution.py:276
  53.3 1.1 %multiply_add_fusion.2 = f32[4,128,128]{2,1,0:T(8,128)S(1)} fusion(f32[4,128,128]{2,1,0:T(8,128)S(1)} %collective-permute-done.4, f32[4,128,128]{2,1,0:T(8,128)S(1)} %multiply_add_fusion.4, f32[]{:T(128)} %bitcast.13, f32[]{:T(128)} %bitcast.2), kind=kLoop, calls=%fused_computation.27 | loop fusion | flops 196608 | bytes 786440 | tf_op jit(solution)/shard_map/add | solution.py:291
  54.4 3.5 %fusion.3 = (f32[4,128,128]{2,1,0:T(8,128)S(1)}, f32[4,128,128]{2,1,0:T(8,128)S(1)}) fusion(f32[5,4,128,128]{3,2,1,0:T(8,128)S(1)} %convert_element_type.45, f32[]{:T(128)} %bitcast.17, f32[]{:T(128)} %bitcast.9, f32[4,128,128]{2,1,0:T(8,128)} %collective-permute-done.5, f32[4,128,128]{2,1,0:T(8,128)S(1)} %collective-permute-done.3, ...), kind=kLoop, calls=%fused_computation.7 | loop fusion | flops 458752 | bytes 1572880 | tf_op jit(solution)/shard_map/add | solution.py:282
  57.9 0.5 collective-permute-start.7
  58.4 1.7 %collective-permute-start.6 = (f32[4,128,128]{2,1,0:T(8,128)S(1)}, f32[4,128,128]{2,1,0:T(8,128)S(1)}, u32[]{:S(2)}, u32[]{:S(2)}) collective-permute-start(f32[4,128,128]{2,1,0:T(8,128)S(1)} %multiply_add_fusion.2), channel_id=1, source_target_pairs={{0,64},{8,72},{16,80},{24,88},{32,96},{40,104},{48,112},{56,120},{... | collective-permute-start | bytes 786440 | tf_op jit(solution)/shard_map/ppermute | solution.py:276
  60.1 7.4 %shard_map.105 = (f32[4,128,1024]{2,1,0:T(8,128)}, f32[4,128,1024]{2,1,0:T(8,128)}, f32[4,1024,128]{2,1,0:T(8,128)}, f32[4,1024,128]{2,1,0:T(8,128)}, f32[4,16,1024]{2,1,0:T(8,128)}) custom-call(bf16[4,1024,128]{2,1,0:T(8,128)(2,1)} %q_ref.11, ...), custom_call_target="tpu_custom_call", output_to_operand_aliasing={{0}: (5, {}), {1}: (6, {}), {2}: (7, {}), {3}: (8, {}), {4}... | custom-call | flops 1006632960 | bytes 3276800 | tf_op jit(solution)/shard_map/pallas_call | solution.py:104
  67.5 0.6 fusion.15
  68.1 0.0 collective-permute-done.7
  68.1 0.0 collective-permute-done.6
  68.1 1.3 %add_convert_fusion.1 = bf16[4,128,128]{2,1,0:T(8,128)(2,1)S(1)} fusion(f32[4,128,128]{2,1,0:T(8,128)S(1)} %collective-permute-done.6, f32[4,128,128]{2,1,0:T(8,128)S(1)} %multiply_add_fusion.2, f32[]{:T(128)} %bitcast.16, f32[]{:T(128)} %bitcast.12), kind=kLoop, calls=%fused_computation.21 | loop fusion | flops 262144 | bytes 655368 | tf_op jit(solution)/shard_map/convert_element_type | solution.py:273
  69.5 1.4 %collective-permute-start.8 = (bf16[4,128,128]{2,1,0:T(8,128)(2,1)S(1)}, bf16[4,128,128]{2,1,0:T(8,128)(2,1)S(1)}, u32[]{:S(2)}, u32[]{:S(2)}) collective-permute-start(bf16[4,128,128]{2,1,0:T(8,128)(2,1)S(1)} %add_convert_fusion.1), channel_id=1, source_target_pairs={{0,128},{8,136},{16,144},{24,152},{32,160},{40,168},{48,176},{56,1... | collective-permute-start | bytes 393224 | tf_op jit(solution)/shard_map/ppermute | solution.py:272
  70.9 1.9 %fusion.1 = f32[4,128,128]{2,1,0:T(8,128)S(1)} fusion(f32[5,4,128,128]{3,2,1,0:T(8,128)S(1)} %convert_element_type.45, f32[]{:T(128)} %bitcast.19, f32[]{:T(128)} %bitcast.6, f32[4,128,128]{2,1,0:T(8,128)S(1)} %collective-permute-done.7, f32[4,128,128]{2,1,0:T(8,128)S(1)} %get-tuple-element.132, f32[]{:T(128)} %bitcast.3), kind=kLoop, calls=%fused_computation.4 | loop fusion | flops 327680 | bytes 1048588 | tf_op jit(solution)/shard_map/add | solution.py:282
  72.7 0.1 collective-permute-start.9
  72.8 0.7 fusion.17
  73.6 2.5 %collective-permute-done.8 = bf16[4,128,128]{2,1,0:T(8,128)(2,1)S(1)} collective-permute-done((bf16[4,128,128]{2,1,0:T(8,128)(2,1)S(1)}, bf16[4,128,128]{2,1,0:T(8,128)(2,1)S(1)}, u32[]{:S(2)}, u32[]{:S(2)}) %collective-permute-start.8) | collective-permute-done | bytes 131104 | tf_op jit(solution)/shard_map/ppermute | solution.py:272
  76.0 0.6 fusion.19.ls_ref
  76.7 1.1 %copy.30.lst_ref = bf16[5,4,128,128]{3,2,1,0:T(8,128)(2,1)} copy(bf16[5,4,128,128]{2,3,1,0:T(8,128)(2,1)S(1)} %bitcast.59) | data formatting | bytes 1310720 | tf_op jit(solution)/shard_map/transpose | solution.py:198
  77.8 2.0 %add_convert_fusion.kst_ref = bf16[4,128,128]{2,1,0:T(8,128)(2,1)} fusion(f32[4,128,128]{2,1,0:T(8,128)S(1)} %collective-permute-done.9, f32[]{:T(128)} %bitcast.4, f32[4,128,128]{2,1,0:T(8,128)S(1)} %collective-permute-done.7, f32[4,128,128]{2,1,0:T(8,128)S(1)} %get-tuple-element.132, f32[]{:T(128)} %bitcast.3), kind=kLoop, calls=%fused_computation.18 | loop fusion | flops 327680 | bytes 917512 | tf_op jit(solution)/shard_map/convert_element_type | solution.py:295
  79.7 9.0 %shard_map.106 = (bf16[4,1024,128]{2,1,0:T(8,128)(2,1)}, bf16[4,1024,128]{2,1,0:T(8,128)(2,1)}, bf16[4,1024,128]{2,1,0:T(8,128)(2,1)}, bf16[4,1024,128]{2,1,0:T(8,128)(2,1)}, f32[4,16,1024]{2,1,0:T(8,128)}) custom-call(bf16[4,1024,128]{2,1,0:T(8,128)(2,1)} %q_ref.11, bf16[4,1024,128]{2,1,0:T(8,128)(2,1)} %k_ref.11, bf16[4,1024,128]{2,1,0:T(8,128)(2,1)} %v_ref.11, ...), custom_call_target="tpu_custom_call" | custom-call | flops 1610612736 | bytes 17825792 | tf_op jit(solution)/shard_map/pallas_call | solution.py:199
  88.7 1.8 %copy.31 = f32[16,4,1024]{2,1,0:T(4,128)} copy(f32[16,4,1024]{2,0,1:T(8,128)} %bitcast.60) | data formatting | bytes 524288
  (13 shorter events, 0.1 us)
Async XLA Ops:
  0.6 7.1 %copy-start = (s32[32,32]{1,0:T(8,128)S(1)}, s32[32,32]{1,0:T(8,128)}, u32[]{:S(2)}) copy-start(s32[32,32]{1,0:T(8,128)} %param.11) | copy-start | bytes 12292
  7.7 14.9 %collective-permute-start = (bf16[4,128,128]{2,1,0:T(8,128)(2,1)}, bf16[4,128,128]{2,1,0:T(8,128)(2,1)S(1)}, u32[]{:S(2)}, u32[]{:S(2)}) collective-permute-start(bf16[4,128,128]{2,1,0:T(8,128)(2,1)} %get-tuple-element.64), channel_id=1, source_target_pairs={{0,8},{8,0},{16,24},{24,16},{32,40},{40,32},{48,56},{56,48},{64,72... | collective-permute-start | bytes 393224 | tf_op jit(solution)/shard_map/ppermute | solution.py:272
  11.5 11.1 %collective-permute-start.1 = (bf16[4,128,128]{2,1,0:T(8,128)(2,1)S(1)}, bf16[4,128,128]{2,1,0:T(8,128)(2,1)S(1)}, u32[]{:S(2)}, u32[]{:S(2)}) collective-permute-start(bf16[4,128,128]{2,1,0:T(8,128)(2,1)S(1)} %fusion.20), channel_id=1, source_target_pairs={{0,128},{8,136},{16,144},{24,152},{32,160},{40,168},{48,176},{56,1... | collective-permute-start | bytes 393224 | tf_op jit(solution)/shard_map/ppermute | solution.py:280
  14.5 10.0 %copy-start.2 = (bf16[4,128,128]{2,1,0:T(8,128)(2,1)S(1)}, bf16[4,128,128]{2,1,0:T(8,128)(2,1)}, u32[]{:S(2)}) copy-start(bf16[4,128,128]{2,1,0:T(8,128)(2,1)} %get-tuple-element.64) | copy-start | bytes 393220
  24.0 11.5 %collective-permute-start.3 = (f32[4,128,128]{2,1,0:T(8,128)S(1)}, f32[4,128,128]{2,1,0:T(8,128)S(1)}, u32[]{:S(2)}, u32[]{:S(2)}) collective-permute-start(f32[4,128,128]{2,1,0:T(8,128)S(1)} %fusion.7), channel_id=1, source_target_pairs={{0,64},{8,72},{16,80},{24,88},{32,96},{40,104},{48,112},{56,120},{... | collective-permute-start | bytes 786440 | tf_op jit(solution)/shard_map/ppermute | solution.py:284
  25.8 9.7 %collective-permute-start.2 = (f32[4,128,128]{2,1,0:T(8,128)S(1)}, f32[4,128,128]{2,1,0:T(8,128)S(1)}, u32[]{:S(2)}, u32[]{:S(2)}) collective-permute-start(f32[4,128,128]{2,1,0:T(8,128)S(1)} %multiply_add_fusion.5), channel_id=1, source_target_pairs={{0,16},{8,24},{16,0},{24,8},{32,48},{40,56},{48,32},{56,40},{64,80... | collective-permute-start | bytes 786440 | tf_op jit(solution)/shard_map/ppermute | solution.py:276
  38.1 13.1 %collective-permute-start.5 = (f32[4,128,128]{2,1,0:T(8,128)}, f32[4,128,128]{2,1,0:T(8,128)}, u32[]{:S(2)}, u32[]{:S(2)}) collective-permute-start(f32[4,128,128]{2,1,0:T(8,128)} %fusion.5), channel_id=1, source_target_pairs={{0,32},{8,40},{16,48},{24,56},{32,0},{40,8},{48,16},{56,24},{64,96... | collective-permute-start | bytes 786440 | tf_op jit(solution)/shard_map/ppermute | solution.py:284
  42.2 11.1 %collective-permute-start.4 = (f32[4,128,128]{2,1,0:T(8,128)S(1)}, f32[4,128,128]{2,1,0:T(8,128)S(1)}, u32[]{:S(2)}, u32[]{:S(2)}) collective-permute-start(f32[4,128,128]{2,1,0:T(8,128)S(1)} %multiply_add_fusion.4), channel_id=1, source_target_pairs={{0,32},{8,40},{16,48},{24,56},{32,0},{40,8},{48,16},{56,24},{64,96... | collective-permute-start | bytes 786440 | tf_op jit(solution)/shard_map/ppermute | solution.py:276
  57.9 10.2 %collective-permute-start.7 = (f32[4,128,128]{2,1,0:T(8,128)S(1)}, f32[4,128,128]{2,1,0:T(8,128)S(1)}, u32[]{:S(2)}, u32[]{:S(2)}) collective-permute-start(f32[4,128,128]{2,1,0:T(8,128)S(1)} %get-tuple-element.131), channel_id=1, source_target_pairs={{0,16},{8,24},{16,0},{24,8},{32,48},{40,56},{48,32},{56,40},{64,80... | collective-permute-start | bytes 786440 | tf_op jit(solution)/shard_map/ppermute | solution.py:284
  58.4 9.7 %collective-permute-start.6 = (f32[4,128,128]{2,1,0:T(8,128)S(1)}, f32[4,128,128]{2,1,0:T(8,128)S(1)}, u32[]{:S(2)}, u32[]{:S(2)}) collective-permute-start(f32[4,128,128]{2,1,0:T(8,128)S(1)} %multiply_add_fusion.2), channel_id=1, source_target_pairs={{0,64},{8,72},{16,80},{24,88},{32,96},{40,104},{48,112},{56,120},{... | collective-permute-start | bytes 786440 | tf_op jit(solution)/shard_map/ppermute | solution.py:276
  69.5 6.6 %collective-permute-start.8 = (bf16[4,128,128]{2,1,0:T(8,128)(2,1)S(1)}, bf16[4,128,128]{2,1,0:T(8,128)(2,1)S(1)}, u32[]{:S(2)}, u32[]{:S(2)}) collective-permute-start(bf16[4,128,128]{2,1,0:T(8,128)(2,1)S(1)} %add_convert_fusion.1), channel_id=1, source_target_pairs={{0,128},{8,136},{16,144},{24,152},{32,160},{40,168},{48,176},{56,1... | collective-permute-start | bytes 393224 | tf_op jit(solution)/shard_map/ppermute | solution.py:272
  72.7 5.1 %collective-permute-start.9 = (f32[4,128,128]{2,1,0:T(8,128)S(1)}, f32[4,128,128]{2,1,0:T(8,128)S(1)}, u32[]{:S(2)}, u32[]{:S(2)}) collective-permute-start(f32[4,128,128]{2,1,0:T(8,128)S(1)} %fusion.1), channel_id=1, source_target_pairs={{0,8},{8,0},{16,24},{24,16},{32,40},{40,32},{48,56},{56,48},{64,72... | collective-permute-start | bytes 786440 | tf_op jit(solution)/shard_map/ppermute | solution.py:284
  76.6 3.1 %copy-start.1 = (bf16[5,4,128,128]{3,2,1,0:T(8,128)(2,1)}, bf16[5,4,128,128]{3,2,1,0:T(8,128)(2,1)S(1)}, u32[]{:S(2)}) copy-start(bf16[5,4,128,128]{3,2,1,0:T(8,128)(2,1)S(1)} %fusion.19.ls_ref) | copy-start | bytes 1966084

commit v9 on v6

--- a/solution.py
+++ b/solution.py
@@ -121,12 +121,12 @@
     nlev = g_ref.shape[0]
     nbits = gs_ref.shape[0]
     first = nlev - nbits
-    st_ref[...] = dot_tn(k_ref[...], v_ref[...]).astype(st_ref.dtype)
+    st_ref[...] = dot_tn(k_ref[...], v_ref[...]).astype(jnp.bfloat16).astype(st_ref.dtype)
     do_t = jnp.transpose(do_ref[...].astype(jnp.float32))
     q = q_ref[...]
     for b in range(nbits):
         scaled_t = (g_ref[first + b : first + b + 1, :] * do_t).astype(jnp.bfloat16)
-        gs_ref[b] = dot_nn(scaled_t, q).astype(gs_ref.dtype)
+        gs_ref[b] = dot_nn(scaled_t, q).astype(jnp.bfloat16).astype(gs_ref.dtype)
 
 
 def state_part(query_rows, key_rows, value_rows, out_grad, gate_t, nbits):
@@ -144,8 +144,8 @@
             pl.BlockSpec((nbits, None, width, width), lambda h: (0, h, 0, 0)),
         ],
         out_shape=[
-            jax.ShapeDtypeStruct((heads, width, width), bf),
-            jax.ShapeDtypeStruct((nbits, heads, width, width), bf),
+            jax.ShapeDtypeStruct((heads, width, width), jnp.float32),
+            jax.ShapeDtypeStruct((nbits, heads, width, width), jnp.float32),
         ],
         compiler_params=pltpu.CompilerParams(dimension_semantics=("arbitrary",)),
         cost_estimate=pl.CostEstimate(
@@ -157,13 +157,16 @@
 
 
 def final_kernel(q_ref, k_ref, v_ref, do_ref, o_ref, dq_ref, dk_ref, dv_ref, ggl_ref, g_ref,
-                 ls_ref, lst_ref, kst_ref, attn_ref, gq_ref, gk_ref, gv_ref, gg_ref):
+                 ls_ref, kst_ref, attn_ref, gq_ref, gk_ref, gv_ref, gg_ref):
     block_len = q_ref.shape[0]
     nlev = g_ref.shape[0]
     nbits = ls_ref.shape[0]
     first = nlev - nbits
     key_state_t = kst_ref[...]
-    gg_ref[...] = ggl_ref[...]
+    h = pl.program_id(0)
+    state_t = [jnp.transpose(ls_ref[b].astype(jnp.float32)).astype(jnp.bfloat16) for b in range(nbits)]
+    gg = [ggl_ref[lev : lev + 1, :] for lev in range(nlev)]
+    cross_rows = [[] for _ in range(nbits)]
     for i in range(block_len // TILE):
         ts = pl.ds(i * TILE, TILE)
         qi = q_ref[ts, :]
@@ -173,16 +176,20 @@
         grad_q_t = dq_ref[:, ts]
         for b in range(nbits):
             weight = g_ref[first + b : first + b + 1, ts]
-            level_out_t = dot_nt(lst_ref[b], qi)
+            level_out_t = dot_nt(state_t[b], qi)
             level_back_t = dot_nt(ls_ref[b], doi)
             attn_t = attn_t + weight * level_out_t
             grad_q_t = grad_q_t + weight * level_back_t
             dotted = jnp.sum(level_out_t * do_t, axis=0, keepdims=True)
-            gg_ref[first + b : first + b + 1, ts] = weight * dotted
+            cross_rows[b].append(weight * dotted)
         attn_ref[ts, :] = jnp.transpose(attn_t).astype(attn_ref.dtype)
         gq_ref[ts, :] = jnp.transpose(grad_q_t).astype(gq_ref.dtype)
         gk_ref[ts, :] = (dk_ref[ts, :] + dot_nn(v_ref[ts, :], key_state_t)).astype(gk_ref.dtype)
         gv_ref[ts, :] = (dv_ref[ts, :] + dot_nt(k_ref[ts, :], key_state_t)).astype(gv_ref.dtype)
+    for b in range(nbits):
+        gg[first + b] = jnp.concatenate(cross_rows[b], axis=1)
+    for lev in range(nlev):
+        gg_ref[lev, pl.ds(h, 1), :] = gg[lev]
 
 
 def final_part(query_rows, key_rows, value_rows, out_grad, partials, gate_t, level_state, key_state_t):
@@ -195,15 +202,14 @@
     ls_spec = pl.BlockSpec((nbits, None, width, width), lambda h: (0, h, 0, 0))
     ks_spec = pl.BlockSpec((None, width, width), lambda h: (h, 0, 0))
     bf = jnp.bfloat16
-    level_state_t = jnp.swapaxes(level_state, 2, 3)
     return pl.pallas_call(
         final_kernel,
         grid=(heads,),
         in_specs=[row_spec] * 4 + [col_spec] * 2 + [row_spec] * 2
-        + [gate_spec, gate_spec, ls_spec, ls_spec, ks_spec],
-        out_specs=[row_spec] * 4 + [gate_spec],
+        + [gate_spec, gate_spec, ls_spec, ks_spec],
+        out_specs=[row_spec] * 4 + [pl.BlockSpec((nlev, heads, block_len), lambda h: (0, 0, 0))],
         out_shape=[jax.ShapeDtypeStruct((heads, block_len, width), bf)] * 4
-        + [jax.ShapeDtypeStruct((heads, nlev, block_len), jnp.float32)],
+        + [jax.ShapeDtypeStruct((nlev, heads, block_len), jnp.float32)],
         compiler_params=pltpu.CompilerParams(dimension_semantics=("arbitrary",)),
         cost_estimate=pl.CostEstimate(
             flops=heads * block_len * width * width * 2 * (2 * nbits + 2),
@@ -211,7 +217,7 @@
             bytes_accessed=heads * block_len * (8 * width * 2 + 4 * width * 4 + 4 * nlev * 4),
         ),
     )(query_rows, key_rows, value_rows, out_grad, *partials[:4], partials[4], gate_t,
-      level_state, level_state_t, key_state_t)
+      level_state, key_state_t)
 
 
 def same_doc(block_levels, earlier, later):
@@ -246,9 +252,9 @@
 
     gate_t = weights.transpose(1, 0, 2)
     own_state, grad_state = state_part(query_rows, key_rows, value_rows, out_grad, gate_t, nbits)
-    grad_wide = grad_state.astype(jnp.float32)
+    grad_wide = grad_state
     heads = query_rows.shape[0]
-    fwd_x = own_state.astype(jnp.float32)
+    fwd_x = own_state
     bwd_acc = None
     levels = []
     partials = None
@@ -293,7 +299,7 @@
     attn, grad_q, grad_k, grad_v, grad_gate = final_part(
         query_rows, key_rows, value_rows, out_grad, partials, gate_t, level_state, key_state_t
     )
-    return (attn, grad_q, grad_k, grad_v, grad_gate.transpose(1, 0, 2))
+    return (attn, grad_q, grad_k, grad_v, grad_gate)
 
 
 def solution(mesh):

time: 83.2 us -> 81.6 us (0.981)
  local copies, waits for them, and re-layouts: 6.5 us -> 3.61 us
    unnamed x5 -> x6, local copies, waits for them, and re-layouts: 1.83 us -> 0.1 us
    convert_element_type x1 -> x0, other arithmetic: 1.21 us -> none  [per_device(): grad_wide = grad_state.astype(jnp.float32)]
    transpose x1 -> x0, local copies, waits for them, and re-layouts: 1.14 us -> none  [final_part(): level_state_t = jnp.swapaxes(level_state, 2, 3)]
    convert_element_type x1 -> x2, other arithmetic: 0.06 us -> 1.03 us  [per_device(): fwd_x.astype(jnp.bfloat16)]
    convert_element_type x1, other arithmetic: 0.03 us -> 0.97 us  [per_device(): send.astype(jnp.bfloat16)]
  transfers between devices with their start and end apart: 10 -> 10, of which waited for: 2 -> 2; matrix products, arithmetic and copies ran while one was open for 5% -> 2% of each run, Pallas kernels for 36% -> 37%
where the time goes in v9:
time: 81.6 us; the launch traced here: 80.3 us
  Pallas kernels  44 us (54%)
  starting transfers between devices  11.9 us (15%)
  waiting for transfers between devices  9.2 us (11%)
  between operations  6.66 us (8%)
  other arithmetic  4.92 us (6%)
  local copies, waits for them, and re-layouts  3.61 us (4%)
    pallas_call x4, Pallas kernels, local_part(): pl.pallas_call(local_kernel, grid=(1,), in_specs=in_specs, out_specs=[col...  29.7 us
    pallas_call x1, Pallas kernels, final_part(): pl.pallas_call(final_kernel, grid=(heads,), in_specs=[row_spec] * 4 + [co...  8.97 us
    pallas_call x1, Pallas kernels, state_part(): pl.pallas_call(state_kernel, grid=(heads,), in_specs=[row_spec] * 4 + [ga...  5.31 us
    ppermute x2, waiting for transfers between devices, per_device(): lax.ppermute(fwd_x.astype(jnp.bfloat16), 'ctx', pairs_of(kf, ctx_len))  4.97 us
    ppermute x3, waiting for transfers between devices, per_device(): fwd_got = lax.ppermute(fwd_x, 'ctx', pairs_of(kf, ctx_len))  4.21 us
    ppermute x3, starting transfers between devices, per_device(): fwd_got = lax.ppermute(fwd_x, 'ctx', pairs_of(kf, ctx_len))  4.19 us
    ppermute x4, starting transfers between devices, per_device(): bwd_got = lax.ppermute(send, 'ctx', bwd_pairs)  3.94 us
    ppermute x1, starting transfers between devices, per_device(): lax.ppermute(send.astype(jnp.bfloat16), 'ctx', bwd_pairs)  2.33 us
  transfers between devices with their start and end apart: 10, of which 2 were waited for; matrix products, arithmetic and copies ran while one was open for 2% of the time, Pallas kernels for 37%

profile of v9, /device:TPU:4, one launch (start us, length us, event | category | flops | bytes accessed | tf_op | source)
XLA Modules:
  0.0 80.3 jit_solution(11345975102201141254)
XLA Ops:
  0.6 1.8 %fusion.9.g_ref = f32[4,16,1024]{2,1,0:T(8,128)} fusion(f32[16,4,1024]{2,1,0:T(4,128)} %param.10), kind=kLoop, calls=%fused_computation.18 | loop fusion | bytes 524288 | tf_op jit(solution)/shard_map/transpose | solution.py:253
  2.5 1.7 %fusion.22 = (s32[1,1]{1,0:T(1,128)}, s32[1,1]{1,0:T(1,128)}, s32[1,1]{1,0:T(1,128)}, s32[1,1]{1,0:T(1,128)}, s32[1,1]{1,0:T(1,128)}, /*index=5*/s32[1,1]{1,0:T(...) fusion(s32[32,32]{1,0:T(8,128)} %param.11, s32[]{:T(128)S(6)} %select_n.251, s32[]{:T(128)S(6)} %select_n.249, ...), kind=kLoop, calls=%fused_computation.40 | loop fusion | bytes 112 | tf_op jit(solution)/shard_map/dynamic_slice | solution.py:224
  4.8 5.3 %shard_map.101 = (f32[4,128,128]{2,1,0:T(8,128)}, f32[5,4,128,128]{3,2,1,0:T(8,128)}) custom-call(bf16[4,1024,128]{2,1,0:T(8,128)(2,1)} %q_ref.11, bf16[4,1024,128]{2,1,0:T(8,128)(2,1)} %k_ref.11, bf16[4,1024,128]{2,1,0:T(8,128)(2,1)} %v_ref.11, bf16[4,1024,128]{2,1,0:T(8,128)(2,1)} %do_ref.11, f32[4,16,1024]{2,1,0:T(8,128)} %fusion.9.g_ref), custom_call_target="tpu_custom_call" | custom-call | flops 805306368 | bytes 4456448 | tf_op jit(solution)/shard_map/pallas_call | solution.py:138
  10.1 1.0 %fusion.10 = bf16[4,128,128]{2,1,0:T(8,128)(2,1)S(1)} fusion(f32[5,4,128,128]{3,2,1,0:T(8,128)} %get-tuple-element.56, pred[]{:T(512)S(6)} %and.45), kind=kLoop, calls=%fused_computation.29 | loop fusion | flops 65536 | bytes 262145 | tf_op jit(solution)/shard_map/convert_element_type | solution.py:282
  11.1 2.3 %collective-permute-start.1 = (bf16[4,128,128]{2,1,0:T(8,128)(2,1)S(1)}, bf16[4,128,128]{2,1,0:T(8,128)(2,1)S(1)}, u32[]{:S(2)}, u32[]{:S(2)}) collective-permute-start(bf16[4,128,128]{2,1,0:T(8,128)(2,1)S(1)} %fusion.10), channel_id=1, source_target_pairs={{0,128},{8,136},{16,144},{24,152},{32,160},{40,168},{48,176},{56,1... | collective-permute-start | bytes 393224 | tf_op jit(solution)/shard_map/ppermute | solution.py:282
  13.4 1.0 %convert_element_type.39 = bf16[4,128,128]{2,1,0:T(8,128)(2,1)S(1)} convert(f32[4,128,128]{2,1,0:T(8,128)} %get-tuple-element.55) | non-fusion elementwise | flops 65536 | bytes 393216 | tf_op jit(solution)/shard_map/convert_element_type | solution.py:266
  14.4 0.1 collective-permute-start
  19.5 0.0 copy-start
  19.6 0.0 copy-start.1
  19.6 7.5 %shard_map.102 = (f32[4,128,1024]{2,1,0:T(8,128)}, f32[4,128,1024]{2,1,0:T(8,128)}, f32[4,1024,128]{2,1,0:T(8,128)}, f32[4,1024,128]{2,1,0:T(8,128)}, f32[4,16,1024]{2,1,0:T(8,128)}) custom-call(bf16[4,1024,128]{2,1,0:T(8,128)(2,1)} %q_ref.11, bf16[4,1024,128]{2,1,0:T(8,128)(2,1)} %k_ref.11, bf16[4,1024,128]{2,1,0:T(8,128)(2,1)} %v_ref.11, ...), custom_call_target="tpu_custom_call" | custom-call | flops 1006632960 | bytes 3276800 | tf_op jit(solution)/shard_map/pallas_call | solution.py:104
  27.1 0.0 collective-permute-done.1
  27.1 0.0 collective-permute-done
  27.1 0.0 copy-done
  27.2 0.5 collective-permute-start.3
  27.7 0.0 copy-done.1
  27.7 1.7 %collective-permute-start.2 = (f32[4,128,128]{2,1,0:T(8,128)S(1)}, f32[4,128,128]{2,1,0:T(8,128)S(1)}, u32[]{:S(2)}, u32[]{:S(2)}) collective-permute-start(f32[4,128,128]{2,1,0:T(8,128)S(1)} %add_select_fusion.2), channel_id=1, source_target_pairs={{0,16},{8,24},{16,0},{24,8},{32,48},{40,56},{48,32},{56,40},{64,80... | collective-permute-start | bytes 786440 | tf_op jit(solution)/shard_map/ppermute | solution.py:270
  29.4 7.4 %shard_map.103 = (f32[4,128,1024]{2,1,0:T(8,128)}, f32[4,128,1024]{2,1,0:T(8,128)}, f32[4,1024,128]{2,1,0:T(8,128)}, f32[4,1024,128]{2,1,0:T(8,128)}, f32[4,16,1024]{2,1,0:T(8,128)}) custom-call(bf16[4,1024,128]{2,1,0:T(8,128)(2,1)} %q_ref.11, ...), custom_call_target="tpu_custom_call", output_to_operand_aliasing={{0}: (5, {}), {1}: (6, {}), {2}: (7, {}), {3}: (8, {}), {4}... | custom-call | flops 1006632960 | bytes 3276800 | tf_op jit(solution)/shard_map/pallas_call | solution.py:104
  36.8 0.0 collective-permute-done.3
  36.8 0.0 collective-permute-done.2
  36.8 0.8 fusion.2
  37.6 2.9 %collective-permute-start.5 = (f32[4,128,128]{2,1,0:T(8,128)}, f32[4,128,128]{2,1,0:T(8,128)S(1)}, u32[]{:S(2)}, u32[]{:S(2)}) collective-permute-start(f32[4,128,128]{2,1,0:T(8,128)} %fusion.2), channel_id=1, source_target_pairs={{0,32},{8,40},{16,48},{24,56},{32,0},{40,8},{48,16},{56,24},{64,96... | collective-permute-start | bytes 786440 | tf_op jit(solution)/shard_map/ppermute | solution.py:284
  40.5 0.9 %collective-permute-start.4 = (f32[4,128,128]{2,1,0:T(8,128)S(1)}, f32[4,128,128]{2,1,0:T(8,128)S(1)}, u32[]{:S(2)}, u32[]{:S(2)}) collective-permute-start(f32[4,128,128]{2,1,0:T(8,128)S(1)} %add_select_fusion.1), channel_id=1, source_target_pairs={{0,32},{8,40},{16,48},{24,56},{32,0},{40,8},{48,16},{56,24},{64,96... | collective-permute-start | bytes 786440 | tf_op jit(solution)/shard_map/ppermute | solution.py:270
  41.4 7.4 %shard_map.104 = (f32[4,128,1024]{2,1,0:T(8,128)}, f32[4,128,1024]{2,1,0:T(8,128)}, f32[4,1024,128]{2,1,0:T(8,128)}, f32[4,1024,128]{2,1,0:T(8,128)}, f32[4,16,1024]{2,1,0:T(8,128)}) custom-call(bf16[4,1024,128]{2,1,0:T(8,128)(2,1)} %q_ref.11, ...), custom_call_target="tpu_custom_call", output_to_operand_aliasing={{0}: (5, {}), {1}: (6, {}), {2}: (7, {}), {3}: (8, {}), {4}... | custom-call | flops 1006632960 | bytes 3276800 | tf_op jit(solution)/shard_map/pallas_call | solution.py:104
  48.9 0.0 collective-permute-done.5
  48.9 4.2 %collective-permute-done.4 = f32[4,128,128]{2,1,0:T(8,128)S(1)} collective-permute-done((f32[4,128,128]{2,1,0:T(8,128)S(1)}, f32[4,128,128]{2,1,0:T(8,128)S(1)}, u32[]{:S(2)}, u32[]{:S(2)}) %collective-permute-start.4) | collective-permute-done | bytes 262176 | tf_op jit(solution)/shard_map/ppermute | solution.py:270
  53.1 0.8 fusion.1
  53.9 0.5 collective-permute-start.7
  54.4 1.6 %collective-permute-start.6 = (f32[4,128,128]{2,1,0:T(8,128)S(1)}, f32[4,128,128]{2,1,0:T(8,128)S(1)}, u32[]{:S(2)}, u32[]{:S(2)}) collective-permute-start(f32[4,128,128]{2,1,0:T(8,128)S(1)} %add_select_fusion), channel_id=1, source_target_pairs={{0,64},{8,72},{16,80},{24,88},{32,96},{40,104},{48,112},{56,120},{... | collective-permute-start | bytes 786440 | tf_op jit(solution)/shard_map/ppermute | solution.py:270
  56.0 7.5 %shard_map.105 = (f32[4,128,1024]{2,1,0:T(8,128)}, f32[4,128,1024]{2,1,0:T(8,128)}, f32[4,1024,128]{2,1,0:T(8,128)}, f32[4,1024,128]{2,1,0:T(8,128)}, f32[4,16,1024]{2,1,0:T(8,128)}) custom-call(bf16[4,1024,128]{2,1,0:T(8,128)(2,1)} %q_ref.11, ...), custom_call_target="tpu_custom_call", output_to_operand_aliasing={{0}: (5, {}), {1}: (6, {}), {2}: (7, {}), {3}: (8, {}), {4}... | custom-call | flops 1006632960 | bytes 3276800 | tf_op jit(solution)/shard_map/pallas_call | solution.py:104
  63.5 0.0 collective-permute-done.7
  63.5 0.0 collective-permute-done.6
  63.5 0.1 select_convert_fusion.1
  63.6 1.4 %collective-permute-start.8 = (bf16[4,128,128]{2,1,0:T(8,128)(2,1)S(1)}, bf16[4,128,128]{2,1,0:T(8,128)(2,1)S(1)}, u32[]{:S(2)}, u32[]{:S(2)}) collective-permute-start(bf16[4,128,128]{2,1,0:T(8,128)(2,1)S(1)} %select_convert_fusion.1), channel_id=1, source_target_pairs={{0,128},{8,136},{16,144},{24,152},{32,160},{40,168},{48,176},{56,1... | collective-permute-start | bytes 393224 | tf_op jit(solution)/shard_map/ppermute | solution.py:265
  65.0 0.1 fusion
  65.0 0.1 collective-permute-start.9
  65.2 5.0 %collective-permute-done.8 = bf16[4,128,128]{2,1,0:T(8,128)(2,1)S(1)} collective-permute-done((bf16[4,128,128]{2,1,0:T(8,128)(2,1)S(1)}, bf16[4,128,128]{2,1,0:T(8,128)(2,1)S(1)}, u32[]{:S(2)}, u32[]{:S(2)}) %collective-permute-start.8) | collective-permute-done | bytes 131104 | tf_op jit(solution)/shard_map/ppermute | solution.py:265
  70.2 0.0 copy-start.2
  70.2 0.0 collective-permute-done.9
  70.2 0.9 %fusion.8.kst_ref = bf16[4,128,128]{2,1,0:T(8,128)(2,1)} fusion(f32[4,128,128]{2,1,0:T(8,128)S(1)} %collective-permute-done.9, pred[]{:T(512)} %bitcast.1, pred[]{:T(512)S(6)} %eq.22, f32[4,128,128]{2,1,0:T(8,128)S(1)} %collective-permute-done.7, f32[4,128,128]{2,1,0:T(8,128)S(1)} %get-tuple-element.106, pred[]{:T(512)} %bitcast.4, pred[]{:T(512)S(6)} %eq.21), kind=kLoop, calls=%fused_computation.16 | loop fusion | flops 458752 | bytes 917508 | tf_op jit(solution)/shard_map/convert_element_type | solution.py:298
  71.1 0.1 copy-done.2
  71.2 9.0 %shard_map.106 = (bf16[4,1024,128]{2,1,0:T(8,128)(2,1)}, bf16[4,1024,128]{2,1,0:T(8,128)(2,1)}, bf16[4,1024,128]{2,1,0:T(8,128)(2,1)}, bf16[4,1024,128]{2,1,0:T(8,128)(2,1)}, f32[16,4,1024]{2,1,0:T(4,128)}) custom-call(bf16[4,1024,128]{2,1,0:T(8,128)(2,1)} %q_ref.11, bf16[4,1024,128]{2,1,0:T(8,128)(2,1)} %k_ref.11, bf16[4,1024,128]{2,1,0:T(8,128)(2,1)} %v_ref.11, ...), custom_call_target="tpu_custom_call" | custom-call | flops 1610612736 | bytes 17825792 | tf_op jit(solution)/shard_map/pallas_call | solution.py:205
  (11 shorter events, 0.4 us)
Async XLA Ops:
  11.1 16.0 %collective-permute-start.1 = (bf16[4,128,128]{2,1,0:T(8,128)(2,1)S(1)}, bf16[4,128,128]{2,1,0:T(8,128)(2,1)S(1)}, u32[]{:S(2)}, u32[]{:S(2)}) collective-permute-start(bf16[4,128,128]{2,1,0:T(8,128)(2,1)S(1)} %fusion.10), channel_id=1, source_target_pairs={{0,128},{8,136},{16,144},{24,152},{32,160},{40,168},{48,176},{56,1... | collective-permute-start | bytes 393224 | tf_op jit(solution)/shard_map/ppermute | solution.py:282
  14.4 12.7 %collective-permute-start = (bf16[4,128,128]{2,1,0:T(8,128)(2,1)S(1)}, bf16[4,128,128]{2,1,0:T(8,128)(2,1)S(1)}, u32[]{:S(2)}, u32[]{:S(2)}) collective-permute-start(bf16[4,128,128]{2,1,0:T(8,128)(2,1)S(1)} %convert_element_type.39), channel_id=1, source_target_pairs={{0,8},{8,0},{16,24},{24,16},{32,40},{40,32},{48,56},{56,48},{64,72... | collective-permute-start | bytes 393224 | tf_op jit(solution)/shard_map/ppermute | solution.py:265
  19.5 7.6 %copy-start = (f32[5,4,128,128]{3,2,1,0:T(8,128)S(1)}, f32[5,4,128,128]{3,2,1,0:T(8,128)}, u32[]{:S(2)}) copy-start(f32[5,4,128,128]{3,2,1,0:T(8,128)} %get-tuple-element.56) | copy-start | bytes 3932164
  19.6 8.1 %copy-start.1 = (f32[4,128,128]{2,1,0:T(8,128)S(1)}, f32[4,128,128]{2,1,0:T(8,128)}, u32[]{:S(2)}) copy-start(f32[4,128,128]{2,1,0:T(8,128)} %get-tuple-element.55) | copy-start | bytes 786436
  27.2 9.6 %collective-permute-start.3 = (f32[4,128,128]{2,1,0:T(8,128)S(1)}, f32[4,128,128]{2,1,0:T(8,128)S(1)}, u32[]{:S(2)}, u32[]{:S(2)}) collective-permute-start(f32[4,128,128]{2,1,0:T(8,128)S(1)} %fusion.3), channel_id=1, source_target_pairs={{0,64},{8,72},{16,80},{24,88},{32,96},{40,104},{48,112},{56,120},{... | collective-permute-start | bytes 786440 | tf_op jit(solution)/shard_map/ppermute | solution.py:284
  27.7 9.1 %collective-permute-start.2 = (f32[4,128,128]{2,1,0:T(8,128)S(1)}, f32[4,128,128]{2,1,0:T(8,128)S(1)}, u32[]{:S(2)}, u32[]{:S(2)}) collective-permute-start(f32[4,128,128]{2,1,0:T(8,128)S(1)} %add_select_fusion.2), channel_id=1, source_target_pairs={{0,16},{8,24},{16,0},{24,8},{32,48},{40,56},{48,32},{56,40},{64,80... | collective-permute-start | bytes 786440 | tf_op jit(solution)/shard_map/ppermute | solution.py:270
  37.6 11.3 %collective-permute-start.5 = (f32[4,128,128]{2,1,0:T(8,128)}, f32[4,128,128]{2,1,0:T(8,128)S(1)}, u32[]{:S(2)}, u32[]{:S(2)}) collective-permute-start(f32[4,128,128]{2,1,0:T(8,128)} %fusion.2), channel_id=1, source_target_pairs={{0,32},{8,40},{16,48},{24,56},{32,0},{40,8},{48,16},{56,24},{64,96... | collective-permute-start | bytes 786440 | tf_op jit(solution)/shard_map/ppermute | solution.py:284
  40.5 12.5 %collective-permute-start.4 = (f32[4,128,128]{2,1,0:T(8,128)S(1)}, f32[4,128,128]{2,1,0:T(8,128)S(1)}, u32[]{:S(2)}, u32[]{:S(2)}) collective-permute-start(f32[4,128,128]{2,1,0:T(8,128)S(1)} %add_select_fusion.1), channel_id=1, source_target_pairs={{0,32},{8,40},{16,48},{24,56},{32,0},{40,8},{48,16},{56,24},{64,96... | collective-permute-start | bytes 786440 | tf_op jit(solution)/shard_map/ppermute | solution.py:270
  53.9 9.6 %collective-permute-start.7 = (f32[4,128,128]{2,1,0:T(8,128)}, f32[4,128,128]{2,1,0:T(8,128)S(1)}, u32[]{:S(2)}, u32[]{:S(2)}) collective-permute-start(f32[4,128,128]{2,1,0:T(8,128)} %get-tuple-element.105), channel_id=1, source_target_pairs={{0,16},{8,24},{16,0},{24,8},{32,48},{40,56},{48,32},{56,40},{64,80... | collective-permute-start | bytes 786440 | tf_op jit(solution)/shard_map/ppermute | solution.py:284
  54.4 9.1 %collective-permute-start.6 = (f32[4,128,128]{2,1,0:T(8,128)S(1)}, f32[4,128,128]{2,1,0:T(8,128)S(1)}, u32[]{:S(2)}, u32[]{:S(2)}) collective-permute-start(f32[4,128,128]{2,1,0:T(8,128)S(1)} %add_select_fusion), channel_id=1, source_target_pairs={{0,64},{8,72},{16,80},{24,88},{32,96},{40,104},{48,112},{56,120},{... | collective-permute-start | bytes 786440 | tf_op jit(solution)/shard_map/ppermute | solution.py:270
  63.6 6.6 %collective-permute-start.8 = (bf16[4,128,128]{2,1,0:T(8,128)(2,1)S(1)}, bf16[4,128,128]{2,1,0:T(8,128)(2,1)S(1)}, u32[]{:S(2)}, u32[]{:S(2)}) collective-permute-start(bf16[4,128,128]{2,1,0:T(8,128)(2,1)S(1)} %select_convert_fusion.1), channel_id=1, source_target_pairs={{0,128},{8,136},{16,144},{24,152},{32,160},{40,168},{48,176},{56,1... | collective-permute-start | bytes 393224 | tf_op jit(solution)/shard_map/ppermute | solution.py:265
  65.0 5.2 %collective-permute-start.9 = (f32[4,128,128]{2,1,0:T(8,128)S(1)}, f32[4,128,128]{2,1,0:T(8,128)S(1)}, u32[]{:S(2)}, u32[]{:S(2)}) collective-permute-start(f32[4,128,128]{2,1,0:T(8,128)S(1)} %fusion), channel_id=1, source_target_pairs={{0,8},{8,0},{16,24},{24,16},{32,40},{40,32},{48,56},{56,48},{64,72... | collective-permute-start | bytes 786440 | tf_op jit(solution)/shard_map/ppermute | solution.py:284
  70.2 1.0 %copy-start.2 = (bf16[5,4,128,128]{3,2,1,0:T(8,128)(2,1)}, bf16[5,4,128,128]{3,2,1,0:T(8,128)(2,1)S(1)}, u32[]{:S(2)}) copy-start(bf16[5,4,128,128]{3,2,1,0:T(8,128)(2,1)S(1)} %fusion.20.ls_ref) | copy-start | bytes 1966084

commit v10 on v9

--- a/solution.py
+++ b/solution.py
@@ -221,7 +221,8 @@
 
 
 def same_doc(block_levels, earlier, later):
-    return block_levels[later, earlier] >= 0
+    picked = lax.dynamic_slice(block_levels, (later, earlier), (1, 1))
+    return picked.reshape(1, 1, 1) >= 0
 
 
 def step_masks(block_levels, me, k):

time: 81.6 us -> 81.4 us (level)
  no operation moved by 1% of the time
where the time goes in v10:
time: 81.4 us; the launch traced here: 80.1 us
  Pallas kernels  44 us (54%)
  starting transfers between devices  11.9 us (15%)
  waiting for transfers between devices  9.17 us (11%)
  between operations  6.52 us (8%)
  other arithmetic  4.92 us (6%)
  local copies, waits for them, and re-layouts  3.54 us (4%)
    pallas_call x4, Pallas kernels, local_part(): pl.pallas_call(local_kernel, grid=(1,), in_specs=in_specs, out_specs=[col...  29.7 us
    pallas_call x1, Pallas kernels, final_part(): pl.pallas_call(final_kernel, grid=(heads,), in_specs=[row_spec] * 4 + [co...  8.97 us
    pallas_call x1, Pallas kernels, state_part(): pl.pallas_call(state_kernel, grid=(heads,), in_specs=[row_spec] * 4 + [ga...  5.31 us
    ppermute x2, waiting for transfers between devices, per_device(): lax.ppermute(fwd_x.astype(jnp.bfloat16), 'ctx', pairs_of(kf, ctx_len))  4.95 us
    ppermute x3, waiting for transfers between devices, per_device(): fwd_got = lax.ppermute(fwd_x, 'ctx', pairs_of(kf, ctx_len))  4.21 us
    ppermute x3, starting transfers between devices, per_device(): fwd_got = lax.ppermute(fwd_x, 'ctx', pairs_of(kf, ctx_len))  4.18 us
    ppermute x4, starting transfers between devices, per_device(): bwd_got = lax.ppermute(send, 'ctx', bwd_pairs)  3.94 us
    ppermute x1, starting transfers between devices, per_device(): lax.ppermute(send.astype(jnp.bfloat16), 'ctx', bwd_pairs)  2.33 us
  transfers between devices with their start and end apart: 10, of which 2 were waited for; matrix products, arithmetic and copies ran while one was open for 2% of the time, Pallas kernels for 37%

profile of v10, /device:TPU:4, one launch (start us, length us, event | category | flops | bytes accessed | tf_op | source)
XLA Modules:
  0.0 80.1 jit_solution(16443111513162034773)
XLA Ops:
  0.6 1.8 %fusion.9.g_ref = f32[4,16,1024]{2,1,0:T(8,128)} fusion(f32[16,4,1024]{2,1,0:T(4,128)} %param.10), kind=kLoop, calls=%fused_computation.18 | loop fusion | bytes 524288 | tf_op jit(solution)/shard_map/transpose | solution.py:254
  2.5 1.6 %fusion.22 = (s32[1,1]{1,0:T(1,128)}, s32[1,1]{1,0:T(1,128)}, s32[1,1]{1,0:T(1,128)}, s32[1,1]{1,0:T(1,128)}, s32[1,1]{1,0:T(1,128)}, /*index=5*/s32[1,1]{1,0:T(...) fusion(s32[32,32]{1,0:T(8,128)} %param.11, s32[]{:T(128)S(6)} %select_n.199, s32[]{:T(128)S(6)} %select_n.198, ...), kind=kLoop, calls=%fused_computation.40 | loop fusion | bytes 112 | tf_op jit(solution)/shard_map/dynamic_slice | solution.py:224
  4.7 5.3 %shard_map.101 = (f32[4,128,128]{2,1,0:T(8,128)}, f32[5,4,128,128]{3,2,1,0:T(8,128)}) custom-call(bf16[4,1024,128]{2,1,0:T(8,128)(2,1)} %q_ref.11, bf16[4,1024,128]{2,1,0:T(8,128)(2,1)} %k_ref.11, bf16[4,1024,128]{2,1,0:T(8,128)(2,1)} %v_ref.11, bf16[4,1024,128]{2,1,0:T(8,128)(2,1)} %do_ref.11, f32[4,16,1024]{2,1,0:T(8,128)} %fusion.9.g_ref), custom_call_target="tpu_custom_call" | custom-call | flops 805306368 | bytes 4456448 | tf_op jit(solution)/shard_map/pallas_call | solution.py:138
  10.0 1.0 %fusion.10 = bf16[4,128,128]{2,1,0:T(8,128)(2,1)S(1)} fusion(f32[5,4,128,128]{3,2,1,0:T(8,128)} %get-tuple-element.56, pred[]{:T(512)} %bitcast.4), kind=kLoop, calls=%fused_computation.29 | loop fusion | flops 65536 | bytes 262145 | tf_op jit(solution)/shard_map/convert_element_type | solution.py:283
  11.0 2.3 %collective-permute-start.1 = (bf16[4,128,128]{2,1,0:T(8,128)(2,1)S(1)}, bf16[4,128,128]{2,1,0:T(8,128)(2,1)S(1)}, u32[]{:S(2)}, u32[]{:S(2)}) collective-permute-start(bf16[4,128,128]{2,1,0:T(8,128)(2,1)S(1)} %fusion.10), channel_id=1, source_target_pairs={{0,128},{8,136},{16,144},{24,152},{32,160},{40,168},{48,176},{56,1... | collective-permute-start | bytes 393224 | tf_op jit(solution)/shard_map/ppermute | solution.py:283
  13.4 1.0 %convert_element_type.39 = bf16[4,128,128]{2,1,0:T(8,128)(2,1)S(1)} convert(f32[4,128,128]{2,1,0:T(8,128)} %get-tuple-element.55) | non-fusion elementwise | flops 65536 | bytes 393216 | tf_op jit(solution)/shard_map/convert_element_type | solution.py:267
  14.3 0.1 collective-permute-start
  19.3 0.0 copy-start
  19.3 0.0 copy-start.1
  19.3 7.5 %shard_map.102 = (f32[4,128,1024]{2,1,0:T(8,128)}, f32[4,128,1024]{2,1,0:T(8,128)}, f32[4,1024,128]{2,1,0:T(8,128)}, f32[4,1024,128]{2,1,0:T(8,128)}, f32[4,16,1024]{2,1,0:T(8,128)}) custom-call(bf16[4,1024,128]{2,1,0:T(8,128)(2,1)} %q_ref.11, bf16[4,1024,128]{2,1,0:T(8,128)(2,1)} %k_ref.11, bf16[4,1024,128]{2,1,0:T(8,128)(2,1)} %v_ref.11, ...), custom_call_target="tpu_custom_call" | custom-call | flops 1006632960 | bytes 3276800 | tf_op jit(solution)/shard_map/pallas_call | solution.py:104
  26.9 0.0 collective-permute-done.1
  26.9 0.0 collective-permute-done
  26.9 0.0 copy-done
  27.0 0.5 collective-permute-start.3
  27.5 0.0 copy-done.1
  27.5 1.7 %collective-permute-start.2 = (f32[4,128,128]{2,1,0:T(8,128)S(1)}, f32[4,128,128]{2,1,0:T(8,128)S(1)}, u32[]{:S(2)}, u32[]{:S(2)}) collective-permute-start(f32[4,128,128]{2,1,0:T(8,128)S(1)} %add_select_fusion.2), channel_id=1, source_target_pairs={{0,16},{8,24},{16,0},{24,8},{32,48},{40,56},{48,32},{56,40},{64,80... | collective-permute-start | bytes 786440 | tf_op jit(solution)/shard_map/ppermute | solution.py:271
  29.2 7.4 %shard_map.103 = (f32[4,128,1024]{2,1,0:T(8,128)}, f32[4,128,1024]{2,1,0:T(8,128)}, f32[4,1024,128]{2,1,0:T(8,128)}, f32[4,1024,128]{2,1,0:T(8,128)}, f32[4,16,1024]{2,1,0:T(8,128)}) custom-call(bf16[4,1024,128]{2,1,0:T(8,128)(2,1)} %q_ref.11, ...), custom_call_target="tpu_custom_call", output_to_operand_aliasing={{0}: (5, {}), {1}: (6, {}), {2}: (7, {}), {3}: (8, {}), {4}... | custom-call | flops 1006632960 | bytes 3276800 | tf_op jit(solution)/shard_map/pallas_call | solution.py:104
  36.6 0.0 collective-permute-done.3
  36.6 0.0 collective-permute-done.2
  36.6 0.8 fusion.2
  37.4 2.9 %collective-permute-start.5 = (f32[4,128,128]{2,1,0:T(8,128)}, f32[4,128,128]{2,1,0:T(8,128)S(1)}, u32[]{:S(2)}, u32[]{:S(2)}) collective-permute-start(f32[4,128,128]{2,1,0:T(8,128)} %fusion.2), channel_id=1, source_target_pairs={{0,32},{8,40},{16,48},{24,56},{32,0},{40,8},{48,16},{56,24},{64,96... | collective-permute-start | bytes 786440 | tf_op jit(solution)/shard_map/ppermute | solution.py:285
  40.3 0.9 %collective-permute-start.4 = (f32[4,128,128]{2,1,0:T(8,128)S(1)}, f32[4,128,128]{2,1,0:T(8,128)S(1)}, u32[]{:S(2)}, u32[]{:S(2)}) collective-permute-start(f32[4,128,128]{2,1,0:T(8,128)S(1)} %add_select_fusion.1), channel_id=1, source_target_pairs={{0,32},{8,40},{16,48},{24,56},{32,0},{40,8},{48,16},{56,24},{64,96... | collective-permute-start | bytes 786440 | tf_op jit(solution)/shard_map/ppermute | solution.py:271
  41.2 7.4 %shard_map.104 = (f32[4,128,1024]{2,1,0:T(8,128)}, f32[4,128,1024]{2,1,0:T(8,128)}, f32[4,1024,128]{2,1,0:T(8,128)}, f32[4,1024,128]{2,1,0:T(8,128)}, f32[4,16,1024]{2,1,0:T(8,128)}) custom-call(bf16[4,1024,128]{2,1,0:T(8,128)(2,1)} %q_ref.11, ...), custom_call_target="tpu_custom_call", output_to_operand_aliasing={{0}: (5, {}), {1}: (6, {}), {2}: (7, {}), {3}: (8, {}), {4}... | custom-call | flops 1006632960 | bytes 3276800 | tf_op jit(solution)/shard_map/pallas_call | solution.py:104
  48.6 0.0 collective-permute-done.5
  48.7 4.2 %collective-permute-done.4 = f32[4,128,128]{2,1,0:T(8,128)S(1)} collective-permute-done((f32[4,128,128]{2,1,0:T(8,128)S(1)}, f32[4,128,128]{2,1,0:T(8,128)S(1)}, u32[]{:S(2)}, u32[]{:S(2)}) %collective-permute-start.4) | collective-permute-done | bytes 262176 | tf_op jit(solution)/shard_map/ppermute | solution.py:271
  52.9 0.8 %fusion.1 = (f32[4,128,128]{2,1,0:T(8,128)}, f32[4,128,128]{2,1,0:T(8,128)S(1)}) fusion(f32[5,4,128,128]{3,2,1,0:T(8,128)S(1)} %copy-done, pred[]{:T(512)} %bitcast.19, pred[]{:T(512)} %bitcast.6, pred[]{:T(512)} %eq.21, f32[4,128,128]{2,1,0:T(8,128)S(1)} %collective-permute-done.5, pred[]{:T(512)} %bitcast.12, f32[4,128,128]{2,1,0:T(8,128)S(1)} %collective-permute-done.3, ...), kind=kLoop, calls=%fused_computation.5 | loop fusion | flops 655360 | bytes 1572871 | tf_op jit(solution)/shard_map/jit(_where)/select_n | solution.py:279
  53.7 0.5 collective-permute-start.7
  54.2 1.6 %collective-permute-start.6 = (f32[4,128,128]{2,1,0:T(8,128)S(1)}, f32[4,128,128]{2,1,0:T(8,128)S(1)}, u32[]{:S(2)}, u32[]{:S(2)}) collective-permute-start(f32[4,128,128]{2,1,0:T(8,128)S(1)} %add_select_fusion), channel_id=1, source_target_pairs={{0,64},{8,72},{16,80},{24,88},{32,96},{40,104},{48,112},{56,120},{... | collective-permute-start | bytes 786440 | tf_op jit(solution)/shard_map/ppermute | solution.py:271
  55.8 7.5 %shard_map.105 = (f32[4,128,1024]{2,1,0:T(8,128)}, f32[4,128,1024]{2,1,0:T(8,128)}, f32[4,1024,128]{2,1,0:T(8,128)}, f32[4,1024,128]{2,1,0:T(8,128)}, f32[4,16,1024]{2,1,0:T(8,128)}) custom-call(bf16[4,1024,128]{2,1,0:T(8,128)(2,1)} %q_ref.11, ...), custom_call_target="tpu_custom_call", output_to_operand_aliasing={{0}: (5, {}), {1}: (6, {}), {2}: (7, {}), {3}: (8, {}), {4}... | custom-call | flops 1006632960 | bytes 3276800 | tf_op jit(solution)/shard_map/pallas_call | solution.py:104
  63.3 0.0 collective-permute-done.7
  63.3 0.0 collective-permute-done.6
  63.3 0.1 select_convert_fusion.1
  63.4 1.4 %collective-permute-start.8 = (bf16[4,128,128]{2,1,0:T(8,128)(2,1)S(1)}, bf16[4,128,128]{2,1,0:T(8,128)(2,1)S(1)}, u32[]{:S(2)}, u32[]{:S(2)}) collective-permute-start(bf16[4,128,128]{2,1,0:T(8,128)(2,1)S(1)} %select_convert_fusion.1), channel_id=1, source_target_pairs={{0,128},{8,136},{16,144},{24,152},{32,160},{40,168},{48,176},{56,1... | collective-permute-start | bytes 393224 | tf_op jit(solution)/shard_map/ppermute | solution.py:266
  64.8 0.1 fusion
  64.8 0.1 collective-permute-start.9
  65.0 4.9 %collective-permute-done.8 = bf16[4,128,128]{2,1,0:T(8,128)(2,1)S(1)} collective-permute-done((bf16[4,128,128]{2,1,0:T(8,128)(2,1)S(1)}, bf16[4,128,128]{2,1,0:T(8,128)(2,1)S(1)}, u32[]{:S(2)}, u32[]{:S(2)}) %collective-permute-start.8) | collective-permute-done | bytes 131104 | tf_op jit(solution)/shard_map/ppermute | solution.py:266
  70.0 0.0 copy-start.2
  70.0 0.0 collective-permute-done.9
  70.0 0.9 %fusion.8.kst_ref = bf16[4,128,128]{2,1,0:T(8,128)(2,1)} fusion(f32[4,128,128]{2,1,0:T(8,128)S(1)} %collective-permute-done.9, pred[]{:T(512)} %bitcast.1, pred[]{:T(512)} %eq.22, f32[4,128,128]{2,1,0:T(8,128)S(1)} %collective-permute-done.7, f32[4,128,128]{2,1,0:T(8,128)S(1)} %get-tuple-element.106, pred[]{:T(512)} %bitcast.6, pred[]{:T(512)} %eq.21), kind=kLoop, calls=%fused_computation.16 | loop fusion | flops 458752 | bytes 917508 | tf_op jit(solution)/shard_map/convert_element_type | solution.py:299
  70.9 0.1 copy-done.2
  71.0 9.0 %shard_map.106 = (bf16[4,1024,128]{2,1,0:T(8,128)(2,1)}, bf16[4,1024,128]{2,1,0:T(8,128)(2,1)}, bf16[4,1024,128]{2,1,0:T(8,128)(2,1)}, bf16[4,1024,128]{2,1,0:T(8,128)(2,1)}, f32[16,4,1024]{2,1,0:T(4,128)}) custom-call(bf16[4,1024,128]{2,1,0:T(8,128)(2,1)} %q_ref.11, bf16[4,1024,128]{2,1,0:T(8,128)(2,1)} %k_ref.11, bf16[4,1024,128]{2,1,0:T(8,128)(2,1)} %v_ref.11, ...), custom_call_target="tpu_custom_call" | custom-call | flops 1610612736 | bytes 17825792 | tf_op jit(solution)/shard_map/pallas_call | solution.py:205
  (11 shorter events, 0.4 us)
Async XLA Ops:
  11.0 15.8 %collective-permute-start.1 = (bf16[4,128,128]{2,1,0:T(8,128)(2,1)S(1)}, bf16[4,128,128]{2,1,0:T(8,128)(2,1)S(1)}, u32[]{:S(2)}, u32[]{:S(2)}) collective-permute-start(bf16[4,128,128]{2,1,0:T(8,128)(2,1)S(1)} %fusion.10), channel_id=1, source_target_pairs={{0,128},{8,136},{16,144},{24,152},{32,160},{40,168},{48,176},{56,1... | collective-permute-start | bytes 393224 | tf_op jit(solution)/shard_map/ppermute | solution.py:283
  14.3 12.6 %collective-permute-start = (bf16[4,128,128]{2,1,0:T(8,128)(2,1)S(1)}, bf16[4,128,128]{2,1,0:T(8,128)(2,1)S(1)}, u32[]{:S(2)}, u32[]{:S(2)}) collective-permute-start(bf16[4,128,128]{2,1,0:T(8,128)(2,1)S(1)} %convert_element_type.39), channel_id=1, source_target_pairs={{0,8},{8,0},{16,24},{24,16},{32,40},{40,32},{48,56},{56,48},{64,72... | collective-permute-start | bytes 393224 | tf_op jit(solution)/shard_map/ppermute | solution.py:266
  19.3 7.6 %copy-start = (f32[5,4,128,128]{3,2,1,0:T(8,128)S(1)}, f32[5,4,128,128]{3,2,1,0:T(8,128)}, u32[]{:S(2)}) copy-start(f32[5,4,128,128]{3,2,1,0:T(8,128)} %get-tuple-element.56) | copy-start | bytes 3932164
  19.3 8.1 %copy-start.1 = (f32[4,128,128]{2,1,0:T(8,128)S(1)}, f32[4,128,128]{2,1,0:T(8,128)}, u32[]{:S(2)}) copy-start(f32[4,128,128]{2,1,0:T(8,128)} %get-tuple-element.55) | copy-start | bytes 786436
  27.0 9.6 %collective-permute-start.3 = (f32[4,128,128]{2,1,0:T(8,128)S(1)}, f32[4,128,128]{2,1,0:T(8,128)S(1)}, u32[]{:S(2)}, u32[]{:S(2)}) collective-permute-start(f32[4,128,128]{2,1,0:T(8,128)S(1)} %fusion.3), channel_id=1, source_target_pairs={{0,64},{8,72},{16,80},{24,88},{32,96},{40,104},{48,112},{56,120},{... | collective-permute-start | bytes 786440 | tf_op jit(solution)/shard_map/ppermute | solution.py:285
  27.5 9.1 %collective-permute-start.2 = (f32[4,128,128]{2,1,0:T(8,128)S(1)}, f32[4,128,128]{2,1,0:T(8,128)S(1)}, u32[]{:S(2)}, u32[]{:S(2)}) collective-permute-start(f32[4,128,128]{2,1,0:T(8,128)S(1)} %add_select_fusion.2), channel_id=1, source_target_pairs={{0,16},{8,24},{16,0},{24,8},{32,48},{40,56},{48,32},{56,40},{64,80... | collective-permute-start | bytes 786440 | tf_op jit(solution)/shard_map/ppermute | solution.py:271
  37.4 11.3 %collective-permute-start.5 = (f32[4,128,128]{2,1,0:T(8,128)}, f32[4,128,128]{2,1,0:T(8,128)S(1)}, u32[]{:S(2)}, u32[]{:S(2)}) collective-permute-start(f32[4,128,128]{2,1,0:T(8,128)} %fusion.2), channel_id=1, source_target_pairs={{0,32},{8,40},{16,48},{24,56},{32,0},{40,8},{48,16},{56,24},{64,96... | collective-permute-start | bytes 786440 | tf_op jit(solution)/shard_map/ppermute | solution.py:285
  40.3 12.5 %collective-permute-start.4 = (f32[4,128,128]{2,1,0:T(8,128)S(1)}, f32[4,128,128]{2,1,0:T(8,128)S(1)}, u32[]{:S(2)}, u32[]{:S(2)}) collective-permute-start(f32[4,128,128]{2,1,0:T(8,128)S(1)} %add_select_fusion.1), channel_id=1, source_target_pairs={{0,32},{8,40},{16,48},{24,56},{32,0},{40,8},{48,16},{56,24},{64,96... | collective-permute-start | bytes 786440 | tf_op jit(solution)/shard_map/ppermute | solution.py:271
  53.7 9.6 %collective-permute-start.7 = (f32[4,128,128]{2,1,0:T(8,128)}, f32[4,128,128]{2,1,0:T(8,128)S(1)}, u32[]{:S(2)}, u32[]{:S(2)}) collective-permute-start(f32[4,128,128]{2,1,0:T(8,128)} %get-tuple-element.105), channel_id=1, source_target_pairs={{0,16},{8,24},{16,0},{24,8},{32,48},{40,56},{48,32},{56,40},{64,80... | collective-permute-start | bytes 786440 | tf_op jit(solution)/shard_map/ppermute | solution.py:285
  54.2 9.1 %collective-permute-start.6 = (f32[4,128,128]{2,1,0:T(8,128)S(1)}, f32[4,128,128]{2,1,0:T(8,128)S(1)}, u32[]{:S(2)}, u32[]{:S(2)}) collective-permute-start(f32[4,128,128]{2,1,0:T(8,128)S(1)} %add_select_fusion), channel_id=1, source_target_pairs={{0,64},{8,72},{16,80},{24,88},{32,96},{40,104},{48,112},{56,120},{... | collective-permute-start | bytes 786440 | tf_op jit(solution)/shard_map/ppermute | solution.py:271
  63.4 6.6 %collective-permute-start.8 = (bf16[4,128,128]{2,1,0:T(8,128)(2,1)S(1)}, bf16[4,128,128]{2,1,0:T(8,128)(2,1)S(1)}, u32[]{:S(2)}, u32[]{:S(2)}) collective-permute-start(bf16[4,128,128]{2,1,0:T(8,128)(2,1)S(1)} %select_convert_fusion.1), channel_id=1, source_target_pairs={{0,128},{8,136},{16,144},{24,152},{32,160},{40,168},{48,176},{56,1... | collective-permute-start | bytes 393224 | tf_op jit(solution)/shard_map/ppermute | solution.py:266
  64.8 5.2 %collective-permute-start.9 = (f32[4,128,128]{2,1,0:T(8,128)S(1)}, f32[4,128,128]{2,1,0:T(8,128)S(1)}, u32[]{:S(2)}, u32[]{:S(2)}) collective-permute-start(f32[4,128,128]{2,1,0:T(8,128)S(1)} %fusion), channel_id=1, source_target_pairs={{0,8},{8,0},{16,24},{24,16},{32,40},{40,32},{48,56},{56,48},{64,72... | collective-permute-start | bytes 786440 | tf_op jit(solution)/shard_map/ppermute | solution.py:285
  70.0 1.0 %copy-start.2 = (bf16[5,4,128,128]{3,2,1,0:T(8,128)(2,1)}, bf16[5,4,128,128]{3,2,1,0:T(8,128)(2,1)S(1)}, u32[]{:S(2)}) copy-start(bf16[5,4,128,128]{3,2,1,0:T(8,128)(2,1)S(1)} %fusion.20.ls_ref) | copy-start | bytes 1966084

commit v11 on v10

--- a/solution.py
+++ b/solution.py
@@ -164,7 +164,11 @@
     first = nlev - nbits
     key_state_t = kst_ref[...]
     h = pl.program_id(0)
-    state_t = [jnp.transpose(ls_ref[b].astype(jnp.float32)).astype(jnp.bfloat16) for b in range(nbits)]
+    width = ls_ref.shape[1]
+    state_t = jnp.concatenate(
+        [jnp.transpose(ls_ref[b].astype(jnp.float32)).astype(jnp.bfloat16) for b in range(nbits)], axis=0
+    )
+    state = jnp.concatenate([ls_ref[b] for b in range(nbits)], axis=0)
     gg = [ggl_ref[lev : lev + 1, :] for lev in range(nlev)]
     cross_rows = [[] for _ in range(nbits)]
     for i in range(block_len // TILE):
@@ -174,10 +178,12 @@
         do_t = jnp.transpose(doi.astype(jnp.float32))
         attn_t = o_ref[:, ts]
         grad_q_t = dq_ref[:, ts]
+        out_all = dot_nt(state_t, qi)
+        back_all = dot_nt(state, doi)
         for b in range(nbits):
             weight = g_ref[first + b : first + b + 1, ts]
-            level_out_t = dot_nt(state_t[b], qi)
-            level_back_t = dot_nt(ls_ref[b], doi)
+            level_out_t = out_all[b * width : (b + 1) * width]
+            level_back_t = back_all[b * width : (b + 1) * width]
             attn_t = attn_t + weight * level_out_t
             grad_q_t = grad_q_t + weight * level_back_t
             dotted = jnp.sum(level_out_t * do_t, axis=0, keepdims=True)

time: 81.4 us -> 81.3 us (level)
  no operation moved by 1% of the time
where the time goes in v11:
time: 81.3 us; the launch traced here: 80.1 us
  Pallas kernels  44 us (54%)
  starting transfers between devices  11.9 us (15%)
  waiting for transfers between devices  9.17 us (11%)
  between operations  6.52 us (8%)
  other arithmetic  4.92 us (6%)
  local copies, waits for them, and re-layouts  3.54 us (4%)
    pallas_call x4, Pallas kernels, local_part(): pl.pallas_call(local_kernel, grid=(1,), in_specs=in_specs, out_specs=[col...  29.7 us
    pallas_call x1, Pallas kernels, final_part(): pl.pallas_call(final_kernel, grid=(heads,), in_specs=[row_spec] * 4 + [co...  8.95 us
    pallas_call x1, Pallas kernels, state_part(): pl.pallas_call(state_kernel, grid=(heads,), in_specs=[row_spec] * 4 + [ga...  5.31 us
    ppermute x2, waiting for transfers between devices, per_device(): lax.ppermute(fwd_x.astype(jnp.bfloat16), 'ctx', pairs_of(kf, ctx_len))  4.95 us
    ppermute x3, waiting for transfers between devices, per_device(): fwd_got = lax.ppermute(fwd_x, 'ctx', pairs_of(kf, ctx_len))  4.21 us
    ppermute x3, starting transfers between devices, per_device(): fwd_got = lax.ppermute(fwd_x, 'ctx', pairs_of(kf, ctx_len))  4.18 us
    ppermute x4, starting transfers between devices, per_device(): bwd_got = lax.ppermute(send, 'ctx', bwd_pairs)  3.94 us
    ppermute x1, starting transfers between devices, per_device(): lax.ppermute(send.astype(jnp.bfloat16), 'ctx', bwd_pairs)  2.33 us
  transfers between devices with their start and end apart: 10, of which 2 were waited for; matrix products, arithmetic and copies ran while one was open for 2% of the time, Pallas kernels for 37%

profile of v11, /device:TPU:4, one launch (start us, length us, event | category | flops | bytes accessed | tf_op | source)
XLA Modules:
  0.0 80.1 jit_solution(10726744678489875475)
XLA Ops:
  0.6 1.8 %fusion.9.g_ref = f32[4,16,1024]{2,1,0:T(8,128)} fusion(f32[16,4,1024]{2,1,0:T(4,128)} %param.10), kind=kLoop, calls=%fused_computation.18 | loop fusion | bytes 524288 | tf_op jit(solution)/shard_map/transpose | solution.py:260
  2.5 1.6 %fusion.22 = (s32[1,1]{1,0:T(1,128)}, s32[1,1]{1,0:T(1,128)}, s32[1,1]{1,0:T(1,128)}, s32[1,1]{1,0:T(1,128)}, s32[1,1]{1,0:T(1,128)}, /*index=5*/s32[1,1]{1,0:T(...) fusion(s32[32,32]{1,0:T(8,128)} %param.11, s32[]{:T(128)S(6)} %select_n.199, s32[]{:T(128)S(6)} %select_n.198, ...), kind=kLoop, calls=%fused_computation.40 | loop fusion | bytes 112 | tf_op jit(solution)/shard_map/dynamic_slice | solution.py:230
  4.7 5.3 %shard_map.101 = (f32[4,128,128]{2,1,0:T(8,128)}, f32[5,4,128,128]{3,2,1,0:T(8,128)}) custom-call(bf16[4,1024,128]{2,1,0:T(8,128)(2,1)} %q_ref.11, bf16[4,1024,128]{2,1,0:T(8,128)(2,1)} %k_ref.11, bf16[4,1024,128]{2,1,0:T(8,128)(2,1)} %v_ref.11, bf16[4,1024,128]{2,1,0:T(8,128)(2,1)} %do_ref.11, f32[4,16,1024]{2,1,0:T(8,128)} %fusion.9.g_ref), custom_call_target="tpu_custom_call" | custom-call | flops 805306368 | bytes 4456448 | tf_op jit(solution)/shard_map/pallas_call | solution.py:138
  10.0 1.0 %fusion.10 = bf16[4,128,128]{2,1,0:T(8,128)(2,1)S(1)} fusion(f32[5,4,128,128]{3,2,1,0:T(8,128)} %get-tuple-element.56, pred[]{:T(512)} %bitcast.4), kind=kLoop, calls=%fused_computation.29 | loop fusion | flops 65536 | bytes 262145 | tf_op jit(solution)/shard_map/convert_element_type | solution.py:289
  11.0 2.3 %collective-permute-start.1 = (bf16[4,128,128]{2,1,0:T(8,128)(2,1)S(1)}, bf16[4,128,128]{2,1,0:T(8,128)(2,1)S(1)}, u32[]{:S(2)}, u32[]{:S(2)}) collective-permute-start(bf16[4,128,128]{2,1,0:T(8,128)(2,1)S(1)} %fusion.10), channel_id=1, source_target_pairs={{0,128},{8,136},{16,144},{24,152},{32,160},{40,168},{48,176},{56,1... | collective-permute-start | bytes 393224 | tf_op jit(solution)/shard_map/ppermute | solution.py:289
  13.4 1.0 %convert_element_type.39 = bf16[4,128,128]{2,1,0:T(8,128)(2,1)S(1)} convert(f32[4,128,128]{2,1,0:T(8,128)} %get-tuple-element.55) | non-fusion elementwise | flops 65536 | bytes 393216 | tf_op jit(solution)/shard_map/convert_element_type | solution.py:273
  14.3 0.1 collective-permute-start
  19.3 0.0 copy-start
  19.3 0.0 copy-start.1
  19.3 7.5 %shard_map.102 = (f32[4,128,1024]{2,1,0:T(8,128)}, f32[4,128,1024]{2,1,0:T(8,128)}, f32[4,1024,128]{2,1,0:T(8,128)}, f32[4,1024,128]{2,1,0:T(8,128)}, f32[4,16,1024]{2,1,0:T(8,128)}) custom-call(bf16[4,1024,128]{2,1,0:T(8,128)(2,1)} %q_ref.11, bf16[4,1024,128]{2,1,0:T(8,128)(2,1)} %k_ref.11, bf16[4,1024,128]{2,1,0:T(8,128)(2,1)} %v_ref.11, ...), custom_call_target="tpu_custom_call" | custom-call | flops 1006632960 | bytes 3276800 | tf_op jit(solution)/shard_map/pallas_call | solution.py:104
  26.9 0.0 collective-permute-done.1
  26.9 0.0 collective-permute-done
  26.9 0.0 copy-done
  27.0 0.5 collective-permute-start.3
  27.5 0.0 copy-done.1
  27.5 1.7 %collective-permute-start.2 = (f32[4,128,128]{2,1,0:T(8,128)S(1)}, f32[4,128,128]{2,1,0:T(8,128)S(1)}, u32[]{:S(2)}, u32[]{:S(2)}) collective-permute-start(f32[4,128,128]{2,1,0:T(8,128)S(1)} %add_select_fusion.2), channel_id=1, source_target_pairs={{0,16},{8,24},{16,0},{24,8},{32,48},{40,56},{48,32},{56,40},{64,80... | collective-permute-start | bytes 786440 | tf_op jit(solution)/shard_map/ppermute | solution.py:277
  29.2 7.4 %shard_map.103 = (f32[4,128,1024]{2,1,0:T(8,128)}, f32[4,128,1024]{2,1,0:T(8,128)}, f32[4,1024,128]{2,1,0:T(8,128)}, f32[4,1024,128]{2,1,0:T(8,128)}, f32[4,16,1024]{2,1,0:T(8,128)}) custom-call(bf16[4,1024,128]{2,1,0:T(8,128)(2,1)} %q_ref.11, ...), custom_call_target="tpu_custom_call", output_to_operand_aliasing={{0}: (5, {}), {1}: (6, {}), {2}: (7, {}), {3}: (8, {}), {4}... | custom-call | flops 1006632960 | bytes 3276800 | tf_op jit(solution)/shard_map/pallas_call | solution.py:104
  36.6 0.0 collective-permute-done.3
  36.6 0.0 collective-permute-done.2
  36.6 0.8 fusion.2
  37.4 2.9 %collective-permute-start.5 = (f32[4,128,128]{2,1,0:T(8,128)}, f32[4,128,128]{2,1,0:T(8,128)S(1)}, u32[]{:S(2)}, u32[]{:S(2)}) collective-permute-start(f32[4,128,128]{2,1,0:T(8,128)} %fusion.2), channel_id=1, source_target_pairs={{0,32},{8,40},{16,48},{24,56},{32,0},{40,8},{48,16},{56,24},{64,96... | collective-permute-start | bytes 786440 | tf_op jit(solution)/shard_map/ppermute | solution.py:291
  40.3 0.9 %collective-permute-start.4 = (f32[4,128,128]{2,1,0:T(8,128)S(1)}, f32[4,128,128]{2,1,0:T(8,128)S(1)}, u32[]{:S(2)}, u32[]{:S(2)}) collective-permute-start(f32[4,128,128]{2,1,0:T(8,128)S(1)} %add_select_fusion.1), channel_id=1, source_target_pairs={{0,32},{8,40},{16,48},{24,56},{32,0},{40,8},{48,16},{56,24},{64,96... | collective-permute-start | bytes 786440 | tf_op jit(solution)/shard_map/ppermute | solution.py:277
  41.2 7.4 %shard_map.104 = (f32[4,128,1024]{2,1,0:T(8,128)}, f32[4,128,1024]{2,1,0:T(8,128)}, f32[4,1024,128]{2,1,0:T(8,128)}, f32[4,1024,128]{2,1,0:T(8,128)}, f32[4,16,1024]{2,1,0:T(8,128)}) custom-call(bf16[4,1024,128]{2,1,0:T(8,128)(2,1)} %q_ref.11, ...), custom_call_target="tpu_custom_call", output_to_operand_aliasing={{0}: (5, {}), {1}: (6, {}), {2}: (7, {}), {3}: (8, {}), {4}... | custom-call | flops 1006632960 | bytes 3276800 | tf_op jit(solution)/shard_map/pallas_call | solution.py:104
  48.6 0.0 collective-permute-done.5
  48.7 4.2 %collective-permute-done.4 = f32[4,128,128]{2,1,0:T(8,128)S(1)} collective-permute-done((f32[4,128,128]{2,1,0:T(8,128)S(1)}, f32[4,128,128]{2,1,0:T(8,128)S(1)}, u32[]{:S(2)}, u32[]{:S(2)}) %collective-permute-start.4) | collective-permute-done | bytes 262176 | tf_op jit(solution)/shard_map/ppermute | solution.py:277
  52.9 0.8 %fusion.1 = (f32[4,128,128]{2,1,0:T(8,128)}, f32[4,128,128]{2,1,0:T(8,128)S(1)}) fusion(f32[5,4,128,128]{3,2,1,0:T(8,128)S(1)} %copy-done, pred[]{:T(512)} %bitcast.19, pred[]{:T(512)} %bitcast.6, pred[]{:T(512)} %eq.21, f32[4,128,128]{2,1,0:T(8,128)S(1)} %collective-permute-done.5, pred[]{:T(512)} %bitcast.12, f32[4,128,128]{2,1,0:T(8,128)S(1)} %collective-permute-done.3, ...), kind=kLoop, calls=%fused_computation.5 | loop fusion | flops 655360 | bytes 1572871 | tf_op jit(solution)/shard_map/jit(_where)/select_n | solution.py:285
  53.7 0.5 collective-permute-start.7
  54.2 1.6 %collective-permute-start.6 = (f32[4,128,128]{2,1,0:T(8,128)S(1)}, f32[4,128,128]{2,1,0:T(8,128)S(1)}, u32[]{:S(2)}, u32[]{:S(2)}) collective-permute-start(f32[4,128,128]{2,1,0:T(8,128)S(1)} %add_select_fusion), channel_id=1, source_target_pairs={{0,64},{8,72},{16,80},{24,88},{32,96},{40,104},{48,112},{56,120},{... | collective-permute-start | bytes 786440 | tf_op jit(solution)/shard_map/ppermute | solution.py:277
  55.8 7.5 %shard_map.105 = (f32[4,128,1024]{2,1,0:T(8,128)}, f32[4,128,1024]{2,1,0:T(8,128)}, f32[4,1024,128]{2,1,0:T(8,128)}, f32[4,1024,128]{2,1,0:T(8,128)}, f32[4,16,1024]{2,1,0:T(8,128)}) custom-call(bf16[4,1024,128]{2,1,0:T(8,128)(2,1)} %q_ref.11, ...), custom_call_target="tpu_custom_call", output_to_operand_aliasing={{0}: (5, {}), {1}: (6, {}), {2}: (7, {}), {3}: (8, {}), {4}... | custom-call | flops 1006632960 | bytes 3276800 | tf_op jit(solution)/shard_map/pallas_call | solution.py:104
  63.3 0.0 collective-permute-done.7
  63.3 0.0 collective-permute-done.6
  63.3 0.1 select_convert_fusion.1
  63.4 1.4 %collective-permute-start.8 = (bf16[4,128,128]{2,1,0:T(8,128)(2,1)S(1)}, bf16[4,128,128]{2,1,0:T(8,128)(2,1)S(1)}, u32[]{:S(2)}, u32[]{:S(2)}) collective-permute-start(bf16[4,128,128]{2,1,0:T(8,128)(2,1)S(1)} %select_convert_fusion.1), channel_id=1, source_target_pairs={{0,128},{8,136},{16,144},{24,152},{32,160},{40,168},{48,176},{56,1... | collective-permute-start | bytes 393224 | tf_op jit(solution)/shard_map/ppermute | solution.py:272
  64.8 0.1 fusion
  64.8 0.1 collective-permute-start.9
  65.0 4.9 %collective-permute-done.8 = bf16[4,128,128]{2,1,0:T(8,128)(2,1)S(1)} collective-permute-done((bf16[4,128,128]{2,1,0:T(8,128)(2,1)S(1)}, bf16[4,128,128]{2,1,0:T(8,128)(2,1)S(1)}, u32[]{:S(2)}, u32[]{:S(2)}) %collective-permute-start.8) | collective-permute-done | bytes 131104 | tf_op jit(solution)/shard_map/ppermute | solution.py:272
  70.0 0.0 copy-start.2
  70.0 0.0 collective-permute-done.9
  70.0 0.9 %fusion.8.kst_ref = bf16[4,128,128]{2,1,0:T(8,128)(2,1)} fusion(f32[4,128,128]{2,1,0:T(8,128)S(1)} %collective-permute-done.9, pred[]{:T(512)} %bitcast.1, pred[]{:T(512)} %eq.22, f32[4,128,128]{2,1,0:T(8,128)S(1)} %collective-permute-done.7, f32[4,128,128]{2,1,0:T(8,128)S(1)} %get-tuple-element.106, pred[]{:T(512)} %bitcast.6, pred[]{:T(512)} %eq.21), kind=kLoop, calls=%fused_computation.16 | loop fusion | flops 458752 | bytes 917508 | tf_op jit(solution)/shard_map/convert_element_type | solution.py:305
  70.9 0.1 copy-done.2
  71.0 9.0 %shard_map.106 = (bf16[4,1024,128]{2,1,0:T(8,128)(2,1)}, bf16[4,1024,128]{2,1,0:T(8,128)(2,1)}, bf16[4,1024,128]{2,1,0:T(8,128)(2,1)}, bf16[4,1024,128]{2,1,0:T(8,128)(2,1)}, f32[16,4,1024]{2,1,0:T(4,128)}) custom-call(bf16[4,1024,128]{2,1,0:T(8,128)(2,1)} %q_ref.11, bf16[4,1024,128]{2,1,0:T(8,128)(2,1)} %k_ref.11, bf16[4,1024,128]{2,1,0:T(8,128)(2,1)} %v_ref.11, ...), custom_call_target="tpu_custom_call" | custom-call | flops 1610612736 | bytes 17825792 | tf_op jit(solution)/shard_map/pallas_call | solution.py:211
  (11 shorter events, 0.4 us)
Async XLA Ops:
  11.0 15.8 %collective-permute-start.1 = (bf16[4,128,128]{2,1,0:T(8,128)(2,1)S(1)}, bf16[4,128,128]{2,1,0:T(8,128)(2,1)S(1)}, u32[]{:S(2)}, u32[]{:S(2)}) collective-permute-start(bf16[4,128,128]{2,1,0:T(8,128)(2,1)S(1)} %fusion.10), channel_id=1, source_target_pairs={{0,128},{8,136},{16,144},{24,152},{32,160},{40,168},{48,176},{56,1... | collective-permute-start | bytes 393224 | tf_op jit(solution)/shard_map/ppermute | solution.py:289
  14.3 12.6 %collective-permute-start = (bf16[4,128,128]{2,1,0:T(8,128)(2,1)S(1)}, bf16[4,128,128]{2,1,0:T(8,128)(2,1)S(1)}, u32[]{:S(2)}, u32[]{:S(2)}) collective-permute-start(bf16[4,128,128]{2,1,0:T(8,128)(2,1)S(1)} %convert_element_type.39), channel_id=1, source_target_pairs={{0,8},{8,0},{16,24},{24,16},{32,40},{40,32},{48,56},{56,48},{64,72... | collective-permute-start | bytes 393224 | tf_op jit(solution)/shard_map/ppermute | solution.py:272
  19.3 7.6 %copy-start = (f32[5,4,128,128]{3,2,1,0:T(8,128)S(1)}, f32[5,4,128,128]{3,2,1,0:T(8,128)}, u32[]{:S(2)}) copy-start(f32[5,4,128,128]{3,2,1,0:T(8,128)} %get-tuple-element.56) | copy-start | bytes 3932164
  19.3 8.1 %copy-start.1 = (f32[4,128,128]{2,1,0:T(8,128)S(1)}, f32[4,128,128]{2,1,0:T(8,128)}, u32[]{:S(2)}) copy-start(f32[4,128,128]{2,1,0:T(8,128)} %get-tuple-element.55) | copy-start | bytes 786436
  27.0 9.6 %collective-permute-start.3 = (f32[4,128,128]{2,1,0:T(8,128)S(1)}, f32[4,128,128]{2,1,0:T(8,128)S(1)}, u32[]{:S(2)}, u32[]{:S(2)}) collective-permute-start(f32[4,128,128]{2,1,0:T(8,128)S(1)} %fusion.3), channel_id=1, source_target_pairs={{0,64},{8,72},{16,80},{24,88},{32,96},{40,104},{48,112},{56,120},{... | collective-permute-start | bytes 786440 | tf_op jit(solution)/shard_map/ppermute | solution.py:291
  27.5 9.1 %collective-permute-start.2 = (f32[4,128,128]{2,1,0:T(8,128)S(1)}, f32[4,128,128]{2,1,0:T(8,128)S(1)}, u32[]{:S(2)}, u32[]{:S(2)}) collective-permute-start(f32[4,128,128]{2,1,0:T(8,128)S(1)} %add_select_fusion.2), channel_id=1, source_target_pairs={{0,16},{8,24},{16,0},{24,8},{32,48},{40,56},{48,32},{56,40},{64,80... | collective-permute-start | bytes 786440 | tf_op jit(solution)/shard_map/ppermute | solution.py:277
  37.4 11.3 %collective-permute-start.5 = (f32[4,128,128]{2,1,0:T(8,128)}, f32[4,128,128]{2,1,0:T(8,128)S(1)}, u32[]{:S(2)}, u32[]{:S(2)}) collective-permute-start(f32[4,128,128]{2,1,0:T(8,128)} %fusion.2), channel_id=1, source_target_pairs={{0,32},{8,40},{16,48},{24,56},{32,0},{40,8},{48,16},{56,24},{64,96... | collective-permute-start | bytes 786440 | tf_op jit(solution)/shard_map/ppermute | solution.py:291
  40.3 12.5 %collective-permute-start.4 = (f32[4,128,128]{2,1,0:T(8,128)S(1)}, f32[4,128,128]{2,1,0:T(8,128)S(1)}, u32[]{:S(2)}, u32[]{:S(2)}) collective-permute-start(f32[4,128,128]{2,1,0:T(8,128)S(1)} %add_select_fusion.1), channel_id=1, source_target_pairs={{0,32},{8,40},{16,48},{24,56},{32,0},{40,8},{48,16},{56,24},{64,96... | collective-permute-start | bytes 786440 | tf_op jit(solution)/shard_map/ppermute | solution.py:277
  53.7 9.6 %collective-permute-start.7 = (f32[4,128,128]{2,1,0:T(8,128)}, f32[4,128,128]{2,1,0:T(8,128)S(1)}, u32[]{:S(2)}, u32[]{:S(2)}) collective-permute-start(f32[4,128,128]{2,1,0:T(8,128)} %get-tuple-element.105), channel_id=1, source_target_pairs={{0,16},{8,24},{16,0},{24,8},{32,48},{40,56},{48,32},{56,40},{64,80... | collective-permute-start | bytes 786440 | tf_op jit(solution)/shard_map/ppermute | solution.py:291
  54.2 9.1 %collective-permute-start.6 = (f32[4,128,128]{2,1,0:T(8,128)S(1)}, f32[4,128,128]{2,1,0:T(8,128)S(1)}, u32[]{:S(2)}, u32[]{:S(2)}) collective-permute-start(f32[4,128,128]{2,1,0:T(8,128)S(1)} %add_select_fusion), channel_id=1, source_target_pairs={{0,64},{8,72},{16,80},{24,88},{32,96},{40,104},{48,112},{56,120},{... | collective-permute-start | bytes 786440 | tf_op jit(solution)/shard_map/ppermute | solution.py:277
  63.4 6.6 %collective-permute-start.8 = (bf16[4,128,128]{2,1,0:T(8,128)(2,1)S(1)}, bf16[4,128,128]{2,1,0:T(8,128)(2,1)S(1)}, u32[]{:S(2)}, u32[]{:S(2)}) collective-permute-start(bf16[4,128,128]{2,1,0:T(8,128)(2,1)S(1)} %select_convert_fusion.1), channel_id=1, source_target_pairs={{0,128},{8,136},{16,144},{24,152},{32,160},{40,168},{48,176},{56,1... | collective-permute-start | bytes 393224 | tf_op jit(solution)/shard_map/ppermute | solution.py:272
  64.8 5.2 %collective-permute-start.9 = (f32[4,128,128]{2,1,0:T(8,128)S(1)}, f32[4,128,128]{2,1,0:T(8,128)S(1)}, u32[]{:S(2)}, u32[]{:S(2)}) collective-permute-start(f32[4,128,128]{2,1,0:T(8,128)S(1)} %fusion), channel_id=1, source_target_pairs={{0,8},{8,0},{16,24},{24,16},{32,40},{40,32},{48,56},{56,48},{64,72... | collective-permute-start | bytes 786440 | tf_op jit(solution)/shard_map/ppermute | solution.py:291
  70.0 1.0 %copy-start.2 = (bf16[5,4,128,128]{3,2,1,0:T(8,128)(2,1)}, bf16[5,4,128,128]{3,2,1,0:T(8,128)(2,1)S(1)}, u32[]{:S(2)}) copy-start(bf16[5,4,128,128]{3,2,1,0:T(8,128)(2,1)S(1)} %fusion.20.ls_ref) | copy-start | bytes 1966084

commit v12 on v11

--- a/solution.py
+++ b/solution.py
@@ -124,9 +124,13 @@
     st_ref[...] = dot_tn(k_ref[...], v_ref[...]).astype(jnp.bfloat16).astype(st_ref.dtype)
     do_t = jnp.transpose(do_ref[...].astype(jnp.float32))
     q = q_ref[...]
+    width = q.shape[1]
+    scaled_t = jnp.concatenate(
+        [(g_ref[first + b : first + b + 1, :] * do_t).astype(jnp.bfloat16) for b in range(nbits)], axis=0
+    )
+    states = dot_nn(scaled_t, q).astype(jnp.bfloat16).astype(gs_ref.dtype)
     for b in range(nbits):
-        scaled_t = (g_ref[first + b : first + b + 1, :] * do_t).astype(jnp.bfloat16)
-        gs_ref[b] = dot_nn(scaled_t, q).astype(jnp.bfloat16).astype(gs_ref.dtype)
+        gs_ref[b] = states[b * width : (b + 1) * width]
 
 
 def state_part(query_rows, key_rows, value_rows, out_grad, gate_t, nbits):

time: 81.3 us -> 81.3 us (level)
  no operation moved by 1% of the time
where the time goes in v12:
time: 81.3 us; the launch traced here: 80 us
  Pallas kernels  43.9 us (54%)
  starting transfers between devices  11.9 us (15%)
  waiting for transfers between devices  9.18 us (11%)
  between operations  6.52 us (8%)
  other arithmetic  4.92 us (6%)
  local copies, waits for them, and re-layouts  3.54 us (4%)
    pallas_call x4, Pallas kernels, local_part(): pl.pallas_call(local_kernel, grid=(1,), in_specs=in_specs, out_specs=[col...  29.7 us
    pallas_call x1, Pallas kernels, final_part(): pl.pallas_call(final_kernel, grid=(heads,), in_specs=[row_spec] * 4 + [co...  8.95 us
    pallas_call x1, Pallas kernels, state_part(): pl.pallas_call(state_kernel, grid=(heads,), in_specs=[row_spec] * 4 + [ga...  5.26 us
    ppermute x2, waiting for transfers between devices, per_device(): lax.ppermute(fwd_x.astype(jnp.bfloat16), 'ctx', pairs_of(kf, ctx_len))  4.96 us
    ppermute x3, waiting for transfers between devices, per_device(): fwd_got = lax.ppermute(fwd_x, 'ctx', pairs_of(kf, ctx_len))  4.21 us
    ppermute x3, starting transfers between devices, per_device(): fwd_got = lax.ppermute(fwd_x, 'ctx', pairs_of(kf, ctx_len))  4.18 us
    ppermute x4, starting transfers between devices, per_device(): bwd_got = lax.ppermute(send, 'ctx', bwd_pairs)  3.94 us
    ppermute x1, starting transfers between devices, per_device(): lax.ppermute(send.astype(jnp.bfloat16), 'ctx', bwd_pairs)  2.33 us
  transfers between devices with their start and end apart: 10, of which 2 were waited for; matrix products, arithmetic and copies ran while one was open for 2% of the time, Pallas kernels for 37%

profile of v12, /device:TPU:4, one launch (start us, length us, event | category | flops | bytes accessed | tf_op | source)
XLA Modules:
  0.0 80.0 jit_solution(17251014047832658253)
XLA Ops:
  0.6 1.8 %fusion.9.g_ref = f32[4,16,1024]{2,1,0:T(8,128)} fusion(f32[16,4,1024]{2,1,0:T(4,128)} %param.10), kind=kLoop, calls=%fused_computation.18 | loop fusion | bytes 524288 | tf_op jit(solution)/shard_map/transpose | solution.py:264
  2.5 1.6 %fusion.22 = (s32[1,1]{1,0:T(1,128)}, s32[1,1]{1,0:T(1,128)}, s32[1,1]{1,0:T(1,128)}, s32[1,1]{1,0:T(1,128)}, s32[1,1]{1,0:T(1,128)}, /*index=5*/s32[1,1]{1,0:T(...) fusion(s32[32,32]{1,0:T(8,128)} %param.11, s32[]{:T(128)S(6)} %select_n.199, s32[]{:T(128)S(6)} %select_n.198, ...), kind=kLoop, calls=%fused_computation.40 | loop fusion | bytes 112 | tf_op jit(solution)/shard_map/dynamic_slice | solution.py:234
  4.7 5.3 %shard_map.101 = (f32[4,128,128]{2,1,0:T(8,128)}, f32[5,4,128,128]{3,2,1,0:T(8,128)}) custom-call(bf16[4,1024,128]{2,1,0:T(8,128)(2,1)} %q_ref.11, bf16[4,1024,128]{2,1,0:T(8,128)(2,1)} %k_ref.11, bf16[4,1024,128]{2,1,0:T(8,128)(2,1)} %v_ref.11, bf16[4,1024,128]{2,1,0:T(8,128)(2,1)} %do_ref.11, f32[4,16,1024]{2,1,0:T(8,128)} %fusion.9.g_ref), custom_call_target="tpu_custom_call" | custom-call | flops 805306368 | bytes 4456448 | tf_op jit(solution)/shard_map/pallas_call | solution.py:142
  10.0 1.0 %fusion.10 = bf16[4,128,128]{2,1,0:T(8,128)(2,1)S(1)} fusion(f32[5,4,128,128]{3,2,1,0:T(8,128)} %get-tuple-element.56, pred[]{:T(512)} %bitcast.4), kind=kLoop, calls=%fused_computation.29 | loop fusion | flops 65536 | bytes 262145 | tf_op jit(solution)/shard_map/convert_element_type | solution.py:293
  11.0 2.3 %collective-permute-start.1 = (bf16[4,128,128]{2,1,0:T(8,128)(2,1)S(1)}, bf16[4,128,128]{2,1,0:T(8,128)(2,1)S(1)}, u32[]{:S(2)}, u32[]{:S(2)}) collective-permute-start(bf16[4,128,128]{2,1,0:T(8,128)(2,1)S(1)} %fusion.10), channel_id=1, source_target_pairs={{0,128},{8,136},{16,144},{24,152},{32,160},{40,168},{48,176},{56,1... | collective-permute-start | bytes 393224 | tf_op jit(solution)/shard_map/ppermute | solution.py:293
  13.3 1.0 %convert_element_type.39 = bf16[4,128,128]{2,1,0:T(8,128)(2,1)S(1)} convert(f32[4,128,128]{2,1,0:T(8,128)} %get-tuple-element.55) | non-fusion elementwise | flops 65536 | bytes 393216 | tf_op jit(solution)/shard_map/convert_element_type | solution.py:277
  14.3 0.1 collective-permute-start
  19.3 0.0 copy-start
  19.3 0.0 copy-start.1
  19.3 7.5 %shard_map.102 = (f32[4,128,1024]{2,1,0:T(8,128)}, f32[4,128,1024]{2,1,0:T(8,128)}, f32[4,1024,128]{2,1,0:T(8,128)}, f32[4,1024,128]{2,1,0:T(8,128)}, f32[4,16,1024]{2,1,0:T(8,128)}) custom-call(bf16[4,1024,128]{2,1,0:T(8,128)(2,1)} %q_ref.11, bf16[4,1024,128]{2,1,0:T(8,128)(2,1)} %k_ref.11, bf16[4,1024,128]{2,1,0:T(8,128)(2,1)} %v_ref.11, ...), custom_call_target="tpu_custom_call" | custom-call | flops 1006632960 | bytes 3276800 | tf_op jit(solution)/shard_map/pallas_call | solution.py:104
  26.8 0.0 collective-permute-done.1
  26.8 0.0 collective-permute-done
  26.9 0.0 copy-done
  26.9 0.5 collective-permute-start.3
  27.4 0.0 copy-done.1
  27.5 1.7 %collective-permute-start.2 = (f32[4,128,128]{2,1,0:T(8,128)S(1)}, f32[4,128,128]{2,1,0:T(8,128)S(1)}, u32[]{:S(2)}, u32[]{:S(2)}) collective-permute-start(f32[4,128,128]{2,1,0:T(8,128)S(1)} %add_select_fusion.2), channel_id=1, source_target_pairs={{0,16},{8,24},{16,0},{24,8},{32,48},{40,56},{48,32},{56,40},{64,80... | collective-permute-start | bytes 786440 | tf_op jit(solution)/shard_map/ppermute | solution.py:281
  29.1 7.4 %shard_map.103 = (f32[4,128,1024]{2,1,0:T(8,128)}, f32[4,128,1024]{2,1,0:T(8,128)}, f32[4,1024,128]{2,1,0:T(8,128)}, f32[4,1024,128]{2,1,0:T(8,128)}, f32[4,16,1024]{2,1,0:T(8,128)}) custom-call(bf16[4,1024,128]{2,1,0:T(8,128)(2,1)} %q_ref.11, ...), custom_call_target="tpu_custom_call", output_to_operand_aliasing={{0}: (5, {}), {1}: (6, {}), {2}: (7, {}), {3}: (8, {}), {4}... | custom-call | flops 1006632960 | bytes 3276800 | tf_op jit(solution)/shard_map/pallas_call | solution.py:104
  36.5 0.0 collective-permute-done.3
  36.5 0.0 collective-permute-done.2
  36.6 0.8 fusion.2
  37.3 2.9 %collective-permute-start.5 = (f32[4,128,128]{2,1,0:T(8,128)}, f32[4,128,128]{2,1,0:T(8,128)S(1)}, u32[]{:S(2)}, u32[]{:S(2)}) collective-permute-start(f32[4,128,128]{2,1,0:T(8,128)} %fusion.2), channel_id=1, source_target_pairs={{0,32},{8,40},{16,48},{24,56},{32,0},{40,8},{48,16},{56,24},{64,96... | collective-permute-start | bytes 786440 | tf_op jit(solution)/shard_map/ppermute | solution.py:295
  40.3 0.9 %collective-permute-start.4 = (f32[4,128,128]{2,1,0:T(8,128)S(1)}, f32[4,128,128]{2,1,0:T(8,128)S(1)}, u32[]{:S(2)}, u32[]{:S(2)}) collective-permute-start(f32[4,128,128]{2,1,0:T(8,128)S(1)} %add_select_fusion.1), channel_id=1, source_target_pairs={{0,32},{8,40},{16,48},{24,56},{32,0},{40,8},{48,16},{56,24},{64,96... | collective-permute-start | bytes 786440 | tf_op jit(solution)/shard_map/ppermute | solution.py:281
  41.2 7.4 %shard_map.104 = (f32[4,128,1024]{2,1,0:T(8,128)}, f32[4,128,1024]{2,1,0:T(8,128)}, f32[4,1024,128]{2,1,0:T(8,128)}, f32[4,1024,128]{2,1,0:T(8,128)}, f32[4,16,1024]{2,1,0:T(8,128)}) custom-call(bf16[4,1024,128]{2,1,0:T(8,128)(2,1)} %q_ref.11, ...), custom_call_target="tpu_custom_call", output_to_operand_aliasing={{0}: (5, {}), {1}: (6, {}), {2}: (7, {}), {3}: (8, {}), {4}... | custom-call | flops 1006632960 | bytes 3276800 | tf_op jit(solution)/shard_map/pallas_call | solution.py:104
  48.6 0.0 collective-permute-done.5
  48.6 4.2 %collective-permute-done.4 = f32[4,128,128]{2,1,0:T(8,128)S(1)} collective-permute-done((f32[4,128,128]{2,1,0:T(8,128)S(1)}, f32[4,128,128]{2,1,0:T(8,128)S(1)}, u32[]{:S(2)}, u32[]{:S(2)}) %collective-permute-start.4) | collective-permute-done | bytes 262176 | tf_op jit(solution)/shard_map/ppermute | solution.py:281
  52.9 0.8 %fusion.1 = (f32[4,128,128]{2,1,0:T(8,128)}, f32[4,128,128]{2,1,0:T(8,128)S(1)}) fusion(f32[5,4,128,128]{3,2,1,0:T(8,128)S(1)} %copy-done, pred[]{:T(512)} %bitcast.19, pred[]{:T(512)} %bitcast.6, pred[]{:T(512)} %eq.21, f32[4,128,128]{2,1,0:T(8,128)S(1)} %collective-permute-done.5, pred[]{:T(512)} %bitcast.12, f32[4,128,128]{2,1,0:T(8,128)S(1)} %collective-permute-done.3, ...), kind=kLoop, calls=%fused_computation.5 | loop fusion | flops 655360 | bytes 1572871 | tf_op jit(solution)/shard_map/jit(_where)/select_n | solution.py:289
  53.7 0.5 collective-permute-start.7
  54.1 1.6 %collective-permute-start.6 = (f32[4,128,128]{2,1,0:T(8,128)S(1)}, f32[4,128,128]{2,1,0:T(8,128)S(1)}, u32[]{:S(2)}, u32[]{:S(2)}) collective-permute-start(f32[4,128,128]{2,1,0:T(8,128)S(1)} %add_select_fusion), channel_id=1, source_target_pairs={{0,64},{8,72},{16,80},{24,88},{32,96},{40,104},{48,112},{56,120},{... | collective-permute-start | bytes 786440 | tf_op jit(solution)/shard_map/ppermute | solution.py:281
  55.8 7.5 %shard_map.105 = (f32[4,128,1024]{2,1,0:T(8,128)}, f32[4,128,1024]{2,1,0:T(8,128)}, f32[4,1024,128]{2,1,0:T(8,128)}, f32[4,1024,128]{2,1,0:T(8,128)}, f32[4,16,1024]{2,1,0:T(8,128)}) custom-call(bf16[4,1024,128]{2,1,0:T(8,128)(2,1)} %q_ref.11, ...), custom_call_target="tpu_custom_call", output_to_operand_aliasing={{0}: (5, {}), {1}: (6, {}), {2}: (7, {}), {3}: (8, {}), {4}... | custom-call | flops 1006632960 | bytes 3276800 | tf_op jit(solution)/shard_map/pallas_call | solution.py:104
  63.3 0.0 collective-permute-done.7
  63.3 0.0 collective-permute-done.6
  63.3 0.1 select_convert_fusion.1
  63.3 1.4 %collective-permute-start.8 = (bf16[4,128,128]{2,1,0:T(8,128)(2,1)S(1)}, bf16[4,128,128]{2,1,0:T(8,128)(2,1)S(1)}, u32[]{:S(2)}, u32[]{:S(2)}) collective-permute-start(bf16[4,128,128]{2,1,0:T(8,128)(2,1)S(1)} %select_convert_fusion.1), channel_id=1, source_target_pairs={{0,128},{8,136},{16,144},{24,152},{32,160},{40,168},{48,176},{56,1... | collective-permute-start | bytes 393224 | tf_op jit(solution)/shard_map/ppermute | solution.py:276
  64.7 0.1 fusion
  64.8 0.1 collective-permute-start.9
  64.9 5.0 %collective-permute-done.8 = bf16[4,128,128]{2,1,0:T(8,128)(2,1)S(1)} collective-permute-done((bf16[4,128,128]{2,1,0:T(8,128)(2,1)S(1)}, bf16[4,128,128]{2,1,0:T(8,128)(2,1)S(1)}, u32[]{:S(2)}, u32[]{:S(2)}) %collective-permute-start.8) | collective-permute-done | bytes 131104 | tf_op jit(solution)/shard_map/ppermute | solution.py:276
  69.9 0.0 copy-start.2
  70.0 0.0 collective-permute-done.9
  70.0 0.9 %fusion.8.kst_ref = bf16[4,128,128]{2,1,0:T(8,128)(2,1)} fusion(f32[4,128,128]{2,1,0:T(8,128)S(1)} %collective-permute-done.9, pred[]{:T(512)} %bitcast.1, pred[]{:T(512)} %eq.22, f32[4,128,128]{2,1,0:T(8,128)S(1)} %collective-permute-done.7, f32[4,128,128]{2,1,0:T(8,128)S(1)} %get-tuple-element.106, pred[]{:T(512)} %bitcast.6, pred[]{:T(512)} %eq.21), kind=kLoop, calls=%fused_computation.16 | loop fusion | flops 458752 | bytes 917508 | tf_op jit(solution)/shard_map/convert_element_type | solution.py:309
  70.8 0.1 copy-done.2
  70.9 9.0 %shard_map.106 = (bf16[4,1024,128]{2,1,0:T(8,128)(2,1)}, bf16[4,1024,128]{2,1,0:T(8,128)(2,1)}, bf16[4,1024,128]{2,1,0:T(8,128)(2,1)}, bf16[4,1024,128]{2,1,0:T(8,128)(2,1)}, f32[16,4,1024]{2,1,0:T(4,128)}) custom-call(bf16[4,1024,128]{2,1,0:T(8,128)(2,1)} %q_ref.11, bf16[4,1024,128]{2,1,0:T(8,128)(2,1)} %k_ref.11, bf16[4,1024,128]{2,1,0:T(8,128)(2,1)} %v_ref.11, ...), custom_call_target="tpu_custom_call" | custom-call | flops 1610612736 | bytes 17825792 | tf_op jit(solution)/shard_map/pallas_call | solution.py:215
  (11 shorter events, 0.4 us)
Async XLA Ops:
  11.0 15.8 %collective-permute-start.1 = (bf16[4,128,128]{2,1,0:T(8,128)(2,1)S(1)}, bf16[4,128,128]{2,1,0:T(8,128)(2,1)S(1)}, u32[]{:S(2)}, u32[]{:S(2)}) collective-permute-start(bf16[4,128,128]{2,1,0:T(8,128)(2,1)S(1)} %fusion.10), channel_id=1, source_target_pairs={{0,128},{8,136},{16,144},{24,152},{32,160},{40,168},{48,176},{56,1... | collective-permute-start | bytes 393224 | tf_op jit(solution)/shard_map/ppermute | solution.py:293
  14.3 12.6 %collective-permute-start = (bf16[4,128,128]{2,1,0:T(8,128)(2,1)S(1)}, bf16[4,128,128]{2,1,0:T(8,128)(2,1)S(1)}, u32[]{:S(2)}, u32[]{:S(2)}) collective-permute-start(bf16[4,128,128]{2,1,0:T(8,128)(2,1)S(1)} %convert_element_type.39), channel_id=1, source_target_pairs={{0,8},{8,0},{16,24},{24,16},{32,40},{40,32},{48,56},{56,48},{64,72... | collective-permute-start | bytes 393224 | tf_op jit(solution)/shard_map/ppermute | solution.py:276
  19.3 7.6 %copy-start = (f32[5,4,128,128]{3,2,1,0:T(8,128)S(1)}, f32[5,4,128,128]{3,2,1,0:T(8,128)}, u32[]{:S(2)}) copy-start(f32[5,4,128,128]{3,2,1,0:T(8,128)} %get-tuple-element.56) | copy-start | bytes 3932164
  19.3 8.1 %copy-start.1 = (f32[4,128,128]{2,1,0:T(8,128)S(1)}, f32[4,128,128]{2,1,0:T(8,128)}, u32[]{:S(2)}) copy-start(f32[4,128,128]{2,1,0:T(8,128)} %get-tuple-element.55) | copy-start | bytes 786436
  26.9 9.6 %collective-permute-start.3 = (f32[4,128,128]{2,1,0:T(8,128)S(1)}, f32[4,128,128]{2,1,0:T(8,128)S(1)}, u32[]{:S(2)}, u32[]{:S(2)}) collective-permute-start(f32[4,128,128]{2,1,0:T(8,128)S(1)} %fusion.3), channel_id=1, source_target_pairs={{0,64},{8,72},{16,80},{24,88},{32,96},{40,104},{48,112},{56,120},{... | collective-permute-start | bytes 786440 | tf_op jit(solution)/shard_map/ppermute | solution.py:295
  27.5 9.1 %collective-permute-start.2 = (f32[4,128,128]{2,1,0:T(8,128)S(1)}, f32[4,128,128]{2,1,0:T(8,128)S(1)}, u32[]{:S(2)}, u32[]{:S(2)}) collective-permute-start(f32[4,128,128]{2,1,0:T(8,128)S(1)} %add_select_fusion.2), channel_id=1, source_target_pairs={{0,16},{8,24},{16,0},{24,8},{32,48},{40,56},{48,32},{56,40},{64,80... | collective-permute-start | bytes 786440 | tf_op jit(solution)/shard_map/ppermute | solution.py:281
  37.3 11.3 %collective-permute-start.5 = (f32[4,128,128]{2,1,0:T(8,128)}, f32[4,128,128]{2,1,0:T(8,128)S(1)}, u32[]{:S(2)}, u32[]{:S(2)}) collective-permute-start(f32[4,128,128]{2,1,0:T(8,128)} %fusion.2), channel_id=1, source_target_pairs={{0,32},{8,40},{16,48},{24,56},{32,0},{40,8},{48,16},{56,24},{64,96... | collective-permute-start | bytes 786440 | tf_op jit(solution)/shard_map/ppermute | solution.py:295
  40.3 12.5 %collective-permute-start.4 = (f32[4,128,128]{2,1,0:T(8,128)S(1)}, f32[4,128,128]{2,1,0:T(8,128)S(1)}, u32[]{:S(2)}, u32[]{:S(2)}) collective-permute-start(f32[4,128,128]{2,1,0:T(8,128)S(1)} %add_select_fusion.1), channel_id=1, source_target_pairs={{0,32},{8,40},{16,48},{24,56},{32,0},{40,8},{48,16},{56,24},{64,96... | collective-permute-start | bytes 786440 | tf_op jit(solution)/shard_map/ppermute | solution.py:281
  53.7 9.6 %collective-permute-start.7 = (f32[4,128,128]{2,1,0:T(8,128)}, f32[4,128,128]{2,1,0:T(8,128)S(1)}, u32[]{:S(2)}, u32[]{:S(2)}) collective-permute-start(f32[4,128,128]{2,1,0:T(8,128)} %get-tuple-element.105), channel_id=1, source_target_pairs={{0,16},{8,24},{16,0},{24,8},{32,48},{40,56},{48,32},{56,40},{64,80... | collective-permute-start | bytes 786440 | tf_op jit(solution)/shard_map/ppermute | solution.py:295
  54.1 9.1 %collective-permute-start.6 = (f32[4,128,128]{2,1,0:T(8,128)S(1)}, f32[4,128,128]{2,1,0:T(8,128)S(1)}, u32[]{:S(2)}, u32[]{:S(2)}) collective-permute-start(f32[4,128,128]{2,1,0:T(8,128)S(1)} %add_select_fusion), channel_id=1, source_target_pairs={{0,64},{8,72},{16,80},{24,88},{32,96},{40,104},{48,112},{56,120},{... | collective-permute-start | bytes 786440 | tf_op jit(solution)/shard_map/ppermute | solution.py:281
  63.3 6.6 %collective-permute-start.8 = (bf16[4,128,128]{2,1,0:T(8,128)(2,1)S(1)}, bf16[4,128,128]{2,1,0:T(8,128)(2,1)S(1)}, u32[]{:S(2)}, u32[]{:S(2)}) collective-permute-start(bf16[4,128,128]{2,1,0:T(8,128)(2,1)S(1)} %select_convert_fusion.1), channel_id=1, source_target_pairs={{0,128},{8,136},{16,144},{24,152},{32,160},{40,168},{48,176},{56,1... | collective-permute-start | bytes 393224 | tf_op jit(solution)/shard_map/ppermute | solution.py:276
  64.8 5.2 %collective-permute-start.9 = (f32[4,128,128]{2,1,0:T(8,128)S(1)}, f32[4,128,128]{2,1,0:T(8,128)S(1)}, u32[]{:S(2)}, u32[]{:S(2)}) collective-permute-start(f32[4,128,128]{2,1,0:T(8,128)S(1)} %fusion), channel_id=1, source_target_pairs={{0,8},{8,0},{16,24},{24,16},{32,40},{40,32},{48,56},{56,48},{64,72... | collective-permute-start | bytes 786440 | tf_op jit(solution)/shard_map/ppermute | solution.py:295
  69.9 1.0 %copy-start.2 = (bf16[5,4,128,128]{3,2,1,0:T(8,128)(2,1)}, bf16[5,4,128,128]{3,2,1,0:T(8,128)(2,1)S(1)}, u32[]{:S(2)}) copy-start(bf16[5,4,128,128]{3,2,1,0:T(8,128)(2,1)S(1)} %fusion.20.ls_ref) | copy-start | bytes 1966084

commit v13 on v11

--- a/solution.py
+++ b/solution.py
@@ -4,6 +4,11 @@
 from jax.experimental import pallas as pl
 from jax.experimental.pallas import tpu as pltpu
 from jax.sharding import PartitionSpec as P
+import functools
+
+
+def gate_rows(g_ref, h):
+    return jnp.concatenate([g_ref[lev, pl.ds(h, 1), :] for lev in range(g_ref.shape[0])], axis=0)
 
 
 TILE = 256
@@ -29,7 +34,8 @@
     return lax.dot_general(a, b, (((1,), (0,)), ((), ())), preferred_element_type=jnp.float32)
 
 
-def local_kernel(q_ref, k_ref, v_ref, do_ref, g_ref, *refs):
+def local_kernel(h, q_ref, k_ref, v_ref, do_ref, g_ref, *refs):
+    gate = gate_rows(g_ref, h)
     o_ref, dq_ref, dk_ref, dv_ref, gg_ref = refs[-5:]
     block_len = q_ref.shape[0]
     tiles = block_len // TILE
@@ -50,7 +56,7 @@
         doi = do_ref[ts, :]
         kj = k_ref[ss, :]
         vj = v_ref[ss, :]
-        gi = g_ref[:, ts]
+        gi = gate[:, t0 : t0 + size]
         scores = dot_nt(kj, qi)
         back = dot_nt(vj, doi)
         prod = scores * back
@@ -79,12 +85,12 @@
             for b in range(a):
                 pair(i * TILE + a * SUB, i * TILE + b * SUB, SUB, log_sub + (a ^ b).bit_length())
             pair(i * TILE + a * SUB, i * TILE + a * SUB, SUB, None)
-    gg_ref[...] = gg_ref[...] * g_ref[...]
+    gg_ref[...] = gg_ref[...] * gate
 
 
 def local_part(query_rows, key_rows, value_rows, out_grad, gate_t, h, outs):
     heads, block_len, width = query_rows.shape
-    nlev = gate_t.shape[1]
+    nlev = gate_t.shape[0]
     f32 = jnp.float32
     pairs = (block_len // TILE) * (block_len // TILE + 1) // 2
     flops = pairs * 6 * 2 * TILE * TILE * width
@@ -94,15 +100,16 @@
     row_spec = pl.BlockSpec((None, block_len, width), lambda i: (h, 0, 0))
     col_spec = pl.BlockSpec((None, width, block_len), lambda i: (h, 0, 0))
     gate_spec = pl.BlockSpec((None, nlev, block_len), lambda i: (h, 0, 0))
+    full_gate = pl.BlockSpec((nlev, heads, block_len), lambda i: (0, 0, 0))
     args = (query_rows, key_rows, value_rows, out_grad, gate_t)
-    in_specs = [row_spec] * 4 + [gate_spec]
+    in_specs = [row_spec] * 4 + [full_gate]
     aliases = {}
     if outs is not None:
         args = args + tuple(outs)
         in_specs = in_specs + [pl.BlockSpec(memory_space=pl.ANY)] * 5
         aliases = {5 + n: n for n in range(5)}
     return pl.pallas_call(
-        local_kernel,
+        functools.partial(local_kernel, h),
         grid=(1,),
         in_specs=in_specs,
         out_specs=[col_spec] * 2 + [row_spec] * 2 + [gate_spec],
@@ -119,21 +126,22 @@
 
 def state_kernel(q_ref, k_ref, v_ref, do_ref, g_ref, st_ref, gs_ref):
     nlev = g_ref.shape[0]
+    gate = gate_rows(g_ref, pl.program_id(0))
     nbits = gs_ref.shape[0]
     first = nlev - nbits
     st_ref[...] = dot_tn(k_ref[...], v_ref[...]).astype(jnp.bfloat16).astype(st_ref.dtype)
     do_t = jnp.transpose(do_ref[...].astype(jnp.float32))
     q = q_ref[...]
     for b in range(nbits):
-        scaled_t = (g_ref[first + b : first + b + 1, :] * do_t).astype(jnp.bfloat16)
+        scaled_t = (gate[first + b : first + b + 1, :] * do_t).astype(jnp.bfloat16)
         gs_ref[b] = dot_nn(scaled_t, q).astype(jnp.bfloat16).astype(gs_ref.dtype)
 
 
 def state_part(query_rows, key_rows, value_rows, out_grad, gate_t, nbits):
     heads, block_len, width = query_rows.shape
-    nlev = gate_t.shape[1]
+    nlev = gate_t.shape[0]
     row_spec = pl.BlockSpec((None, block_len, width), lambda h: (h, 0, 0))
-    gate_spec = pl.BlockSpec((None, nlev, block_len), lambda h: (h, 0, 0))
+    gate_spec = pl.BlockSpec((nlev, heads, block_len), lambda h: (0, 0, 0))
     bf = jnp.bfloat16
     return pl.pallas_call(
         state_kernel,
@@ -164,6 +172,7 @@
     first = nlev - nbits
     key_state_t = kst_ref[...]
     h = pl.program_id(0)
+    gate = gate_rows(g_ref, h)
     width = ls_ref.shape[1]
     state_t = jnp.concatenate(
         [jnp.transpose(ls_ref[b].astype(jnp.float32)).astype(jnp.bfloat16) for b in range(nbits)], axis=0
@@ -181,7 +190,7 @@
         out_all = dot_nt(state_t, qi)
         back_all = dot_nt(state, doi)
         for b in range(nbits):
-            weight = g_ref[first + b : first + b + 1, ts]
+            weight = gate[first + b : first + b + 1, i * TILE : (i + 1) * TILE]
             level_out_t = out_all[b * width : (b + 1) * width]
             level_back_t = back_all[b * width : (b + 1) * width]
             attn_t = attn_t + weight * level_out_t
@@ -200,8 +209,9 @@
 
 def final_part(query_rows, key_rows, value_rows, out_grad, partials, gate_t, level_state, key_state_t):
     heads, block_len, width = query_rows.shape
-    nlev = gate_t.shape[1]
+    nlev = gate_t.shape[0]
     nbits = level_state.shape[0]
+    full_gate = pl.BlockSpec((nlev, heads, block_len), lambda h: (0, 0, 0))
     row_spec = pl.BlockSpec((None, block_len, width), lambda h: (h, 0, 0))
     col_spec = pl.BlockSpec((None, width, block_len), lambda h: (h, 0, 0))
     gate_spec = pl.BlockSpec((None, nlev, block_len), lambda h: (h, 0, 0))
@@ -212,7 +222,7 @@
         final_kernel,
         grid=(heads,),
         in_specs=[row_spec] * 4 + [col_spec] * 2 + [row_spec] * 2
-        + [gate_spec, gate_spec, ls_spec, ks_spec],
+        + [gate_spec, full_gate, ls_spec, ks_spec],
         out_specs=[row_spec] * 4 + [pl.BlockSpec((nlev, heads, block_len), lambda h: (0, 0, 0))],
         out_shape=[jax.ShapeDtypeStruct((heads, block_len, width), bf)] * 4
         + [jax.ShapeDtypeStruct((nlev, heads, block_len), jnp.float32)],
@@ -257,7 +267,7 @@
     me = lax.axis_index("ctx")
     weights = jnp.exp(level_gate)
 
-    gate_t = weights.transpose(1, 0, 2)
+    gate_t = weights
     own_state, grad_state = state_part(query_rows, key_rows, value_rows, out_grad, gate_t, nbits)
     grad_wide = grad_state
     heads = query_rows.shape[0]

time: 81.3 us -> 81.7 us (level)
    transpose x1 -> x0, local copies, waits for them, and re-layouts: 1.84 us -> none  [per_device(): gate_t = weights.transpose(1, 0, 2)]
    exp x0 -> x1, local copies, waits for them, and re-layouts: none -> 1.73 us  [per_device(): weights = jnp.exp(level_gate)]
where the time goes in v13:
time: 81.7 us; the launch traced here: 80.4 us
  Pallas kernels  44.5 us (54%)
  starting transfers between devices  11.9 us (15%)
  waiting for transfers between devices  9.13 us (11%)
  between operations  6.52 us (8%)
  other arithmetic  4.92 us (6%)
  local copies, waits for them, and re-layouts  3.44 us (4%)
    pallas_call x4, Pallas kernels, local_part(): pl.pallas_call(functools.partial(local_kernel, h), grid=(1,), in_specs=in...  30 us
    pallas_call x1, Pallas kernels, final_part(): pl.pallas_call(final_kernel, grid=(heads,), in_specs=[row_spec] * 4 + [co...  8.99 us
    pallas_call x1, Pallas kernels, state_part(): pl.pallas_call(state_kernel, grid=(heads,), in_specs=[row_spec] * 4 + [ga...  5.55 us
    ppermute x2, waiting for transfers between devices, per_device(): lax.ppermute(fwd_x.astype(jnp.bfloat16), 'ctx', pairs_of(kf, ctx_len))  4.97 us
    ppermute x3, starting transfers between devices, per_device(): fwd_got = lax.ppermute(fwd_x, 'ctx', pairs_of(kf, ctx_len))  4.17 us
    ppermute x3, waiting for transfers between devices, per_device(): fwd_got = lax.ppermute(fwd_x, 'ctx', pairs_of(kf, ctx_len))  4.15 us
    ppermute x4, starting transfers between devices, per_device(): bwd_got = lax.ppermute(send, 'ctx', bwd_pairs)  3.94 us
    ppermute x1, starting transfers between devices, per_device(): lax.ppermute(send.astype(jnp.bfloat16), 'ctx', bwd_pairs)  2.33 us
  transfers between devices with their start and end apart: 10, of which 2 were waited for; matrix products, arithmetic and copies ran while one was open for 2% of the time, Pallas kernels for 37%

profile of v13, /device:TPU:4, one launch (start us, length us, event | category | flops | bytes accessed | tf_op | source)
XLA Modules:
  0.0 80.4 jit_solution(2099374049071425551)
XLA Ops:
  0.6 1.7 %exp.3.g_ref = f32[16,4,1024]{2,1,0:T(4,128)} exponential(f32[16,4,1024]{2,1,0:T(4,128)} %param.10) | non-fusion elementwise | bytes 524288 | tf_op jit(solution)/shard_map/exp | solution.py:268
  2.4 1.6 %fusion.21 = (s32[1,1]{1,0:T(1,128)}, s32[1,1]{1,0:T(1,128)}, s32[1,1]{1,0:T(1,128)}, s32[1,1]{1,0:T(1,128)}, s32[1,1]{1,0:T(1,128)}, /*index=5*/s32[1,1]{1,0:T(...) fusion(s32[32,32]{1,0:T(8,128)} %param.11, s32[]{:T(128)S(6)} %select_n.199, s32[]{:T(128)S(6)} %select_n.198, ...), kind=kLoop, calls=%fused_computation.38 | loop fusion | bytes 112 | tf_op jit(solution)/shard_map/dynamic_slice | solution.py:240
  4.6 5.6 %shard_map.101 = (f32[4,128,128]{2,1,0:T(8,128)}, f32[5,4,128,128]{3,2,1,0:T(8,128)}) custom-call(bf16[4,1024,128]{2,1,0:T(8,128)(2,1)} %q_ref.11, bf16[4,1024,128]{2,1,0:T(8,128)(2,1)} %k_ref.11, bf16[4,1024,128]{2,1,0:T(8,128)(2,1)} %v_ref.11, bf16[4,1024,128]{2,1,0:T(8,128)(2,1)} %do_ref.11, f32[16,4,1024]{2,1,0:T(4,128)} %exp.3.g_ref), custom_call_target="tpu_custom_call" | custom-call | flops 805306368 | bytes 4456448 | tf_op jit(solution)/shard_map/pallas_call | solution.py:146
  10.2 1.0 %fusion.9 = bf16[4,128,128]{2,1,0:T(8,128)(2,1)S(1)} fusion(f32[5,4,128,128]{3,2,1,0:T(8,128)} %get-tuple-element.56, pred[]{:T(512)} %bitcast.3), kind=kLoop, calls=%fused_computation.27 | loop fusion | flops 65536 | bytes 262145 | tf_op jit(solution)/shard_map/convert_element_type | solution.py:299
  11.2 2.3 %collective-permute-start.1 = (bf16[4,128,128]{2,1,0:T(8,128)(2,1)S(1)}, bf16[4,128,128]{2,1,0:T(8,128)(2,1)S(1)}, u32[]{:S(2)}, u32[]{:S(2)}) collective-permute-start(bf16[4,128,128]{2,1,0:T(8,128)(2,1)S(1)} %fusion.9), channel_id=1, source_target_pairs={{0,128},{8,136},{16,144},{24,152},{32,160},{40,168},{48,176},{56,1... | collective-permute-start | bytes 393224 | tf_op jit(solution)/shard_map/ppermute | solution.py:299
  13.5 1.0 %convert_element_type.39 = bf16[4,128,128]{2,1,0:T(8,128)(2,1)S(1)} convert(f32[4,128,128]{2,1,0:T(8,128)} %get-tuple-element.55) | non-fusion elementwise | flops 65536 | bytes 393216 | tf_op jit(solution)/shard_map/convert_element_type | solution.py:283
  14.5 0.1 collective-permute-start
  19.5 0.0 copy-start
  19.5 0.0 copy-start.1
  19.5 7.6 %shard_map.102 = (f32[4,128,1024]{2,1,0:T(8,128)}, f32[4,128,1024]{2,1,0:T(8,128)}, f32[4,1024,128]{2,1,0:T(8,128)}, f32[4,1024,128]{2,1,0:T(8,128)}, f32[4,16,1024]{2,1,0:T(8,128)}) custom-call(bf16[4,1024,128]{2,1,0:T(8,128)(2,1)} %q_ref.11, bf16[4,1024,128]{2,1,0:T(8,128)(2,1)} %k_ref.11, bf16[4,1024,128]{2,1,0:T(8,128)(2,1)} %v_ref.11, ...), custom_call_target="tpu_custom_call" | custom-call | flops 1006632960 | bytes 3276800 | tf_op jit(solution)/shard_map/pallas_call | solution.py:111
  27.1 0.0 collective-permute-done.1
  27.1 0.0 collective-permute-done
  27.1 0.0 copy-done
  27.2 0.5 collective-permute-start.3
  27.7 0.0 copy-done.1
  27.7 1.7 %collective-permute-start.2 = (f32[4,128,128]{2,1,0:T(8,128)S(1)}, f32[4,128,128]{2,1,0:T(8,128)S(1)}, u32[]{:S(2)}, u32[]{:S(2)}) collective-permute-start(f32[4,128,128]{2,1,0:T(8,128)S(1)} %add_select_fusion.2), channel_id=1, source_target_pairs={{0,16},{8,24},{16,0},{24,8},{32,48},{40,56},{48,32},{56,40},{64,80... | collective-permute-start | bytes 786440 | tf_op jit(solution)/shard_map/ppermute | solution.py:287
  29.4 7.4 %shard_map.103 = (f32[4,128,1024]{2,1,0:T(8,128)}, f32[4,128,1024]{2,1,0:T(8,128)}, f32[4,1024,128]{2,1,0:T(8,128)}, f32[4,1024,128]{2,1,0:T(8,128)}, f32[4,16,1024]{2,1,0:T(8,128)}) custom-call(bf16[4,1024,128]{2,1,0:T(8,128)(2,1)} %q_ref.11, ...), custom_call_target="tpu_custom_call", output_to_operand_aliasing={{0}: (5, {}), {1}: (6, {}), {2}: (7, {}), {3}: (8, {}), {4}... | custom-call | flops 1006632960 | bytes 3276800 | tf_op jit(solution)/shard_map/pallas_call | solution.py:111
  36.8 0.0 collective-permute-done.3
  36.9 0.0 collective-permute-done.2
  36.9 0.8 fusion.2
  37.6 2.9 %collective-permute-start.5 = (f32[4,128,128]{2,1,0:T(8,128)}, f32[4,128,128]{2,1,0:T(8,128)S(1)}, u32[]{:S(2)}, u32[]{:S(2)}) collective-permute-start(f32[4,128,128]{2,1,0:T(8,128)} %fusion.2), channel_id=1, source_target_pairs={{0,32},{8,40},{16,48},{24,56},{32,0},{40,8},{48,16},{56,24},{64,96... | collective-permute-start | bytes 786440 | tf_op jit(solution)/shard_map/ppermute | solution.py:301
  40.6 0.9 %collective-permute-start.4 = (f32[4,128,128]{2,1,0:T(8,128)S(1)}, f32[4,128,128]{2,1,0:T(8,128)S(1)}, u32[]{:S(2)}, u32[]{:S(2)}) collective-permute-start(f32[4,128,128]{2,1,0:T(8,128)S(1)} %add_select_fusion.1), channel_id=1, source_target_pairs={{0,32},{8,40},{16,48},{24,56},{32,0},{40,8},{48,16},{56,24},{64,96... | collective-permute-start | bytes 786440 | tf_op jit(solution)/shard_map/ppermute | solution.py:287
  41.5 7.4 %shard_map.104 = (f32[4,128,1024]{2,1,0:T(8,128)}, f32[4,128,1024]{2,1,0:T(8,128)}, f32[4,1024,128]{2,1,0:T(8,128)}, f32[4,1024,128]{2,1,0:T(8,128)}, f32[4,16,1024]{2,1,0:T(8,128)}) custom-call(bf16[4,1024,128]{2,1,0:T(8,128)(2,1)} %q_ref.11, ...), custom_call_target="tpu_custom_call", output_to_operand_aliasing={{0}: (5, {}), {1}: (6, {}), {2}: (7, {}), {3}: (8, {}), {4}... | custom-call | flops 1006632960 | bytes 3276800 | tf_op jit(solution)/shard_map/pallas_call | solution.py:111
  49.0 0.0 collective-permute-done.5
  49.0 4.1 %collective-permute-done.4 = f32[4,128,128]{2,1,0:T(8,128)S(1)} collective-permute-done((f32[4,128,128]{2,1,0:T(8,128)S(1)}, f32[4,128,128]{2,1,0:T(8,128)S(1)}, u32[]{:S(2)}, u32[]{:S(2)}) %collective-permute-start.4) | collective-permute-done | bytes 262176 | tf_op jit(solution)/shard_map/ppermute | solution.py:287
  53.2 0.8 fusion.1
  54.0 0.4 collective-permute-start.7
  54.4 1.6 %collective-permute-start.6 = (f32[4,128,128]{2,1,0:T(8,128)S(1)}, f32[4,128,128]{2,1,0:T(8,128)S(1)}, u32[]{:S(2)}, u32[]{:S(2)}) collective-permute-start(f32[4,128,128]{2,1,0:T(8,128)S(1)} %add_select_fusion), channel_id=1, source_target_pairs={{0,64},{8,72},{16,80},{24,88},{32,96},{40,104},{48,112},{56,120},{... | collective-permute-start | bytes 786440 | tf_op jit(solution)/shard_map/ppermute | solution.py:287
  56.1 7.5 %shard_map.105 = (f32[4,128,1024]{2,1,0:T(8,128)}, f32[4,128,1024]{2,1,0:T(8,128)}, f32[4,1024,128]{2,1,0:T(8,128)}, f32[4,1024,128]{2,1,0:T(8,128)}, f32[4,16,1024]{2,1,0:T(8,128)}) custom-call(bf16[4,1024,128]{2,1,0:T(8,128)(2,1)} %q_ref.11, ...), custom_call_target="tpu_custom_call", output_to_operand_aliasing={{0}: (5, {}), {1}: (6, {}), {2}: (7, {}), {3}: (8, {}), {4}... | custom-call | flops 1006632960 | bytes 3276800 | tf_op jit(solution)/shard_map/pallas_call | solution.py:111
  63.6 0.0 collective-permute-done.7
  63.6 0.0 collective-permute-done.6
  63.6 0.1 select_convert_fusion.1
  63.7 1.4 %collective-permute-start.8 = (bf16[4,128,128]{2,1,0:T(8,128)(2,1)S(1)}, bf16[4,128,128]{2,1,0:T(8,128)(2,1)S(1)}, u32[]{:S(2)}, u32[]{:S(2)}) collective-permute-start(bf16[4,128,128]{2,1,0:T(8,128)(2,1)S(1)} %select_convert_fusion.1), channel_id=1, source_target_pairs={{0,128},{8,136},{16,144},{24,152},{32,160},{40,168},{48,176},{56,1... | collective-permute-start | bytes 393224 | tf_op jit(solution)/shard_map/ppermute | solution.py:282
  65.1 0.1 fusion
  65.2 0.1 collective-permute-start.9
  65.3 5.0 %collective-permute-done.8 = bf16[4,128,128]{2,1,0:T(8,128)(2,1)S(1)} collective-permute-done((bf16[4,128,128]{2,1,0:T(8,128)(2,1)S(1)}, bf16[4,128,128]{2,1,0:T(8,128)(2,1)S(1)}, u32[]{:S(2)}, u32[]{:S(2)}) %collective-permute-start.8) | collective-permute-done | bytes 131104 | tf_op jit(solution)/shard_map/ppermute | solution.py:282
  70.3 0.0 copy-start.2
  70.3 0.0 collective-permute-done.9
  70.3 0.9 %fusion.8.kst_ref = bf16[4,128,128]{2,1,0:T(8,128)(2,1)} fusion(f32[4,128,128]{2,1,0:T(8,128)S(1)} %collective-permute-done.9, pred[]{:T(512)} %bitcast, pred[]{:T(512)} %eq.22, f32[4,128,128]{2,1,0:T(8,128)S(1)} %collective-permute-done.7, f32[4,128,128]{2,1,0:T(8,128)S(1)} %get-tuple-element.106, pred[]{:T(512)} %bitcast.5, pred[]{:T(512)} %eq.21), kind=kLoop, calls=%fused_computation.16 | loop fusion | flops 458752 | bytes 917508 | tf_op jit(solution)/shard_map/convert_element_type | solution.py:315
  71.2 0.1 copy-done.2
  71.3 9.0 %shard_map.106 = (bf16[4,1024,128]{2,1,0:T(8,128)(2,1)}, bf16[4,1024,128]{2,1,0:T(8,128)(2,1)}, bf16[4,1024,128]{2,1,0:T(8,128)(2,1)}, bf16[4,1024,128]{2,1,0:T(8,128)(2,1)}, f32[16,4,1024]{2,1,0:T(4,128)}) custom-call(bf16[4,1024,128]{2,1,0:T(8,128)(2,1)} %q_ref.11, bf16[4,1024,128]{2,1,0:T(8,128)(2,1)} %k_ref.11, bf16[4,1024,128]{2,1,0:T(8,128)(2,1)} %v_ref.11, ...), custom_call_target="tpu_custom_call" | custom-call | flops 1610612736 | bytes 17825792 | tf_op jit(solution)/shard_map/pallas_call | solution.py:221
  (11 shorter events, 0.4 us)
Async XLA Ops:
  11.2 15.9 %collective-permute-start.1 = (bf16[4,128,128]{2,1,0:T(8,128)(2,1)S(1)}, bf16[4,128,128]{2,1,0:T(8,128)(2,1)S(1)}, u32[]{:S(2)}, u32[]{:S(2)}) collective-permute-start(bf16[4,128,128]{2,1,0:T(8,128)(2,1)S(1)} %fusion.9), channel_id=1, source_target_pairs={{0,128},{8,136},{16,144},{24,152},{32,160},{40,168},{48,176},{56,1... | collective-permute-start | bytes 393224 | tf_op jit(solution)/shard_map/ppermute | solution.py:299
  14.5 12.6 %collective-permute-start = (bf16[4,128,128]{2,1,0:T(8,128)(2,1)S(1)}, bf16[4,128,128]{2,1,0:T(8,128)(2,1)S(1)}, u32[]{:S(2)}, u32[]{:S(2)}) collective-permute-start(bf16[4,128,128]{2,1,0:T(8,128)(2,1)S(1)} %convert_element_type.39), channel_id=1, source_target_pairs={{0,8},{8,0},{16,24},{24,16},{32,40},{40,32},{48,56},{56,48},{64,72... | collective-permute-start | bytes 393224 | tf_op jit(solution)/shard_map/ppermute | solution.py:282
  19.5 7.7 %copy-start = (f32[5,4,128,128]{3,2,1,0:T(8,128)S(1)}, f32[5,4,128,128]{3,2,1,0:T(8,128)}, u32[]{:S(2)}) copy-start(f32[5,4,128,128]{3,2,1,0:T(8,128)} %get-tuple-element.56) | copy-start | bytes 3932164
  19.5 8.2 %copy-start.1 = (f32[4,128,128]{2,1,0:T(8,128)S(1)}, f32[4,128,128]{2,1,0:T(8,128)}, u32[]{:S(2)}) copy-start(f32[4,128,128]{2,1,0:T(8,128)} %get-tuple-element.55) | copy-start | bytes 786436
  27.2 9.7 %collective-permute-start.3 = (f32[4,128,128]{2,1,0:T(8,128)S(1)}, f32[4,128,128]{2,1,0:T(8,128)S(1)}, u32[]{:S(2)}, u32[]{:S(2)}) collective-permute-start(f32[4,128,128]{2,1,0:T(8,128)S(1)} %fusion.3), channel_id=1, source_target_pairs={{0,64},{8,72},{16,80},{24,88},{32,96},{40,104},{48,112},{56,120},{... | collective-permute-start | bytes 786440 | tf_op jit(solution)/shard_map/ppermute | solution.py:301
  27.7 9.1 %collective-permute-start.2 = (f32[4,128,128]{2,1,0:T(8,128)S(1)}, f32[4,128,128]{2,1,0:T(8,128)S(1)}, u32[]{:S(2)}, u32[]{:S(2)}) collective-permute-start(f32[4,128,128]{2,1,0:T(8,128)S(1)} %add_select_fusion.2), channel_id=1, source_target_pairs={{0,16},{8,24},{16,0},{24,8},{32,48},{40,56},{48,32},{56,40},{64,80... | collective-permute-start | bytes 786440 | tf_op jit(solution)/shard_map/ppermute | solution.py:287
  37.6 11.3 %collective-permute-start.5 = (f32[4,128,128]{2,1,0:T(8,128)}, f32[4,128,128]{2,1,0:T(8,128)S(1)}, u32[]{:S(2)}, u32[]{:S(2)}) collective-permute-start(f32[4,128,128]{2,1,0:T(8,128)} %fusion.2), channel_id=1, source_target_pairs={{0,32},{8,40},{16,48},{24,56},{32,0},{40,8},{48,16},{56,24},{64,96... | collective-permute-start | bytes 786440 | tf_op jit(solution)/shard_map/ppermute | solution.py:301
  40.6 12.5 %collective-permute-start.4 = (f32[4,128,128]{2,1,0:T(8,128)S(1)}, f32[4,128,128]{2,1,0:T(8,128)S(1)}, u32[]{:S(2)}, u32[]{:S(2)}) collective-permute-start(f32[4,128,128]{2,1,0:T(8,128)S(1)} %add_select_fusion.1), channel_id=1, source_target_pairs={{0,32},{8,40},{16,48},{24,56},{32,0},{40,8},{48,16},{56,24},{64,96... | collective-permute-start | bytes 786440 | tf_op jit(solution)/shard_map/ppermute | solution.py:287
  54.0 9.6 %collective-permute-start.7 = (f32[4,128,128]{2,1,0:T(8,128)}, f32[4,128,128]{2,1,0:T(8,128)S(1)}, u32[]{:S(2)}, u32[]{:S(2)}) collective-permute-start(f32[4,128,128]{2,1,0:T(8,128)} %get-tuple-element.105), channel_id=1, source_target_pairs={{0,16},{8,24},{16,0},{24,8},{32,48},{40,56},{48,32},{56,40},{64,80... | collective-permute-start | bytes 786440 | tf_op jit(solution)/shard_map/ppermute | solution.py:301
  54.4 9.2 %collective-permute-start.6 = (f32[4,128,128]{2,1,0:T(8,128)S(1)}, f32[4,128,128]{2,1,0:T(8,128)S(1)}, u32[]{:S(2)}, u32[]{:S(2)}) collective-permute-start(f32[4,128,128]{2,1,0:T(8,128)S(1)} %add_select_fusion), channel_id=1, source_target_pairs={{0,64},{8,72},{16,80},{24,88},{32,96},{40,104},{48,112},{56,120},{... | collective-permute-start | bytes 786440 | tf_op jit(solution)/shard_map/ppermute | solution.py:287
  63.7 6.6 %collective-permute-start.8 = (bf16[4,128,128]{2,1,0:T(8,128)(2,1)S(1)}, bf16[4,128,128]{2,1,0:T(8,128)(2,1)S(1)}, u32[]{:S(2)}, u32[]{:S(2)}) collective-permute-start(bf16[4,128,128]{2,1,0:T(8,128)(2,1)S(1)} %select_convert_fusion.1), channel_id=1, source_target_pairs={{0,128},{8,136},{16,144},{24,152},{32,160},{40,168},{48,176},{56,1... | collective-permute-start | bytes 393224 | tf_op jit(solution)/shard_map/ppermute | solution.py:282
  65.2 5.2 %collective-permute-start.9 = (f32[4,128,128]{2,1,0:T(8,128)S(1)}, f32[4,128,128]{2,1,0:T(8,128)S(1)}, u32[]{:S(2)}, u32[]{:S(2)}) collective-permute-start(f32[4,128,128]{2,1,0:T(8,128)S(1)} %fusion), channel_id=1, source_target_pairs={{0,8},{8,0},{16,24},{24,16},{32,40},{40,32},{48,56},{56,48},{64,72... | collective-permute-start | bytes 786440 | tf_op jit(solution)/shard_map/ppermute | solution.py:301
  70.3 1.0 %copy-start.2 = (bf16[5,4,128,128]{3,2,1,0:T(8,128)(2,1)}, bf16[5,4,128,128]{3,2,1,0:T(8,128)(2,1)S(1)}, u32[]{:S(2)}) copy-start(bf16[5,4,128,128]{3,2,1,0:T(8,128)(2,1)S(1)} %fusion.19.ls_ref) | copy-start | bytes 1966084

commit v14 on v11

--- a/solution.py
+++ b/solution.py
@@ -8,6 +8,7 @@
 
 TILE = 256
 SUB = 128
+ROWS = 512
 
 
 def bit_length_small(numbers, count):
@@ -171,8 +172,8 @@
     state = jnp.concatenate([ls_ref[b] for b in range(nbits)], axis=0)
     gg = [ggl_ref[lev : lev + 1, :] for lev in range(nlev)]
     cross_rows = [[] for _ in range(nbits)]
-    for i in range(block_len // TILE):
-        ts = pl.ds(i * TILE, TILE)
+    for i in range(block_len // ROWS):
+        ts = pl.ds(i * ROWS, ROWS)
         qi = q_ref[ts, :]
         doi = do_ref[ts, :]
         do_t = jnp.transpose(doi.astype(jnp.float32))

time: 81.3 us -> 81.3 us (level)
  no operation moved by 1% of the time
where the time goes in v14:
time: 81.3 us; the launch traced here: 80.1 us
  Pallas kernels  44 us (54%)
  starting transfers between devices  11.9 us (15%)
  waiting for transfers between devices  9.17 us (11%)
  between operations  6.52 us (8%)
  other arithmetic  4.92 us (6%)
  local copies, waits for them, and re-layouts  3.54 us (4%)
    pallas_call x4, Pallas kernels, local_part(): pl.pallas_call(local_kernel, grid=(1,), in_specs=in_specs, out_specs=[col...  29.7 us
    pallas_call x1, Pallas kernels, final_part(): pl.pallas_call(final_kernel, grid=(heads,), in_specs=[row_spec] * 4 + [co...  8.95 us
    pallas_call x1, Pallas kernels, state_part(): pl.pallas_call(state_kernel, grid=(heads,), in_specs=[row_spec] * 4 + [ga...  5.31 us
    ppermute x2, waiting for transfers between devices, per_device(): lax.ppermute(fwd_x.astype(jnp.bfloat16), 'ctx', pairs_of(kf, ctx_len))  4.95 us
    ppermute x3, waiting for transfers between devices, per_device(): fwd_got = lax.ppermute(fwd_x, 'ctx', pairs_of(kf, ctx_len))  4.21 us
    ppermute x3, starting transfers between devices, per_device(): fwd_got = lax.ppermute(fwd_x, 'ctx', pairs_of(kf, ctx_len))  4.18 us
    ppermute x4, starting transfers between devices, per_device(): bwd_got = lax.ppermute(send, 'ctx', bwd_pairs)  3.94 us
    ppermute x1, starting transfers between devices, per_device(): lax.ppermute(send.astype(jnp.bfloat16), 'ctx', bwd_pairs)  2.33 us
  transfers between devices with their start and end apart: 10, of which 2 were waited for; matrix products, arithmetic and copies ran while one was open for 2% of the time, Pallas kernels for 37%

profile of v14, /device:TPU:4, one launch (start us, length us, event | category | flops | bytes accessed | tf_op | source)
XLA Modules:
  0.0 80.1 jit_solution(2890483450954415029)
XLA Ops:
  0.6 1.8 %fusion.9.g_ref = f32[4,16,1024]{2,1,0:T(8,128)} fusion(f32[16,4,1024]{2,1,0:T(4,128)} %param.10), kind=kLoop, calls=%fused_computation.18 | loop fusion | bytes 524288 | tf_op jit(solution)/shard_map/transpose | solution.py:261
  2.5 1.6 %fusion.22 = (s32[1,1]{1,0:T(1,128)}, s32[1,1]{1,0:T(1,128)}, s32[1,1]{1,0:T(1,128)}, s32[1,1]{1,0:T(1,128)}, s32[1,1]{1,0:T(1,128)}, /*index=5*/s32[1,1]{1,0:T(...) fusion(s32[32,32]{1,0:T(8,128)} %param.11, s32[]{:T(128)S(6)} %select_n.199, s32[]{:T(128)S(6)} %select_n.198, ...), kind=kLoop, calls=%fused_computation.40 | loop fusion | bytes 112 | tf_op jit(solution)/shard_map/dynamic_slice | solution.py:231
  4.7 5.3 %shard_map.101 = (f32[4,128,128]{2,1,0:T(8,128)}, f32[5,4,128,128]{3,2,1,0:T(8,128)}) custom-call(bf16[4,1024,128]{2,1,0:T(8,128)(2,1)} %q_ref.11, bf16[4,1024,128]{2,1,0:T(8,128)(2,1)} %k_ref.11, bf16[4,1024,128]{2,1,0:T(8,128)(2,1)} %v_ref.11, bf16[4,1024,128]{2,1,0:T(8,128)(2,1)} %do_ref.11, f32[4,16,1024]{2,1,0:T(8,128)} %fusion.9.g_ref), custom_call_target="tpu_custom_call" | custom-call | flops 805306368 | bytes 4456448 | tf_op jit(solution)/shard_map/pallas_call | solution.py:139
  10.0 1.0 %fusion.10 = bf16[4,128,128]{2,1,0:T(8,128)(2,1)S(1)} fusion(f32[5,4,128,128]{3,2,1,0:T(8,128)} %get-tuple-element.56, pred[]{:T(512)} %bitcast.4), kind=kLoop, calls=%fused_computation.29 | loop fusion | flops 65536 | bytes 262145 | tf_op jit(solution)/shard_map/convert_element_type | solution.py:290
  11.0 2.3 %collective-permute-start.1 = (bf16[4,128,128]{2,1,0:T(8,128)(2,1)S(1)}, bf16[4,128,128]{2,1,0:T(8,128)(2,1)S(1)}, u32[]{:S(2)}, u32[]{:S(2)}) collective-permute-start(bf16[4,128,128]{2,1,0:T(8,128)(2,1)S(1)} %fusion.10), channel_id=1, source_target_pairs={{0,128},{8,136},{16,144},{24,152},{32,160},{40,168},{48,176},{56,1... | collective-permute-start | bytes 393224 | tf_op jit(solution)/shard_map/ppermute | solution.py:290
  13.4 1.0 %convert_element_type.39 = bf16[4,128,128]{2,1,0:T(8,128)(2,1)S(1)} convert(f32[4,128,128]{2,1,0:T(8,128)} %get-tuple-element.55) | non-fusion elementwise | flops 65536 | bytes 393216 | tf_op jit(solution)/shard_map/convert_element_type | solution.py:274
  14.3 0.1 collective-permute-start
  19.3 0.0 copy-start
  19.3 0.0 copy-start.1
  19.3 7.5 %shard_map.102 = (f32[4,128,1024]{2,1,0:T(8,128)}, f32[4,128,1024]{2,1,0:T(8,128)}, f32[4,1024,128]{2,1,0:T(8,128)}, f32[4,1024,128]{2,1,0:T(8,128)}, f32[4,16,1024]{2,1,0:T(8,128)}) custom-call(bf16[4,1024,128]{2,1,0:T(8,128)(2,1)} %q_ref.11, bf16[4,1024,128]{2,1,0:T(8,128)(2,1)} %k_ref.11, bf16[4,1024,128]{2,1,0:T(8,128)(2,1)} %v_ref.11, ...), custom_call_target="tpu_custom_call" | custom-call | flops 1006632960 | bytes 3276800 | tf_op jit(solution)/shard_map/pallas_call | solution.py:105
  26.9 0.0 collective-permute-done.1
  26.9 0.0 collective-permute-done
  26.9 0.0 copy-done
  27.0 0.5 collective-permute-start.3
  27.5 0.0 copy-done.1
  27.5 1.7 %collective-permute-start.2 = (f32[4,128,128]{2,1,0:T(8,128)S(1)}, f32[4,128,128]{2,1,0:T(8,128)S(1)}, u32[]{:S(2)}, u32[]{:S(2)}) collective-permute-start(f32[4,128,128]{2,1,0:T(8,128)S(1)} %add_select_fusion.2), channel_id=1, source_target_pairs={{0,16},{8,24},{16,0},{24,8},{32,48},{40,56},{48,32},{56,40},{64,80... | collective-permute-start | bytes 786440 | tf_op jit(solution)/shard_map/ppermute | solution.py:278
  29.2 7.4 %shard_map.103 = (f32[4,128,1024]{2,1,0:T(8,128)}, f32[4,128,1024]{2,1,0:T(8,128)}, f32[4,1024,128]{2,1,0:T(8,128)}, f32[4,1024,128]{2,1,0:T(8,128)}, f32[4,16,1024]{2,1,0:T(8,128)}) custom-call(bf16[4,1024,128]{2,1,0:T(8,128)(2,1)} %q_ref.11, ...), custom_call_target="tpu_custom_call", output_to_operand_aliasing={{0}: (5, {}), {1}: (6, {}), {2}: (7, {}), {3}: (8, {}), {4}... | custom-call | flops 1006632960 | bytes 3276800 | tf_op jit(solution)/shard_map/pallas_call | solution.py:105
  36.6 0.0 collective-permute-done.3
  36.6 0.0 collective-permute-done.2
  36.6 0.8 fusion.2
  37.4 2.9 %collective-permute-start.5 = (f32[4,128,128]{2,1,0:T(8,128)}, f32[4,128,128]{2,1,0:T(8,128)S(1)}, u32[]{:S(2)}, u32[]{:S(2)}) collective-permute-start(f32[4,128,128]{2,1,0:T(8,128)} %fusion.2), channel_id=1, source_target_pairs={{0,32},{8,40},{16,48},{24,56},{32,0},{40,8},{48,16},{56,24},{64,96... | collective-permute-start | bytes 786440 | tf_op jit(solution)/shard_map/ppermute | solution.py:292
  40.3 0.9 %collective-permute-start.4 = (f32[4,128,128]{2,1,0:T(8,128)S(1)}, f32[4,128,128]{2,1,0:T(8,128)S(1)}, u32[]{:S(2)}, u32[]{:S(2)}) collective-permute-start(f32[4,128,128]{2,1,0:T(8,128)S(1)} %add_select_fusion.1), channel_id=1, source_target_pairs={{0,32},{8,40},{16,48},{24,56},{32,0},{40,8},{48,16},{56,24},{64,96... | collective-permute-start | bytes 786440 | tf_op jit(solution)/shard_map/ppermute | solution.py:278
  41.2 7.4 %shard_map.104 = (f32[4,128,1024]{2,1,0:T(8,128)}, f32[4,128,1024]{2,1,0:T(8,128)}, f32[4,1024,128]{2,1,0:T(8,128)}, f32[4,1024,128]{2,1,0:T(8,128)}, f32[4,16,1024]{2,1,0:T(8,128)}) custom-call(bf16[4,1024,128]{2,1,0:T(8,128)(2,1)} %q_ref.11, ...), custom_call_target="tpu_custom_call", output_to_operand_aliasing={{0}: (5, {}), {1}: (6, {}), {2}: (7, {}), {3}: (8, {}), {4}... | custom-call | flops 1006632960 | bytes 3276800 | tf_op jit(solution)/shard_map/pallas_call | solution.py:105
  48.6 0.0 collective-permute-done.5
  48.7 4.2 %collective-permute-done.4 = f32[4,128,128]{2,1,0:T(8,128)S(1)} collective-permute-done((f32[4,128,128]{2,1,0:T(8,128)S(1)}, f32[4,128,128]{2,1,0:T(8,128)S(1)}, u32[]{:S(2)}, u32[]{:S(2)}) %collective-permute-start.4) | collective-permute-done | bytes 262176 | tf_op jit(solution)/shard_map/ppermute | solution.py:278
  52.9 0.8 %fusion.1 = (f32[4,128,128]{2,1,0:T(8,128)}, f32[4,128,128]{2,1,0:T(8,128)S(1)}) fusion(f32[5,4,128,128]{3,2,1,0:T(8,128)S(1)} %copy-done, pred[]{:T(512)} %bitcast.19, pred[]{:T(512)} %bitcast.6, pred[]{:T(512)} %eq.21, f32[4,128,128]{2,1,0:T(8,128)S(1)} %collective-permute-done.5, pred[]{:T(512)} %bitcast.12, f32[4,128,128]{2,1,0:T(8,128)S(1)} %collective-permute-done.3, ...), kind=kLoop, calls=%fused_computation.5 | loop fusion | flops 655360 | bytes 1572871 | tf_op jit(solution)/shard_map/jit(_where)/select_n | solution.py:286
  53.7 0.5 collective-permute-start.7
  54.2 1.6 %collective-permute-start.6 = (f32[4,128,128]{2,1,0:T(8,128)S(1)}, f32[4,128,128]{2,1,0:T(8,128)S(1)}, u32[]{:S(2)}, u32[]{:S(2)}) collective-permute-start(f32[4,128,128]{2,1,0:T(8,128)S(1)} %add_select_fusion), channel_id=1, source_target_pairs={{0,64},{8,72},{16,80},{24,88},{32,96},{40,104},{48,112},{56,120},{... | collective-permute-start | bytes 786440 | tf_op jit(solution)/shard_map/ppermute | solution.py:278
  55.8 7.5 %shard_map.105 = (f32[4,128,1024]{2,1,0:T(8,128)}, f32[4,128,1024]{2,1,0:T(8,128)}, f32[4,1024,128]{2,1,0:T(8,128)}, f32[4,1024,128]{2,1,0:T(8,128)}, f32[4,16,1024]{2,1,0:T(8,128)}) custom-call(bf16[4,1024,128]{2,1,0:T(8,128)(2,1)} %q_ref.11, ...), custom_call_target="tpu_custom_call", output_to_operand_aliasing={{0}: (5, {}), {1}: (6, {}), {2}: (7, {}), {3}: (8, {}), {4}... | custom-call | flops 1006632960 | bytes 3276800 | tf_op jit(solution)/shard_map/pallas_call | solution.py:105
  63.3 0.0 collective-permute-done.7
  63.3 0.0 collective-permute-done.6
  63.3 0.1 select_convert_fusion.1
  63.4 1.4 %collective-permute-start.8 = (bf16[4,128,128]{2,1,0:T(8,128)(2,1)S(1)}, bf16[4,128,128]{2,1,0:T(8,128)(2,1)S(1)}, u32[]{:S(2)}, u32[]{:S(2)}) collective-permute-start(bf16[4,128,128]{2,1,0:T(8,128)(2,1)S(1)} %select_convert_fusion.1), channel_id=1, source_target_pairs={{0,128},{8,136},{16,144},{24,152},{32,160},{40,168},{48,176},{56,1... | collective-permute-start | bytes 393224 | tf_op jit(solution)/shard_map/ppermute | solution.py:273
  64.8 0.1 fusion
  64.8 0.1 collective-permute-start.9
  65.0 4.9 %collective-permute-done.8 = bf16[4,128,128]{2,1,0:T(8,128)(2,1)S(1)} collective-permute-done((bf16[4,128,128]{2,1,0:T(8,128)(2,1)S(1)}, bf16[4,128,128]{2,1,0:T(8,128)(2,1)S(1)}, u32[]{:S(2)}, u32[]{:S(2)}) %collective-permute-start.8) | collective-permute-done | bytes 131104 | tf_op jit(solution)/shard_map/ppermute | solution.py:273
  70.0 0.0 copy-start.2
  70.0 0.0 collective-permute-done.9
  70.0 0.9 %fusion.8.kst_ref = bf16[4,128,128]{2,1,0:T(8,128)(2,1)} fusion(f32[4,128,128]{2,1,0:T(8,128)S(1)} %collective-permute-done.9, pred[]{:T(512)} %bitcast.1, pred[]{:T(512)} %eq.22, f32[4,128,128]{2,1,0:T(8,128)S(1)} %collective-permute-done.7, f32[4,128,128]{2,1,0:T(8,128)S(1)} %get-tuple-element.106, pred[]{:T(512)} %bitcast.6, pred[]{:T(512)} %eq.21), kind=kLoop, calls=%fused_computation.16 | loop fusion | flops 458752 | bytes 917508 | tf_op jit(solution)/shard_map/convert_element_type | solution.py:306
  70.9 0.1 copy-done.2
  71.0 8.9 %shard_map.106 = (bf16[4,1024,128]{2,1,0:T(8,128)(2,1)}, bf16[4,1024,128]{2,1,0:T(8,128)(2,1)}, bf16[4,1024,128]{2,1,0:T(8,128)(2,1)}, bf16[4,1024,128]{2,1,0:T(8,128)(2,1)}, f32[16,4,1024]{2,1,0:T(4,128)}) custom-call(bf16[4,1024,128]{2,1,0:T(8,128)(2,1)} %q_ref.11, bf16[4,1024,128]{2,1,0:T(8,128)(2,1)} %k_ref.11, bf16[4,1024,128]{2,1,0:T(8,128)(2,1)} %v_ref.11, ...), custom_call_target="tpu_custom_call" | custom-call | flops 1610612736 | bytes 17825792 | tf_op jit(solution)/shard_map/pallas_call | solution.py:212
  (11 shorter events, 0.4 us)
Async XLA Ops:
  11.0 15.8 %collective-permute-start.1 = (bf16[4,128,128]{2,1,0:T(8,128)(2,1)S(1)}, bf16[4,128,128]{2,1,0:T(8,128)(2,1)S(1)}, u32[]{:S(2)}, u32[]{:S(2)}) collective-permute-start(bf16[4,128,128]{2,1,0:T(8,128)(2,1)S(1)} %fusion.10), channel_id=1, source_target_pairs={{0,128},{8,136},{16,144},{24,152},{32,160},{40,168},{48,176},{56,1... | collective-permute-start | bytes 393224 | tf_op jit(solution)/shard_map/ppermute | solution.py:290
  14.3 12.6 %collective-permute-start = (bf16[4,128,128]{2,1,0:T(8,128)(2,1)S(1)}, bf16[4,128,128]{2,1,0:T(8,128)(2,1)S(1)}, u32[]{:S(2)}, u32[]{:S(2)}) collective-permute-start(bf16[4,128,128]{2,1,0:T(8,128)(2,1)S(1)} %convert_element_type.39), channel_id=1, source_target_pairs={{0,8},{8,0},{16,24},{24,16},{32,40},{40,32},{48,56},{56,48},{64,72... | collective-permute-start | bytes 393224 | tf_op jit(solution)/shard_map/ppermute | solution.py:273
  19.3 7.6 %copy-start = (f32[5,4,128,128]{3,2,1,0:T(8,128)S(1)}, f32[5,4,128,128]{3,2,1,0:T(8,128)}, u32[]{:S(2)}) copy-start(f32[5,4,128,128]{3,2,1,0:T(8,128)} %get-tuple-element.56) | copy-start | bytes 3932164
  19.3 8.1 %copy-start.1 = (f32[4,128,128]{2,1,0:T(8,128)S(1)}, f32[4,128,128]{2,1,0:T(8,128)}, u32[]{:S(2)}) copy-start(f32[4,128,128]{2,1,0:T(8,128)} %get-tuple-element.55) | copy-start | bytes 786436
  27.0 9.6 %collective-permute-start.3 = (f32[4,128,128]{2,1,0:T(8,128)S(1)}, f32[4,128,128]{2,1,0:T(8,128)S(1)}, u32[]{:S(2)}, u32[]{:S(2)}) collective-permute-start(f32[4,128,128]{2,1,0:T(8,128)S(1)} %fusion.3), channel_id=1, source_target_pairs={{0,64},{8,72},{16,80},{24,88},{32,96},{40,104},{48,112},{56,120},{... | collective-permute-start | bytes 786440 | tf_op jit(solution)/shard_map/ppermute | solution.py:292
  27.5 9.1 %collective-permute-start.2 = (f32[4,128,128]{2,1,0:T(8,128)S(1)}, f32[4,128,128]{2,1,0:T(8,128)S(1)}, u32[]{:S(2)}, u32[]{:S(2)}) collective-permute-start(f32[4,128,128]{2,1,0:T(8,128)S(1)} %add_select_fusion.2), channel_id=1, source_target_pairs={{0,16},{8,24},{16,0},{24,8},{32,48},{40,56},{48,32},{56,40},{64,80... | collective-permute-start | bytes 786440 | tf_op jit(solution)/shard_map/ppermute | solution.py:278
  37.4 11.3 %collective-permute-start.5 = (f32[4,128,128]{2,1,0:T(8,128)}, f32[4,128,128]{2,1,0:T(8,128)S(1)}, u32[]{:S(2)}, u32[]{:S(2)}) collective-permute-start(f32[4,128,128]{2,1,0:T(8,128)} %fusion.2), channel_id=1, source_target_pairs={{0,32},{8,40},{16,48},{24,56},{32,0},{40,8},{48,16},{56,24},{64,96... | collective-permute-start | bytes 786440 | tf_op jit(solution)/shard_map/ppermute | solution.py:292
  40.3 12.5 %collective-permute-start.4 = (f32[4,128,128]{2,1,0:T(8,128)S(1)}, f32[4,128,128]{2,1,0:T(8,128)S(1)}, u32[]{:S(2)}, u32[]{:S(2)}) collective-permute-start(f32[4,128,128]{2,1,0:T(8,128)S(1)} %add_select_fusion.1), channel_id=1, source_target_pairs={{0,32},{8,40},{16,48},{24,56},{32,0},{40,8},{48,16},{56,24},{64,96... | collective-permute-start | bytes 786440 | tf_op jit(solution)/shard_map/ppermute | solution.py:278
  53.7 9.6 %collective-permute-start.7 = (f32[4,128,128]{2,1,0:T(8,128)}, f32[4,128,128]{2,1,0:T(8,128)S(1)}, u32[]{:S(2)}, u32[]{:S(2)}) collective-permute-start(f32[4,128,128]{2,1,0:T(8,128)} %get-tuple-element.105), channel_id=1, source_target_pairs={{0,16},{8,24},{16,0},{24,8},{32,48},{40,56},{48,32},{56,40},{64,80... | collective-permute-start | bytes 786440 | tf_op jit(solution)/shard_map/ppermute | solution.py:292
  54.2 9.1 %collective-permute-start.6 = (f32[4,128,128]{2,1,0:T(8,128)S(1)}, f32[4,128,128]{2,1,0:T(8,128)S(1)}, u32[]{:S(2)}, u32[]{:S(2)}) collective-permute-start(f32[4,128,128]{2,1,0:T(8,128)S(1)} %add_select_fusion), channel_id=1, source_target_pairs={{0,64},{8,72},{16,80},{24,88},{32,96},{40,104},{48,112},{56,120},{... | collective-permute-start | bytes 786440 | tf_op jit(solution)/shard_map/ppermute | solution.py:278
  63.4 6.6 %collective-permute-start.8 = (bf16[4,128,128]{2,1,0:T(8,128)(2,1)S(1)}, bf16[4,128,128]{2,1,0:T(8,128)(2,1)S(1)}, u32[]{:S(2)}, u32[]{:S(2)}) collective-permute-start(bf16[4,128,128]{2,1,0:T(8,128)(2,1)S(1)} %select_convert_fusion.1), channel_id=1, source_target_pairs={{0,128},{8,136},{16,144},{24,152},{32,160},{40,168},{48,176},{56,1... | collective-permute-start | bytes 393224 | tf_op jit(solution)/shard_map/ppermute | solution.py:273
  64.8 5.2 %collective-permute-start.9 = (f32[4,128,128]{2,1,0:T(8,128)S(1)}, f32[4,128,128]{2,1,0:T(8,128)S(1)}, u32[]{:S(2)}, u32[]{:S(2)}) collective-permute-start(f32[4,128,128]{2,1,0:T(8,128)S(1)} %fusion), channel_id=1, source_target_pairs={{0,8},{8,0},{16,24},{24,16},{32,40},{40,32},{48,56},{56,48},{64,72... | collective-permute-start | bytes 786440 | tf_op jit(solution)/shard_map/ppermute | solution.py:292
  70.0 1.0 %copy-start.2 = (bf16[5,4,128,128]{3,2,1,0:T(8,128)(2,1)}, bf16[5,4,128,128]{3,2,1,0:T(8,128)(2,1)S(1)}, u32[]{:S(2)}) copy-start(bf16[5,4,128,128]{3,2,1,0:T(8,128)(2,1)S(1)} %fusion.20.ls_ref) | copy-start | bytes 1966084
